TPU v7x, 32 devices: a whole 2x2x4 slice. The times are simulated.
32 devices in a mesh: seq: 4 (over z), tp: 4 (over y, x), dp: 2 (over core).
Axes of the slice: x: 2, y: 2, z: 4, core: 2. Of those that a mesh axis runs over, the one named last changes fastest.
Arguments:
- hidden_states: bfloat16 [2048, 7168], P(('dp', 'seq'), 'tp'), parts along dimension 0, may hold values from -120 to 120
- input_gain: float32 [7168], P('tp'), may hold values from 0.1 to 1.9
- query_down: bfloat16 [7168, 1536], P('tp', 'seq'), may hold values from -0.0625 to 0.0625
- memory_down: bfloat16 [7168, 576], P('tp', 'seq'), may hold values from -0.0625 to 0.0625
- query_gain: float32 [1536], replicated, may hold values from 0.1 to 1.9
- memory_gain: float32 [512], replicated, may hold values from 0.1 to 1.9
- query_up: bfloat16 [1536, 12288], P('seq', 'tp'), may hold values from -16 to 16
- key_up: bfloat16 [512, 8192], P('seq', 'tp'), may hold values from -0.25 to 0.25
- value_up: bfloat16 [512, 8192], P('seq', 'tp'), may hold values from -0.25 to 0.25
- segment_ids: int32 [2048], P(('dp', 'seq')), parts along dimension 0, may hold values from 0 to 11, never falling along the last dimension, each value on 1 to 256 neighbouring positions
Outputs:
- attended: bfloat16 [2048, 8192], P(('dp', 'seq'), 'tp'), parts along dimension 0
There are 2 independent parts, one for each index of `dp`. A program takes and returns all parts, laid end to end along the dimension named above; an argument that names none is the same for every part. Nothing has to cross between parts.
Inputs may be any that keep to these rules, and one draw needn't show every extreme that they name: `segment_ids`: ids never fall along the group; each of the 12 documents has 1 to 256 tokens and one has exactly 256.
All inputs are finite; a program needn't handle non-finite values.
Results may differ from a plain program's by a relative error of at most 0.0065.
The roundings to bfloat16 on the way count: a program that leaves them out, or rounds other values in their place, can miss the bound.
Values may be sent and summed in bfloat16 or wider, within the bound.
No kernel may reach another device: no remote copies, remote signals or barrier semaphores. Data moves between devices by JAX's collectives and lax.ppermute only.
A program may use at most 128 MiB of HBM per device.

v0:
```python
import jax
import jax.numpy as jnp
from jax import lax
from jax.sharding import PartitionSpec as P

D = 7168
KVRANK = 512
NOPE = 128
ROPE = 64
VDIM = 128
DOCS = 12


epsilon = 1e-06


def rms_scale(entries, gain_vector):
    return (
        entries * lax.rsqrt(jnp.mean(entries * entries, -1, keepdims=True) + epsilon) * gain_vector
    )


def rotate(entries, position):
    half_width = entries.shape[-1] // 2
    frequency = jnp.power(10000.0, -2.0 * jnp.arange(half_width, dtype=jnp.float32) / ROPE)
    angles = position.astype(jnp.float32)[..., None] * frequency
    cosine = jnp.cos(angles)
    sine_part = jnp.sin(angles)
    first_half = entries[..., :half_width]
    second_half = entries[..., half_width:]
    return jnp.concatenate(
        [
            first_half * cosine - second_half * sine_part,
            second_half * cosine + first_half * sine_part,
        ],
        -1,
    )


def compress(query_sums, memory_sums, query_gain, memory_gain, position):
    compressed_query = rms_scale(query_sums, query_gain).astype(jnp.bfloat16)
    compressed_memory = rms_scale(memory_sums[:, :KVRANK], memory_gain).astype(jnp.bfloat16)
    key_rope = rotate(memory_sums[:, KVRANK:], position).astype(jnp.bfloat16)
    return (compressed_query, compressed_memory, key_rope)


def expand(latent_rows, key_up, value_up):
    key_sums = jnp.dot(
        latent_rows,
        lax.all_gather(key_up, "seq", axis=0, tiled=True),
        preferred_element_type=jnp.float32,
    )
    value_sums = jnp.dot(
        latent_rows,
        lax.all_gather(value_up, "seq", axis=0, tiled=True),
        preferred_element_type=jnp.float32,
    )
    return (key_sums.astype(jnp.bfloat16), value_sums.astype(jnp.bfloat16))


def heads_attention(query_all, key_all, value_all, group_ids, score_scale, doc_most):
    total_rows = query_all.shape[0]
    block_rows = min(512, total_rows)
    key_index = jnp.arange(total_rows, dtype=jnp.int32)
    results = []
    for block in range(total_rows // block_rows):
        lower = block * block_rows
        upper = lower + block_rows
        key_low = max(0, lower - doc_most)
        scores = (
            jnp.einsum(
                "qhd,khd->hqk",
                query_all[lower:upper],
                key_all[key_low:upper],
                preferred_element_type=jnp.float32,
            )
            * score_scale
        )
        allowed = (group_ids[lower:upper, None] == group_ids[None, key_low:upper]) & (
            key_index[lower:upper, None] >= key_index[None, key_low:upper]
        )
        scores = jnp.where(allowed[None], scores, -jnp.inf)
        row_max = jnp.max(scores, -1, keepdims=True)
        probs_full = jnp.exp(scores - row_max)
        denominator = jnp.sum(probs_full, -1)
        weights = probs_full.astype(jnp.bfloat16)
        weighted = jnp.einsum(
            "hqk,khd->qhd", weights, value_all[key_low:upper], preferred_element_type=jnp.float32
        )
        results.append((weighted / jnp.transpose(denominator)[:, :, None]).astype(jnp.bfloat16))
    return jnp.concatenate(results, 0)


def body(
    hidden_states,
    input_gain,
    query_down,
    memory_down,
    query_gain,
    memory_gain,
    query_up,
    key_up,
    value_up,
    segment_ids,
):
    tok_count = hidden_states.shape[0]
    seq_count = lax.axis_size("seq")
    total_rows = tok_count * seq_count
    doc_most = total_rows // 4
    own_start = lax.axis_index("seq") * tok_count
    own_tokens = own_start + jnp.arange(tok_count, dtype=jnp.int32)
    onehot = segment_ids[:, None] == jnp.arange(DOCS, dtype=jnp.int32)[None, :]
    first_index = jnp.min(jnp.where(onehot, own_tokens[:, None], total_rows), 0)
    starts = lax.pmin(first_index, "seq")
    position = own_tokens - jnp.sum(jnp.where(onehot, starts[None, :], 0), 1)
    inputs = hidden_states.astype(jnp.float32)
    square_sums = lax.psum(jnp.sum(inputs * inputs, 1), "tp")
    normed = (inputs * lax.rsqrt(square_sums / D + epsilon)[:, None] * input_gain).astype(
        jnp.bfloat16
    )

    def project(weight_piece):
        return jnp.dot(normed, weight_piece, preferred_element_type=jnp.float32)

    query_latent = project(lax.all_gather(query_down, "seq", axis=1, tiled=True))
    memory_latent = project(lax.all_gather(memory_down, "seq", axis=1, tiled=True))
    query_sums, memory_sums = lax.psum((query_latent, memory_latent), "tp")
    compressed_query, compressed_memory, key_rope = compress(
        query_sums, memory_sums, query_gain, memory_gain, position
    )
    query_sums_up = jnp.dot(
        compressed_query,
        lax.all_gather(query_up, "seq", axis=0, tiled=True),
        preferred_element_type=jnp.float32,
    )
    local_heads = query_up.shape[1] // (NOPE + ROPE)
    query_full = query_sums_up.reshape(tok_count, local_heads, NOPE + ROPE)
    query = jnp.concatenate(
        [query_full[..., :NOPE], rotate(query_full[..., NOPE:], position[:, None])], -1
    ).astype(jnp.bfloat16)
    group_ids = lax.all_gather(segment_ids, "seq", axis=0, tiled=True)
    score_scale = (NOPE + ROPE) ** (-0.5)
    key_nope, value_rows = expand(compressed_memory, key_up, value_up)
    query_all, key_nope_all, value_all = (
        lax.all_to_all(query, "seq", split_axis=1, concat_axis=0, tiled=True),
        lax.all_to_all(
            key_nope.reshape(tok_count, local_heads, NOPE),
            "seq",
            split_axis=1,
            concat_axis=0,
            tiled=True,
        ),
        lax.all_to_all(
            value_rows.reshape(tok_count, local_heads, VDIM),
            "seq",
            split_axis=1,
            concat_axis=0,
            tiled=True,
        ),
    )
    rope_all = lax.all_gather(key_rope, "seq", axis=0, tiled=True)
    head_count = key_nope_all.shape[1]
    key_all = jnp.concatenate(
        [key_nope_all, jnp.broadcast_to(rope_all[:, None, :], (total_rows, head_count, ROPE))], -1
    )
    head_output = heads_attention(query_all, key_all, value_all, group_ids, score_scale, doc_most)
    attended = lax.all_to_all(head_output, "seq", split_axis=0, concat_axis=1, tiled=True)
    return attended.reshape(tok_count, local_heads * VDIM)


def solution(mesh):
    in_specs = (
        P(("dp", "seq"), "tp"),
        P("tp"),
        P("tp", "seq"),
        P("tp", "seq"),
        P(),
        P(),
        P("seq", "tp"),
        P("seq", "tp"),
        P("seq", "tp"),
        P(("dp", "seq")),
    )
    out_specs = P(("dp", "seq"), "tp")
    return jax.shard_map(body, mesh=mesh, in_specs=in_specs, out_specs=out_specs, check_vma=False)
```

profile of v0, /device:TPU:0, one launch (start us, length us, event | category | flops | bytes accessed | tf_op | source)
XLA Modules:
  0.0 653.9 jit_solution(14374351158190365708)
XLA Ops:
  8.3 11.4 %psum.21 = f32[256]{0:T(256)S(1)} all-reduce(f32[256]{0:T(256)S(1)} %fusion.15), channel_id=1, replica_groups=mesh['seq'=4,'tp'=4,'dp'=2] {'tp'}, use_global_device_ids=true, to_apply=%region_1.2 | all-reduce | flops 256 | bytes 2048 | tf_op jit(solution)/shard_map/psum | solution.py:117
  19.7 37.1 %all-gather.7.cloned.1.call-done = bf16[1792,576]{0,1:T(8,128)(2,1)} async-done(((bf16[1792,144]{0,1:T(8,128)(2,1)}), bf16[1792,576]{0,1:T(8,128)(2,1)}) %all-gather.7.cloned.1.call-update) | async-done | bytes 2064400 | tf_op jit(solution)/shard_map/all_gather | solution.py:126
  56.8 3.2 fusion.40
  60.0 99.6 %all-gather.11.cloned.1.call-done = bf16[1792,1536]{1,0:T(8,128)(2,1)} async-done(((bf16[1792,384]{1,0:T(8,128)(2,1)}), bf16[1792,1536]{1,0:T(8,128)(2,1)}) %all-gather.11.cloned.1.call-update) | async-done | bytes 5505040 | tf_op jit(solution)/shard_map/all_gather | solution.py:125
  159.6 5.4 fusion.38
  166.7 67.3 %all-reduce.3.cloned.1.call-done = (f32[256,576]{0,1:T(8,128)}, f32[256,1536]{1,0:T(8,128)}) async-done(((f32[256,576]{0,1:T(8,128)}, f32[256,1536]{1,0:T(8,128)}), (f32[256,576]{0,1:T(8,128)}, f32[256,1536]{1,0:T(8,128)})) %all-reduce.3.cloned.1.call-update) | async-done | bytes 2162704 | tf_op jit(solution)/shard_map/psum | solution.py:127
  235.2 46.0 %all-gather.15.cloned.1.call-done = bf16[512,2048]{1,0:T(8,128)(2,1)} async-done(((bf16[128,2048]{1,0:T(8,128)(2,1)}), bf16[512,2048]{1,0:T(8,128)(2,1)}) %all-gather.15.cloned.1.call-update) | async-done | bytes 2097168 | tf_op jit(solution)/shard_map/all_gather | solution.py:50
  281.1 2.6 fusion.19
  285.0 3.5 all-to-all-start.2
  288.7 52.7 %pmin.7 = s32[12]{0:T(128)S(1)} all-reduce(s32[12]{0:T(128)S(1)} %select_reduce_fusion.1), channel_id=1, replica_groups=mesh['seq'=4,'tp'=4,'dp'=2] {'seq'}, use_global_device_ids=true, to_apply=%region_7.8 | all-reduce | flops 12 | bytes 96 | tf_op jit(solution)/shard_map/pmin | solution.py:114
  341.5 7.2 %all-gather.9.cloned.1.call-done = bf16[512,2048]{1,0:T(8,128)(2,1)} async-done(((bf16[128,2048]{1,0:T(8,128)(2,1)}), bf16[512,2048]{1,0:T(8,128)(2,1)}) %all-gather.9.cloned.1.call-update) | async-done | bytes 2097168 | tf_op jit(solution)/shard_map/all_gather | solution.py:55
  348.7 2.4 fusion.18
  353.5 3.6 all-to-all-start
  357.3 178.3 %all-gather.13.cloned.1.call-done = bf16[1536,3072]{1,0:T(8,128)(2,1)} async-done(((bf16[384,3072]{1,0:T(8,128)(2,1)}), bf16[1536,3072]{1,0:T(8,128)(2,1)}) %all-gather.13.cloned.1.call-update) | async-done | bytes 9437200 | tf_op jit(solution)/shard_map/all_gather | solution.py:133
  535.6 6.5 fusion.32
  543.7 3.6 all-to-all-start.1
  547.3 31.8 %all-gather = s32[4,1,256]{2,1,0:T(1,128)S(1)} all-gather(s32[1,1,256]{2,1,0:T(1,128)S(1)} %bitcast.67), channel_id=1, replica_groups=mesh['seq'=4,'tp'=4,'dp'=2] {'seq'}, dimensions={0}, use_global_device_ids=true | all-gather | bytes 5120 | tf_op jit(solution)/shard_map/all_gather | solution.py:141
  581.2 20.5 %all_gather.27 = bf16[1024,64]{0,1:T(8,128)(2,1)S(1)} all-gather(bf16[256,64]{0,1:T(8,128)(2,1)S(1)} %pad_maximum_fusion.4), channel_id=1, replica_groups=mesh['seq'=4,'tp'=4,'dp'=2] {'seq'}, dimensions={0}, use_global_device_ids=true | all-gather | bytes 163840 | tf_op jit(solution)/shard_map/all_gather | solution.py:161
  602.6 1.7 copy.53
  613.3 1.7 fusion
  615.0 1.8 fusion.1
  616.8 2.4 divide_convert_fusion
  620.1 25.1 %all_to_all.63 = bf16[1024,4,128]{2,1,0:T(4,128)(2,1)S(1)} all-to-all(bf16[1024,4,128]{2,1,0:T(4,128)(2,1)S(1)} %copy.58), channel_id=1, replica_groups=mesh['seq'=4,'tp'=4,'dp'=2] {'seq'}, dimensions={0} | all-to-all | bytes 2097152 | tf_op jit(solution)/shard_map/all_to_all | solution.py:167
  645.5 1.6 reshape.246
  (83 shorter events, 23.4 us)
Async XLA Ops:
  6.5 1.5 copy-start.6
  6.5 50.2 %copy-start.10 = (f32[1792]{0:T(1024)S(1)}, f32[1792]{0:T(1024)}, u32[]{:S(2)}) copy-start(f32[1792]{0:T(1024)} %param.11) | copy-start | bytes 21508
  6.5 50.2 %all-gather.7.cloned.1.call-start = ((), (), s32[]{:S(2)}) async-start(), calls=%async_computation.4 | async-start | bytes 2580480 | tf_op jit(solution)/shard_map/all_gather | solution.py:126
  7.3 152.3 %all-gather.11.cloned.1.call-start = ((), (), s32[]{:S(2)}) async-start(), calls=%async_computation.6 | async-start | bytes 6881280 | tf_op jit(solution)/shard_map/all_gather | solution.py:125
  8.0 226.0 %all-reduce.3.cloned.1.call-start = ((), (), s32[]{:S(2)}) async-start(), calls=%async_computation.9 | async-start | bytes 4325376 | tf_op jit(solution)/shard_map/psum | solution.py:127
  165.0 116.2 %copy-start.8 = (f32[512]{0:T(512)S(1)}, f32[512]{0:T(512)}, u32[]{:S(2)}) copy-start(f32[512]{0:T(512)} %param.15) | copy-start | bytes 6148
  165.0 116.2 %all-gather.15.cloned.1.call-start = ((), (), s32[]{:S(2)}) async-start(), calls=%async_computation.8 | async-start | bytes 2621440 | tf_op jit(solution)/shard_map/all_gather | solution.py:50
  165.6 183.1 %all-gather.9.cloned.1.call-start = ((), (), s32[]{:S(2)}) async-start(), calls=%async_computation.5 | async-start | bytes 2621440 | tf_op jit(solution)/shard_map/all_gather | solution.py:55
  166.1 369.5 %all-gather.13.cloned.1.call-start = ((), (), s32[]{:S(2)}) async-start(), calls=%async_computation.7 | async-start | bytes 11796480 | tf_op jit(solution)/shard_map/all_gather | solution.py:133
  283.7 4.8 copy-start.9
  283.8 64.9 %copy-start = (f32[256,576]{0,1:T(8,128)S(1)}, f32[256,576]{0,1:T(8,128)}, u32[]{:S(2)}) copy-start(f32[256,576]{0,1:T(8,128)} %get-tuple-element.5) | copy-start | bytes 1769476
  285.0 67.5 %all-to-all-start.2 = ((bf16[256,16,128]{2,0,1:T(8,128)(2,1)}), bf16[256,16,128]{2,0,1:T(8,128)(2,1)S(1)}, u32[]{:S(2)}, u32[]{:S(2)}) async-start(bf16[256,16,128]{2,0,1:T(8,128)(2,1)} %bitcast.53), calls=%async_computation.2 | async-start | bytes 2097152 | tf_op jit(solution)/shard_map/all_to_all | solution.py:146
  341.5 10.8 %copy-start.3 = (f32[256,1536]{1,0:T(8,128)S(1)}, f32[256,1536]{1,0:T(8,128)}, u32[]{:S(2)}) copy-start(f32[256,1536]{1,0:T(8,128)} %get-tuple-element.6) | copy-start | bytes 4718596
  352.3 183.3 %copy-start.11 = (f32[1536]{0:T(1024)S(1)}, f32[1536]{0:T(1024)}, u32[]{:S(2)}) copy-start(f32[1536]{0:T(1024)} %param.14) | copy-start | bytes 18436
  352.5 1.0 copy-start.1
  353.5 190.2 %all-to-all-start = ((bf16[256,16,128]{2,0,1:T(8,128)(2,1)}), bf16[256,16,128]{2,0,1:T(8,128)(2,1)S(1)}, u32[]{:S(2)}, u32[]{:S(2)}) async-start(bf16[256,16,128]{2,0,1:T(8,128)(2,1)} %bitcast.54), calls=%async_computation | async-start | bytes 2097152 | tf_op jit(solution)/shard_map/all_to_all | solution.py:153
  543.7 64.7 %all-to-all-start.1 = ((bf16[256,16,192]{0,2,1:T(8,128)(2,1)}), bf16[256,16,192]{0,2,1:T(8,128)(2,1)S(1)}, u32[]{:S(2)}, u32[]{:S(2)}) async-start(bf16[256,16,192]{0,2,1:T(8,128)(2,1)} %pad_maximum_fusion), calls=%async_computation.1 | async-start | bytes 3145728 | tf_op jit(solution)/shard_map/all_to_all | solution.py:145
  608.6 1.0 copy-start.4
  608.6 1.3 copy-start.5
  610.9 1.0 copy-start.7
  611.9 1.4 copy-start.2
Sparse Core Ops, SparseCore 0:
  8.9 47.8 all-gather.6
  58.4 101.1 all-gather.10
  165.1 68.8 all-reduce.2
  235.5 45.6 all-gather.14
  282.6 66.0 all-gather.8
  350.1 185.4 all-gather.12
where the time goes:
time: 655 us; the launch traced here: 654 us
  waiting for transfers between devices  438 us (67%)
  blocking collectives  141 us (22%)
  matrix products  26.6 us (4%)
  local copies, waits for them, and re-layouts  14.5 us (2%)
  between operations  13.8 us (2%)
  starting transfers between devices  10.8 us (2%)
  other arithmetic  8.32 us (1%)
    all_gather x1, waiting for transfers between devices, body(): lax.all_gather(query_up, 'seq', axis=0, tiled=True)  178 us
    all_gather x1, waiting for transfers between devices, body(): lax.all_gather(query_down, 'seq', axis=1, tiled=True)  99.6 us
    psum x1, waiting for transfers between devices, body(): query_sums, memory_sums = lax.psum((query_latent, memory_latent), 'tp')  67.3 us
    pmin x1, blocking collectives, body(): starts = lax.pmin(first_index, 'seq')  52.7 us
    all_gather x1, waiting for transfers between devices, expand(): lax.all_gather(key_up, 'seq', axis=0, tiled=True)  46 us
    all_gather x1, waiting for transfers between devices, body(): lax.all_gather(memory_down, 'seq', axis=1, tiled=True)  37.1 us
    all_gather x1, blocking collectives, body(): group_ids = lax.all_gather(segment_ids, 'seq', axis=0, tiled=True)  31.8 us
    all_to_all x1, blocking collectives, body(): lax.all_to_all(head_output, 'seq', split_axis=0, concat_axis=1, tiled=True)  25.1 us
  transfers between devices with their start and end apart: 9, of which 6 were waited for; matrix products, arithmetic and copies ran while one was open for 4% of the time, Pallas kernels for 0%

commit v1 on v0

v1 whole, which is shorter than its diff:
```python
import jax
import jax.numpy as jnp
from jax import lax
from jax.sharding import PartitionSpec as P

KVRANK = 512
NOPE = 128
ROPE = 64
VDIM = 128
DOCS = 12


epsilon = 1e-06


def rms_scale(entries, gain_vector):
    return (
        entries * lax.rsqrt(jnp.mean(entries * entries, -1, keepdims=True) + epsilon) * gain_vector
    )


def rotate(entries, position):
    half_width = entries.shape[-1] // 2
    frequency = jnp.power(10000.0, -2.0 * jnp.arange(half_width, dtype=jnp.float32) / ROPE)
    angles = position.astype(jnp.float32)[..., None] * frequency
    cosine = jnp.cos(angles)
    sine_part = jnp.sin(angles)
    first_half = entries[..., :half_width]
    second_half = entries[..., half_width:]
    return jnp.concatenate(
        [
            first_half * cosine - second_half * sine_part,
            second_half * cosine + first_half * sine_part,
        ],
        -1,
    )


def heads_attention(query_all, key_all, value_all, group_ids, score_scale, doc_most):
    total_rows = query_all.shape[0]
    block_rows = min(512, total_rows)
    key_index = jnp.arange(total_rows, dtype=jnp.int32)
    results = []
    for block in range(total_rows // block_rows):
        lower = block * block_rows
        upper = lower + block_rows
        key_low = max(0, lower - doc_most)
        scores = (
            jnp.einsum(
                "qhd,khd->hqk",
                query_all[lower:upper],
                key_all[key_low:upper],
                preferred_element_type=jnp.float32,
            )
            * score_scale
        )
        allowed = (group_ids[lower:upper, None] == group_ids[None, key_low:upper]) & (
            key_index[lower:upper, None] >= key_index[None, key_low:upper]
        )
        scores = jnp.where(allowed[None], scores, -jnp.inf)
        row_max = jnp.max(scores, -1, keepdims=True)
        probs_full = jnp.exp(scores - row_max)
        denominator = jnp.sum(probs_full, -1)
        weights = probs_full.astype(jnp.bfloat16)
        weighted = jnp.einsum(
            "hqk,khd->qhd", weights, value_all[key_low:upper], preferred_element_type=jnp.float32
        )
        results.append((weighted / jnp.transpose(denominator)[:, :, None]).astype(jnp.bfloat16))
    return jnp.concatenate(results, 0)


def body(
    hidden_states,
    input_gain,
    query_down,
    memory_down,
    query_gain,
    memory_gain,
    query_up,
    key_up,
    value_up,
    segment_ids,
):
    tok_count = hidden_states.shape[0]
    seq_count = lax.axis_size("seq")
    tp_count = lax.axis_size("tp")
    seq_index = lax.axis_index("seq")
    tp_index = lax.axis_index("tp")
    width = hidden_states.shape[1] * tp_count
    total_rows = tok_count * seq_count
    doc_most = total_rows // 4
    qrank_piece = query_down.shape[1]
    memory_piece = memory_down.shape[1]
    qrank = qrank_piece * seq_count
    memory_cols = memory_piece * seq_count

    group_ids = lax.all_gather(segment_ids, "seq", axis=0, tiled=True)
    token_index = jnp.arange(total_rows, dtype=jnp.int32)
    onehot = group_ids[:, None] == jnp.arange(DOCS, dtype=jnp.int32)[None, :]
    starts = jnp.min(jnp.where(onehot, token_index[:, None], total_rows), 0)
    position = token_index - jnp.sum(jnp.where(onehot, starts[None, :], 0), 1)

    inputs = hidden_states.astype(jnp.float32)
    square_sums = lax.psum(jnp.sum(inputs * inputs, 1), "tp")
    normed = (inputs * lax.rsqrt(square_sums / width + epsilon)[:, None] * input_gain).astype(
        jnp.bfloat16
    )

    down_piece = jnp.concatenate([query_down, memory_down], 1)
    down_all = lax.all_gather(down_piece, "seq", axis=1, tiled=True)
    partial = jnp.dot(normed, down_all, preferred_element_type=jnp.float32)
    latent_rows = lax.psum_scatter(partial, "tp", scatter_dimension=0, tiled=True)
    chunk = latent_rows.shape[0]
    latent_rows = latent_rows.reshape(chunk, seq_count, qrank_piece + memory_piece)
    query_sums = latent_rows[:, :, :qrank_piece].reshape(chunk, qrank)
    memory_sums = latent_rows[:, :, qrank_piece:].reshape(chunk, memory_cols)
    chunk_position = lax.dynamic_slice(
        position, (seq_index * tok_count + tp_index * chunk,), (chunk,)
    )
    compressed_query = rms_scale(query_sums, query_gain).astype(jnp.bfloat16)
    compressed_memory = rms_scale(memory_sums[:, :KVRANK], memory_gain).astype(jnp.bfloat16)
    key_rope = rotate(memory_sums[:, KVRANK:], chunk_position).astype(jnp.bfloat16)
    packed = jnp.concatenate([compressed_query, compressed_memory, key_rope], 1)
    packed = lax.all_gather(packed, "seq", axis=0, tiled=False)
    packed = lax.all_gather(packed, "tp", axis=0, tiled=False)
    latent = jnp.transpose(packed, (1, 0, 2, 3)).reshape(total_rows, packed.shape[-1])
    cq_all = latent[:, :qrank]
    cm_all = latent[:, qrank : qrank + KVRANK]
    rope_all = latent[:, qrank + KVRANK :]

    local_heads = query_up.shape[1] // (NOPE + ROPE)
    heads = local_heads // seq_count
    query_w = lax.all_to_all(
        query_up.reshape(query_up.shape[0], seq_count, heads * (NOPE + ROPE)),
        "seq",
        split_axis=1,
        concat_axis=0,
        tiled=True,
    ).reshape(qrank, heads * (NOPE + ROPE))
    key_w = lax.all_to_all(
        key_up.reshape(key_up.shape[0], seq_count, heads * NOPE),
        "seq",
        split_axis=1,
        concat_axis=0,
        tiled=True,
    ).reshape(KVRANK, heads * NOPE)
    value_w = lax.all_to_all(
        value_up.reshape(value_up.shape[0], seq_count, heads * VDIM),
        "seq",
        split_axis=1,
        concat_axis=0,
        tiled=True,
    ).reshape(KVRANK, heads * VDIM)

    query_full = jnp.dot(cq_all, query_w, preferred_element_type=jnp.float32).reshape(
        total_rows, heads, NOPE + ROPE
    )
    query = jnp.concatenate(
        [query_full[..., :NOPE], rotate(query_full[..., NOPE:], position[:, None])], -1
    ).astype(jnp.bfloat16)
    key_nope = (
        jnp.dot(cm_all, key_w, preferred_element_type=jnp.float32)
        .astype(jnp.bfloat16)
        .reshape(total_rows, heads, NOPE)
    )
    value = (
        jnp.dot(cm_all, value_w, preferred_element_type=jnp.float32)
        .astype(jnp.bfloat16)
        .reshape(total_rows, heads, VDIM)
    )
    key_all = jnp.concatenate(
        [key_nope, jnp.broadcast_to(rope_all[:, None, :], (total_rows, heads, ROPE))], -1
    )
    score_scale = (NOPE + ROPE) ** (-0.5)
    head_output = heads_attention(query, key_all, value, group_ids, score_scale, doc_most)
    attended = lax.all_to_all(head_output, "seq", split_axis=0, concat_axis=1, tiled=True)
    return attended.reshape(tok_count, local_heads * VDIM)


def solution(mesh):
    in_specs = (
        P(("dp", "seq"), "tp"),
        P("tp"),
        P("tp", "seq"),
        P("tp", "seq"),
        P(),
        P(),
        P("seq", "tp"),
        P("seq", "tp"),
        P("seq", "tp"),
        P(("dp", "seq")),
    )
    out_specs = P(("dp", "seq"), "tp")
    return jax.shard_map(body, mesh=mesh, in_specs=in_specs, out_specs=out_specs, check_vma=False)
```

time: 655 us -> 380 us (0.58)
  waiting for transfers between devices: 438 us -> 251 us
  blocking collectives: 141 us -> 46.9 us
  local copies, waits for them, and re-layouts: 14.5 us -> 24.8 us
  matrix products: 26.6 us -> 18.2 us
    all_gather x5 -> x3, waiting for transfers between devices: 368 us -> 157 us  [the longest x1 127 us: body(): down_all = lax.all_gather(down_piece, 'seq', axis=1, tiled=True)]
    all_to_all x3, waiting for transfers between devices: 0.01 us -> 68.2 us  [the longest x1 46.6 us: body(): lax.all_to_all(query_up.reshape(query_up.shape[0], seq_count, heads * (NO...]
    psum x1 -> x0, waiting for transfers between devices: 67.3 us -> none  [body(): query_sums, memory_sums = lax.psum((query_latent, memory_latent), 'tp')]
    pmin x1 -> x0, blocking collectives: 52.7 us -> none  [body(): starts = lax.pmin(first_index, 'seq')]
    reduce_scatter x0 -> x1, waiting for transfers between devices: none -> 26.4 us  [body(): lax.psum_scatter(partial, 'tp', scatter_dimension=0, tiled=True)]
    all_gather x1, blocking collectives: 31.8 us -> 7.86 us  [body(): group_ids = lax.all_gather(segment_ids, 'seq', axis=0, tiled=True)]
    all_gather x1 -> x0, blocking collectives: 20.5 us -> none  [body(): rope_all = lax.all_gather(key_rope, 'seq', axis=0, tiled=True)]
    dot_general x5 -> x4, matrix products: 20.1 us -> 12.1 us  [the longest x1 6.93 us: body(): partial = jnp.dot(normed, down_all, preferred_element_type=jnp.float32)]
  transfers between devices with their start and end apart: 9 -> 7, of which waited for: 6 -> 6; matrix products, arithmetic and copies ran while one was open for 4% -> 5% of each run, Pallas kernels for 0% -> 0%
where the time goes in v1:
time: 380 us; the launch traced here: 379 us
  waiting for transfers between devices  251 us (66%)
  blocking collectives  46.9 us (12%)
  local copies, waits for them, and re-layouts  24.8 us (7%)
  matrix products  18.2 us (5%)
  between operations  13.6 us (4%)
  other arithmetic  13.2 us (3%)
  starting transfers between devices  10.9 us (3%)
    all_gather x1, waiting for transfers between devices, body(): down_all = lax.all_gather(down_piece, 'seq', axis=1, tiled=True)  127 us
    all_to_all x1, waiting for transfers between devices, body(): lax.all_to_all(query_up.reshape(query_up.shape[0], seq_count, heads * (NO...  46.6 us
    all_gather x1, waiting for transfers between devices, body(): packed = lax.all_gather(packed, 'seq', axis=0, tiled=False)  29.2 us
    all_to_all x1, blocking collectives, body(): lax.all_to_all(head_output, 'seq', split_axis=0, concat_axis=1, tiled=True)  27.7 us
    reduce_scatter x1, waiting for transfers between devices, body(): lax.psum_scatter(partial, 'tp', scatter_dimension=0, tiled=True)  26.4 us
    all_to_all x1, waiting for transfers between devices, body(): lax.all_to_all(key_up.reshape(key_up.shape[0], seq_count, heads * NOPE),...  13.3 us
    psum x1, blocking collectives, body(): square_sums = lax.psum(jnp.sum(inputs * inputs, 1), 'tp')  11.4 us
    unnamed x38, local copies, waits for them, and re-layouts  9.38 us
  transfers between devices with their start and end apart: 7, of which 6 were waited for; matrix products, arithmetic and copies ran while one was open for 5% of the time, Pallas kernels for 0%

profile of v1, /device:TPU:0, one launch (start us, length us, event | category | flops | bytes accessed | tf_op | source)
XLA Modules:
  0.0 378.8 jit_solution(2457869246093978417)
XLA Ops:
  6.5 1.8 copy.69
  8.4 2.6 pad_maximum_fusion
  11.3 11.4 %psum.7 = f32[256]{0:T(256)S(1)} all-reduce(f32[256]{0:T(256)S(1)} %fusion.16), channel_id=1, replica_groups=mesh['seq'=4,'tp'=4,'dp'=2] {'tp'}, use_global_device_ids=true, to_apply=%region_1.2 | all-reduce | flops 256 | bytes 2048 | tf_op jit(solution)/shard_map/psum | solution.py:104
  22.7 127.4 %all-gather.7.cloned.1.call-done = bf16[1792,2112]{0,1:T(8,128)(2,1)} async-done(((bf16[1792,528]{0,1:T(8,128)(2,1)}), bf16[1792,2112]{0,1:T(8,128)(2,1)}) %all-gather.7.cloned.1.call-update) | async-done | bytes 7569424 | tf_op jit(solution)/shard_map/all_gather | solution.py:110
  150.1 6.9 %fusion.33 = f32[256,2112]{1,0:T(8,128)} fusion(bf16[1792,2112]{0,1:T(8,128)(2,1)} %all-gather.7.cloned.1.call-done, bf16[256,1792]{1,0:T(8,128)(2,1)S(1)} %copy-done.5, f32[1792]{0:T(1024)S(1)} %copy-done.14, f32[256]{0:T(256)S(1)} %add_rsqrt_fusion), kind=kOutput, calls=%fused_computation.43 | convolution fusion | flops 1939603456 | bytes 10657792 | tf_op jit(solution)/shard_map/dot_general | solution.py:111
  157.1 7.9 %all-gather.2 = s32[4,1,256]{2,1,0:T(1,128)S(1)} all-gather(s32[1,1,256]{2,1,0:T(1,128)S(1)} %bitcast.83), channel_id=1, replica_groups=mesh['seq'=4,'tp'=4,'dp'=2] {'seq'}, dimensions={0}, use_global_device_ids=true | all-gather | bytes 5120 | tf_op jit(solution)/shard_map/all_gather | solution.py:97
  165.3 26.4 %reduce-scatter.2.cloned.1.call-done = f32[64,2112]{1,0:T(8,128)} async-done(((f32[256,2112]{1,0:T(8,128)}), f32[64,2112]{1,0:T(8,128)}) %reduce-scatter.2.cloned.1.call-update) | async-done | bytes 540688 | tf_op jit(solution)/shard_map/reduce_scatter | solution.py:112
  195.7 29.2 %all-gather.9.cloned.1.call-done = bf16[256,2112]{1,0:T(8,128)(2,1)} async-done(((bf16[64,2112]{1,0:T(8,128)(2,1)}), bf16[256,2112]{1,0:T(8,128)(2,1)}) %all-gather.9.cloned.1.call-update) | async-done | bytes 1081360 | tf_op jit(solution)/shard_map/all_gather | solution.py:124
  225.9 3.5 all-to-all-start.2
  230.4 13.3 %all-to-all-done.2 = bf16[128,4,512]{0,2,1:T(8,128)(2,1)S(1)} async-done(((bf16[128,4,512]{0,2,1:T(8,128)(2,1)}), bf16[128,4,512]{0,2,1:T(8,128)(2,1)S(1)}, u32[]{:S(2)}, u32[]{:S(2)}) %all-to-all-start.2) | async-done | bytes 524320 | tf_op jit(solution)/shard_map/all_to_all | solution.py:140
  243.7 3.5 all-to-all-start
  247.1 3.0 copy.77
  250.2 2.7 copy.78
  252.8 8.3 %all-to-all-done = bf16[128,4,512]{0,2,1:T(8,128)(2,1)S(1)} async-done(((bf16[128,4,512]{0,2,1:T(8,128)(2,1)}), bf16[128,4,512]{0,2,1:T(8,128)(2,1)S(1)}, u32[]{:S(2)}, u32[]{:S(2)}) %all-to-all-start) | async-done | bytes 524320 | tf_op jit(solution)/shard_map/all_to_all | solution.py:147
  261.2 3.8 %all-to-all-start.1 = ((bf16[384,4,768]{2,0,1:T(8,128)(2,1)}), bf16[384,4,768]{2,0,1:T(8,128)(2,1)S(1)}, u32[]{:S(2)}, u32[]{:S(2)}) async-start(bf16[384,4,768]{2,0,1:T(8,128)(2,1)} %copy.78), calls=%async_computation.2 | async-start | bytes 4718592 | tf_op jit(solution)/shard_map/all_to_all | solution.py:133
  265.6 1.8 multiply_cosine_fusion
  268.4 1.8 compare_and_fusion
  271.5 46.6 %all-to-all-done.1 = bf16[384,4,768]{2,0,1:T(8,128)(2,1)S(1)} async-done(((bf16[384,4,768]{2,0,1:T(8,128)(2,1)}), bf16[384,4,768]{2,0,1:T(8,128)(2,1)S(1)}, u32[]{:S(2)}, u32[]{:S(2)}) %all-to-all-start.1) | async-done | bytes 2359328 | tf_op jit(solution)/shard_map/all_to_all | solution.py:133
  318.1 2.4 copy.79
  320.6 2.6 copy.74
  324.9 2.6 fusion.6
  329.1 1.8 convolution_convert_fusion
  339.6 2.1 divide_convert_fusion
  342.6 27.7 %all_to_all.60 = bf16[1024,4,128]{2,1,0:T(4,128)(2,1)S(1)} all-to-all(bf16[1024,4,128]{2,1,0:T(4,128)(2,1)S(1)} %copy.84), channel_id=1, replica_groups=mesh['seq'=4,'tp'=4,'dp'=2] {'seq'}, dimensions={0} | all-to-all | bytes 2097152 | tf_op jit(solution)/shard_map/all_to_all | solution.py:176
  (96 shorter events, 24.2 us)
Async XLA Ops:
  6.5 143.5 %all-gather.7.cloned.1.call-start = ((), (), s32[]{:S(2)}) async-start(), calls=%async_computation.5 | async-start | bytes 9461760 | tf_op jit(solution)/shard_map/all_gather | solution.py:110
  8.3 2.7 copy-start.5
  8.4 141.7 %copy-start.14 = (f32[1792]{0:T(1024)S(1)}, f32[1792]{0:T(1024)}, u32[]{:S(2)}) copy-start(f32[1792]{0:T(1024)} %param.11) | copy-start | bytes 21508
  11.0 180.7 %reduce-scatter.2.cloned.1.call-start = ((), (), s32[]{:S(2)}) async-start(), calls=%async_computation.6 | async-start | bytes 2785280 | tf_op jit(solution)/shard_map/reduce_scatter | solution.py:112
  22.7 134.4 %copy-start.13 = (s32[256]{0:T(256)S(1)}, s32[256]{0:T(256)}, u32[]{:S(2)}) copy-start(s32[256]{0:T(256)} %param.19) | copy-start | bytes 3076
  157.0 37.4 %copy-start.11 = (f32[512]{0:T(512)S(1)}, f32[512]{0:T(512)}, u32[]{:S(2)}) copy-start(f32[512]{0:T(512)} %param.15) | copy-start | bytes 6148
  157.0 37.7 %copy-start.10 = (f32[1536]{0:T(1024)S(1)}, f32[1536]{0:T(1024)}, u32[]{:S(2)}) copy-start(f32[1536]{0:T(1024)} %param.14) | copy-start | bytes 18436
  157.0 67.8 %all-gather.9.cloned.1.call-start = ((), (), s32[]{:S(2)}) async-start(), calls=%async_computation.7 | async-start | bytes 1392640 | tf_op jit(solution)/shard_map/all_gather | solution.py:124
  165.0 30.7 %copy-start.12 = (f32[32]{0:T(128)}, f32[32]{0:T(128)S(1)}, u32[]{:S(2)}) copy-start(f32[32]{0:T(128)S(1)} %multiply_power_fusion) | copy-start | bytes 388
  193.2 31.8 %copy-start.7 = (bf16[128,2048]{1,0:T(8,128)(2,1)S(1)}, bf16[128,2048]{1,0:T(8,128)(2,1)}, u32[]{:S(2)}) copy-start(bf16[128,2048]{1,0:T(8,128)(2,1)} %param.17) | copy-start | bytes 1572868
  194.0 35.4 %copy-start.8 = (bf16[128,2048]{1,0:T(8,128)(2,1)S(1)}, bf16[128,2048]{1,0:T(8,128)(2,1)}, u32[]{:S(2)}) copy-start(bf16[128,2048]{1,0:T(8,128)(2,1)} %param.18) | copy-start | bytes 1572868
  195.7 124.9 %all-gather.11.cloned.1.call-start = ((), (), s32[]{:S(2)}) async-start(), calls=%async_computation.8 | async-start | bytes 5570560 | tf_op jit(solution)/shard_map/all_gather | solution.py:125
  225.9 17.7 %all-to-all-start.2 = ((bf16[128,4,512]{0,2,1:T(8,128)(2,1)}), bf16[128,4,512]{0,2,1:T(8,128)(2,1)S(1)}, u32[]{:S(2)}, u32[]{:S(2)}) async-start(bf16[128,4,512]{0,2,1:T(8,128)(2,1)} %bitcast.20), calls=%async_computation.3 | async-start | bytes 1048576 | tf_op jit(solution)/shard_map/all_to_all | solution.py:140
  243.7 17.5 %all-to-all-start = ((bf16[128,4,512]{0,2,1:T(8,128)(2,1)}), bf16[128,4,512]{0,2,1:T(8,128)(2,1)S(1)}, u32[]{:S(2)}, u32[]{:S(2)}) async-start(bf16[128,4,512]{0,2,1:T(8,128)(2,1)} %bitcast.7), calls=%async_computation.1 | async-start | bytes 1048576 | tf_op jit(solution)/shard_map/all_to_all | solution.py:147
  261.2 57.0 %all-to-all-start.1 = ((bf16[384,4,768]{2,0,1:T(8,128)(2,1)}), bf16[384,4,768]{2,0,1:T(8,128)(2,1)S(1)}, u32[]{:S(2)}, u32[]{:S(2)}) async-start(bf16[384,4,768]{2,0,1:T(8,128)(2,1)} %copy.78), calls=%async_computation.2 | async-start | bytes 4718592 | tf_op jit(solution)/shard_map/all_to_all | solution.py:133
  323.2 1.7 copy-start
  324.0 3.5 copy-start.1
  324.9 4.3 %copy-start.9 = (bf16[4,128,1,512]{3,1,0,2:T(8,128)(2,1)S(1)}, bf16[4,128,1,512]{3,1,0,2:T(8,128)(2,1)}, u32[]{:S(2)}) copy-start(bf16[4,128,1,512]{3,1,0,2:T(8,128)(2,1)} %copy.81) | copy-start | bytes 1572868
  327.5 1.6 copy-start.3
  327.5 3.5 copy-start.6
  330.9 1.8 copy-start.4
  331.0 1.7 copy-start.15
  335.5 1.0 slice-start
  337.9 1.7 slice-start.1
  (1 other events, 1.0 us)
Sparse Core Ops, SparseCore 0:
  11.1 138.9 all-gather.6
  157.2 34.4 reduce-scatter.1
  195.8 29.0 all-gather.8
  226.6 54.1 all-gather.10

commit v2 on v1

--- a/solution.py
+++ b/solution.py
@@ -106,9 +106,27 @@
         jnp.bfloat16
     )
 
+    dp_index = lax.axis_index("dp")
+    dp_count = lax.axis_size("dp")
     down_piece = jnp.concatenate([query_down, memory_down], 1)
-    down_all = lax.all_gather(down_piece, "seq", axis=1, tiled=True)
-    partial = jnp.dot(normed, down_all, preferred_element_type=jnp.float32)
+    half_rows = down_piece.shape[0] // dp_count
+    own_rows = lax.dynamic_slice_in_dim(down_piece, dp_index * half_rows, half_rows, 0)
+    own_all = lax.all_gather(own_rows, "seq", axis=1, tiled=True)
+    partial = jnp.dot(
+        lax.dynamic_slice_in_dim(normed, dp_index * half_rows, half_rows, 1),
+        own_all,
+        preferred_element_type=jnp.float32,
+    )
+    for shift in range(1, dp_count):
+        peer = (dp_index + dp_count - shift) % dp_count
+        peer_all = lax.ppermute(
+            own_all, "dp", perm=[(i, (i + shift) % dp_count) for i in range(dp_count)]
+        )
+        partial = partial + jnp.dot(
+            lax.dynamic_slice_in_dim(normed, peer * half_rows, half_rows, 1),
+            peer_all,
+            preferred_element_type=jnp.float32,
+        )
     latent_rows = lax.psum_scatter(partial, "tp", scatter_dimension=0, tiled=True)
     chunk = latent_rows.shape[0]
     latent_rows = latent_rows.reshape(chunk, seq_count, qrank_piece + memory_piece)
@@ -121,36 +139,40 @@
     compressed_memory = rms_scale(memory_sums[:, :KVRANK], memory_gain).astype(jnp.bfloat16)
     key_rope = rotate(memory_sums[:, KVRANK:], chunk_position).astype(jnp.bfloat16)
     packed = jnp.concatenate([compressed_query, compressed_memory, key_rope], 1)
-    packed = lax.all_gather(packed, "seq", axis=0, tiled=False)
-    packed = lax.all_gather(packed, "tp", axis=0, tiled=False)
-    latent = jnp.transpose(packed, (1, 0, 2, 3)).reshape(total_rows, packed.shape[-1])
+    latent = lax.all_gather(packed, ("seq", "tp"), axis=0, tiled=True)
     cq_all = latent[:, :qrank]
     cm_all = latent[:, qrank : qrank + KVRANK]
     rope_all = latent[:, qrank + KVRANK :]
 
     local_heads = query_up.shape[1] // (NOPE + ROPE)
     heads = local_heads // seq_count
-    query_w = lax.all_to_all(
-        query_up.reshape(query_up.shape[0], seq_count, heads * (NOPE + ROPE)),
-        "seq",
-        split_axis=1,
-        concat_axis=0,
-        tiled=True,
-    ).reshape(qrank, heads * (NOPE + ROPE))
-    key_w = lax.all_to_all(
-        key_up.reshape(key_up.shape[0], seq_count, heads * NOPE),
-        "seq",
-        split_axis=1,
-        concat_axis=0,
-        tiled=True,
-    ).reshape(KVRANK, heads * NOPE)
-    value_w = lax.all_to_all(
-        value_up.reshape(value_up.shape[0], seq_count, heads * VDIM),
-        "seq",
-        split_axis=1,
-        concat_axis=0,
-        tiled=True,
-    ).reshape(KVRANK, heads * VDIM)
+
+    def head_columns(weight, head_width):
+        rows = weight.shape[0]
+        cols = heads * head_width // dp_count
+        own = lax.dynamic_slice_in_dim(
+            weight.reshape(rows, seq_count, heads * head_width), dp_index * cols, cols, 2
+        )
+        own = lax.all_to_all(own, "seq", split_axis=1, concat_axis=0, tiled=True)
+        own = own.reshape(rows * seq_count, cols)
+        pieces = [own]
+        for shift in range(1, dp_count):
+            pieces.append(
+                lax.ppermute(
+                    own, "dp", perm=[(i, (i + shift) % dp_count) for i in range(dp_count)]
+                )
+            )
+        ordered = []
+        for core in range(dp_count):
+            pick = pieces[0]
+            for k in range(1, dp_count):
+                pick = jnp.where((dp_index + dp_count - k) % dp_count == core, pieces[k], pick)
+            ordered.append(pick)
+        return jnp.concatenate(ordered, 1)
+
+    query_w = head_columns(query_up, NOPE + ROPE)
+    key_w = head_columns(key_up, NOPE)
+    value_w = head_columns(value_up, VDIM)
 
     query_full = jnp.dot(cq_all, query_w, preferred_element_type=jnp.float32).reshape(
         total_rows, heads, NOPE + ROPE

time: 380 us -> 301 us (0.79)
  waiting for transfers between devices: 251 us -> 174 us
  local copies, waits for them, and re-layouts: 24.8 us -> 16.8 us
  matrix products: 18.2 us -> 23.6 us
    all_gather x3 -> x2, waiting for transfers between devices: 157 us -> 89 us  [the longest x1 76.8 us: body(): own_all = lax.all_gather(own_rows, 'seq', axis=1, tiled=True)]
    all_to_all x3, waiting for transfers between devices: 68.2 us -> 60.5 us  [head_columns(): own = lax.all_to_all(own, 'seq', split_axis=1, concat_axis=0, tiled=True)]
    reshape x2 -> x0, local copies, waits for them, and re-layouts: 5.14 us -> none  [the longest x1 2.7 us: body(): query_up.reshape(query_up.shape[0], seq_count, heads * (NOPE + ROPE))]
    select_n x0 -> x3, other arithmetic: none -> 4.49 us  [head_columns(): jnp.where((dp_index + dp_count - k) % dp_count == core, pieces[k], pick)]
    unnamed x38 -> x32, local copies, waits for them, and re-layouts: 9.38 us -> 7.32 us
    dot_general x1 -> x2, matrix products: 6.93 us -> 8.38 us  [the longest x1 4.89 us: body(): jnp.dot(lax.dynamic_slice_in_dim(normed, peer * half_rows, half_rows, 1),...]
  transfers between devices with their start and end apart: 7 -> 10, of which waited for: 6 -> 7; matrix products, arithmetic and copies ran while one was open for 5% -> 6% of each run, Pallas kernels for 0% -> 0%
where the time goes in v2:
time: 301 us; the launch traced here: 300 us
  waiting for transfers between devices  174 us (58%)
  blocking collectives  46.7 us (16%)
  matrix products  23.6 us (8%)
  local copies, waits for them, and re-layouts  16.8 us (6%)
  between operations  13.7 us (5%)
  other arithmetic  13.1 us (4%)
  starting transfers between devices  12 us (4%)
    all_gather x1, waiting for transfers between devices, body(): own_all = lax.all_gather(own_rows, 'seq', axis=1, tiled=True)  76.8 us
    all_to_all x3, waiting for transfers between devices, head_columns(): own = lax.all_to_all(own, 'seq', split_axis=1, concat_axis=0, tiled=True)  60.5 us
    all_to_all x1, blocking collectives, body(): lax.all_to_all(head_output, 'seq', split_axis=0, concat_axis=1, tiled=True)  28.5 us
    reduce_scatter x1, waiting for transfers between devices, body(): lax.psum_scatter(partial, 'tp', scatter_dimension=0, tiled=True)  24.4 us
    all_gather x1, waiting for transfers between devices, body(): latent = lax.all_gather(packed, ('seq', 'tp'), axis=0, tiled=True)  12.2 us
    all_to_all x3, starting transfers between devices, head_columns(): own = lax.all_to_all(own, 'seq', split_axis=1, concat_axis=0, tiled=True)  11.7 us
    psum x1, blocking collectives, body(): square_sums = lax.psum(jnp.sum(inputs * inputs, 1), 'tp')  9.84 us
    all_gather x1, blocking collectives, body(): group_ids = lax.all_gather(segment_ids, 'seq', axis=0, tiled=True)  8.43 us
  transfers between devices with their start and end apart: 10, of which 7 were waited for; matrix products, arithmetic and copies ran while one was open for 6% of the time, Pallas kernels for 0%

profile of v2, /device:TPU:0, one launch (start us, length us, event | category | flops | bytes accessed | tf_op | source)
XLA Modules:
  0.0 299.9 jit_solution(7188480454968841016)
XLA Ops:
  6.5 1.9 copy.60
  9.5 76.8 %all-gather.4.cloned.1.call-done = bf16[896,2112]{0,1:T(8,128)(2,1)} async-done(((bf16[896,528]{0,1:T(8,128)(2,1)}), bf16[896,2112]{0,1:T(8,128)(2,1)}) %all-gather.4.cloned.1.call-update) | async-done | bytes 3784720 | tf_op jit(solution)/shard_map/all_gather | solution.py:114
  86.6 9.8 %psum.7 = f32[256]{0:T(256)S(1)} all-reduce(f32[256]{0:T(256)S(1)} %fusion.20), channel_id=1, replica_groups=mesh['seq'=4,'tp'=4,'dp'=2] {'tp'}, use_global_device_ids=true, to_apply=%region_1.2 | all-reduce | flops 256 | bytes 2048 | tf_op jit(solution)/shard_map/psum | solution.py:104
  96.8 3.5 %fusion.50 = f32[256,2112]{1,0:T(8,128)S(1)} fusion(bf16[896,2112]{0,1:T(8,128)(2,1)} %all-gather.4.cloned.1.call-done, bf16[256,1792]{1,0:T(8,128)(2,1)S(1)} %fusion.22, s32[]{:T(128)S(6)} %select_n.88), kind=kOutput, calls=%fused_computation.64 | convolution fusion | flops 968884224 | bytes 6406148 | tf_op jit(solution)/shard_map/dot_general | solution.py:115
  100.3 4.9 %convolution_add_fusion = f32[256,2112]{1,0:T(8,128)} fusion(f32[256,2112]{1,0:T(8,128)S(1)} %fusion.50, bf16[896,2112]{0,1:T(8,128)(2,1)} %collective-permute-done, bf16[256,1792]{1,0:T(8,128)(2,1)S(1)} %fusion.22, s32[]{:T(128)S(6)} %select_n.90), kind=kOutput, calls=%fused_computation.7 | convolution fusion | flops 969424896 | bytes 8634372 | tf_op jit(solution)/shard_map/dot_general | solution.py:125
  105.3 8.4 %all-gather = s32[4,1,256]{2,1,0:T(1,128)S(1)} all-gather(s32[1,1,256]{2,1,0:T(1,128)S(1)} %bitcast.74), channel_id=1, replica_groups=mesh['seq'=4,'tp'=4,'dp'=2] {'seq'}, dimensions={0}, use_global_device_ids=true | all-gather | bytes 5120 | tf_op jit(solution)/shard_map/all_gather | solution.py:97
  114.0 24.4 %reduce-scatter.2.cloned.1.call-done = f32[64,2112]{1,0:T(8,128)} async-done(((f32[256,2112]{1,0:T(8,128)}), f32[64,2112]{1,0:T(8,128)}) %reduce-scatter.2.cloned.1.call-update) | async-done | bytes 540688 | tf_op jit(solution)/shard_map/reduce_scatter | solution.py:130
  142.3 3.0 %copy.67 = bf16[384,3072]{0,1:T(8,128)(2,1)S(1)} copy(bf16[384,3072]{1,0:T(8,128)(2,1)} %param.16) | data formatting | bytes 4718592 | tf_op args[6]
  146.5 4.7 %all-to-all-start.1 = ((bf16[384,4,384]{0,2,1:T(8,128)(2,1)}), bf16[384,4,384]{0,2,1:T(8,128)(2,1)S(1)}, u32[]{:S(2)}, u32[]{:S(2)}) async-start(bf16[384,4,384]{0,2,1:T(8,128)(2,1)} %constant_dynamic-slice_fusion.1), calls=%async_computation.2 | async-start | bytes 2359296 | tf_op jit(solution)/shard_map/all_to_all | solution.py:156
  152.3 33.3 %all-to-all-done.1 = bf16[384,4,384]{0,2,1:T(8,128)(2,1)S(1)} async-done(((bf16[384,4,384]{0,2,1:T(8,128)(2,1)}), bf16[384,4,384]{0,2,1:T(8,128)(2,1)S(1)}, u32[]{:S(2)}, u32[]{:S(2)}) %all-to-all-start.1) | async-done | bytes 1179680 | tf_op jit(solution)/shard_map/all_to_all | solution.py:156
  185.6 3.4 %all-to-all-start.2 = ((bf16[128,4,256]{0,2,1:T(8,128)(2,1)}), bf16[128,4,256]{0,2,1:T(8,128)(2,1)S(1)}, u32[]{:S(2)}, u32[]{:S(2)}) async-start(bf16[128,4,256]{0,2,1:T(8,128)(2,1)} %constant_dynamic-slice_fusion), calls=%async_computation.3 | async-start | bytes 524288 | tf_op jit(solution)/shard_map/all_to_all | solution.py:156
  190.9 13.3 %all-to-all-done.2 = bf16[128,4,256]{0,2,1:T(8,128)(2,1)S(1)} async-done(((bf16[128,4,256]{0,2,1:T(8,128)(2,1)}), bf16[128,4,256]{0,2,1:T(8,128)(2,1)S(1)}, u32[]{:S(2)}, u32[]{:S(2)}) %all-to-all-start.2) | async-done | bytes 262176 | tf_op jit(solution)/shard_map/all_to_all | solution.py:156
  204.2 3.6 %all-to-all-start = ((bf16[128,4,256]{0,2,1:T(8,128)(2,1)}), bf16[128,4,256]{0,2,1:T(8,128)(2,1)S(1)}, u32[]{:S(2)}, u32[]{:S(2)}) async-start(bf16[128,4,256]{0,2,1:T(8,128)(2,1)} %constant_dynamic-slice_fusion.2), calls=%async_computation.1 | async-start | bytes 524288 | tf_op jit(solution)/shard_map/all_to_all | solution.py:156
  208.7 13.9 %all-to-all-done = bf16[128,4,256]{0,2,1:T(8,128)(2,1)S(1)} async-done(((bf16[128,4,256]{0,2,1:T(8,128)(2,1)}), bf16[128,4,256]{0,2,1:T(8,128)(2,1)S(1)}, u32[]{:S(2)}, u32[]{:S(2)}) %all-to-all-start) | async-done | bytes 262176 | tf_op jit(solution)/shard_map/all_to_all | solution.py:156
  225.1 2.9 broadcast_select_fusion.1
  228.0 12.2 %all-gather.6.cloned.1.call-done = bf16[1024,2112]{1,0:T(8,128)(2,1)} async-done(((bf16[64,2112]{1,0:T(8,128)(2,1)}), bf16[1024,2112]{1,0:T(8,128)(2,1)}) %all-gather.6.cloned.1.call-update) | async-done | bytes 4325392 | tf_op jit(solution)/shard_map/all_gather | solution.py:142
  240.2 2.2 convolution_convert_fusion.1
  242.4 5.0 %fusion.6 = f32[1024,768]{0,1:T(8,128)S(1)} fusion(bf16[1024,2112]{1,0:T(8,128)(2,1)} %all-gather.6.cloned.1.call-done, bf16[1536,384]{1,0:T(8,128)(2,1)S(1)} %copy-done.4, bf16[1536,384]{1,0:T(8,128)(2,1)S(1)} %copy-done.3), kind=kOutput, calls=%fused_computation.11 | convolution fusion | flops 2420637696 | bytes 8650752 | tf_op jit(solution)/shard_map/dot_general | solution.py:177
  247.4 1.7 copy-done.2
  250.9 2.0 convolution_convert_fusion
  254.0 1.7 fusion
  258.1 1.9 fusion.1
  260.0 2.1 divide_convert_fusion
  263.0 28.5 %all_to_all.60 = bf16[1024,4,128]{2,1,0:T(4,128)(2,1)S(1)} all-to-all(bf16[1024,4,128]{2,1,0:T(4,128)(2,1)S(1)} %copy.73), channel_id=1, replica_groups=mesh['seq'=4,'tp'=4,'dp'=2] {'seq'}, dimensions={0} | all-to-all | bytes 2097152 | tf_op jit(solution)/shard_map/all_to_all | solution.py:198
  (102 shorter events, 21.4 us)
Async XLA Ops:
  6.5 1.9 copy-start.7
  6.5 79.8 %all-gather.4.cloned.1.call-start = ((), (), s32[]{:S(2)}) async-start(), calls=%async_computation.5 | async-start | bytes 4730880 | tf_op jit(solution)/shard_map/all_gather | solution.py:114
  8.4 77.9 %copy-start = (bf16[256,1792]{1,0:T(8,128)(2,1)S(1)}, bf16[256,1792]{1,0:T(8,128)(2,1)}, u32[]{:S(2)}) copy-start(bf16[256,1792]{1,0:T(8,128)(2,1)} %param.10) | copy-start | bytes 2752516
  8.4 88.0 %copy-start.9 = (f32[1792]{0:T(1024)S(1)}, f32[1792]{0:T(1024)}, u32[]{:S(2)}) copy-start(f32[1792]{0:T(1024)} %param.11) | copy-start | bytes 21508
  9.5 128.9 %reduce-scatter.2.cloned.1.call-start = ((), (), s32[]{:S(2)}) async-start(), calls=%async_computation.6 | async-start | bytes 2785280 | tf_op jit(solution)/shard_map/reduce_scatter | solution.py:130
  86.3 13.9 %collective-permute-start = (bf16[896,2112]{0,1:T(8,128)(2,1)}, bf16[896,2112]{0,1:T(8,128)(2,1)}, u32[]{:S(2)}, u32[]{:S(2)}) collective-permute-start(bf16[896,2112]{0,1:T(8,128)(2,1)} %all-gather.4.cloned.1.call-done), channel_id=1, source_target_pairs={{0,1},{1,0},{2,3},{3,2},{4,5},{5,4},{6,7},{7,6},{8,9},{9,8},{10,11... | collective-permute-start | bytes 11354120 | tf_op jit(solution)/shard_map/ppermute | solution.py:122
  100.2 5.0 %copy-start.12 = (s32[256]{0:T(256)S(1)}, s32[256]{0:T(256)}, u32[]{:S(2)}) copy-start(s32[256]{0:T(256)} %param.19) | copy-start | bytes 3076
  105.2 35.6 %copy-start.11 = (f32[512]{0:T(512)S(1)}, f32[512]{0:T(512)}, u32[]{:S(2)}) copy-start(f32[512]{0:T(512)} %param.15) | copy-start | bytes 6148
  105.2 135.0 %all-gather.6.cloned.1.call-start = ((), (), s32[]{:S(2)}) async-start(), calls=%async_computation.7 | async-start | bytes 4734976 | tf_op jit(solution)/shard_map/all_gather | solution.py:142
  114.0 27.4 %copy-start.10 = (f32[1536]{0:T(1024)S(1)}, f32[1536]{0:T(1024)}, u32[]{:S(2)}) copy-start(f32[1536]{0:T(1024)} %param.14) | copy-start | bytes 18436
  145.3 5.9 %copy-start.5 = (bf16[128,2048]{1,0:T(8,128)(2,1)S(1)}, bf16[128,2048]{1,0:T(8,128)(2,1)}, u32[]{:S(2)}) copy-start(bf16[128,2048]{1,0:T(8,128)(2,1)} %param.17) | copy-start | bytes 1572868
  146.5 42.5 %copy-start.6 = (bf16[128,2048]{1,0:T(8,128)(2,1)S(1)}, bf16[128,2048]{1,0:T(8,128)(2,1)}, u32[]{:S(2)}) copy-start(bf16[128,2048]{1,0:T(8,128)(2,1)} %param.18) | copy-start | bytes 1572868
  146.5 39.0 %all-to-all-start.1 = ((bf16[384,4,384]{0,2,1:T(8,128)(2,1)}), bf16[384,4,384]{0,2,1:T(8,128)(2,1)S(1)}, u32[]{:S(2)}, u32[]{:S(2)}) async-start(bf16[384,4,384]{0,2,1:T(8,128)(2,1)} %constant_dynamic-slice_fusion.1), calls=%async_computation.2 | async-start | bytes 2359296 | tf_op jit(solution)/shard_map/all_to_all | solution.py:156
  185.6 18.6 %all-to-all-start.2 = ((bf16[128,4,256]{0,2,1:T(8,128)(2,1)}), bf16[128,4,256]{0,2,1:T(8,128)(2,1)S(1)}, u32[]{:S(2)}, u32[]{:S(2)}) async-start(bf16[128,4,256]{0,2,1:T(8,128)(2,1)} %constant_dynamic-slice_fusion), calls=%async_computation.3 | async-start | bytes 524288 | tf_op jit(solution)/shard_map/all_to_all | solution.py:156
  190.9 34.3 %collective-permute-start.2 = (bf16[1536,384]{1,0:T(8,128)(2,1)S(1)}, bf16[1536,384]{1,0:T(8,128)(2,1)}, u32[]{:S(2)}, u32[]{:S(2)}) collective-permute-start(bf16[1536,384]{1,0:T(8,128)(2,1)S(1)} %bitcast.50), channel_id=1, source_target_pairs={{0,1},{1,0},{2,3},{3,2},{4,5},{5,4},{6,7},{7,6},{8,9},{9,8},{10,11... | collective-permute-start | bytes 3538952 | tf_op jit(solution)/shard_map/ppermute | solution.py:161
  204.2 18.4 %all-to-all-start = ((bf16[128,4,256]{0,2,1:T(8,128)(2,1)}), bf16[128,4,256]{0,2,1:T(8,128)(2,1)S(1)}, u32[]{:S(2)}, u32[]{:S(2)}) async-start(bf16[128,4,256]{0,2,1:T(8,128)(2,1)} %constant_dynamic-slice_fusion.2), calls=%async_computation.1 | async-start | bytes 524288 | tf_op jit(solution)/shard_map/all_to_all | solution.py:156
  208.3 15.0 %collective-permute-start.3 = (bf16[512,256]{1,0:T(8,128)(2,1)S(1)}, bf16[512,256]{1,0:T(8,128)(2,1)S(1)}, u32[]{:S(2)}, u32[]{:S(2)}) collective-permute-start(bf16[512,256]{1,0:T(8,128)(2,1)S(1)} %bitcast.64), channel_id=1, source_target_pairs={{0,1},{1,0},{2,3},{3,2},{4,5},{5,4},{6,7},{7,6},{8,9},{9,8},{10,11... | collective-permute-start | bytes 786440 | tf_op jit(solution)/shard_map/ppermute | solution.py:161
  222.7 1.6 collective-permute-start.1
  240.2 2.2 copy-start.3
  240.2 2.2 copy-start.4
  242.4 5.0 %copy-start.1 = (bf16[1024,512]{0,1:T(8,128)(2,1)}, bf16[1024,512]{0,1:T(8,128)(2,1)S(1)}, u32[]{:S(2)}) copy-start(bf16[1024,512]{0,1:T(8,128)(2,1)S(1)} %convolution_convert_fusion.1) | copy-start | bytes 3145732
  247.4 1.7 copy-start.2
  247.4 1.8 slice-start.2
  258.1 1.9 slice-start.1
  (2 other events, 2.6 us)
Sparse Core Ops, SparseCore 0:
  9.6 76.6 all-gather.3
  105.3 33.0 reduce-scatter.1
  142.4 97.6 all-gather.5

commit v3 on v2

--- a/solution.py
+++ b/solution.py
@@ -95,10 +95,6 @@
     memory_cols = memory_piece * seq_count
 
     group_ids = lax.all_gather(segment_ids, "seq", axis=0, tiled=True)
-    token_index = jnp.arange(total_rows, dtype=jnp.int32)
-    onehot = group_ids[:, None] == jnp.arange(DOCS, dtype=jnp.int32)[None, :]
-    starts = jnp.min(jnp.where(onehot, token_index[:, None], total_rows), 0)
-    position = token_index - jnp.sum(jnp.where(onehot, starts[None, :], 0), 1)
 
     inputs = hidden_states.astype(jnp.float32)
     square_sums = lax.psum(jnp.sum(inputs * inputs, 1), "tp")
@@ -112,6 +108,7 @@
     half_rows = down_piece.shape[0] // dp_count
     own_rows = lax.dynamic_slice_in_dim(down_piece, dp_index * half_rows, half_rows, 0)
     own_all = lax.all_gather(own_rows, "seq", axis=1, tiled=True)
+    own_all, normed, group_ids = lax.optimization_barrier((own_all, normed, group_ids))
     partial = jnp.dot(
         lax.dynamic_slice_in_dim(normed, dp_index * half_rows, half_rows, 1),
         own_all,
@@ -128,6 +125,11 @@
             preferred_element_type=jnp.float32,
         )
     latent_rows = lax.psum_scatter(partial, "tp", scatter_dimension=0, tiled=True)
+
+    token_index = jnp.arange(total_rows, dtype=jnp.int32)
+    onehot = group_ids[:, None] == jnp.arange(DOCS, dtype=jnp.int32)[None, :]
+    starts = jnp.min(jnp.where(onehot, token_index[:, None], total_rows), 0)
+    position = token_index - jnp.sum(jnp.where(onehot, starts[None, :], 0), 1)
     chunk = latent_rows.shape[0]
     latent_rows = latent_rows.reshape(chunk, seq_count, qrank_piece + memory_piece)
     query_sums = latent_rows[:, :, :qrank_piece].reshape(chunk, qrank)
@@ -139,7 +141,9 @@
     compressed_memory = rms_scale(memory_sums[:, :KVRANK], memory_gain).astype(jnp.bfloat16)
     key_rope = rotate(memory_sums[:, KVRANK:], chunk_position).astype(jnp.bfloat16)
     packed = jnp.concatenate([compressed_query, compressed_memory, key_rope], 1)
-    latent = lax.all_gather(packed, ("seq", "tp"), axis=0, tiled=True)
+    packed = lax.all_gather(packed, "seq", axis=0, tiled=False)
+    packed = lax.all_gather(packed, "tp", axis=0, tiled=False)
+    latent = jnp.transpose(packed, (1, 0, 2, 3)).reshape(total_rows, packed.shape[-1])
     cq_all = latent[:, :qrank]
     cm_all = latent[:, qrank : qrank + KVRANK]
     rope_all = latent[:, qrank + KVRANK :]
@@ -194,8 +198,20 @@
         [key_nope, jnp.broadcast_to(rope_all[:, None, :], (total_rows, heads, ROPE))], -1
     )
     score_scale = (NOPE + ROPE) ** (-0.5)
-    head_output = heads_attention(query, key_all, value, group_ids, score_scale, doc_most)
-    attended = lax.all_to_all(head_output, "seq", split_axis=0, concat_axis=1, tiled=True)
+    groups = 2 if heads % 2 == 0 else 1
+    per_group = heads // groups
+    attended = []
+    for group in range(groups):
+        picked = slice(group * per_group, (group + 1) * per_group)
+        head_output = heads_attention(
+            query[:, picked], key_all[:, picked], value[:, picked], group_ids, score_scale, doc_most
+        )
+        attended.append(
+            lax.all_to_all(head_output, "seq", split_axis=0, concat_axis=1, tiled=True).reshape(
+                tok_count, seq_count, per_group, VDIM
+            )
+        )
+    attended = jnp.concatenate(attended, 2)
     return attended.reshape(tok_count, local_heads * VDIM)
 
 

time: 301 us -> 301 us (level)
  blocking collectives: 46.7 us -> 39.6 us
  local copies, waits for them, and re-layouts: 16.8 us -> 23.8 us
  waiting for transfers between devices: 174 us -> 169 us
    all_gather x1, waiting for transfers between devices: 76.8 us -> 52.8 us  [body(): own_all = lax.all_gather(own_rows, 'seq', axis=1, tiled=True)]
    all_to_all x3, waiting for transfers between devices: 60.5 us -> 39.4 us  [head_columns(): own = lax.all_to_all(own, 'seq', split_axis=1, concat_axis=0, tiled=True)]
    all_gather x1 -> x2, waiting for transfers between devices: 12.2 us -> 29.2 us  [the longest x1 29.2 us: body(): packed = lax.all_gather(packed, 'seq', axis=0, tiled=False)]
    all_to_all x1, blocking collectives: 28.5 us -> 16.6 us  [body(): lax.all_to_all(head_output, 'seq', split_axis=0, concat_axis=1, tiled=True)]
    reduce_scatter x1, waiting for transfers between devices: 24.4 us -> 34.6 us  [body(): lax.psum_scatter(partial, 'tp', scatter_dimension=0, tiled=True)]
    all_to_all x0 -> x1, waiting for transfers between devices: none -> 8.68 us  [body(): lax.all_to_all(head_output, 'seq', split_axis=0, concat_axis=1, tiled=True)]
    all_to_all x0 -> x1, starting transfers between devices: none -> 4.13 us  [body(): lax.all_to_all(head_output, 'seq', split_axis=0, concat_axis=1, tiled=True)]
    ppermute x1, waiting for transfers between devices: 0.01 us -> 3.43 us  [body(): lax.ppermute(own_all, 'dp', perm=[(i, (i + shift) % dp_count) for i in ra...]
  transfers between devices with their start and end apart: 10 -> 12, of which waited for: 7 -> 9; matrix products, arithmetic and copies ran while one was open for 6% -> 7% of each run, Pallas kernels for 0% -> 0%
where the time goes in v3:
time: 301 us; the launch traced here: 300 us
  waiting for transfers between devices  169 us (56%)
  blocking collectives  39.6 us (13%)
  matrix products  24.9 us (8%)
  local copies, waits for them, and re-layouts  23.8 us (8%)
  starting transfers between devices  15 us (5%)
  other arithmetic  14.3 us (5%)
  between operations  13.8 us (5%)
    all_gather x1, waiting for transfers between devices, body(): own_all = lax.all_gather(own_rows, 'seq', axis=1, tiled=True)  52.8 us
    all_to_all x3, waiting for transfers between devices, head_columns(): own = lax.all_to_all(own, 'seq', split_axis=1, concat_axis=0, tiled=True)  39.4 us
    reduce_scatter x1, waiting for transfers between devices, body(): lax.psum_scatter(partial, 'tp', scatter_dimension=0, tiled=True)  34.6 us
    all_gather x1, waiting for transfers between devices, body(): packed = lax.all_gather(packed, 'seq', axis=0, tiled=False)  29.2 us
    all_to_all x1, blocking collectives, body(): lax.all_to_all(head_output, 'seq', split_axis=0, concat_axis=1, tiled=True)  16.6 us
    all_gather x1, blocking collectives, body(): group_ids = lax.all_gather(segment_ids, 'seq', axis=0, tiled=True)  11.7 us
    psum x1, blocking collectives, body(): square_sums = lax.psum(jnp.sum(inputs * inputs, 1), 'tp')  11.4 us
    all_to_all x3, starting transfers between devices, head_columns(): own = lax.all_to_all(own, 'seq', split_axis=1, concat_axis=0, tiled=True)  10.5 us
  transfers between devices with their start and end apart: 12, of which 9 were waited for; matrix products, arithmetic and copies ran while one was open for 7% of the time, Pallas kernels for 0%

profile of v3, /device:TPU:0, one launch (start us, length us, event | category | flops | bytes accessed | tf_op | source)
XLA Modules:
  0.0 300.2 jit_solution(3262502907540813024)
XLA Ops:
  10.2 11.4 %psum.7 = f32[256]{0:T(256)S(1)} all-reduce(f32[256]{0:T(256)S(1)} %fusion.13), channel_id=1, replica_groups=mesh['seq'=4,'tp'=4,'dp'=2] {'tp'}, use_global_device_ids=true, to_apply=%region_1.0 | all-reduce | flops 256 | bytes 2048 | tf_op jit(solution)/shard_map/psum | solution.py:100
  21.6 11.7 %all-gather.2 = s32[4,1,256]{2,1,0:T(1,128)S(1)} all-gather(s32[1,1,256]{2,1,0:T(1,128)S(1)} %bitcast.99), channel_id=1, replica_groups=mesh['seq'=4,'tp'=4,'dp'=2] {'seq'}, dimensions={0}, use_global_device_ids=true | all-gather | bytes 5120 | tf_op jit(solution)/shard_map/all_gather | solution.py:97
  33.5 52.8 %all-gather.7.cloned.1.call-done = bf16[896,2112]{0,1:T(8,128)(2,1)} async-done(((bf16[896,528]{0,1:T(8,128)(2,1)}), bf16[896,2112]{0,1:T(8,128)(2,1)}) %all-gather.7.cloned.1.call-update) | async-done | bytes 3784720 | tf_op jit(solution)/shard_map/all_gather | solution.py:110
  86.4 3.5 %fusion.73 = f32[256,2112]{1,0:T(8,128)S(1)} fusion(bf16[896,2112]{0,1:T(8,128)(2,1)} %all-gather.7.cloned.1.call-done, bf16[256,1792]{1,0:T(8,128)(2,1)S(1)} %fusion.15, s32[]{:T(128)S(6)} %select_n.94), kind=kOutput, calls=%fused_computation.91 | convolution fusion | flops 968884224 | bytes 6406148 | tf_op jit(solution)/shard_map/dot_general | solution.py:112
  89.8 3.4 %collective-permute-done = bf16[896,2112]{0,1:T(8,128)(2,1)} collective-permute-done((bf16[896,2112]{0,1:T(8,128)(2,1)}, bf16[896,2112]{0,1:T(8,128)(2,1)}, u32[]{:S(2)}, u32[]{:S(2)}) %collective-permute-start) | collective-permute-done | bytes 3784736 | tf_op jit(solution)/shard_map/ppermute | solution.py:119
  93.3 4.9 %convolution_add_fusion = f32[256,2112]{1,0:T(8,128)} fusion(f32[256,2112]{1,0:T(8,128)S(1)} %fusion.73, bf16[896,2112]{0,1:T(8,128)(2,1)} %collective-permute-done, bf16[256,1792]{1,0:T(8,128)(2,1)S(1)} %fusion.15, s32[]{:T(128)S(6)} %select_n.96), kind=kOutput, calls=%fused_computation | convolution fusion | flops 969424896 | bytes 8634372 | tf_op jit(solution)/shard_map/dot_general | solution.py:122
  98.6 34.6 %reduce-scatter.2.cloned.1.call-done = f32[64,2112]{1,0:T(8,128)} async-done(((f32[256,2112]{1,0:T(8,128)}), f32[64,2112]{1,0:T(8,128)}) %reduce-scatter.2.cloned.1.call-update) | async-done | bytes 540688 | tf_op jit(solution)/shard_map/reduce_scatter | solution.py:127
  137.2 29.2 %all-gather.9.cloned.1.call-done = bf16[256,2112]{1,0:T(8,128)(2,1)} async-done(((bf16[64,2112]{1,0:T(8,128)(2,1)}), bf16[256,2112]{1,0:T(8,128)(2,1)}) %all-gather.9.cloned.1.call-update) | async-done | bytes 1081360 | tf_op jit(solution)/shard_map/all_gather | solution.py:144
  166.4 3.0 copy.69
  170.7 3.5 %all-to-all-start.1 = ((bf16[384,4,384]{0,2,1:T(8,128)(2,1)}), bf16[384,4,384]{0,2,1:T(8,128)(2,1)S(1)}, u32[]{:S(2)}, u32[]{:S(2)}) async-start(bf16[384,4,384]{0,2,1:T(8,128)(2,1)} %constant_dynamic-slice_fusion), calls=%async_computation.2 | async-start | bytes 2359296 | tf_op jit(solution)/shard_map/all_to_all | solution.py:160
  175.2 27.3 %all-to-all-done.1 = bf16[384,4,384]{0,2,1:T(8,128)(2,1)S(1)} async-done(((bf16[384,4,384]{0,2,1:T(8,128)(2,1)}), bf16[384,4,384]{0,2,1:T(8,128)(2,1)S(1)}, u32[]{:S(2)}, u32[]{:S(2)}) %all-to-all-start.1) | async-done | bytes 1179680 | tf_op jit(solution)/shard_map/all_to_all | solution.py:160
  202.5 3.4 %all-to-all-start.2 = ((bf16[128,4,256]{0,2,1:T(8,128)(2,1)}), bf16[128,4,256]{0,2,1:T(8,128)(2,1)S(1)}, u32[]{:S(2)}, u32[]{:S(2)}) async-start(bf16[128,4,256]{0,2,1:T(8,128)(2,1)} %constant_dynamic-slice_fusion.2), calls=%async_computation.3 | async-start | bytes 524288 | tf_op jit(solution)/shard_map/all_to_all | solution.py:160
  208.9 5.5 %all-to-all-done.2 = bf16[128,4,256]{0,2,1:T(8,128)(2,1)S(1)} async-done(((bf16[128,4,256]{0,2,1:T(8,128)(2,1)}), bf16[128,4,256]{0,2,1:T(8,128)(2,1)S(1)}, u32[]{:S(2)}, u32[]{:S(2)}) %all-to-all-start.2) | async-done | bytes 262176 | tf_op jit(solution)/shard_map/all_to_all | solution.py:160
  214.3 3.6 %all-to-all-start = ((bf16[128,4,256]{0,2,1:T(8,128)(2,1)}), bf16[128,4,256]{0,2,1:T(8,128)(2,1)S(1)}, u32[]{:S(2)}, u32[]{:S(2)}) async-start(bf16[128,4,256]{0,2,1:T(8,128)(2,1)} %constant_dynamic-slice_fusion.1), calls=%async_computation.1 | async-start | bytes 524288 | tf_op jit(solution)/shard_map/all_to_all | solution.py:160
  218.1 6.6 %all-to-all-done = bf16[128,4,256]{0,2,1:T(8,128)(2,1)S(1)} async-done(((bf16[128,4,256]{0,2,1:T(8,128)(2,1)}), bf16[128,4,256]{0,2,1:T(8,128)(2,1)S(1)}, u32[]{:S(2)}, u32[]{:S(2)}) %all-to-all-start) | async-done | bytes 262176 | tf_op jit(solution)/shard_map/all_to_all | solution.py:160
  229.6 2.8 copy.66
  232.6 2.8 fusion
  238.7 2.0 convolution_convert_fusion
  242.5 2.3 fusion.16
  253.7 4.1 %all-to-all-start.3 = ((bf16[1024,2,128]{2,1,0:T(2,128)(2,1)}), bf16[1024,2,128]{2,1,0:T(2,128)(2,1)}, u32[]{:S(2)}, u32[]{:S(2)}) async-start(bf16[1024,2,128]{2,1,0:T(2,128)(2,1)} %copy.75), calls=%async_computation.4 | async-start | bytes 1048576 | tf_op jit(solution)/shard_map/all_to_all | solution.py:210
  257.8 2.1 fusion.18
  264.2 8.7 %all-to-all-done.3 = bf16[1024,2,128]{2,1,0:T(2,128)(2,1)} async-done(((bf16[1024,2,128]{2,1,0:T(2,128)(2,1)}), bf16[1024,2,128]{2,1,0:T(2,128)(2,1)}, u32[]{:S(2)}, u32[]{:S(2)}) %all-to-all-start.3) | async-done | bytes 524320 | tf_op jit(solution)/shard_map/all_to_all | solution.py:210
  272.9 16.6 %all_to_all.75 = bf16[1024,2,128]{2,1,0:T(2,128)(2,1)S(1)} all-to-all(bf16[1024,2,128]{2,1,0:T(2,128)(2,1)S(1)} %copy.77), channel_id=1, replica_groups=mesh['seq'=4,'tp'=4,'dp'=2] {'seq'}, dimensions={0} | all-to-all | bytes 1048576 | tf_op jit(solution)/shard_map/all_to_all | solution.py:210
  289.5 2.1 pad_maximum_fusion.1
  (117 shorter events, 38.5 us)
Async XLA Ops:
  6.5 1.9 copy-start.9
  6.5 79.8 %all-gather.7.cloned.1.call-start = ((), (), s32[]{:S(2)}) async-start(), calls=%async_computation.6 | async-start | bytes 4730880 | tf_op jit(solution)/shard_map/all_gather | solution.py:110
  8.4 13.1 %copy-start.14 = (s32[256]{0:T(256)S(1)}, s32[256]{0:T(256)}, u32[]{:S(2)}) copy-start(s32[256]{0:T(256)} %param.19) | copy-start | bytes 3076
  8.4 24.8 %copy-start.11 = (f32[1792]{0:T(1024)S(1)}, f32[1792]{0:T(1024)}, u32[]{:S(2)}) copy-start(f32[1792]{0:T(1024)} %param.11) | copy-start | bytes 21508
  9.5 123.7 %reduce-scatter.2.cloned.1.call-start = ((), (), s32[]{:S(2)}) async-start(), calls=%async_computation.7 | async-start | bytes 2785280 | tf_op jit(solution)/shard_map/reduce_scatter | solution.py:127
  86.4 6.9 %collective-permute-start = (bf16[896,2112]{0,1:T(8,128)(2,1)}, bf16[896,2112]{0,1:T(8,128)(2,1)}, u32[]{:S(2)}, u32[]{:S(2)}) collective-permute-start(bf16[896,2112]{0,1:T(8,128)(2,1)} %all-gather.7.cloned.1.call-done), channel_id=1, source_target_pairs={{0,1},{1,0},{2,3},{3,2},{4,5},{5,4},{6,7},{7,6},{8,9},{9,8},{10,11... | collective-permute-start | bytes 11354120 | tf_op jit(solution)/shard_map/ppermute | solution.py:119
  98.2 37.8 %copy-start.13 = (f32[512]{0:T(512)S(1)}, f32[512]{0:T(512)}, u32[]{:S(2)}) copy-start(f32[512]{0:T(512)} %param.15) | copy-start | bytes 6148
  98.2 68.2 %all-gather.9.cloned.1.call-start = ((), (), s32[]{:S(2)}) async-start(), calls=%async_computation.8 | async-start | bytes 1392640 | tf_op jit(solution)/shard_map/all_gather | solution.py:144
  137.2 92.4 %all-gather.11.cloned.1.call-start = ((), (), s32[]{:S(2)}) async-start(), calls=%async_computation.9 | async-start | bytes 5570560 | tf_op jit(solution)/shard_map/all_gather | solution.py:145
  169.5 4.7 %copy-start.8 = (bf16[128,2048]{1,0:T(8,128)(2,1)S(1)}, bf16[128,2048]{1,0:T(8,128)(2,1)}, u32[]{:S(2)}) copy-start(bf16[128,2048]{1,0:T(8,128)(2,1)} %param.17) | copy-start | bytes 1572868
  170.7 31.8 %all-to-all-start.1 = ((bf16[384,4,384]{0,2,1:T(8,128)(2,1)}), bf16[384,4,384]{0,2,1:T(8,128)(2,1)S(1)}, u32[]{:S(2)}, u32[]{:S(2)}) async-start(bf16[384,4,384]{0,2,1:T(8,128)(2,1)} %constant_dynamic-slice_fusion), calls=%async_computation.2 | async-start | bytes 2359296 | tf_op jit(solution)/shard_map/all_to_all | solution.py:160
  202.5 11.8 %all-to-all-start.2 = ((bf16[128,4,256]{0,2,1:T(8,128)(2,1)}), bf16[128,4,256]{0,2,1:T(8,128)(2,1)S(1)}, u32[]{:S(2)}, u32[]{:S(2)}) async-start(bf16[128,4,256]{0,2,1:T(8,128)(2,1)} %constant_dynamic-slice_fusion.2), calls=%async_computation.3 | async-start | bytes 524288 | tf_op jit(solution)/shard_map/all_to_all | solution.py:160
  206.7 19.8 %collective-permute-start.2 = (bf16[1536,384]{1,0:T(8,128)(2,1)S(1)}, bf16[1536,384]{1,0:T(8,128)(2,1)S(1)}, u32[]{:S(2)}, u32[]{:S(2)}) collective-permute-start(bf16[1536,384]{1,0:T(8,128)(2,1)S(1)} %bitcast.75), channel_id=1, source_target_pairs={{0,1},{1,0},{2,3},{3,2},{4,5},{5,4},{6,7},{7,6},{8,9},{9,8},{10,11... | collective-permute-start | bytes 3538952 | tf_op jit(solution)/shard_map/ppermute | solution.py:165
  214.3 10.4 %all-to-all-start = ((bf16[128,4,256]{0,2,1:T(8,128)(2,1)}), bf16[128,4,256]{0,2,1:T(8,128)(2,1)S(1)}, u32[]{:S(2)}, u32[]{:S(2)}) async-start(bf16[128,4,256]{0,2,1:T(8,128)(2,1)} %constant_dynamic-slice_fusion.1), calls=%async_computation.1 | async-start | bytes 524288 | tf_op jit(solution)/shard_map/all_to_all | solution.py:160
  218.1 7.0 %collective-permute-start.3 = (bf16[512,256]{1,0:T(8,128)(2,1)S(1)}, bf16[512,256]{1,0:T(8,128)(2,1)S(1)}, u32[]{:S(2)}, u32[]{:S(2)}) collective-permute-start(bf16[512,256]{1,0:T(8,128)(2,1)S(1)} %bitcast.89), channel_id=1, source_target_pairs={{0,1},{1,0},{2,3},{3,2},{4,5},{5,4},{6,7},{7,6},{8,9},{9,8},{10,11... | collective-permute-start | bytes 786440 | tf_op jit(solution)/shard_map/ppermute | solution.py:165
  224.9 1.6 collective-permute-start.1
  229.2 17.6 %copy-start.6 = (pred[512,512]{0,1:T(8,128)(4,1)}, pred[512,512]{0,1:T(8,128)(4,1)S(1)}, u32[]{:S(2)}) copy-start(pred[512,512]{0,1:T(8,128)(4,1)S(1)} %compare_and_fusion.1) | copy-start | bytes 786436
  229.6 2.8 copy-start.4
  229.6 3.0 copy-start.5
  232.4 2.9 copy-start
  235.4 1.7 copy-start.3
  246.8 2.6 copy-start.15
  253.7 19.3 %all-to-all-start.3 = ((bf16[1024,2,128]{2,1,0:T(2,128)(2,1)}), bf16[1024,2,128]{2,1,0:T(2,128)(2,1)}, u32[]{:S(2)}, u32[]{:S(2)}) async-start(bf16[1024,2,128]{2,1,0:T(2,128)(2,1)} %copy.75), calls=%async_computation.4 | async-start | bytes 1048576 | tf_op jit(solution)/shard_map/all_to_all | solution.py:210
  259.9 1.9 copy-start.16
  (5 other events, 7.9 us)
Sparse Core Ops, SparseCore 0:
  9.6 76.7 all-gather.6
  98.3 34.8 reduce-scatter.1
  137.3 29.0 all-gather.8
  168.1 54.1 all-gather.10

commit v4 on v3

--- a/solution.py
+++ b/solution.py
@@ -67,6 +67,22 @@
         )
         results.append((weighted / jnp.transpose(denominator)[:, :, None]).astype(jnp.bfloat16))
     return jnp.concatenate(results, 0)
+
+
+def shifted(values, axis_name, count, shift):
+    return lax.ppermute(values, axis_name, perm=[(i, (i + shift) % count) for i in range(count)])
+
+
+def gather_chunks(chunk, seq_index, seq_count, tp_index, tp_count):
+    from_seq = [chunk] + [shifted(chunk, "seq", seq_count, k) for k in range(1, seq_count)]
+    plane = jnp.stack(from_seq)
+    grid = [plane] + [shifted(plane, "tp", tp_count, k) for k in range(1, tp_count)]
+    grid = jnp.stack(grid, 1)
+    seq_order = (seq_index - jnp.arange(seq_count)) % seq_count
+    tp_order = (tp_index - jnp.arange(tp_count)) % tp_count
+    grid = jnp.take(grid, seq_order, axis=0)
+    grid = jnp.take(grid, tp_order, axis=1)
+    return grid.reshape(seq_count * tp_count * chunk.shape[0], chunk.shape[1])
 
 
 def body(
@@ -141,9 +157,7 @@
     compressed_memory = rms_scale(memory_sums[:, :KVRANK], memory_gain).astype(jnp.bfloat16)
     key_rope = rotate(memory_sums[:, KVRANK:], chunk_position).astype(jnp.bfloat16)
     packed = jnp.concatenate([compressed_query, compressed_memory, key_rope], 1)
-    packed = lax.all_gather(packed, "seq", axis=0, tiled=False)
-    packed = lax.all_gather(packed, "tp", axis=0, tiled=False)
-    latent = jnp.transpose(packed, (1, 0, 2, 3)).reshape(total_rows, packed.shape[-1])
+    latent = gather_chunks(packed, seq_index, seq_count, tp_index, tp_count)
     cq_all = latent[:, :qrank]
     cm_all = latent[:, qrank : qrank + KVRANK]
     rope_all = latent[:, qrank + KVRANK :]

time: 301 us -> 326 us (1.083)
  local copies, waits for them, and re-layouts: 23.8 us -> 38.6 us
  waiting for transfers between devices: 169 us -> 156 us
  other arithmetic: 14.3 us -> 26 us
  starting transfers between devices: 15 us -> 26.2 us
    ppermute x0 -> x6, waiting for transfers between devices: none -> 60.1 us  [shifted(): lax.ppermute(values, axis_name, perm=[(i, (i + shift) % count) for i in r...]
    reduce_scatter x1, waiting for transfers between devices: 34.6 us -> 0.01 us  [body(): lax.psum_scatter(partial, 'tp', scatter_dimension=0, tiled=True)]
    all_gather x2 -> x0, waiting for transfers between devices: 29.2 us -> none  [the longest x1 29.2 us: body(): packed = lax.all_gather(packed, 'seq', axis=0, tiled=False)]
    gather x0 -> x3, local copies, waits for them, and re-layouts: none -> 13.3 us  [the longest x2 7.96 us: gather_chunks(): grid = jnp.take(grid, tp_order, axis=1)]
    ppermute x0 -> x6, starting transfers between devices: none -> 7.46 us  [shifted(): lax.ppermute(values, axis_name, perm=[(i, (i + shift) % count) for i in r...]
    all_to_all x3, waiting for transfers between devices: 39.4 us -> 33.4 us  [head_columns(): own = lax.all_to_all(own, 'seq', split_axis=1, concat_axis=0, tiled=True)]
    select_n x0 -> x4, other arithmetic: none -> 5.81 us  [the longest x2 4.85 us: gather_chunks(): grid = jnp.take(grid, seq_order, axis=0)]
    all_to_all x1, starting transfers between devices: 4.13 us -> 7.81 us  [body(): lax.all_to_all(head_output, 'seq', split_axis=0, concat_axis=1, tiled=True)]
  transfers between devices with their start and end apart: 12 -> 16, of which waited for: 9 -> 11; matrix products, arithmetic and copies ran while one was open for 7% -> 10% of each run, Pallas kernels for 0% -> 0%
where the time goes in v4:
time: 326 us; the launch traced here: 325 us
  waiting for transfers between devices  156 us (48%)
  blocking collectives  40.8 us (13%)
  local copies, waits for them, and re-layouts  38.6 us (12%)
  starting transfers between devices  26.2 us (8%)
  other arithmetic  26 us (8%)
  matrix products  23.6 us (7%)
  between operations  14.1 us (4%)
    ppermute x6, waiting for transfers between devices, shifted(): lax.ppermute(values, axis_name, perm=[(i, (i + shift) % count) for i in r...  60.1 us
    all_gather x1, waiting for transfers between devices, body(): own_all = lax.all_gather(own_rows, 'seq', axis=1, tiled=True)  52.8 us
    all_to_all x3, waiting for transfers between devices, head_columns(): own = lax.all_to_all(own, 'seq', split_axis=1, concat_axis=0, tiled=True)  33.4 us
    all_to_all x1, blocking collectives, body(): lax.all_to_all(head_output, 'seq', split_axis=0, concat_axis=1, tiled=True)  17.7 us
    all_gather x1, blocking collectives, body(): group_ids = lax.all_gather(segment_ids, 'seq', axis=0, tiled=True)  11.7 us
    psum x1, blocking collectives, body(): square_sums = lax.psum(jnp.sum(inputs * inputs, 1), 'tp')  11.4 us
    unnamed x58, local copies, waits for them, and re-layouts  11.4 us
    all_to_all x3, starting transfers between devices, head_columns(): own = lax.all_to_all(own, 'seq', split_axis=1, concat_axis=0, tiled=True)  10.3 us
  transfers between devices with their start and end apart: 16, of which 11 were waited for; matrix products, arithmetic and copies ran while one was open for 10% of the time, Pallas kernels for 0%

profile of v4, /device:TPU:0, one launch (start us, length us, event | category | flops | bytes accessed | tf_op | source)
XLA Modules:
  0.0 325.1 jit_solution(8680553785938687881)
XLA Ops:
  10.2 11.4 %psum.7 = f32[256]{0:T(256)S(1)} all-reduce(f32[256]{0:T(256)S(1)} %fusion.13), channel_id=1, replica_groups=mesh['seq'=4,'tp'=4,'dp'=2] {'tp'}, use_global_device_ids=true, to_apply=%region_1.0 | all-reduce | flops 256 | bytes 2048 | tf_op jit(solution)/shard_map/psum | solution.py:116
  21.6 11.7 %all-gather = s32[4,1,256]{2,1,0:T(1,128)S(1)} all-gather(s32[1,1,256]{2,1,0:T(1,128)S(1)} %bitcast.112), channel_id=1, replica_groups=mesh['seq'=4,'tp'=4,'dp'=2] {'seq'}, dimensions={0}, use_global_device_ids=true | all-gather | bytes 5120 | tf_op jit(solution)/shard_map/all_gather | solution.py:113
  33.5 52.8 %all-gather.3.cloned.1.call-done = bf16[896,2112]{0,1:T(8,128)(2,1)} async-done(((bf16[896,528]{0,1:T(8,128)(2,1)}), bf16[896,2112]{0,1:T(8,128)(2,1)}) %all-gather.3.cloned.1.call-update) | async-done | bytes 3784720 | tf_op jit(solution)/shard_map/all_gather | solution.py:126
  86.4 3.5 %fusion.73 = f32[256,2112]{1,0:T(8,128)S(1)} fusion(bf16[896,2112]{0,1:T(8,128)(2,1)} %all-gather.3.cloned.1.call-done, bf16[256,1792]{1,0:T(8,128)(2,1)S(1)} %fusion.15, s32[]{:T(128)S(6)} %select_n.170), kind=kOutput, calls=%fused_computation.97 | convolution fusion | flops 968884224 | bytes 6406148 | tf_op jit(solution)/shard_map/dot_general | solution.py:128
  89.8 3.4 %collective-permute-done = bf16[896,2112]{0,1:T(8,128)(2,1)} collective-permute-done((bf16[896,2112]{0,1:T(8,128)(2,1)}, bf16[896,2112]{0,1:T(8,128)(2,1)}, u32[]{:S(2)}, u32[]{:S(2)}) %collective-permute-start) | collective-permute-done | bytes 3784736 | tf_op jit(solution)/shard_map/ppermute | solution.py:135
  93.3 4.9 %convolution_add_fusion = f32[256,2112]{1,0:T(8,128)} fusion(f32[256,2112]{1,0:T(8,128)S(1)} %fusion.73, bf16[896,2112]{0,1:T(8,128)(2,1)} %collective-permute-done, bf16[256,1792]{1,0:T(8,128)(2,1)S(1)} %fusion.15, s32[]{:T(128)S(6)} %select_n.172), kind=kOutput, calls=%fused_computation.5 | convolution fusion | flops 969424896 | bytes 8634372 | tf_op jit(solution)/shard_map/dot_general | solution.py:138
  100.2 3.4 %all-to-all-start.2 = ((bf16[128,4,256]{0,2,1:T(8,128)(2,1)}), bf16[128,4,256]{0,2,1:T(8,128)(2,1)S(1)}, u32[]{:S(2)}, u32[]{:S(2)}) async-start(bf16[128,4,256]{0,2,1:T(8,128)(2,1)} %constant_dynamic-slice_fusion.2), calls=%async_computation.3 | async-start | bytes 524288 | tf_op jit(solution)/shard_map/all_to_all | solution.py:174
  104.6 8.4 %all-to-all-done.2 = bf16[128,4,256]{0,2,1:T(8,128)(2,1)S(1)} async-done(((bf16[128,4,256]{0,2,1:T(8,128)(2,1)}), bf16[128,4,256]{0,2,1:T(8,128)(2,1)S(1)}, u32[]{:S(2)}, u32[]{:S(2)}) %all-to-all-start.2) | async-done | bytes 262176 | tf_op jit(solution)/shard_map/all_to_all | solution.py:174
  113.0 3.4 %all-to-all-start = ((bf16[128,4,256]{0,2,1:T(8,128)(2,1)}), bf16[128,4,256]{0,2,1:T(8,128)(2,1)S(1)}, u32[]{:S(2)}, u32[]{:S(2)}) async-start(bf16[128,4,256]{0,2,1:T(8,128)(2,1)} %constant_dynamic-slice_fusion.1), calls=%async_computation.1 | async-start | bytes 524288 | tf_op jit(solution)/shard_map/all_to_all | solution.py:174
  116.4 3.0 copy.69
  120.6 2.8 all-to-all-done
  123.4 3.5 %all-to-all-start.1 = ((bf16[384,4,384]{0,2,1:T(8,128)(2,1)}), bf16[384,4,384]{0,2,1:T(8,128)(2,1)S(1)}, u32[]{:S(2)}, u32[]{:S(2)}) async-start(bf16[384,4,384]{0,2,1:T(8,128)(2,1)} %constant_dynamic-slice_fusion), calls=%async_computation.2 | async-start | bytes 2359296 | tf_op jit(solution)/shard_map/all_to_all | solution.py:174
  130.5 22.2 %all-to-all-done.1 = bf16[384,4,384]{0,2,1:T(8,128)(2,1)S(1)} async-done(((bf16[384,4,384]{0,2,1:T(8,128)(2,1)}), bf16[384,4,384]{0,2,1:T(8,128)(2,1)S(1)}, u32[]{:S(2)}, u32[]{:S(2)}) %all-to-all-start.1) | async-done | bytes 1179680 | tf_op jit(solution)/shard_map/all_to_all | solution.py:174
  166.4 3.9 %collective-permute-done.1 = bf16[64,2112]{1,0:T(8,128)(2,1)S(1)} collective-permute-done((bf16[64,2112]{1,0:T(8,128)(2,1)S(1)}, bf16[64,2112]{1,0:T(8,128)(2,1)S(1)}, u32[]{:S(2)}, u32[]{:S(2)}) %collective-permute-start.1) | collective-permute-done | bytes 270368 | tf_op jit(solution)/shard_map/ppermute | solution.py:73
  170.4 11.0 %collective-permute-done.2 = bf16[64,2112]{1,0:T(8,128)(2,1)S(1)} collective-permute-done((bf16[64,2112]{1,0:T(8,128)(2,1)S(1)}, bf16[64,2112]{1,0:T(8,128)(2,1)S(1)}, u32[]{:S(2)}, u32[]{:S(2)}) %collective-permute-start.2) | collective-permute-done | bytes 270368 | tf_op jit(solution)/shard_map/ppermute | solution.py:73
  188.1 20.9 %collective-permute-done.6 = bf16[4,64,2112]{2,1,0:T(8,128)(2,1)S(1)} collective-permute-done((bf16[4,64,2112]{2,1,0:T(8,128)(2,1)S(1)}, bf16[4,64,2112]{2,1,0:T(8,128)(2,1)S(1)}, u32[]{:S(2)}, u32[]{:S(2)}) %collective-permute-start.6) | collective-permute-done | bytes 1081376 | tf_op jit(solution)/shard_map/ppermute | solution.py:73
  209.1 23.1 %collective-permute-done.4 = bf16[4,64,2112]{2,1,0:T(8,128)(2,1)S(1)} collective-permute-done((bf16[4,64,2112]{2,1,0:T(8,128)(2,1)S(1)}, bf16[4,64,2112]{2,1,0:T(8,128)(2,1)S(1)}, u32[]{:S(2)}, u32[]{:S(2)}) %collective-permute-start.4) | collective-permute-done | bytes 1081376 | tf_op jit(solution)/shard_map/ppermute | solution.py:73
  235.8 5.3 %gather_fusion = bf16[4,4,64,2112]{3,2,1,0:T(8,128)(2,1)} fusion(bf16[4,4,64,2112]{3,2,0,1:T(8,128)(2,1)} %pad_maximum_fusion, s32[1024]{0:T(1024)S(1)} %pad_clamp_fusion.1), kind=kCustom, calls=%fused_computation | custom fusion | bytes 8650768 | tf_op jit(solution)/shard_map/jit(_take)/gather | solution.py:83
  241.1 4.8 %broadcast_select_fusion = bf16[4,4,64,2112]{3,2,1,0:T(8,128)(2,1)} fusion(bf16[4,4,64,2112]{3,2,1,0:T(8,128)(2,1)} %gather_fusion, pred[4]{0:T(512)(128)(4,1)S(1)} %copy-done.20), kind=kLoop, calls=%fused_computation.4 | loop fusion | flops 2162688 | bytes 8650756 | tf_op jit(solution)/shard_map/jit(_take)/select_n | solution.py:83
  245.9 5.3 %gather_fusion.1 = bf16[4,4,64,2112]{3,2,1,0:T(8,128)(2,1)} fusion(bf16[4,4,64,2112]{3,2,1,0:T(8,128)(2,1)} %broadcast_select_fusion, s32[1024]{0:T(1024)S(1)} %pad_clamp_fusion), kind=kCustom, calls=%fused_computation.1 | custom fusion | bytes 8650768 | tf_op jit(solution)/shard_map/jit(_take)/gather | solution.py:84
  255.6 2.8 fusion
  276.2 7.8 %all-to-all-start.3 = ((bf16[1024,2,128]{2,1,0:T(2,128)(2,1)}), bf16[1024,2,128]{2,1,0:T(2,128)(2,1)}, u32[]{:S(2)}, u32[]{:S(2)}) async-start(bf16[1024,2,128]{2,1,0:T(2,128)(2,1)} %copy.75), calls=%async_computation.4 | async-start | bytes 1048576 | tf_op jit(solution)/shard_map/all_to_all | solution.py:224
  290.5 5.9 %all-to-all-done.3 = bf16[1024,2,128]{2,1,0:T(2,128)(2,1)} async-done(((bf16[1024,2,128]{2,1,0:T(2,128)(2,1)}), bf16[1024,2,128]{2,1,0:T(2,128)(2,1)}, u32[]{:S(2)}, u32[]{:S(2)}) %all-to-all-start.3) | async-done | bytes 524320 | tf_op jit(solution)/shard_map/all_to_all | solution.py:224
  296.4 17.7 %all_to_all.75 = bf16[1024,2,128]{2,1,0:T(2,128)(2,1)S(1)} all-to-all(bf16[1024,2,128]{2,1,0:T(2,128)(2,1)S(1)} %copy.77), channel_id=1, replica_groups=mesh['seq'=4,'tp'=4,'dp'=2] {'seq'}, dimensions={0} | all-to-all | bytes 1048576 | tf_op jit(solution)/shard_map/all_to_all | solution.py:224
  (157 shorter events, 67.8 us)
Async XLA Ops:
  6.5 79.8 %all-gather.3.cloned.1.call-start = ((), (), s32[]{:S(2)}) async-start(), calls=%async_computation.6 | async-start | bytes 4730880 | tf_op jit(solution)/shard_map/all_gather | solution.py:126
  8.4 13.1 %copy-start.21 = (s32[256]{0:T(256)S(1)}, s32[256]{0:T(256)}, u32[]{:S(2)}) copy-start(s32[256]{0:T(256)} %param.19) | copy-start | bytes 3076
  8.4 24.8 %copy-start.16 = (f32[1792]{0:T(1024)S(1)}, f32[1792]{0:T(1024)}, u32[]{:S(2)}) copy-start(f32[1792]{0:T(1024)} %param.11) | copy-start | bytes 21508
  9.5 144.4 %reduce-scatter.2.cloned.1.call-start = ((), (), s32[]{:S(2)}) async-start(), calls=%async_computation.7 | async-start | bytes 2785280 | tf_op jit(solution)/shard_map/reduce_scatter | solution.py:143
  86.4 6.9 %collective-permute-start = (bf16[896,2112]{0,1:T(8,128)(2,1)}, bf16[896,2112]{0,1:T(8,128)(2,1)}, u32[]{:S(2)}, u32[]{:S(2)}) collective-permute-start(bf16[896,2112]{0,1:T(8,128)(2,1)} %all-gather.3.cloned.1.call-done), channel_id=1, source_target_pairs={{0,1},{1,0},{2,3},{3,2},{4,5},{5,4},{6,7},{7,6},{8,9},{9,8},{10,11... | collective-permute-start | bytes 11354120 | tf_op jit(solution)/shard_map/ppermute | solution.py:135
  98.2 5.5 %copy-start.9 = (bf16[128,2048]{1,0:T(8,128)(2,1)S(1)}, bf16[128,2048]{1,0:T(8,128)(2,1)}, u32[]{:S(2)}) copy-start(bf16[128,2048]{1,0:T(8,128)(2,1)} %param.18) | copy-start | bytes 1572868
  100.2 12.8 %all-to-all-start.2 = ((bf16[128,4,256]{0,2,1:T(8,128)(2,1)}), bf16[128,4,256]{0,2,1:T(8,128)(2,1)S(1)}, u32[]{:S(2)}, u32[]{:S(2)}) async-start(bf16[128,4,256]{0,2,1:T(8,128)(2,1)} %constant_dynamic-slice_fusion.2), calls=%async_computation.3 | async-start | bytes 524288 | tf_op jit(solution)/shard_map/all_to_all | solution.py:174
  113.0 10.4 %all-to-all-start = ((bf16[128,4,256]{0,2,1:T(8,128)(2,1)}), bf16[128,4,256]{0,2,1:T(8,128)(2,1)S(1)}, u32[]{:S(2)}, u32[]{:S(2)}) async-start(bf16[128,4,256]{0,2,1:T(8,128)(2,1)} %constant_dynamic-slice_fusion.1), calls=%async_computation.1 | async-start | bytes 524288 | tf_op jit(solution)/shard_map/all_to_all | solution.py:174
  123.4 29.3 %all-to-all-start.1 = ((bf16[384,4,384]{0,2,1:T(8,128)(2,1)}), bf16[384,4,384]{0,2,1:T(8,128)(2,1)S(1)}, u32[]{:S(2)}, u32[]{:S(2)}) async-start(bf16[384,4,384]{0,2,1:T(8,128)(2,1)} %constant_dynamic-slice_fusion), calls=%async_computation.2 | async-start | bytes 2359296 | tf_op jit(solution)/shard_map/all_to_all | solution.py:174
  128.2 27.2 %copy-start.15 = (s32[1024]{0:T(1024)}, s32[1024]{0:T(1024)S(1)}, u32[]{:S(2)}) copy-start(s32[1024]{0:T(1024)S(1)} %iota.46) | copy-start | bytes 12292
  129.2 31.8 %collective-permute-start.9 = (bf16[512,256]{1,0:T(8,128)(2,1)}, bf16[512,256]{1,0:T(8,128)(2,1)}, u32[]{:S(2)}, u32[]{:S(2)}) collective-permute-start(bf16[512,256]{1,0:T(8,128)(2,1)} %bitcast.28), channel_id=1, source_target_pairs={{0,1},{1,0},{2,3},{3,2},{4,5},{5,4},{6,7},{7,6},{8,9},{9,8},{10,11... | collective-permute-start | bytes 786440 | tf_op jit(solution)/shard_map/ppermute | solution.py:179
  130.0 34.6 %collective-permute-start.7 = (bf16[512,256]{1,0:T(8,128)(2,1)}, bf16[512,256]{1,0:T(8,128)(2,1)}, u32[]{:S(2)}, u32[]{:S(2)}) collective-permute-start(bf16[512,256]{1,0:T(8,128)(2,1)} %bitcast.18), channel_id=1, source_target_pairs={{0,1},{1,0},{2,3},{3,2},{4,5},{5,4},{6,7},{7,6},{8,9},{9,8},{10,11... | collective-permute-start | bytes 786440 | tf_op jit(solution)/shard_map/ppermute | solution.py:179
  153.5 4.5 %copy-start.17 = (f32[1536]{0:T(1024)S(1)}, f32[1536]{0:T(1024)}, u32[]{:S(2)}) copy-start(f32[1536]{0:T(1024)} %param.14) | copy-start | bytes 18436
  153.5 31.6 %collective-permute-start.8 = (bf16[1536,384]{1,0:T(8,128)(2,1)S(1)}, bf16[1536,384]{1,0:T(8,128)(2,1)S(1)}, u32[]{:S(2)}, u32[]{:S(2)}) collective-permute-start(bf16[1536,384]{1,0:T(8,128)(2,1)S(1)} %bitcast.85), channel_id=1, source_target_pairs={{0,1},{1,0},{2,3},{3,2},{4,5},{5,4},{6,7},{7,6},{8,9},{9,8},{10,11... | collective-permute-start | bytes 3538952 | tf_op jit(solution)/shard_map/ppermute | solution.py:179
  158.8 11.5 %collective-permute-start.1 = (bf16[64,2112]{1,0:T(8,128)(2,1)S(1)}, bf16[64,2112]{1,0:T(8,128)(2,1)S(1)}, u32[]{:S(2)}, u32[]{:S(2)}) collective-permute-start(bf16[64,2112]{1,0:T(8,128)(2,1)S(1)} %concatenate.35), channel_id=1, source_target_pairs={{0,8},{8,16},{16,24},{24,0},{1,9},{9,17},{17,25},{25,1},{2,10},{10... | collective-permute-start | bytes 811016 | tf_op jit(solution)/shard_map/ppermute | solution.py:73
  158.9 22.5 %collective-permute-start.2 = (bf16[64,2112]{1,0:T(8,128)(2,1)S(1)}, bf16[64,2112]{1,0:T(8,128)(2,1)S(1)}, u32[]{:S(2)}, u32[]{:S(2)}) collective-permute-start(bf16[64,2112]{1,0:T(8,128)(2,1)S(1)} %concatenate.35), channel_id=1, source_target_pairs={{0,16},{8,24},{16,0},{24,8},{1,17},{9,25},{17,1},{25,9},{2,18},{10... | collective-permute-start | bytes 811016 | tf_op jit(solution)/shard_map/ppermute | solution.py:73
  160.9 20.5 %collective-permute-start.3 = (bf16[64,2112]{1,0:T(8,128)(2,1)S(1)}, bf16[64,2112]{1,0:T(8,128)(2,1)S(1)}, u32[]{:S(2)}, u32[]{:S(2)}) collective-permute-start(bf16[64,2112]{1,0:T(8,128)(2,1)S(1)} %concatenate.35), channel_id=1, source_target_pairs={{0,24},{8,0},{16,8},{24,16},{1,25},{9,1},{17,9},{25,17},{2,26},{10... | collective-permute-start | bytes 811016 | tf_op jit(solution)/shard_map/ppermute | solution.py:73
  181.6 5.9 %slice-start.3 = ((s32[1024]{0:T(1024)}), s32[512]{0:T(512)S(1)}, s32[]{:S(2)}) async-start(s32[1024]{0:T(1024)} %copy-done.15), calls=%async_computation.11 | async-start | bytes 4096 | tf_op jit(solution)/shard_map/slice | solution.py:58
  181.6 27.5 %collective-permute-start.6 = (bf16[4,64,2112]{2,1,0:T(8,128)(2,1)S(1)}, bf16[4,64,2112]{2,1,0:T(8,128)(2,1)S(1)}, u32[]{:S(2)}, u32[]{:S(2)}) collective-permute-start(bf16[4,64,2112]{2,1,0:T(8,128)(2,1)S(1)} %get-tuple-element.20), channel_id=1, source_target_pairs={{0,6},{2,0},{4,2},{6,4},{1,7},{3,1},{5,3},{7,5},{8,14},{10,8},{12,... | collective-permute-start | bytes 3244040 | tf_op jit(solution)/shard_map/ppermute | solution.py:73
  184.1 48.1 %collective-permute-start.4 = (bf16[4,64,2112]{2,1,0:T(8,128)(2,1)S(1)}, bf16[4,64,2112]{2,1,0:T(8,128)(2,1)S(1)}, u32[]{:S(2)}, u32[]{:S(2)}) collective-permute-start(bf16[4,64,2112]{2,1,0:T(8,128)(2,1)S(1)} %get-tuple-element.20), channel_id=1, source_target_pairs={{0,2},{2,4},{4,6},{6,0},{1,3},{3,5},{5,7},{7,1},{8,10},{10,12},{12... | collective-permute-start | bytes 3244040 | tf_op jit(solution)/shard_map/ppermute | solution.py:73
  184.1 49.2 %collective-permute-start.5 = (bf16[4,64,2112]{2,1,0:T(8,128)(2,1)S(1)}, bf16[4,64,2112]{2,1,0:T(8,128)(2,1)S(1)}, u32[]{:S(2)}, u32[]{:S(2)}) collective-permute-start(bf16[4,64,2112]{2,1,0:T(8,128)(2,1)S(1)} %get-tuple-element.20), channel_id=1, source_target_pairs={{0,4},{2,6},{4,0},{6,2},{1,5},{3,7},{5,1},{7,3},{8,12},{10,14},{12... | collective-permute-start | bytes 3244040 | tf_op jit(solution)/shard_map/ppermute | solution.py:73
  187.7 81.6 %copy-start.6 = (pred[512,512]{0,1:T(8,128)(4,1)}, pred[512,512]{0,1:T(8,128)(4,1)S(1)}, u32[]{:S(2)}) copy-start(pred[512,512]{0,1:T(8,128)(4,1)S(1)} %compare_and_fusion.1) | copy-start | bytes 786436
  235.8 5.3 %copy-start.20 = (pred[4]{0:T(512)(128)(4,1)S(1)}, pred[4]{0:T(512)(128)(4,1)}, u32[]{:S(2)}) copy-start(pred[4]{0:T(512)(128)(4,1)} %get-tuple-element.41) | copy-start | bytes 16
  276.2 20.2 %all-to-all-start.3 = ((bf16[1024,2,128]{2,1,0:T(2,128)(2,1)}), bf16[1024,2,128]{2,1,0:T(2,128)(2,1)}, u32[]{:S(2)}, u32[]{:S(2)}) async-start(bf16[1024,2,128]{2,1,0:T(2,128)(2,1)} %copy.75), calls=%async_computation.4 | async-start | bytes 1048576 | tf_op jit(solution)/shard_map/all_to_all | solution.py:224
  (20 other events, 44.6 us)
Sparse Core Ops, SparseCore 0:
  9.6 76.7 all-gather.2
  98.3 34.8 reduce-scatter.1

commit v5 on v4

--- a/solution.py
+++ b/solution.py
@@ -77,11 +77,12 @@
     from_seq = [chunk] + [shifted(chunk, "seq", seq_count, k) for k in range(1, seq_count)]
     plane = jnp.stack(from_seq)
     grid = [plane] + [shifted(plane, "tp", tp_count, k) for k in range(1, tp_count)]
-    grid = jnp.stack(grid, 1)
-    seq_order = (seq_index - jnp.arange(seq_count)) % seq_count
-    tp_order = (tp_index - jnp.arange(tp_count)) % tp_count
-    grid = jnp.take(grid, seq_order, axis=0)
-    grid = jnp.take(grid, tp_order, axis=1)
+    grid = jnp.stack(grid, 1).reshape(seq_count * tp_count, chunk.shape[0], chunk.shape[1])
+    source = jnp.arange(seq_count * tp_count)
+    order = ((seq_index - source // tp_count) % seq_count) * tp_count + (
+        tp_index - source % tp_count
+    ) % tp_count
+    grid = jnp.take(grid, order, axis=0)
     return grid.reshape(seq_count * tp_count * chunk.shape[0], chunk.shape[1])
 
 
@@ -140,27 +141,38 @@
             peer_all,
             preferred_element_type=jnp.float32,
         )
-    latent_rows = lax.psum_scatter(partial, "tp", scatter_dimension=0, tiled=True)
 
     token_index = jnp.arange(total_rows, dtype=jnp.int32)
     onehot = group_ids[:, None] == jnp.arange(DOCS, dtype=jnp.int32)[None, :]
     starts = jnp.min(jnp.where(onehot, token_index[:, None], total_rows), 0)
     position = token_index - jnp.sum(jnp.where(onehot, starts[None, :], 0), 1)
-    chunk = latent_rows.shape[0]
-    latent_rows = latent_rows.reshape(chunk, seq_count, qrank_piece + memory_piece)
-    query_sums = latent_rows[:, :, :qrank_piece].reshape(chunk, qrank)
-    memory_sums = latent_rows[:, :, qrank_piece:].reshape(chunk, memory_cols)
+
+    partial = partial.reshape(tok_count, seq_count, qrank_piece + memory_piece)
+    query_partial = partial[:, :, :qrank_piece].reshape(tok_count, qrank)
+    memory_partial = partial[:, :, qrank_piece:].reshape(tok_count, memory_cols)
+    chunk = tok_count // tp_count
     chunk_position = lax.dynamic_slice(
         position, (seq_index * tok_count + tp_index * chunk,), (chunk,)
     )
+
+    query_sums = lax.psum_scatter(query_partial, "tp", scatter_dimension=0, tiled=True)
     compressed_query = rms_scale(query_sums, query_gain).astype(jnp.bfloat16)
+    cq_all = lax.all_gather(compressed_query, "seq", axis=0, tiled=False)
+    cq_all = lax.all_gather(cq_all, "tp", axis=0, tiled=False)
+    cq_all = jnp.transpose(cq_all, (1, 0, 2, 3)).reshape(total_rows, qrank)
+
+    blocks = memory_partial.reshape(tp_count, chunk, memory_cols)
+    memory_sums = lax.dynamic_index_in_dim(blocks, tp_index, 0, keepdims=False)
+    for k in range(1, tp_count):
+        sent = lax.dynamic_index_in_dim(blocks, (tp_index + k) % tp_count, 0, keepdims=False)
+        memory_sums = memory_sums + shifted(sent, "tp", tp_count, k)
     compressed_memory = rms_scale(memory_sums[:, :KVRANK], memory_gain).astype(jnp.bfloat16)
     key_rope = rotate(memory_sums[:, KVRANK:], chunk_position).astype(jnp.bfloat16)
-    packed = jnp.concatenate([compressed_query, compressed_memory, key_rope], 1)
-    latent = gather_chunks(packed, seq_index, seq_count, tp_index, tp_count)
-    cq_all = latent[:, :qrank]
-    cm_all = latent[:, qrank : qrank + KVRANK]
-    rope_all = latent[:, qrank + KVRANK :]
+    memory_all = gather_chunks(
+        jnp.concatenate([compressed_memory, key_rope], 1), seq_index, seq_count, tp_index, tp_count
+    )
+    cm_all = memory_all[:, :KVRANK]
+    rope_all = memory_all[:, KVRANK:]
 
     local_heads = query_up.shape[1] // (NOPE + ROPE)
     heads = local_heads // seq_count

time: 326 us -> 325 us (level)
  waiting for transfers between devices: 156 us -> 138 us
  blocking collectives: 40.8 us -> 57.9 us
  other arithmetic: 26 us -> 20 us
  local copies, waits for them, and re-layouts: 38.6 us -> 43 us
    all_gather x0 -> x1, blocking collectives: none -> 18.4 us  [body(): cq_all = lax.all_gather(compressed_query, 'seq', axis=0, tiled=False)]
    ppermute x6 -> x9, waiting for transfers between devices: 60.1 us -> 44.7 us  [shifted(): lax.ppermute(values, axis_name, perm=[(i, (i + shift) % count) for i in r...]
    gather x3 -> x1, local copies, waits for them, and re-layouts: 13.3 us -> 2.1 us  [gather_chunks(): grid = jnp.take(grid, order, axis=0)]
    all_to_all x3, waiting for transfers between devices: 33.4 us -> 27.4 us  [head_columns(): own = lax.all_to_all(own, 'seq', split_axis=1, concat_axis=0, tiled=True)]
    select_n x4 -> x2, other arithmetic: 5.81 us -> 0.33 us  [gather_chunks(): grid = jnp.take(grid, order, axis=0)]
    all_to_all x1, starting transfers between devices: 7.81 us -> 3.69 us  [body(): lax.all_to_all(head_output, 'seq', split_axis=0, concat_axis=1, tiled=True)]
    all_to_all x1, waiting for transfers between devices: 5.94 us -> 9.75 us  [body(): lax.all_to_all(head_output, 'seq', split_axis=0, concat_axis=1, tiled=True)]
    ppermute x6 -> x9, starting transfers between devices: 7.46 us -> 11.1 us  [shifted(): lax.ppermute(values, axis_name, perm=[(i, (i + shift) % count) for i in r...]
  transfers between devices with their start and end apart: 16 -> 20, of which waited for: 11 -> 13; matrix products, arithmetic and copies ran while one was open for 10% -> 16% of each run, Pallas kernels for 0% -> 0%
where the time goes in v5:
time: 325 us; the launch traced here: 324 us
  waiting for transfers between devices  138 us (42%)
  blocking collectives  57.9 us (18%)
  local copies, waits for them, and re-layouts  43 us (13%)
  starting transfers between devices  27.9 us (9%)
  matrix products  23.1 us (7%)
  other arithmetic  20 us (6%)
  between operations  13.7 us (4%)
    all_gather x1, waiting for transfers between devices, body(): own_all = lax.all_gather(own_rows, 'seq', axis=1, tiled=True)  52.8 us
    ppermute x9, waiting for transfers between devices, shifted(): lax.ppermute(values, axis_name, perm=[(i, (i + shift) % count) for i in r...  44.7 us
    all_to_all x3, waiting for transfers between devices, head_columns(): own = lax.all_to_all(own, 'seq', split_axis=1, concat_axis=0, tiled=True)  27.4 us
    all_gather x1, blocking collectives, body(): cq_all = lax.all_gather(compressed_query, 'seq', axis=0, tiled=False)  18.4 us
    all_to_all x1, blocking collectives, body(): lax.all_to_all(head_output, 'seq', split_axis=0, concat_axis=1, tiled=True)  16.4 us
    unnamed x52, local copies, waits for them, and re-layouts  13.5 us
    all_to_all x3, starting transfers between devices, head_columns(): own = lax.all_to_all(own, 'seq', split_axis=1, concat_axis=0, tiled=True)  12.5 us
    all_gather x1, blocking collectives, body(): group_ids = lax.all_gather(segment_ids, 'seq', axis=0, tiled=True)  11.7 us
  transfers between devices with their start and end apart: 20, of which 13 were waited for; matrix products, arithmetic and copies ran while one was open for 16% of the time, Pallas kernels for 0%

profile of v5, /device:TPU:0, one launch (start us, length us, event | category | flops | bytes accessed | tf_op | source)
XLA Modules:
  0.0 323.9 jit_solution(1992948258061367824)
XLA Ops:
  10.2 11.4 %psum.7 = f32[256]{0:T(256)S(1)} all-reduce(f32[256]{0:T(256)S(1)} %fusion.8), channel_id=1, replica_groups=mesh['seq'=4,'tp'=4,'dp'=2] {'tp'}, use_global_device_ids=true, to_apply=%region_1.0 | all-reduce | flops 256 | bytes 2048 | tf_op jit(solution)/shard_map/psum | solution.py:117
  21.6 11.7 %all-gather.2 = s32[4,1,256]{2,1,0:T(1,128)S(1)} all-gather(s32[1,1,256]{2,1,0:T(1,128)S(1)} %bitcast.136), channel_id=1, replica_groups=mesh['seq'=4,'tp'=4,'dp'=2] {'seq'}, dimensions={0}, use_global_device_ids=true | all-gather | bytes 5120 | tf_op jit(solution)/shard_map/all_gather | solution.py:114
  33.5 52.8 %all-gather.6.cloned.1.call-done = bf16[896,2112]{0,1:T(8,128)(2,1)} async-done(((bf16[896,528]{0,1:T(8,128)(2,1)}), bf16[896,2112]{0,1:T(8,128)(2,1)}) %all-gather.6.cloned.1.call-update) | async-done | bytes 3784720 | tf_op jit(solution)/shard_map/all_gather | solution.py:127
  86.4 3.4 %fusion.68 = f32[256,2112]{0,1:T(8,128)S(1)} fusion(bf16[896,2112]{0,1:T(8,128)(2,1)} %all-gather.6.cloned.1.call-done, bf16[256,1792]{1,0:T(8,128)(2,1)S(1)} %fusion.10, s32[]{:T(128)S(6)} %select_n.207), kind=kOutput, calls=%fused_computation.91 | convolution fusion | flops 968884224 | bytes 6406148 | tf_op jit(solution)/shard_map/dot_general | solution.py:129
  89.8 3.5 %collective-permute-done = bf16[896,2112]{0,1:T(8,128)(2,1)} collective-permute-done((bf16[896,2112]{0,1:T(8,128)(2,1)}, bf16[896,2112]{0,1:T(8,128)(2,1)}, u32[]{:S(2)}, u32[]{:S(2)}) %collective-permute-start) | collective-permute-done | bytes 3784736 | tf_op jit(solution)/shard_map/ppermute | solution.py:136
  93.3 3.5 %convolution_add_fusion = f32[256,2112]{0,1:T(8,128)S(1)} fusion(f32[256,2112]{0,1:T(8,128)S(1)} %fusion.68, bf16[896,2112]{0,1:T(8,128)(2,1)} %collective-permute-done, bf16[256,1792]{1,0:T(8,128)(2,1)S(1)} %fusion.10, s32[]{:T(128)S(6)} %select_n.209), kind=kOutput, calls=%fused_computation.1 | convolution fusion | flops 969424896 | bytes 8568836 | tf_op jit(solution)/shard_map/dot_general | solution.py:139
  98.1 3.1 copy.164
  102.2 3.4 %all-to-all-start.2 = ((bf16[128,4,256]{0,2,1:T(8,128)(2,1)}), bf16[128,4,256]{0,2,1:T(8,128)(2,1)S(1)}, u32[]{:S(2)}, u32[]{:S(2)}) async-start(bf16[128,4,256]{0,2,1:T(8,128)(2,1)} %constant_dynamic-slice_fusion.2), calls=%async_computation.3 | async-start | bytes 524288 | tf_op jit(solution)/shard_map/all_to_all | solution.py:186
  107.8 7.2 %all-to-all-done.2 = bf16[128,4,256]{0,2,1:T(8,128)(2,1)S(1)} async-done(((bf16[128,4,256]{0,2,1:T(8,128)(2,1)}), bf16[128,4,256]{0,2,1:T(8,128)(2,1)S(1)}, u32[]{:S(2)}, u32[]{:S(2)}) %all-to-all-start.2) | async-done | bytes 262176 | tf_op jit(solution)/shard_map/all_to_all | solution.py:186
  115.1 4.0 %all-to-all-start = ((bf16[128,4,256]{0,2,1:T(8,128)(2,1)}), bf16[128,4,256]{0,2,1:T(8,128)(2,1)}, u32[]{:S(2)}, u32[]{:S(2)}) async-start(bf16[128,4,256]{0,2,1:T(8,128)(2,1)} %constant_dynamic-slice_fusion.1), calls=%async_computation | async-start | bytes 524288 | tf_op jit(solution)/shard_map/all_to_all | solution.py:186
  119.1 4.3 %copy.149 = bf16[384,3072]{0,1:T(8,128)(2,1)} copy(bf16[384,3072]{1,0:T(8,128)(2,1)} %param.16) | data formatting | bytes 4718592 | tf_op args[6]
  126.3 5.0 %all-to-all-start.1 = ((bf16[384,4,384]{2,0,1:T(8,128)(2,1)}), bf16[384,4,384]{2,0,1:T(8,128)(2,1)S(1)}, u32[]{:S(2)}, u32[]{:S(2)}) async-start(bf16[384,4,384]{2,0,1:T(8,128)(2,1)} %copy.150), calls=%async_computation.2 | async-start | bytes 2359296 | tf_op jit(solution)/shard_map/all_to_all | solution.py:186
  137.6 20.2 %all-to-all-done.1 = bf16[384,4,384]{2,0,1:T(8,128)(2,1)S(1)} async-done(((bf16[384,4,384]{2,0,1:T(8,128)(2,1)}), bf16[384,4,384]{2,0,1:T(8,128)(2,1)S(1)}, u32[]{:S(2)}, u32[]{:S(2)}) %all-to-all-start.1) | async-done | bytes 1179680 | tf_op jit(solution)/shard_map/all_to_all | solution.py:186
  164.7 18.4 %all-gather = bf16[256,1536]{1,0:T(8,128)(2,1)} all-gather(bf16[64,1536]{1,0:T(8,128)(2,1)S(1)} %multiply_convert_fusion), channel_id=2, replica_groups=mesh['seq'=4,'tp'=4,'dp'=2] {'seq'}, dimensions={0}, use_global_device_ids=true | all-gather | bytes 983040 | tf_op jit(solution)/shard_map/all_gather | solution.py:160
  191.7 12.2 %collective-permute-done.3 = f32[64,576]{0,1:T(8,128)S(1)} collective-permute-done((f32[64,576]{0,1:T(8,128)S(1)}, f32[64,576]{0,1:T(8,128)S(1)}, u32[]{:S(2)}, u32[]{:S(2)}) %collective-permute-start.3) | collective-permute-done | bytes 147488 | tf_op jit(solution)/shard_map/ppermute | solution.py:73
  203.9 4.5 %collective-permute-done.2 = f32[64,576]{0,1:T(8,128)S(1)} collective-permute-done((f32[64,576]{0,1:T(8,128)S(1)}, f32[64,576]{0,1:T(8,128)S(1)}, u32[]{:S(2)}, u32[]{:S(2)}) %collective-permute-start.2) | collective-permute-done | bytes 147488 | tf_op jit(solution)/shard_map/ppermute | solution.py:73
  208.4 2.6 collective-permute-done.1
  218.5 4.7 %collective-permute-done.5 = bf16[64,576]{0,1:T(8,128)(2,1)S(1)} collective-permute-done((bf16[64,576]{0,1:T(8,128)(2,1)S(1)}, bf16[64,576]{0,1:T(8,128)(2,1)S(1)}, u32[]{:S(2)}, u32[]{:S(2)}) %collective-permute-start.5) | collective-permute-done | bytes 73760 | tf_op jit(solution)/shard_map/ppermute | solution.py:73
  230.1 11.7 %collective-permute-done.9 = bf16[4,64,576]{2,1,0:T(8,128)(2,1)S(1)} collective-permute-done((bf16[4,64,576]{2,1,0:T(8,128)(2,1)S(1)}, bf16[4,64,576]{2,1,0:T(8,128)(2,1)S(1)}, u32[]{:S(2)}, u32[]{:S(2)}) %collective-permute-start.9) | collective-permute-done | bytes 294944 | tf_op jit(solution)/shard_map/ppermute | solution.py:73
  245.0 4.7 %collective-permute-done.7 = bf16[4,64,576]{2,1,0:T(8,128)(2,1)S(1)} collective-permute-done((bf16[4,64,576]{2,1,0:T(8,128)(2,1)S(1)}, bf16[4,64,576]{2,1,0:T(8,128)(2,1)S(1)}, u32[]{:S(2)}, u32[]{:S(2)}) %collective-permute-start.7) | collective-permute-done | bytes 294944 | tf_op jit(solution)/shard_map/ppermute | solution.py:73
  252.6 2.9 copy.144
  280.2 3.7 %all-to-all-start.4 = ((bf16[1024,2,128]{2,1,0:T(2,128)(2,1)}), bf16[1024,2,128]{2,1,0:T(2,128)(2,1)S(1)}, u32[]{:S(2)}, u32[]{:S(2)}) async-start(bf16[1024,2,128]{2,1,0:T(2,128)(2,1)} %copy.160), calls=%async_computation.5 | async-start | bytes 1048576 | tf_op jit(solution)/shard_map/all_to_all | solution.py:236
  288.1 9.8 %all-to-all-done.4 = bf16[1024,2,128]{2,1,0:T(2,128)(2,1)S(1)} async-done(((bf16[1024,2,128]{2,1,0:T(2,128)(2,1)}), bf16[1024,2,128]{2,1,0:T(2,128)(2,1)S(1)}, u32[]{:S(2)}, u32[]{:S(2)}) %all-to-all-start.4) | async-done | bytes 524320 | tf_op jit(solution)/shard_map/all_to_all | solution.py:236
  297.9 16.4 %all_to_all.75 = bf16[1024,2,128]{2,1,0:T(2,128)(2,1)S(1)} all-to-all(bf16[1024,2,128]{2,1,0:T(2,128)(2,1)S(1)} %copy.158), channel_id=1, replica_groups=mesh['seq'=4,'tp'=4,'dp'=2] {'seq'}, dimensions={0} | all-to-all | bytes 1048576 | tf_op jit(solution)/shard_map/all_to_all | solution.py:236
  (163 shorter events, 85.0 us)
Async XLA Ops:
  6.5 79.8 %all-gather.6.cloned.1.call-start = ((), (), s32[]{:S(2)}) async-start(), calls=%async_computation.6 | async-start | bytes 4730880 | tf_op jit(solution)/shard_map/all_gather | solution.py:127
  8.4 24.8 %copy-start.15 = (f32[1792]{0:T(1024)S(1)}, f32[1792]{0:T(1024)}, u32[]{:S(2)}) copy-start(f32[1792]{0:T(1024)} %param.11) | copy-start | bytes 21508
  9.5 153.0 %reduce-scatter.2.cloned.1.call-start = ((), (), s32[]{:S(2)}) async-start(), calls=%async_computation.7 | async-start | bytes 1966080 | tf_op jit(solution)/shard_map/reduce_scatter | solution.py:158
  86.4 6.9 %collective-permute-start = (bf16[896,2112]{0,1:T(8,128)(2,1)}, bf16[896,2112]{0,1:T(8,128)(2,1)}, u32[]{:S(2)}, u32[]{:S(2)}) collective-permute-start(bf16[896,2112]{0,1:T(8,128)(2,1)} %all-gather.6.cloned.1.call-done), channel_id=1, source_target_pairs={{0,1},{1,0},{2,3},{3,2},{4,5},{5,4},{6,7},{7,6},{8,9},{9,8},{10,11... | collective-permute-start | bytes 11354120 | tf_op jit(solution)/shard_map/ppermute | solution.py:136
  102.2 12.8 %all-to-all-start.2 = ((bf16[128,4,256]{0,2,1:T(8,128)(2,1)}), bf16[128,4,256]{0,2,1:T(8,128)(2,1)S(1)}, u32[]{:S(2)}, u32[]{:S(2)}) async-start(bf16[128,4,256]{0,2,1:T(8,128)(2,1)} %constant_dynamic-slice_fusion.2), calls=%async_computation.3 | async-start | bytes 524288 | tf_op jit(solution)/shard_map/all_to_all | solution.py:186
  115.1 11.2 %all-to-all-start = ((bf16[128,4,256]{0,2,1:T(8,128)(2,1)}), bf16[128,4,256]{0,2,1:T(8,128)(2,1)}, u32[]{:S(2)}, u32[]{:S(2)}) async-start(bf16[128,4,256]{0,2,1:T(8,128)(2,1)} %constant_dynamic-slice_fusion.1), calls=%async_computation | async-start | bytes 524288 | tf_op jit(solution)/shard_map/all_to_all | solution.py:186
  126.3 31.6 %all-to-all-start.1 = ((bf16[384,4,384]{2,0,1:T(8,128)(2,1)}), bf16[384,4,384]{2,0,1:T(8,128)(2,1)S(1)}, u32[]{:S(2)}, u32[]{:S(2)}) async-start(bf16[384,4,384]{2,0,1:T(8,128)(2,1)} %copy.150), calls=%async_computation.2 | async-start | bytes 2359296 | tf_op jit(solution)/shard_map/all_to_all | solution.py:186
  131.3 130.8 %all-gather.8.cloned.1.call-start = ((), (), s32[]{:S(2)}) async-start(), calls=%async_computation.8 | async-start | bytes 3932160 | tf_op jit(solution)/shard_map/all_gather | solution.py:161
  133.1 2.6 collective-permute-start.12
  134.9 25.6 %collective-permute-start.10 = (bf16[512,256]{1,0:T(8,128)(2,1)}, bf16[512,256]{1,0:T(8,128)(2,1)}, u32[]{:S(2)}, u32[]{:S(2)}) collective-permute-start(bf16[512,256]{1,0:T(8,128)(2,1)} %bitcast.121), channel_id=1, source_target_pairs={{0,1},{1,0},{2,3},{3,2},{4,5},{5,4},{6,7},{7,6},{8,9},{9,8},{10,11... | collective-permute-start | bytes 786440 | tf_op jit(solution)/shard_map/ppermute | solution.py:191
  135.7 26.8 %copy-start.14 = (s32[1024]{0:T(1024)}, s32[1024]{0:T(1024)S(1)}, u32[]{:S(2)}) copy-start(s32[1024]{0:T(1024)S(1)} %iota.42) | copy-start | bytes 12292
  137.6 26.0 %copy-start.16 = (f32[1536]{0:T(1024)S(1)}, f32[1536]{0:T(1024)}, u32[]{:S(2)}) copy-start(f32[1536]{0:T(1024)} %param.14) | copy-start | bytes 18436
  160.5 22.7 %collective-permute-start.11 = (bf16[1536,384]{0,1:T(8,128)(2,1)S(1)}, bf16[1536,384]{0,1:T(8,128)(2,1)}, u32[]{:S(2)}, u32[]{:S(2)}) collective-permute-start(bf16[1536,384]{0,1:T(8,128)(2,1)S(1)} %copy.151), channel_id=1, source_target_pairs={{0,1},{1,0},{2,3},{3,2},{4,5},{5,4},{6,7},{7,6},{8,9},{9,8},{10,11... | collective-permute-start | bytes 3538952 | tf_op jit(solution)/shard_map/ppermute | solution.py:191
  187.0 28.0 %slice-start = ((s32[1024]{0:T(1024)}), s32[512]{0:T(512)S(1)}, s32[]{:S(2)}) async-start(s32[1024]{0:T(1024)} %copy-done.14), calls=%async_computation.9 | async-start | bytes 4096 | tf_op jit(solution)/shard_map/slice | solution.py:58
  188.1 15.8 %collective-permute-start.3 = (f32[64,576]{0,1:T(8,128)S(1)}, f32[64,576]{0,1:T(8,128)S(1)}, u32[]{:S(2)}, u32[]{:S(2)}) collective-permute-start(f32[64,576]{0,1:T(8,128)S(1)} %bitcast.126), channel_id=1, source_target_pairs={{0,6},{2,0},{4,2},{6,4},{1,7},{3,1},{5,3},{7,5},{8,14},{10,8},{12,... | collective-permute-start | bytes 442376 | tf_op jit(solution)/shard_map/ppermute | solution.py:73
  190.5 17.9 %collective-permute-start.2 = (f32[64,576]{0,1:T(8,128)S(1)}, f32[64,576]{0,1:T(8,128)S(1)}, u32[]{:S(2)}, u32[]{:S(2)}) collective-permute-start(f32[64,576]{0,1:T(8,128)S(1)} %bitcast.125), channel_id=1, source_target_pairs={{0,4},{2,6},{4,0},{6,2},{1,5},{3,7},{5,1},{7,3},{8,12},{10,14},{12... | collective-permute-start | bytes 442376 | tf_op jit(solution)/shard_map/ppermute | solution.py:73
  191.1 19.9 %collective-permute-start.1 = (f32[64,576]{0,1:T(8,128)S(1)}, f32[64,576]{0,1:T(8,128)S(1)}, u32[]{:S(2)}, u32[]{:S(2)}) collective-permute-start(f32[64,576]{0,1:T(8,128)S(1)} %bitcast.124), channel_id=1, source_target_pairs={{0,2},{2,4},{4,6},{6,0},{1,3},{3,5},{5,7},{7,1},{8,10},{10,12},{12... | collective-permute-start | bytes 442376 | tf_op jit(solution)/shard_map/ppermute | solution.py:73
  211.5 6.9 %collective-permute-start.6 = (bf16[64,576]{0,1:T(8,128)(2,1)S(1)}, bf16[64,576]{0,1:T(8,128)(2,1)S(1)}, u32[]{:S(2)}, u32[]{:S(2)}) collective-permute-start(bf16[64,576]{0,1:T(8,128)(2,1)S(1)} %get-tuple-element.32), channel_id=1, source_target_pairs={{0,24},{8,0},{16,8},{24,16},{1,25},{9,1},{17,9},{25,17},{2,26},{10... | collective-permute-start | bytes 221192 | tf_op jit(solution)/shard_map/ppermute | solution.py:73
  213.9 9.3 %collective-permute-start.5 = (bf16[64,576]{0,1:T(8,128)(2,1)S(1)}, bf16[64,576]{0,1:T(8,128)(2,1)S(1)}, u32[]{:S(2)}, u32[]{:S(2)}) collective-permute-start(bf16[64,576]{0,1:T(8,128)(2,1)S(1)} %get-tuple-element.32), channel_id=1, source_target_pairs={{0,16},{8,24},{16,0},{24,8},{1,17},{9,25},{17,1},{25,9},{2,18},{10... | collective-permute-start | bytes 221192 | tf_op jit(solution)/shard_map/ppermute | solution.py:73
  213.9 9.3 %collective-permute-start.4 = (bf16[64,576]{0,1:T(8,128)(2,1)S(1)}, bf16[64,576]{0,1:T(8,128)(2,1)S(1)}, u32[]{:S(2)}, u32[]{:S(2)}) collective-permute-start(bf16[64,576]{0,1:T(8,128)(2,1)S(1)} %get-tuple-element.32), channel_id=1, source_target_pairs={{0,8},{8,16},{16,24},{24,0},{1,9},{9,17},{17,25},{25,1},{2,10},{10... | collective-permute-start | bytes 221192 | tf_op jit(solution)/shard_map/ppermute | solution.py:73
  223.6 18.2 %collective-permute-start.9 = (bf16[4,64,576]{2,1,0:T(8,128)(2,1)S(1)}, bf16[4,64,576]{2,1,0:T(8,128)(2,1)S(1)}, u32[]{:S(2)}, u32[]{:S(2)}) collective-permute-start(bf16[4,64,576]{2,1,0:T(8,128)(2,1)S(1)} %copy.138), channel_id=1, source_target_pairs={{0,6},{2,0},{4,2},{6,4},{1,7},{3,1},{5,3},{7,5},{8,14},{10,8},{12,... | collective-permute-start | bytes 884744 | tf_op jit(solution)/shard_map/ppermute | solution.py:73
  225.5 18.4 %collective-permute-start.8 = (bf16[4,64,576]{2,1,0:T(8,128)(2,1)S(1)}, bf16[4,64,576]{2,1,0:T(8,128)(2,1)S(1)}, u32[]{:S(2)}, u32[]{:S(2)}) collective-permute-start(bf16[4,64,576]{2,1,0:T(8,128)(2,1)S(1)} %copy.138), channel_id=1, source_target_pairs={{0,4},{2,6},{4,0},{6,2},{1,5},{3,7},{5,1},{7,3},{8,12},{10,14},{12... | collective-permute-start | bytes 884744 | tf_op jit(solution)/shard_map/ppermute | solution.py:73
  227.7 21.9 %collective-permute-start.7 = (bf16[4,64,576]{2,1,0:T(8,128)(2,1)S(1)}, bf16[4,64,576]{2,1,0:T(8,128)(2,1)S(1)}, u32[]{:S(2)}, u32[]{:S(2)}) collective-permute-start(bf16[4,64,576]{2,1,0:T(8,128)(2,1)S(1)} %copy.138), channel_id=1, source_target_pairs={{0,2},{2,4},{4,6},{6,0},{1,3},{3,5},{5,7},{7,1},{8,10},{10,12},{12... | collective-permute-start | bytes 884744 | tf_op jit(solution)/shard_map/ppermute | solution.py:73
  280.2 17.7 %all-to-all-start.4 = ((bf16[1024,2,128]{2,1,0:T(2,128)(2,1)}), bf16[1024,2,128]{2,1,0:T(2,128)(2,1)S(1)}, u32[]{:S(2)}, u32[]{:S(2)}) async-start(bf16[1024,2,128]{2,1,0:T(2,128)(2,1)} %copy.160), calls=%async_computation.5 | async-start | bytes 1048576 | tf_op jit(solution)/shard_map/all_to_all | solution.py:236
  (21 other events, 78.7 us)
Sparse Core Ops, SparseCore 0:
  9.6 76.7 all-gather.5
  101.3 29.6 reduce-scatter.1
  183.3 62.8 all-gather.7

commit v6 on v3

--- a/solution.py
+++ b/solution.py
@@ -108,46 +108,6 @@
     half_rows = down_piece.shape[0] // dp_count
     own_rows = lax.dynamic_slice_in_dim(down_piece, dp_index * half_rows, half_rows, 0)
     own_all = lax.all_gather(own_rows, "seq", axis=1, tiled=True)
-    own_all, normed, group_ids = lax.optimization_barrier((own_all, normed, group_ids))
-    partial = jnp.dot(
-        lax.dynamic_slice_in_dim(normed, dp_index * half_rows, half_rows, 1),
-        own_all,
-        preferred_element_type=jnp.float32,
-    )
-    for shift in range(1, dp_count):
-        peer = (dp_index + dp_count - shift) % dp_count
-        peer_all = lax.ppermute(
-            own_all, "dp", perm=[(i, (i + shift) % dp_count) for i in range(dp_count)]
-        )
-        partial = partial + jnp.dot(
-            lax.dynamic_slice_in_dim(normed, peer * half_rows, half_rows, 1),
-            peer_all,
-            preferred_element_type=jnp.float32,
-        )
-    latent_rows = lax.psum_scatter(partial, "tp", scatter_dimension=0, tiled=True)
-
-    token_index = jnp.arange(total_rows, dtype=jnp.int32)
-    onehot = group_ids[:, None] == jnp.arange(DOCS, dtype=jnp.int32)[None, :]
-    starts = jnp.min(jnp.where(onehot, token_index[:, None], total_rows), 0)
-    position = token_index - jnp.sum(jnp.where(onehot, starts[None, :], 0), 1)
-    chunk = latent_rows.shape[0]
-    latent_rows = latent_rows.reshape(chunk, seq_count, qrank_piece + memory_piece)
-    query_sums = latent_rows[:, :, :qrank_piece].reshape(chunk, qrank)
-    memory_sums = latent_rows[:, :, qrank_piece:].reshape(chunk, memory_cols)
-    chunk_position = lax.dynamic_slice(
-        position, (seq_index * tok_count + tp_index * chunk,), (chunk,)
-    )
-    compressed_query = rms_scale(query_sums, query_gain).astype(jnp.bfloat16)
-    compressed_memory = rms_scale(memory_sums[:, :KVRANK], memory_gain).astype(jnp.bfloat16)
-    key_rope = rotate(memory_sums[:, KVRANK:], chunk_position).astype(jnp.bfloat16)
-    packed = jnp.concatenate([compressed_query, compressed_memory, key_rope], 1)
-    packed = lax.all_gather(packed, "seq", axis=0, tiled=False)
-    packed = lax.all_gather(packed, "tp", axis=0, tiled=False)
-    latent = jnp.transpose(packed, (1, 0, 2, 3)).reshape(total_rows, packed.shape[-1])
-    cq_all = latent[:, :qrank]
-    cm_all = latent[:, qrank : qrank + KVRANK]
-    rope_all = latent[:, qrank + KVRANK :]
-
     local_heads = query_up.shape[1] // (NOPE + ROPE)
     heads = local_heads // seq_count
 
@@ -178,6 +138,48 @@
     key_w = head_columns(key_up, NOPE)
     value_w = head_columns(value_up, VDIM)
 
+    own_all, normed, group_ids, query_w, key_w, value_w = lax.optimization_barrier(
+        (own_all, normed, group_ids, query_w, key_w, value_w)
+    )
+    partial = jnp.dot(
+        lax.dynamic_slice_in_dim(normed, dp_index * half_rows, half_rows, 1),
+        own_all,
+        preferred_element_type=jnp.float32,
+    )
+    for shift in range(1, dp_count):
+        peer = (dp_index + dp_count - shift) % dp_count
+        peer_all = lax.ppermute(
+            own_all, "dp", perm=[(i, (i + shift) % dp_count) for i in range(dp_count)]
+        )
+        partial = partial + jnp.dot(
+            lax.dynamic_slice_in_dim(normed, peer * half_rows, half_rows, 1),
+            peer_all,
+            preferred_element_type=jnp.float32,
+        )
+    latent_rows = lax.psum_scatter(partial, "tp", scatter_dimension=0, tiled=True)
+
+    token_index = jnp.arange(total_rows, dtype=jnp.int32)
+    onehot = group_ids[:, None] == jnp.arange(DOCS, dtype=jnp.int32)[None, :]
+    starts = jnp.min(jnp.where(onehot, token_index[:, None], total_rows), 0)
+    position = token_index - jnp.sum(jnp.where(onehot, starts[None, :], 0), 1)
+    chunk = latent_rows.shape[0]
+    latent_rows = latent_rows.reshape(chunk, seq_count, qrank_piece + memory_piece)
+    query_sums = latent_rows[:, :, :qrank_piece].reshape(chunk, qrank)
+    memory_sums = latent_rows[:, :, qrank_piece:].reshape(chunk, memory_cols)
+    chunk_position = lax.dynamic_slice(
+        position, (seq_index * tok_count + tp_index * chunk,), (chunk,)
+    )
+    compressed_query = rms_scale(query_sums, query_gain).astype(jnp.bfloat16)
+    compressed_memory = rms_scale(memory_sums[:, :KVRANK], memory_gain).astype(jnp.bfloat16)
+    key_rope = rotate(memory_sums[:, KVRANK:], chunk_position).astype(jnp.bfloat16)
+    packed = jnp.concatenate([compressed_query, compressed_memory, key_rope], 1)
+    packed = lax.all_gather(packed, "seq", axis=0, tiled=False)
+    packed = lax.all_gather(packed, "tp", axis=0, tiled=False)
+    latent = jnp.transpose(packed, (1, 0, 2, 3)).reshape(total_rows, packed.shape[-1])
+    cq_all = latent[:, :qrank]
+    cm_all = latent[:, qrank : qrank + KVRANK]
+    rope_all = latent[:, qrank + KVRANK :]
+
     query_full = jnp.dot(cq_all, query_w, preferred_element_type=jnp.float32).reshape(
         total_rows, heads, NOPE + ROPE
     )

time: 301 us -> 337 us (1.12)
  waiting for transfers between devices: 169 us -> 193 us
  starting transfers between devices: 15 us -> 24.8 us
  other arithmetic: 14.3 us -> 18.1 us
    all_gather x1, waiting for transfers between devices: 0.02 us -> 54.5 us  [body(): packed = lax.all_gather(packed, 'tp', axis=0, tiled=False)]
    all_gather x1, waiting for transfers between devices: 52.8 us -> 0.01 us  [body(): own_all = lax.all_gather(own_rows, 'seq', axis=1, tiled=True)]
    all_to_all x3, waiting for transfers between devices: 39.4 us -> 65.6 us  [head_columns(): own = lax.all_to_all(own, 'seq', split_axis=1, concat_axis=0, tiled=True)]
    all_to_all x3, starting transfers between devices: 10.5 us -> 19.3 us  [head_columns(): own = lax.all_to_all(own, 'seq', split_axis=1, concat_axis=0, tiled=True)]
    unnamed x40 -> x42, local copies, waits for them, and re-layouts: 9.92 us -> 9.7 us
  transfers between devices with their start and end apart: 12 -> 12, of which waited for: 9 -> 8; matrix products, arithmetic and copies ran while one was open for 7% -> 8% of each run, Pallas kernels for 0% -> 0%
where the time goes in v6:
time: 337 us; the launch traced here: 336 us
  waiting for transfers between devices  193 us (57%)
  blocking collectives  37.8 us (11%)
  starting transfers between devices  24.8 us (7%)
  local copies, waits for them, and re-layouts  24.4 us (7%)
  matrix products  24.4 us (7%)
  other arithmetic  18.1 us (5%)
  between operations  13.7 us (4%)
    all_to_all x3, waiting for transfers between devices, head_columns(): own = lax.all_to_all(own, 'seq', split_axis=1, concat_axis=0, tiled=True)  65.6 us
    all_gather x1, waiting for transfers between devices, body(): packed = lax.all_gather(packed, 'tp', axis=0, tiled=False)  54.5 us
    reduce_scatter x1, waiting for transfers between devices, body(): lax.psum_scatter(partial, 'tp', scatter_dimension=0, tiled=True)  32.4 us
    all_gather x1, waiting for transfers between devices, body(): packed = lax.all_gather(packed, 'seq', axis=0, tiled=False)  29 us
    all_to_all x3, starting transfers between devices, head_columns(): own = lax.all_to_all(own, 'seq', split_axis=1, concat_axis=0, tiled=True)  19.3 us
    all_to_all x1, blocking collectives, body(): lax.all_to_all(head_output, 'seq', split_axis=0, concat_axis=1, tiled=True)  16.4 us
    all_gather x1, blocking collectives, body(): group_ids = lax.all_gather(segment_ids, 'seq', axis=0, tiled=True)  11.4 us
    psum x1, blocking collectives, body(): square_sums = lax.psum(jnp.sum(inputs * inputs, 1), 'tp')  9.96 us
  transfers between devices with their start and end apart: 12, of which 8 were waited for; matrix products, arithmetic and copies ran while one was open for 8% of the time, Pallas kernels for 0%

profile of v6, /device:TPU:0, one launch (start us, length us, event | category | flops | bytes accessed | tf_op | source)
XLA Modules:
  0.0 336.4 jit_solution(17549075251054353968)
XLA Ops:
  10.5 6.3 %all-to-all-start.2 = ((bf16[128,4,256]{0,2,1:T(8,128)(2,1)}), bf16[128,4,256]{0,2,1:T(8,128)(2,1)S(1)}, u32[]{:S(2)}, u32[]{:S(2)}) async-start(bf16[128,4,256]{0,2,1:T(8,128)(2,1)} %constant_dynamic-slice_fusion), calls=%async_computation.2 | async-start | bytes 524288 | tf_op jit(solution)/shard_map/all_to_all | solution.py:120
  16.9 3.1 copy.62
  21.1 8.2 %all-to-all-done.2 = bf16[128,4,256]{0,2,1:T(8,128)(2,1)S(1)} async-done(((bf16[128,4,256]{0,2,1:T(8,128)(2,1)}), bf16[128,4,256]{0,2,1:T(8,128)(2,1)S(1)}, u32[]{:S(2)}, u32[]{:S(2)}) %all-to-all-start.2) | async-done | bytes 262176 | tf_op jit(solution)/shard_map/all_to_all | solution.py:120
  29.3 6.7 %all-to-all-start = ((bf16[384,4,384]{0,2,1:T(8,128)(2,1)}), bf16[384,4,384]{0,2,1:T(8,128)(2,1)S(1)}, u32[]{:S(2)}, u32[]{:S(2)}) async-start(bf16[384,4,384]{0,2,1:T(8,128)(2,1)} %constant_dynamic-slice_fusion.2), calls=%async_computation | async-start | bytes 2359296 | tf_op jit(solution)/shard_map/all_to_all | solution.py:120
  37.1 57.2 %all-to-all-done = bf16[384,4,384]{0,2,1:T(8,128)(2,1)S(1)} async-done(((bf16[384,4,384]{0,2,1:T(8,128)(2,1)}), bf16[384,4,384]{0,2,1:T(8,128)(2,1)S(1)}, u32[]{:S(2)}, u32[]{:S(2)}) %all-to-all-start) | async-done | bytes 1179680 | tf_op jit(solution)/shard_map/all_to_all | solution.py:120
  94.3 6.2 %all-to-all-start.1 = ((bf16[128,4,256]{0,2,1:T(8,128)(2,1)}), bf16[128,4,256]{0,2,1:T(8,128)(2,1)}, u32[]{:S(2)}, u32[]{:S(2)}) async-start(bf16[128,4,256]{0,2,1:T(8,128)(2,1)} %constant_dynamic-slice_fusion.1), calls=%async_computation.1 | async-start | bytes 524288 | tf_op jit(solution)/shard_map/all_to_all | solution.py:120
  100.8 10.0 %psum.7 = f32[256]{0:T(256)S(1)} all-reduce(f32[256]{0:T(256)S(1)} %fusion.10), channel_id=1, replica_groups=mesh['seq'=4,'tp'=4,'dp'=2] {'tp'}, use_global_device_ids=true, to_apply=%region_1.0 | all-reduce | flops 256 | bytes 2048 | tf_op jit(solution)/shard_map/psum | solution.py:100
  114.0 11.4 %all-gather.2 = s32[4,1,256]{2,1,0:T(1,128)S(1)} all-gather(s32[1,1,256]{2,1,0:T(1,128)} %bitcast.101), channel_id=1, replica_groups=mesh['seq'=4,'tp'=4,'dp'=2] {'seq'}, dimensions={0}, use_global_device_ids=true | all-gather | bytes 5120 | tf_op jit(solution)/shard_map/all_gather | solution.py:97
  131.7 3.5 %fusion.64 = f32[256,2112]{1,0:T(8,128)S(1)} fusion(bf16[896,2112]{0,1:T(8,128)(2,1)} %all-gather.7.cloned.1.call-done, bf16[256,1792]{1,0:T(8,128)(2,1)S(1)} %fusion.12, s32[]{:T(128)S(6)} %select_n.94), kind=kOutput, calls=%fused_computation.85 | convolution fusion | flops 968884224 | bytes 6406148 | tf_op jit(solution)/shard_map/dot_general | solution.py:144
  135.1 3.4 %collective-permute-done.3 = bf16[896,2112]{0,1:T(8,128)(2,1)} collective-permute-done((bf16[896,2112]{0,1:T(8,128)(2,1)}, bf16[896,2112]{0,1:T(8,128)(2,1)}, u32[]{:S(2)}, u32[]{:S(2)}) %collective-permute-start.3) | collective-permute-done | bytes 3784736 | tf_op jit(solution)/shard_map/ppermute | solution.py:151
  138.6 4.9 %convolution_add_fusion = f32[256,2112]{1,0:T(8,128)} fusion(f32[256,2112]{1,0:T(8,128)S(1)} %fusion.64, bf16[896,2112]{0,1:T(8,128)(2,1)} %collective-permute-done.3, bf16[256,1792]{1,0:T(8,128)(2,1)S(1)} %fusion.12, s32[]{:T(128)S(6)} %select_n.108), kind=kOutput, calls=%fused_computation | convolution fusion | flops 969424896 | bytes 8634372 | tf_op jit(solution)/shard_map/dot_general | solution.py:154
  143.9 32.4 %reduce-scatter.2.cloned.1.call-done = f32[64,2112]{1,0:T(8,128)} async-done(((f32[256,2112]{1,0:T(8,128)}), f32[64,2112]{1,0:T(8,128)}) %reduce-scatter.2.cloned.1.call-update) | async-done | bytes 540688 | tf_op jit(solution)/shard_map/reduce_scatter | solution.py:159
  180.5 29.0 %all-gather.9.cloned.1.call-done = bf16[256,2112]{1,0:T(8,128)(2,1)} async-done(((bf16[64,2112]{1,0:T(8,128)(2,1)}), bf16[256,2112]{1,0:T(8,128)(2,1)}) %all-gather.9.cloned.1.call-update) | async-done | bytes 1081360 | tf_op jit(solution)/shard_map/all_gather | solution.py:176
  210.8 54.5 %all-gather.11.cloned.1.call-done = bf16[16,64,2112]{2,1,0:T(8,128)(2,1)} async-done(((bf16[4,64,2112]{2,1,0:T(8,128)(2,1)}), bf16[16,64,2112]{2,1,0:T(8,128)(2,1)}) %all-gather.11.cloned.1.call-update) | async-done | bytes 4325392 | tf_op jit(solution)/shard_map/all_gather | solution.py:177
  265.3 2.8 copy.72
  268.3 2.8 fusion
  274.8 2.0 convolution_convert_fusion.1
  281.3 2.3 fusion.13
  288.3 2.0 copy.75
  290.3 4.6 %all-to-all-start.3 = ((bf16[1024,2,128]{2,1,0:T(2,128)(2,1)}), bf16[1024,2,128]{2,1,0:T(2,128)(2,1)}, u32[]{:S(2)}, u32[]{:S(2)}) async-start(bf16[1024,2,128]{2,1,0:T(2,128)(2,1)} %copy.75), calls=%async_computation.4 | async-start | bytes 1048576 | tf_op jit(solution)/shard_map/all_to_all | solution.py:212
  294.9 2.1 fusion.15
  301.3 8.0 %all-to-all-done.3 = bf16[1024,2,128]{2,1,0:T(2,128)(2,1)} async-done(((bf16[1024,2,128]{2,1,0:T(2,128)(2,1)}), bf16[1024,2,128]{2,1,0:T(2,128)(2,1)}, u32[]{:S(2)}, u32[]{:S(2)}) %all-to-all-start.3) | async-done | bytes 524320 | tf_op jit(solution)/shard_map/all_to_all | solution.py:212
  309.3 16.4 %all_to_all.75 = bf16[1024,2,128]{2,1,0:T(2,128)(2,1)S(1)} all-to-all(bf16[1024,2,128]{2,1,0:T(2,128)(2,1)S(1)} %copy.77), channel_id=1, replica_groups=mesh['seq'=4,'tp'=4,'dp'=2] {'seq'}, dimensions={0} | all-to-all | bytes 1048576 | tf_op jit(solution)/shard_map/all_to_all | solution.py:212
  325.7 2.1 pad_maximum_fusion.2
  (121 shorter events, 40.8 us)
Async XLA Ops:
  6.5 1.9 copy-start.11
  6.5 125.1 %all-gather.7.cloned.1.call-start = ((), (), s32[]{:S(2)}) async-start(), calls=%async_computation.6 | async-start | bytes 4730880 | tf_op jit(solution)/shard_map/all_gather | solution.py:110
  10.5 18.8 %all-to-all-start.2 = ((bf16[128,4,256]{0,2,1:T(8,128)(2,1)}), bf16[128,4,256]{0,2,1:T(8,128)(2,1)S(1)}, u32[]{:S(2)}, u32[]{:S(2)}) async-start(bf16[128,4,256]{0,2,1:T(8,128)(2,1)} %constant_dynamic-slice_fusion), calls=%async_computation.2 | async-start | bytes 524288 | tf_op jit(solution)/shard_map/all_to_all | solution.py:120
  21.1 14.9 %copy-start.8 = (bf16[128,2048]{1,0:T(8,128)(2,1)S(1)}, bf16[128,2048]{1,0:T(8,128)(2,1)}, u32[]{:S(2)}) copy-start(bf16[128,2048]{1,0:T(8,128)(2,1)} %param.17) | copy-start | bytes 1572868
  21.1 79.4 %copy-start.1 = (bf16[256,1792]{1,0:T(8,128)(2,1)S(1)}, bf16[256,1792]{1,0:T(8,128)(2,1)}, u32[]{:S(2)}) copy-start(bf16[256,1792]{1,0:T(8,128)(2,1)} %param.10) | copy-start | bytes 2752516
  29.3 65.0 %all-to-all-start = ((bf16[384,4,384]{0,2,1:T(8,128)(2,1)}), bf16[384,4,384]{0,2,1:T(8,128)(2,1)S(1)}, u32[]{:S(2)}, u32[]{:S(2)}) async-start(bf16[384,4,384]{0,2,1:T(8,128)(2,1)} %constant_dynamic-slice_fusion.2), calls=%async_computation | async-start | bytes 2359296 | tf_op jit(solution)/shard_map/all_to_all | solution.py:120
  94.3 18.2 %all-to-all-start.1 = ((bf16[128,4,256]{0,2,1:T(8,128)(2,1)}), bf16[128,4,256]{0,2,1:T(8,128)(2,1)}, u32[]{:S(2)}, u32[]{:S(2)}) async-start(bf16[128,4,256]{0,2,1:T(8,128)(2,1)} %constant_dynamic-slice_fusion.1), calls=%async_computation.1 | async-start | bytes 524288 | tf_op jit(solution)/shard_map/all_to_all | solution.py:120
  100.5 13.2 %copy-start.12 = (f32[1792]{0:T(1024)S(1)}, f32[1792]{0:T(1024)}, u32[]{:S(2)}) copy-start(f32[1792]{0:T(1024)} %param.11) | copy-start | bytes 21508
  100.5 75.8 %reduce-scatter.2.cloned.1.call-start = ((), (), s32[]{:S(2)}) async-start(), calls=%async_computation.7 | async-start | bytes 2785280 | tf_op jit(solution)/shard_map/reduce_scatter | solution.py:159
  111.5 17.0 %collective-permute-start = (bf16[1536,384]{1,0:T(8,128)(2,1)S(1)}, bf16[1536,384]{1,0:T(8,128)(2,1)}, u32[]{:S(2)}, u32[]{:S(2)}) collective-permute-start(bf16[1536,384]{1,0:T(8,128)(2,1)S(1)} %bitcast.78), channel_id=1, source_target_pairs={{0,1},{1,0},{2,3},{3,2},{4,5},{5,4},{6,7},{7,6},{8,9},{9,8},{10,11... | collective-permute-start | bytes 3538952 | tf_op jit(solution)/shard_map/ppermute | solution.py:125
  111.8 13.7 %collective-permute-start.2 = (bf16[512,256]{1,0:T(8,128)(2,1)S(1)}, bf16[512,256]{1,0:T(8,128)(2,1)}, u32[]{:S(2)}, u32[]{:S(2)}) collective-permute-start(bf16[512,256]{1,0:T(8,128)(2,1)S(1)} %bitcast.92), channel_id=1, source_target_pairs={{0,1},{1,0},{2,3},{3,2},{4,5},{5,4},{6,7},{7,6},{8,9},{9,8},{10,11... | collective-permute-start | bytes 786440 | tf_op jit(solution)/shard_map/ppermute | solution.py:125
  113.6 12.8 %collective-permute-start.1 = (bf16[512,256]{1,0:T(8,128)(2,1)S(1)}, bf16[512,256]{1,0:T(8,128)(2,1)}, u32[]{:S(2)}, u32[]{:S(2)}) collective-permute-start(bf16[512,256]{1,0:T(8,128)(2,1)S(1)} %bitcast.93), channel_id=1, source_target_pairs={{0,1},{1,0},{2,3},{3,2},{4,5},{5,4},{6,7},{7,6},{8,9},{9,8},{10,11... | collective-permute-start | bytes 786440 | tf_op jit(solution)/shard_map/ppermute | solution.py:125
  131.7 6.9 %collective-permute-start.3 = (bf16[896,2112]{0,1:T(8,128)(2,1)}, bf16[896,2112]{0,1:T(8,128)(2,1)}, u32[]{:S(2)}, u32[]{:S(2)}) collective-permute-start(bf16[896,2112]{0,1:T(8,128)(2,1)} %all-gather.7.cloned.1.call-done), channel_id=1, source_target_pairs={{0,1},{1,0},{2,3},{3,2},{4,5},{5,4},{6,7},{7,6},{8,9},{9,8},{10,11... | collective-permute-start | bytes 11354120 | tf_op jit(solution)/shard_map/ppermute | solution.py:151
  143.5 35.5 %copy-start.14 = (f32[512]{0:T(512)S(1)}, f32[512]{0:T(512)}, u32[]{:S(2)}) copy-start(f32[512]{0:T(512)} %param.15) | copy-start | bytes 6148
  143.5 66.0 %all-gather.9.cloned.1.call-start = ((), (), s32[]{:S(2)}) async-start(), calls=%async_computation.8 | async-start | bytes 1392640 | tf_op jit(solution)/shard_map/all_gather | solution.py:176
  180.2 85.1 %all-gather.11.cloned.1.call-start = ((), (), s32[]{:S(2)}) async-start(), calls=%async_computation.9 | async-start | bytes 5570560 | tf_op jit(solution)/shard_map/all_gather | solution.py:177
  210.4 73.2 %copy-start.5 = (pred[512,512]{0,1:T(8,128)(4,1)}, pred[512,512]{0,1:T(8,128)(4,1)S(1)}, u32[]{:S(2)}) copy-start(pred[512,512]{0,1:T(8,128)(4,1)S(1)} %compare_and_fusion.1) | copy-start | bytes 786436
  265.3 3.0 copy-start.2
  268.1 4.8 %copy-start = (bf16[4,4,64,2112]{3,2,1,0:T(8,128)(2,1)}, bf16[4,4,64,2112]{3,2,1,0:T(8,128)(2,1)S(1)}, u32[]{:S(2)}) copy-start(bf16[4,4,64,2112]{3,2,1,0:T(8,128)(2,1)S(1)} %copy.72) | copy-start | bytes 12976132
  271.1 1.8 copy-start.10
  272.9 1.9 copy-start.9
  276.8 9.4 %copy-start.15 = (bf16[1024,512]{0,1:T(8,128)(2,1)}, bf16[1024,512]{0,1:T(8,128)(2,1)S(1)}, u32[]{:S(2)}) copy-start(bf16[1024,512]{0,1:T(8,128)(2,1)S(1)} %convolution_convert_fusion.1) | copy-start | bytes 3145732
  290.3 19.0 %all-to-all-start.3 = ((bf16[1024,2,128]{2,1,0:T(2,128)(2,1)}), bf16[1024,2,128]{2,1,0:T(2,128)(2,1)}, u32[]{:S(2)}, u32[]{:S(2)}) async-start(bf16[1024,2,128]{2,1,0:T(2,128)(2,1)} %copy.75), calls=%async_computation.4 | async-start | bytes 1048576 | tf_op jit(solution)/shard_map/all_to_all | solution.py:212
  297.0 1.9 copy-start.16
  (6 other events, 8.8 us)
Sparse Core Ops, SparseCore 0:
  9.6 108.3 all-gather.6
  143.6 32.5 reduce-scatter.1
  180.3 29.0 all-gather.8
  211.2 54.1 all-gather.10

commit v7 on v3

--- a/solution.py
+++ b/solution.py
@@ -1,6 +1,10 @@
+import functools
+
 import jax
 import jax.numpy as jnp
 from jax import lax
+from jax.experimental import pallas as pl
+from jax.experimental.pallas import tpu as pltpu
 from jax.sharding import PartitionSpec as P
 
 KVRANK = 512
@@ -67,6 +71,70 @@
         )
         results.append((weighted / jnp.transpose(denominator)[:, :, None]).astype(jnp.bfloat16))
     return jnp.concatenate(results, 0)
+
+
+def attention_kernel(
+    query_ref, key_ref, rope_ref, value_ref, ids_col_ref, ids_row_ref, out_ref, *, block, window, doc_most, scale
+):
+    lower = pl.program_id(1) * block
+    start = pl.multiple_of(jnp.maximum(lower - doc_most, 0), block)
+    query = query_ref[0]
+    keys = key_ref[0, pl.ds(start, window), :]
+    rope = rope_ref[pl.ds(start, window), :]
+    values = value_ref[0, pl.ds(start, window), :]
+    dims = (((1,), (1,)), ((), ()))
+    scores = lax.dot_general(query[:, :NOPE], keys, dims, preferred_element_type=jnp.float32)
+    scores = scores + lax.dot_general(
+        query[:, NOPE:], rope, dims, preferred_element_type=jnp.float32
+    )
+    scores = scores * scale
+    query_index = lower + lax.broadcasted_iota(jnp.int32, (block, window), 0)
+    key_index = start + lax.broadcasted_iota(jnp.int32, (block, window), 1)
+    allowed = (ids_col_ref[...] == ids_row_ref[:, pl.ds(start, window)]) & (
+        query_index >= key_index
+    )
+    scores = jnp.where(allowed, scores, -jnp.inf)
+    row_max = jnp.max(scores, -1, keepdims=True)
+    probs = jnp.exp(scores - row_max)
+    denominator = jnp.sum(probs, -1, keepdims=True)
+    weighted = jnp.dot(probs.astype(jnp.bfloat16), values, preferred_element_type=jnp.float32)
+    out_ref[0] = (weighted / denominator).astype(out_ref.dtype)
+
+
+def heads_attention_kernel(query, key_nope, key_rope, value, group_ids, score_scale, doc_most):
+    heads, total_rows, _ = query.shape
+    block = min(256, total_rows)
+    window = min(total_rows, doc_most + block)
+    kernel = functools.partial(
+        attention_kernel, block=block, window=window, doc_most=doc_most, scale=score_scale
+    )
+    flops = 2 * heads * total_rows * window * (NOPE + ROPE + VDIM)
+    return pl.pallas_call(
+        kernel,
+        grid=(heads, total_rows // block),
+        in_specs=[
+            pl.BlockSpec((1, block, NOPE + ROPE), lambda h, i: (h, i, 0)),
+            pl.BlockSpec((1, total_rows, NOPE), lambda h, i: (h, 0, 0)),
+            pl.BlockSpec((total_rows, ROPE), lambda h, i: (0, 0)),
+            pl.BlockSpec((1, total_rows, VDIM), lambda h, i: (h, 0, 0)),
+            pl.BlockSpec((block, 1), lambda h, i: (i, 0)),
+            pl.BlockSpec((1, total_rows), lambda h, i: (0, 0)),
+        ],
+        out_specs=pl.BlockSpec((1, block, VDIM), lambda h, i: (h, i, 0)),
+        out_shape=jax.ShapeDtypeStruct((heads, total_rows, VDIM), jnp.bfloat16),
+        cost_estimate=pl.CostEstimate(
+            flops=flops,
+            transcendentals=heads * total_rows * window,
+            bytes_accessed=2 * heads * total_rows * (NOPE + ROPE + NOPE + VDIM + VDIM),
+        ),
+    )(
+        query,
+        key_nope,
+        key_rope,
+        value,
+        group_ids.reshape(total_rows, 1),
+        group_ids.reshape(1, total_rows),
+    )
 
 
 def body(
@@ -178,40 +246,27 @@
     key_w = head_columns(key_up, NOPE)
     value_w = head_columns(value_up, VDIM)
 
-    query_full = jnp.dot(cq_all, query_w, preferred_element_type=jnp.float32).reshape(
-        total_rows, heads, NOPE + ROPE
+    query_full = jnp.einsum(
+        "td,dhe->hte",
+        cq_all,
+        query_w.reshape(qrank, heads, NOPE + ROPE),
+        preferred_element_type=jnp.float32,
     )
     query = jnp.concatenate(
-        [query_full[..., :NOPE], rotate(query_full[..., NOPE:], position[:, None])], -1
+        [query_full[..., :NOPE], rotate(query_full[..., NOPE:], position[None, :])], -1
     ).astype(jnp.bfloat16)
-    key_nope = (
-        jnp.dot(cm_all, key_w, preferred_element_type=jnp.float32)
-        .astype(jnp.bfloat16)
-        .reshape(total_rows, heads, NOPE)
-    )
-    value = (
-        jnp.dot(cm_all, value_w, preferred_element_type=jnp.float32)
-        .astype(jnp.bfloat16)
-        .reshape(total_rows, heads, VDIM)
-    )
-    key_all = jnp.concatenate(
-        [key_nope, jnp.broadcast_to(rope_all[:, None, :], (total_rows, heads, ROPE))], -1
-    )
+    key_nope = jnp.einsum(
+        "td,dhe->hte", cm_all, key_w.reshape(KVRANK, heads, NOPE), preferred_element_type=jnp.float32
+    ).astype(jnp.bfloat16)
+    value = jnp.einsum(
+        "td,dhe->hte", cm_all, value_w.reshape(KVRANK, heads, VDIM), preferred_element_type=jnp.float32
+    ).astype(jnp.bfloat16)
     score_scale = (NOPE + ROPE) ** (-0.5)
-    groups = 2 if heads % 2 == 0 else 1
-    per_group = heads // groups
-    attended = []
-    for group in range(groups):
-        picked = slice(group * per_group, (group + 1) * per_group)
-        head_output = heads_attention(
-            query[:, picked], key_all[:, picked], value[:, picked], group_ids, score_scale, doc_most
-        )
-        attended.append(
-            lax.all_to_all(head_output, "seq", split_axis=0, concat_axis=1, tiled=True).reshape(
-                tok_count, seq_count, per_group, VDIM
-            )
-        )
-    attended = jnp.concatenate(attended, 2)
+    head_output = heads_attention_kernel(
+        query, key_nope, rope_all, value, group_ids, score_scale, doc_most
+    )
+    attended = lax.all_to_all(head_output, "seq", split_axis=1, concat_axis=0, tiled=True)
+    attended = jnp.transpose(attended, (1, 0, 2))
     return attended.reshape(tok_count, local_heads * VDIM)
 
 

time: 301 us -> 300 us (level)
  Pallas kernels: 0 us -> 14.8 us
  blocking collectives: 39.6 us -> 51.8 us
  waiting for transfers between devices: 169 us -> 158 us
  matrix products: 24.9 us -> 15.2 us
  other arithmetic: 14.3 us -> 10.5 us
    pallas_call x0 -> x1, Pallas kernels: none -> 14.8 us  [heads_attention_kernel(): pl.pallas_call(kernel, grid=(heads, total_rows // block), in_specs=[pl.Bl...]
    all_to_all x1, blocking collectives: 16.6 us -> 28.7 us  [body(): lax.all_to_all(head_output, 'seq', split_axis=1, concat_axis=0, tiled=True)]
    dot_general x11 -> x3, matrix products: 16.5 us -> 6.86 us  [the longest x1 3.42 us: body(): jnp.einsum('td,dhe->hte', cq_all, query_w.reshape(qrank, heads, NOPE + RO...]
    all_to_all x1 -> x0, waiting for transfers between devices: 8.68 us -> none  [body(): lax.all_to_all(head_output, 'seq', split_axis=0, concat_axis=1, tiled=True)]
    all_to_all x1 -> x0, starting transfers between devices: 4.13 us -> none  [body(): lax.all_to_all(head_output, 'seq', split_axis=0, concat_axis=1, tiled=True)]
    all_to_all x3, waiting for transfers between devices: 39.4 us -> 35.9 us  [head_columns(): own = lax.all_to_all(own, 'seq', split_axis=1, concat_axis=0, tiled=True)]
    unnamed x40 -> x28, local copies, waits for them, and re-layouts: 9.92 us -> 7 us
  transfers between devices with their start and end apart: 12 -> 11, of which waited for: 9 -> 8; matrix products, arithmetic and copies ran while one was open for 7% -> 6% of each run, Pallas kernels for 0% -> 0%
where the time goes in v7:
time: 300 us; the launch traced here: 299 us
  waiting for transfers between devices  158 us (53%)
  blocking collectives  51.8 us (17%)
  local copies, waits for them, and re-layouts  23.6 us (8%)
  matrix products  15.2 us (5%)
  Pallas kernels  14.8 us (5%)
  between operations  13.6 us (5%)
  starting transfers between devices  12 us (4%)
  other arithmetic  10.5 us (4%)
    all_gather x1, waiting for transfers between devices, body(): own_all = lax.all_gather(own_rows, 'seq', axis=1, tiled=True)  52.8 us
    all_to_all x3, waiting for transfers between devices, head_columns(): own = lax.all_to_all(own, 'seq', split_axis=1, concat_axis=0, tiled=True)  35.9 us
    reduce_scatter x1, waiting for transfers between devices, body(): lax.psum_scatter(partial, 'tp', scatter_dimension=0, tiled=True)  34.6 us
    all_gather x1, waiting for transfers between devices, body(): packed = lax.all_gather(packed, 'seq', axis=0, tiled=False)  29.2 us
    all_to_all x1, blocking collectives, body(): lax.all_to_all(head_output, 'seq', split_axis=1, concat_axis=0, tiled=True)  28.7 us
    pallas_call x1, Pallas kernels, heads_attention_kernel(): pl.pallas_call(kernel, grid=(heads, total_rows // block), in_specs=[pl.Bl...  14.8 us
    all_gather x1, blocking collectives, body(): group_ids = lax.all_gather(segment_ids, 'seq', axis=0, tiled=True)  11.7 us
    psum x1, blocking collectives, body(): square_sums = lax.psum(jnp.sum(inputs * inputs, 1), 'tp')  11.4 us
  transfers between devices with their start and end apart: 11, of which 8 were waited for; matrix products, arithmetic and copies ran while one was open for 6% of the time, Pallas kernels for 0%

profile of v7, /device:TPU:0, one launch (start us, length us, event | category | flops | bytes accessed | tf_op | source)
XLA Modules:
  0.0 299.1 jit_solution(3251331805918792881)
XLA Ops:
  6.5 1.9 copy.115
  10.2 11.4 %psum.7 = f32[256]{0:T(256)S(1)} all-reduce(f32[256]{0:T(256)S(1)} %fusion.2), channel_id=1, replica_groups=mesh['seq'=4,'tp'=4,'dp'=2] {'tp'}, use_global_device_ids=true, to_apply=%region_1.0 | all-reduce | flops 256 | bytes 2048 | tf_op jit(solution)/shard_map/psum | solution.py:168
  21.6 11.7 %all-gather.2 = s32[4,1,256]{2,1,0:T(1,128)S(1)} all-gather(s32[1,1,256]{2,1,0:T(1,128)S(1)} %bitcast.86), channel_id=1, replica_groups=mesh['seq'=4,'tp'=4,'dp'=2] {'seq'}, dimensions={0}, use_global_device_ids=true | all-gather | bytes 5120 | tf_op jit(solution)/shard_map/all_gather | solution.py:165
  33.5 52.8 %all-gather.7.cloned.1.call-done = bf16[896,2112]{0,1:T(8,128)(2,1)} async-done(((bf16[896,528]{0,1:T(8,128)(2,1)}), bf16[896,2112]{0,1:T(8,128)(2,1)}) %all-gather.7.cloned.1.call-update) | async-done | bytes 3784720 | tf_op jit(solution)/shard_map/all_gather | solution.py:178
  86.4 3.5 %fusion.9 = f32[256,2112]{1,0:T(8,128)S(1)} fusion(bf16[896,2112]{0,1:T(8,128)(2,1)} %all-gather.7.cloned.1.call-done, bf16[256,1792]{1,0:T(8,128)(2,1)S(1)} %fusion.4, s32[]{:T(128)S(6)} %select_n.86), kind=kOutput, calls=%fused_computation.29 | convolution fusion | flops 968884224 | bytes 6406148 | tf_op jit(solution)/shard_map/dot_general | solution.py:180
  89.8 3.4 %collective-permute-done.1 = bf16[896,2112]{0,1:T(8,128)(2,1)} collective-permute-done((bf16[896,2112]{0,1:T(8,128)(2,1)}, bf16[896,2112]{0,1:T(8,128)(2,1)}, u32[]{:S(2)}, u32[]{:S(2)}) %collective-permute-start.1) | collective-permute-done | bytes 3784736 | tf_op jit(solution)/shard_map/ppermute | solution.py:187
  93.3 4.9 %convolution_add_fusion = f32[256,2112]{1,0:T(8,128)} fusion(f32[256,2112]{1,0:T(8,128)S(1)} %fusion.9, bf16[896,2112]{0,1:T(8,128)(2,1)} %collective-permute-done.1, bf16[256,1792]{1,0:T(8,128)(2,1)S(1)} %fusion.4, s32[]{:T(128)S(6)} %select_n.87), kind=kOutput, calls=%fused_computation | convolution fusion | flops 969424896 | bytes 8634372 | tf_op jit(solution)/shard_map/dot_general | solution.py:190
  98.6 34.6 %reduce-scatter.2.cloned.1.call-done = f32[64,2112]{1,0:T(8,128)} async-done(((f32[256,2112]{1,0:T(8,128)}), f32[64,2112]{1,0:T(8,128)}) %reduce-scatter.2.cloned.1.call-update) | async-done | bytes 540688 | tf_op jit(solution)/shard_map/reduce_scatter | solution.py:195
  137.2 29.2 %all-gather.9.cloned.1.call-done = bf16[256,2112]{1,0:T(8,128)(2,1)} async-done(((bf16[64,2112]{1,0:T(8,128)(2,1)}), bf16[256,2112]{1,0:T(8,128)(2,1)}) %all-gather.9.cloned.1.call-update) | async-done | bytes 1081360 | tf_op jit(solution)/shard_map/all_gather | solution.py:212
  167.6 4.0 %all-to-all-start.2 = ((bf16[128,4,256]{2,0,1:T(8,128)(2,1)}), bf16[128,4,256]{2,0,1:T(8,128)(2,1)}, u32[]{:S(2)}, u32[]{:S(2)}) async-start(bf16[128,4,256]{2,0,1:T(8,128)(2,1)} %copy.129), calls=%async_computation.3 | async-start | bytes 524288 | tf_op jit(solution)/shard_map/all_to_all | solution.py:228
  171.7 3.1 %copy.110 = bf16[384,3072]{0,1:T(8,128)(2,1)S(1)} copy(bf16[384,3072]{1,0:T(8,128)(2,1)} %param.16) | data formatting | bytes 4718592 | tf_op args[6]
  176.4 4.0 %all-to-all-done.2 = bf16[128,4,256]{2,0,1:T(8,128)(2,1)} async-done(((bf16[128,4,256]{2,0,1:T(8,128)(2,1)}), bf16[128,4,256]{2,0,1:T(8,128)(2,1)}, u32[]{:S(2)}, u32[]{:S(2)}) %all-to-all-start.2) | async-done | bytes 262176 | tf_op jit(solution)/shard_map/all_to_all | solution.py:228
  180.4 3.5 %all-to-all-start = ((bf16[384,4,384]{2,0,1:T(8,128)(2,1)}), bf16[384,4,384]{2,0,1:T(8,128)(2,1)S(1)}, u32[]{:S(2)}, u32[]{:S(2)}) async-start(bf16[384,4,384]{2,0,1:T(8,128)(2,1)} %copy.111), calls=%async_computation | async-start | bytes 2359296 | tf_op jit(solution)/shard_map/all_to_all | solution.py:228
  185.1 26.0 %all-to-all-done = bf16[384,4,384]{2,0,1:T(8,128)(2,1)S(1)} async-done(((bf16[384,4,384]{2,0,1:T(8,128)(2,1)}), bf16[384,4,384]{2,0,1:T(8,128)(2,1)S(1)}, u32[]{:S(2)}, u32[]{:S(2)}) %all-to-all-start) | async-done | bytes 1179680 | tf_op jit(solution)/shard_map/all_to_all | solution.py:228
  211.1 3.6 %all-to-all-start.1 = ((bf16[128,4,256]{2,0,1:T(8,128)(2,1)}), bf16[128,4,256]{2,0,1:T(8,128)(2,1)S(1)}, u32[]{:S(2)}, u32[]{:S(2)}) async-start(bf16[128,4,256]{2,0,1:T(8,128)(2,1)} %copy.123), calls=%async_computation.2 | async-start | bytes 524288 | tf_op jit(solution)/shard_map/all_to_all | solution.py:228
  217.1 5.8 %all-to-all-done.1 = bf16[128,4,256]{2,0,1:T(8,128)(2,1)S(1)} async-done(((bf16[128,4,256]{2,0,1:T(8,128)(2,1)}), bf16[128,4,256]{2,0,1:T(8,128)(2,1)S(1)}, u32[]{:S(2)}, u32[]{:S(2)}) %all-to-all-start.1) | async-done | bytes 262176 | tf_op jit(solution)/shard_map/all_to_all | solution.py:228
  228.9 1.9 multiply_cosine_fusion
  230.8 2.6 copy.120
  234.2 3.4 %fusion.1 = f32[4,1024,192]{2,1,0:T(8,128)S(1)} fusion(bf16[1536,4,192]{0,2,1:T(8,128)(2,1)S(1)} %bitcast.73, bf16[1024,2112]{1,0:T(8,128)(2,1)S(1)} %bitcast.62), kind=kOutput, calls=%fused_computation.6 | convolution fusion | flops 2415919104 | bytes 8650752 | tf_op jit(solution)/shard_map/td,dhe->hte/dot_general | solution.py:249
  238.7 1.7 fusion.5.key_ref
  242.9 2.0 pad_maximum_fusion.1.query_ref
  244.8 14.8 %shard_map.100 = bf16[4,1024,128]{2,1,0:T(8,128)(2,1)} custom-call(bf16[4,1024,192]{2,1,0:T(8,128)(2,1)} %pad_maximum_fusion.1.query_ref, bf16[4,1024,128]{2,1,0:T(8,128)(2,1)} %fusion.5.key_ref, bf16[1024,64]{1,0:T(8,128)(2,1)} %slice.61.rope_ref, bf16[4,1024,128]{2,1,0:T(8,128)(2,1)} %fusion.6.value_ref, s32[1024,1]{1,0:T(8,128)} %copy.134.ids_col_ref, ...), custom_call_target="tpu_custom_call" | custom-call | flops 1342177280 | bytes 4718592 | tf_op jit(solution)/shard_map/pallas_call | solution.py:112
  259.6 2.0 copy.135
  261.7 28.7 %all_to_all.63 = bf16[4,1024,128]{2,0,1:T(4,128)(2,1)S(1)} all-to-all(bf16[4,1024,128]{2,0,1:T(4,128)(2,1)S(1)} %copy.135), channel_id=1, replica_groups=mesh['seq'=4,'tp'=4,'dp'=2] {'seq'}, dimensions={1} | all-to-all | bytes 2097152 | tf_op jit(solution)/shard_map/all_to_all | solution.py:268
  (87 shorter events, 24.9 us)
Async XLA Ops:
  6.5 1.9 copy-start.5
  6.5 79.8 %all-gather.7.cloned.1.call-start = ((), (), s32[]{:S(2)}) async-start(), calls=%async_computation.5 | async-start | bytes 4730880 | tf_op jit(solution)/shard_map/all_gather | solution.py:178
  8.4 1.5 copy-start
  8.4 13.1 %copy-start.10 = (s32[256]{0:T(256)S(1)}, s32[256]{0:T(256)}, u32[]{:S(2)}) copy-start(s32[256]{0:T(256)} %param.19) | copy-start | bytes 3076
  8.4 24.8 %copy-start.7 = (f32[1792]{0:T(1024)S(1)}, f32[1792]{0:T(1024)}, u32[]{:S(2)}) copy-start(f32[1792]{0:T(1024)} %param.11) | copy-start | bytes 21508
  9.5 123.7 %reduce-scatter.2.cloned.1.call-start = ((), (), s32[]{:S(2)}) async-start(), calls=%async_computation.6 | async-start | bytes 2785280 | tf_op jit(solution)/shard_map/reduce_scatter | solution.py:195
  33.2 194.6 %copy-start.6 = (s32[4,1,256]{2,1,0:T(1,128)}, s32[4,1,256]{2,1,0:T(1,128)S(1)}, u32[]{:S(2)}) copy-start(s32[4,1,256]{2,1,0:T(1,128)S(1)} %all-gather.2) | copy-start | bytes 12292
  86.4 6.9 %collective-permute-start.1 = (bf16[896,2112]{0,1:T(8,128)(2,1)}, bf16[896,2112]{0,1:T(8,128)(2,1)}, u32[]{:S(2)}, u32[]{:S(2)}) collective-permute-start(bf16[896,2112]{0,1:T(8,128)(2,1)} %all-gather.7.cloned.1.call-done), channel_id=1, source_target_pairs={{0,1},{1,0},{2,3},{3,2},{4,5},{5,4},{6,7},{7,6},{8,9},{9,8},{10,11... | collective-permute-start | bytes 11354120 | tf_op jit(solution)/shard_map/ppermute | solution.py:187
  98.2 68.2 %all-gather.9.cloned.1.call-start = ((), (), s32[]{:S(2)}) async-start(), calls=%async_computation.7 | async-start | bytes 1392640 | tf_op jit(solution)/shard_map/all_gather | solution.py:212
  98.2 37.4 %copy-start.9 = (f32[512]{0:T(512)S(1)}, f32[512]{0:T(512)}, u32[]{:S(2)}) copy-start(f32[512]{0:T(512)} %param.15) | copy-start | bytes 6148
  134.7 1.5 copy-start.8
  135.3 31.1 %copy-start.1 = (bf16[128,2048]{1,0:T(8,128)(2,1)S(1)}, bf16[128,2048]{1,0:T(8,128)(2,1)}, u32[]{:S(2)}) copy-start(bf16[128,2048]{1,0:T(8,128)(2,1)} %param.18) | copy-start | bytes 1572868
  137.2 93.6 %all-gather.11.cloned.1.call-start = ((), (), s32[]{:S(2)}) async-start(), calls=%async_computation.8 | async-start | bytes 5570560 | tf_op jit(solution)/shard_map/all_gather | solution.py:213
  167.6 12.8 %all-to-all-start.2 = ((bf16[128,4,256]{2,0,1:T(8,128)(2,1)}), bf16[128,4,256]{2,0,1:T(8,128)(2,1)}, u32[]{:S(2)}, u32[]{:S(2)}) async-start(bf16[128,4,256]{2,0,1:T(8,128)(2,1)} %copy.129), calls=%async_computation.3 | async-start | bytes 524288 | tf_op jit(solution)/shard_map/all_to_all | solution.py:228
  174.9 9.0 %copy-start.2 = (bf16[128,2048]{1,0:T(8,128)(2,1)S(1)}, bf16[128,2048]{1,0:T(8,128)(2,1)}, u32[]{:S(2)}) copy-start(bf16[128,2048]{1,0:T(8,128)(2,1)} %param.17) | copy-start | bytes 1572868
  180.4 30.7 %all-to-all-start = ((bf16[384,4,384]{2,0,1:T(8,128)(2,1)}), bf16[384,4,384]{2,0,1:T(8,128)(2,1)S(1)}, u32[]{:S(2)}, u32[]{:S(2)}) async-start(bf16[384,4,384]{2,0,1:T(8,128)(2,1)} %copy.111), calls=%async_computation | async-start | bytes 2359296 | tf_op jit(solution)/shard_map/all_to_all | solution.py:228
  211.1 11.8 %all-to-all-start.1 = ((bf16[128,4,256]{2,0,1:T(8,128)(2,1)}), bf16[128,4,256]{2,0,1:T(8,128)(2,1)S(1)}, u32[]{:S(2)}, u32[]{:S(2)}) async-start(bf16[128,4,256]{2,0,1:T(8,128)(2,1)} %copy.123), calls=%async_computation.2 | async-start | bytes 524288 | tf_op jit(solution)/shard_map/all_to_all | solution.py:228
  215.4 12.1 %collective-permute-start = (bf16[1536,384]{0,1:T(8,128)(2,1)S(1)}, bf16[1536,384]{0,1:T(8,128)(2,1)S(1)}, u32[]{:S(2)}, u32[]{:S(2)}) collective-permute-start(bf16[1536,384]{0,1:T(8,128)(2,1)S(1)} %copy.112), channel_id=1, source_target_pairs={{0,1},{1,0},{2,3},{3,2},{4,5},{5,4},{6,7},{7,6},{8,9},{9,8},{10,11... | collective-permute-start | bytes 3538952 | tf_op jit(solution)/shard_map/ppermute | solution.py:233
  216.6 6.6 %collective-permute-start.3 = (bf16[512,256]{0,1:T(8,128)(2,1)S(1)}, bf16[512,256]{0,1:T(8,128)(2,1)S(1)}, u32[]{:S(2)}, u32[]{:S(2)}) collective-permute-start(bf16[512,256]{0,1:T(8,128)(2,1)S(1)} %copy.130), channel_id=1, source_target_pairs={{0,1},{1,0},{2,3},{3,2},{4,5},{5,4},{6,7},{7,6},{8,9},{9,8},{10,11... | collective-permute-start | bytes 786440 | tf_op jit(solution)/shard_map/ppermute | solution.py:233
  223.1 1.7 collective-permute-start.2
  237.6 1.0 copy-start.3
  237.6 2.8 copy-start.4
Sparse Core Ops, SparseCore 0:
  9.6 76.7 all-gather.6
  98.3 34.8 reduce-scatter.1
  137.3 29.0 all-gather.8
  168.1 54.1 all-gather.10

commit v8 on v7

--- a/solution.py
+++ b/solution.py
@@ -208,13 +208,15 @@
     compressed_query = rms_scale(query_sums, query_gain).astype(jnp.bfloat16)
     compressed_memory = rms_scale(memory_sums[:, :KVRANK], memory_gain).astype(jnp.bfloat16)
     key_rope = rotate(memory_sums[:, KVRANK:], chunk_position).astype(jnp.bfloat16)
-    packed = jnp.concatenate([compressed_query, compressed_memory, key_rope], 1)
-    packed = lax.all_gather(packed, "seq", axis=0, tiled=False)
-    packed = lax.all_gather(packed, "tp", axis=0, tiled=False)
-    latent = jnp.transpose(packed, (1, 0, 2, 3)).reshape(total_rows, packed.shape[-1])
-    cq_all = latent[:, :qrank]
-    cm_all = latent[:, qrank : qrank + KVRANK]
-    rope_all = latent[:, qrank + KVRANK :]
+    def gather_rows(rows):
+        rows = lax.all_gather(rows, "seq", axis=0, tiled=False)
+        rows = lax.all_gather(rows, "tp", axis=0, tiled=False)
+        return jnp.transpose(rows, (1, 0, 2, 3)).reshape(total_rows, rows.shape[-1])
+
+    memory_all = gather_rows(jnp.concatenate([compressed_memory, key_rope], 1))
+    cm_all = memory_all[:, :KVRANK]
+    rope_all = memory_all[:, KVRANK:]
+    cq_all = gather_rows(compressed_query)
 
     local_heads = query_up.shape[1] // (NOPE + ROPE)
     heads = local_heads // seq_count
@@ -262,11 +264,18 @@
         "td,dhe->hte", cm_all, value_w.reshape(KVRANK, heads, VDIM), preferred_element_type=jnp.float32
     ).astype(jnp.bfloat16)
     score_scale = (NOPE + ROPE) ** (-0.5)
-    head_output = heads_attention_kernel(
-        query, key_nope, rope_all, value, group_ids, score_scale, doc_most
-    )
-    attended = lax.all_to_all(head_output, "seq", split_axis=1, concat_axis=0, tiled=True)
-    attended = jnp.transpose(attended, (1, 0, 2))
+    groups = 2 if heads % 2 == 0 else 1
+    per_group = heads // groups
+    attended = []
+    for group in range(groups):
+        picked = slice(group * per_group, (group + 1) * per_group)
+        head_output = heads_attention_kernel(
+            query[picked], key_nope[picked], rope_all, value[picked], group_ids, score_scale, doc_most
+        )
+        head_output = lax.all_to_all(head_output, "seq", split_axis=1, concat_axis=0, tiled=True)
+        attended.append(head_output.reshape(seq_count, per_group, tok_count, VDIM))
+    attended = jnp.stack(attended, 1)
+    attended = jnp.transpose(attended, (3, 0, 1, 2, 4))
     return attended.reshape(tok_count, local_heads * VDIM)
 
 

time: 300 us -> 317 us (1.057)
  blocking collectives: 51.8 us -> 94.2 us
  waiting for transfers between devices: 158 us -> 122 us
  starting transfers between devices: 12 us -> 18.1 us
  local copies, waits for them, and re-layouts: 23.6 us -> 28.6 us
    all_gather x0 -> x2, blocking collectives: none -> 54.7 us  [gather_rows(): rows = lax.all_gather(rows, 'seq', axis=0, tiled=False)]
    all_to_all x3, waiting for transfers between devices: 35.9 us -> 5.82 us  [head_columns(): own = lax.all_to_all(own, 'seq', split_axis=1, concat_axis=0, tiled=True)]
    all_to_all x1, blocking collectives: 28.7 us -> 16.4 us  [body(): lax.all_to_all(head_output, 'seq', split_axis=1, concat_axis=0, tiled=True)]
    all_gather x2, waiting for transfers between devices: 29.2 us -> 18.5 us  [gather_rows(): rows = lax.all_gather(rows, 'tp', axis=0, tiled=False)]
    all_to_all x0 -> x1, waiting for transfers between devices: none -> 4.63 us  [body(): lax.all_to_all(head_output, 'seq', split_axis=1, concat_axis=0, tiled=True)]
    all_to_all x0 -> x1, starting transfers between devices: none -> 4.6 us  [body(): lax.all_to_all(head_output, 'seq', split_axis=1, concat_axis=0, tiled=True)]
    slice x1 -> x4, local copies, waits for them, and re-layouts: 0.73 us -> 4.38 us  [the longest x1 1.5 us: body(): query[picked]]
    pallas_call x1 -> x2, Pallas kernels: 14.8 us -> 16.2 us  [heads_attention_kernel(): pl.pallas_call(kernel, grid=(heads, total_rows // block), in_specs=[pl.Bl...]
  transfers between devices with their start and end apart: 11 -> 12, of which waited for: 8 -> 8; matrix products, arithmetic and copies ran while one was open for 6% -> 9% of each run, Pallas kernels for 0% -> 3%
where the time goes in v8:
time: 317 us; the launch traced here: 316 us
  waiting for transfers between devices  122 us (38%)
  blocking collectives  94.2 us (30%)
  local copies, waits for them, and re-layouts  28.6 us (9%)
  starting transfers between devices  18.1 us (6%)
  Pallas kernels  16.2 us (5%)
  between operations  13.5 us (4%)
  matrix products  13.3 us (4%)
  other arithmetic  10.7 us (3%)
    all_gather x2, blocking collectives, gather_rows(): rows = lax.all_gather(rows, 'seq', axis=0, tiled=False)  54.7 us
    all_gather x1, waiting for transfers between devices, body(): own_all = lax.all_gather(own_rows, 'seq', axis=1, tiled=True)  52.8 us
    reduce_scatter x1, waiting for transfers between devices, body(): lax.psum_scatter(partial, 'tp', scatter_dimension=0, tiled=True)  34.6 us
    all_gather x2, waiting for transfers between devices, gather_rows(): rows = lax.all_gather(rows, 'tp', axis=0, tiled=False)  18.5 us
    all_to_all x1, blocking collectives, body(): lax.all_to_all(head_output, 'seq', split_axis=1, concat_axis=0, tiled=True)  16.4 us
    pallas_call x2, Pallas kernels, heads_attention_kernel(): pl.pallas_call(kernel, grid=(heads, total_rows // block), in_specs=[pl.Bl...  16.2 us
    all_to_all x3, starting transfers between devices, head_columns(): own = lax.all_to_all(own, 'seq', split_axis=1, concat_axis=0, tiled=True)  12.7 us
    all_gather x1, blocking collectives, body(): group_ids = lax.all_gather(segment_ids, 'seq', axis=0, tiled=True)  11.7 us
  transfers between devices with their start and end apart: 12, of which 8 were waited for; matrix products, arithmetic and copies ran while one was open for 9% of the time, Pallas kernels for 3%

profile of v8, /device:TPU:0, one launch (start us, length us, event | category | flops | bytes accessed | tf_op | source)
XLA Modules:
  0.0 316.2 jit_solution(15264957502363008981)
XLA Ops:
  10.2 11.4 %psum.7 = f32[256]{0:T(256)S(1)} all-reduce(f32[256]{0:T(256)S(1)} %fusion), channel_id=1, replica_groups=mesh['seq'=4,'tp'=4,'dp'=2] {'tp'}, use_global_device_ids=true, to_apply=%region_1.0 | all-reduce | flops 256 | bytes 2048 | tf_op jit(solution)/shard_map/psum | solution.py:168
  21.6 11.7 %all-gather.3 = s32[4,1,256]{2,1,0:T(1,128)S(1)} all-gather(s32[1,1,256]{2,1,0:T(1,128)S(1)} %bitcast.90), channel_id=1, replica_groups=mesh['seq'=4,'tp'=4,'dp'=2] {'seq'}, dimensions={0}, use_global_device_ids=true | all-gather | bytes 5120 | tf_op jit(solution)/shard_map/all_gather | solution.py:165
  33.5 52.8 %all-gather.8.cloned.1.call-done = bf16[896,2112]{0,1:T(8,128)(2,1)} async-done(((bf16[896,528]{0,1:T(8,128)(2,1)}), bf16[896,2112]{0,1:T(8,128)(2,1)}) %all-gather.8.cloned.1.call-update) | async-done | bytes 3784720 | tf_op jit(solution)/shard_map/all_gather | solution.py:178
  86.4 3.5 %fusion.7 = f32[256,2112]{1,0:T(8,128)S(1)} fusion(bf16[896,2112]{0,1:T(8,128)(2,1)} %all-gather.8.cloned.1.call-done, bf16[256,1792]{1,0:T(8,128)(2,1)S(1)} %fusion.2, s32[]{:T(128)S(6)} %select_n.86), kind=kOutput, calls=%fused_computation.28 | convolution fusion | flops 968884224 | bytes 6406148 | tf_op jit(solution)/shard_map/dot_general | solution.py:180
  89.8 3.4 %collective-permute-done.1 = bf16[896,2112]{0,1:T(8,128)(2,1)} collective-permute-done((bf16[896,2112]{0,1:T(8,128)(2,1)}, bf16[896,2112]{0,1:T(8,128)(2,1)}, u32[]{:S(2)}, u32[]{:S(2)}) %collective-permute-start.1) | collective-permute-done | bytes 3784736 | tf_op jit(solution)/shard_map/ppermute | solution.py:187
  93.3 4.9 %convolution_add_fusion = f32[256,2112]{1,0:T(8,128)} fusion(f32[256,2112]{1,0:T(8,128)S(1)} %fusion.7, bf16[896,2112]{0,1:T(8,128)(2,1)} %collective-permute-done.1, bf16[256,1792]{1,0:T(8,128)(2,1)S(1)} %fusion.2, s32[]{:T(128)S(6)} %select_n.87), kind=kOutput, calls=%fused_computation | convolution fusion | flops 969424896 | bytes 8634372 | tf_op jit(solution)/shard_map/dot_general | solution.py:190
  98.6 34.6 %reduce-scatter.2.cloned.1.call-done = f32[64,2112]{1,0:T(8,128)} async-done(((f32[256,2112]{1,0:T(8,128)}), f32[64,2112]{1,0:T(8,128)}) %reduce-scatter.2.cloned.1.call-update) | async-done | bytes 540688 | tf_op jit(solution)/shard_map/reduce_scatter | solution.py:195
  135.5 14.9 %all-gather.1 = bf16[256,576]{1,0:T(8,128)(2,1)} all-gather(bf16[64,576]{1,0:T(8,128)(2,1)S(1)} %copy.173), channel_id=3, replica_groups=mesh['seq'=4,'tp'=4,'dp'=2] {'seq'}, dimensions={0}, use_global_device_ids=true | all-gather | bytes 368640 | tf_op jit(solution)/shard_map/all_gather | solution.py:212
  151.7 5.2 %all-to-all-start.1 = ((bf16[128,4,256]{2,0,1:T(8,128)(2,1)}), bf16[128,4,256]{2,0,1:T(8,128)(2,1)}, u32[]{:S(2)}, u32[]{:S(2)}) async-start(bf16[128,4,256]{2,0,1:T(8,128)(2,1)} %copy.168), calls=%async_computation.2 | async-start | bytes 524288 | tf_op jit(solution)/shard_map/all_to_all | solution.py:230
  156.9 3.0 copy.159
  163.8 3.8 %all-to-all-start = ((bf16[384,4,384]{2,0,1:T(8,128)(2,1)}), bf16[384,4,384]{2,0,1:T(8,128)(2,1)S(1)}, u32[]{:S(2)}, u32[]{:S(2)}) async-start(bf16[384,4,384]{2,0,1:T(8,128)(2,1)} %copy.160), calls=%async_computation | async-start | bytes 2359296 | tf_op jit(solution)/shard_map/all_to_all | solution.py:230
  167.7 39.8 %all_gather.30 = bf16[4,64,1536]{2,1,0:T(8,128)(2,1)} all-gather(bf16[1,64,1536]{2,1,0:T(8,128)(2,1)S(1)} %multiply_convert_fusion), channel_id=1, replica_groups=mesh['seq'=4,'tp'=4,'dp'=2] {'seq'}, dimensions={0}, use_global_device_ids=true | all-gather | bytes 983040 | tf_op jit(solution)/shard_map/all_gather | solution.py:212
  208.7 3.7 %all-to-all-start.2 = ((bf16[128,4,256]{2,0,1:T(8,128)(2,1)}), bf16[128,4,256]{2,0,1:T(8,128)(2,1)S(1)}, u32[]{:S(2)}, u32[]{:S(2)}) async-start(bf16[128,4,256]{2,0,1:T(8,128)(2,1)} %copy.177), calls=%async_computation.3 | async-start | bytes 524288 | tf_op jit(solution)/shard_map/all_to_all | solution.py:230
  214.7 4.4 %all-to-all-done.2 = bf16[128,4,256]{2,0,1:T(8,128)(2,1)S(1)} async-done(((bf16[128,4,256]{2,0,1:T(8,128)(2,1)}), bf16[128,4,256]{2,0,1:T(8,128)(2,1)S(1)}, u32[]{:S(2)}, u32[]{:S(2)}) %all-to-all-start.2) | async-done | bytes 262176 | tf_op jit(solution)/shard_map/all_to_all | solution.py:230
  225.1 1.9 multiply_cosine_fusion
  232.9 18.5 %all-gather.10.cloned.1.call-done = bf16[16,64,1536]{2,1,0:T(8,128)(2,1)} async-done(((bf16[4,64,1536]{2,1,0:T(8,128)(2,1)}), bf16[16,64,1536]{2,1,0:T(8,128)(2,1)}) %all-gather.10.cloned.1.call-update) | async-done | bytes 3145744 | tf_op jit(solution)/shard_map/all_gather | solution.py:213
  251.4 2.2 copy.165
  253.6 3.4 %convolution_bitcast_fusion = f32[4,1024,192]{2,1,0:T(8,128)S(1)} fusion(bf16[1536,4,192]{0,2,1:T(8,128)(2,1)S(1)} %bitcast.72, bf16[1024,1536,1]{1,0,2:T(8,128)(2,1)S(1)} %bitcast.68), kind=kOutput, calls=%fused_computation.4 | convolution fusion | flops 2415919104 | bytes 8650752 | tf_op jit(solution)/shard_map/td,dhe->hte/dot_general | solution.py:251
  260.0 8.1 %shard_map.100 = bf16[2,1024,128]{2,1,0:T(8,128)(2,1)} custom-call(bf16[2,1024,192]{2,1,0:T(8,128)(2,1)} %get-tuple-element.15.query_ref, bf16[2,1024,128]{2,1,0:T(8,128)(2,1)} %get-tuple-element.19.key_ref, bf16[1024,64]{1,0:T(8,128)(2,1)} %slice.82.rope_ref, bf16[2,1024,128]{2,1,0:T(8,128)(2,1)} %get-tuple-element.17.value_ref, ...), custom_call_target="tpu_custom_call" | custom-call | flops 671088640 | bytes 2359296 | tf_op jit(solution)/shard_map/pallas_call | solution.py:112
  268.1 2.4 copy.183
  270.5 4.6 %all-to-all-start.3 = ((bf16[2,1024,128]{2,0,1:T(2,128)(2,1)}), bf16[2,1024,128]{2,0,1:T(2,128)(2,1)S(1)}, u32[]{:S(2)}, u32[]{:S(2)}) async-start(bf16[2,1024,128]{2,0,1:T(2,128)(2,1)} %copy.183), calls=%async_computation.4 | async-start | bytes 1048576 | tf_op jit(solution)/shard_map/all_to_all | solution.py:275
  275.1 8.1 %shard_map.101 = bf16[2,1024,128]{2,1,0:T(8,128)(2,1)} custom-call(bf16[2,1024,192]{2,1,0:T(8,128)(2,1)} %get-tuple-element.16.query_ref, bf16[2,1024,128]{2,1,0:T(8,128)(2,1)} %get-tuple-element.20.key_ref, bf16[1024,64]{1,0:T(8,128)(2,1)} %slice.82.rope_ref, bf16[2,1024,128]{2,1,0:T(8,128)(2,1)} %get-tuple-element.18.value_ref, ...), custom_call_target="tpu_custom_call" | custom-call | flops 671088640 | bytes 2359296 | tf_op jit(solution)/shard_map/pallas_call | solution.py:112
  284.8 4.6 %all-to-all-done.3 = bf16[2,1024,128]{2,0,1:T(2,128)(2,1)S(1)} async-done(((bf16[2,1024,128]{2,0,1:T(2,128)(2,1)}), bf16[2,1024,128]{2,0,1:T(2,128)(2,1)S(1)}, u32[]{:S(2)}, u32[]{:S(2)}) %all-to-all-start.3) | async-done | bytes 524320 | tf_op jit(solution)/shard_map/all_to_all | solution.py:275
  289.4 16.4 %all_to_all.75 = bf16[2,1024,128]{2,0,1:T(2,128)(2,1)S(1)} all-to-all(bf16[2,1024,128]{2,0,1:T(2,128)(2,1)S(1)} %copy.185), channel_id=1, replica_groups=mesh['seq'=4,'tp'=4,'dp'=2] {'seq'}, dimensions={1} | all-to-all | bytes 1048576 | tf_op jit(solution)/shard_map/all_to_all | solution.py:275
  (98 shorter events, 35.3 us)
Async XLA Ops:
  6.5 1.9 copy-start.7
  6.5 79.8 %all-gather.8.cloned.1.call-start = ((), (), s32[]{:S(2)}) async-start(), calls=%async_computation.6 | async-start | bytes 4730880 | tf_op jit(solution)/shard_map/all_gather | solution.py:178
  8.4 1.5 copy-start
  8.4 13.1 %copy-start.12 = (s32[256]{0:T(256)S(1)}, s32[256]{0:T(256)}, u32[]{:S(2)}) copy-start(s32[256]{0:T(256)} %param.19) | copy-start | bytes 3076
  8.4 24.8 %copy-start.9 = (f32[1792]{0:T(1024)S(1)}, f32[1792]{0:T(1024)}, u32[]{:S(2)}) copy-start(f32[1792]{0:T(1024)} %param.11) | copy-start | bytes 21508
  9.5 123.8 %reduce-scatter.2.cloned.1.call-start = ((), (), s32[]{:S(2)}) async-start(), calls=%async_computation.7 | async-start | bytes 2785280 | tf_op jit(solution)/shard_map/reduce_scatter | solution.py:195
  33.2 190.8 %copy-start.8 = (s32[4,1,256]{2,1,0:T(1,128)}, s32[4,1,256]{2,1,0:T(1,128)S(1)}, u32[]{:S(2)}) copy-start(s32[4,1,256]{2,1,0:T(1,128)S(1)} %all-gather.3) | copy-start | bytes 12292
  86.4 6.9 %collective-permute-start.1 = (bf16[896,2112]{0,1:T(8,128)(2,1)}, bf16[896,2112]{0,1:T(8,128)(2,1)}, u32[]{:S(2)}, u32[]{:S(2)}) collective-permute-start(bf16[896,2112]{0,1:T(8,128)(2,1)} %all-gather.8.cloned.1.call-done), channel_id=1, source_target_pairs={{0,1},{1,0},{2,3},{3,2},{4,5},{5,4},{6,7},{7,6},{8,9},{9,8},{10,11... | collective-permute-start | bytes 11354120 | tf_op jit(solution)/shard_map/ppermute | solution.py:187
  98.2 36.9 %copy-start.11 = (f32[512]{0:T(512)S(1)}, f32[512]{0:T(512)}, u32[]{:S(2)}) copy-start(f32[512]{0:T(512)} %param.15) | copy-start | bytes 6148
  98.2 128.8 %all-gather.12.cloned.1.call-start = ((), (), s32[]{:S(2)}) async-start(), calls=%async_computation.9 | async-start | bytes 1638400 | tf_op jit(solution)/shard_map/all_gather | solution.py:213
  98.6 51.9 %copy-start.3 = (bf16[128,2048]{1,0:T(8,128)(2,1)S(1)}, bf16[128,2048]{1,0:T(8,128)(2,1)}, u32[]{:S(2)}) copy-start(bf16[128,2048]{1,0:T(8,128)(2,1)} %param.17) | copy-start | bytes 1572868
  134.7 16.1 %copy-start.1 = (f32[64,4,528]{2,1,0:T(4,128)}, f32[64,4,528]{2,1,0:T(4,128)S(1)}, u32[]{:S(2)}) copy-start(f32[64,4,528]{2,1,0:T(4,128)S(1)} %reshape.220) | copy-start | bytes 1622020
  151.7 12.1 %all-to-all-start.1 = ((bf16[128,4,256]{2,0,1:T(8,128)(2,1)}), bf16[128,4,256]{2,0,1:T(8,128)(2,1)}, u32[]{:S(2)}, u32[]{:S(2)}) async-start(bf16[128,4,256]{2,0,1:T(8,128)(2,1)} %copy.168), calls=%async_computation.2 | async-start | bytes 524288 | tf_op jit(solution)/shard_map/all_to_all | solution.py:230
  161.6 6.0 %copy-start.10 = (f32[1536]{0:T(1024)S(1)}, f32[1536]{0:T(1024)}, u32[]{:S(2)}) copy-start(f32[1536]{0:T(1024)} %param.14) | copy-start | bytes 18436
  162.3 45.2 %copy-start.4 = (bf16[128,2048]{1,0:T(8,128)(2,1)S(1)}, bf16[128,2048]{1,0:T(8,128)(2,1)}, u32[]{:S(2)}) copy-start(bf16[128,2048]{1,0:T(8,128)(2,1)} %param.18) | copy-start | bytes 1572868
  163.8 44.9 %all-to-all-start = ((bf16[384,4,384]{2,0,1:T(8,128)(2,1)}), bf16[384,4,384]{2,0,1:T(8,128)(2,1)S(1)}, u32[]{:S(2)}, u32[]{:S(2)}) async-start(bf16[384,4,384]{2,0,1:T(8,128)(2,1)} %copy.160), calls=%async_computation | async-start | bytes 2359296 | tf_op jit(solution)/shard_map/all_to_all | solution.py:230
  167.6 83.8 %all-gather.10.cloned.1.call-start = ((), (), s32[]{:S(2)}) async-start(), calls=%async_computation.8 | async-start | bytes 3932160 | tf_op jit(solution)/shard_map/all_gather | solution.py:213
  208.7 10.4 %all-to-all-start.2 = ((bf16[128,4,256]{2,0,1:T(8,128)(2,1)}), bf16[128,4,256]{2,0,1:T(8,128)(2,1)S(1)}, u32[]{:S(2)}, u32[]{:S(2)}) async-start(bf16[128,4,256]{2,0,1:T(8,128)(2,1)} %copy.177), calls=%async_computation.3 | async-start | bytes 524288 | tf_op jit(solution)/shard_map/all_to_all | solution.py:230
  213.0 10.7 %collective-permute-start = (bf16[1536,384]{0,1:T(8,128)(2,1)S(1)}, bf16[1536,384]{0,1:T(8,128)(2,1)S(1)}, u32[]{:S(2)}, u32[]{:S(2)}) collective-permute-start(bf16[1536,384]{0,1:T(8,128)(2,1)S(1)} %copy.161), channel_id=1, source_target_pairs={{0,1},{1,0},{2,3},{3,2},{4,5},{5,4},{6,7},{7,6},{8,9},{9,8},{10,11... | collective-permute-start | bytes 3538952 | tf_op jit(solution)/shard_map/ppermute | solution.py:235
  214.2 5.2 %collective-permute-start.2 = (bf16[512,256]{0,1:T(8,128)(2,1)S(1)}, bf16[512,256]{0,1:T(8,128)(2,1)S(1)}, u32[]{:S(2)}, u32[]{:S(2)}) collective-permute-start(bf16[512,256]{0,1:T(8,128)(2,1)S(1)} %copy.169), channel_id=1, source_target_pairs={{0,1},{1,0},{2,3},{3,2},{4,5},{5,4},{6,7},{7,6},{8,9},{9,8},{10,11... | collective-permute-start | bytes 786440 | tf_op jit(solution)/shard_map/ppermute | solution.py:235
  219.3 1.7 collective-permute-start.3
  227.0 2.2 copy-start.6
  229.2 1.8 copy-start.5
  270.5 18.9 %all-to-all-start.3 = ((bf16[2,1024,128]{2,0,1:T(2,128)(2,1)}), bf16[2,1024,128]{2,0,1:T(2,128)(2,1)S(1)}, u32[]{:S(2)}, u32[]{:S(2)}) async-start(bf16[2,1024,128]{2,0,1:T(2,128)(2,1)} %copy.183), calls=%async_computation.4 | async-start | bytes 1048576 | tf_op jit(solution)/shard_map/all_to_all | solution.py:275
  (1 other events, 1.5 us)
Sparse Core Ops, SparseCore 0:
  9.6 76.7 all-gather.7
  98.3 34.8 reduce-scatter.1
  150.6 29.3 all-gather.11
  207.6 43.7 all-gather.9

commit v9 on v7

--- a/solution.py
+++ b/solution.py
@@ -209,7 +209,14 @@
     compressed_memory = rms_scale(memory_sums[:, :KVRANK], memory_gain).astype(jnp.bfloat16)
     key_rope = rotate(memory_sums[:, KVRANK:], chunk_position).astype(jnp.bfloat16)
     packed = jnp.concatenate([compressed_query, compressed_memory, key_rope], 1)
-    packed = lax.all_gather(packed, "seq", axis=0, tiled=False)
+    from_seq = [packed] + [
+        lax.ppermute(packed, "seq", perm=[(i, (i + k) % seq_count) for i in range(seq_count)])
+        for k in range(1, seq_count)
+    ]
+    packed = jnp.take(jnp.stack(from_seq), (seq_index - jnp.arange(seq_count)) % seq_count, axis=0)
+    packed, query_up, key_up, value_up = lax.optimization_barrier(
+        (packed, query_up, key_up, value_up)
+    )
     packed = lax.all_gather(packed, "tp", axis=0, tiled=False)
     latent = jnp.transpose(packed, (1, 0, 2, 3)).reshape(total_rows, packed.shape[-1])
     cq_all = latent[:, :qrank]

time: 300 us -> 299 us (level)
  waiting for transfers between devices: 158 us -> 149 us
  starting transfers between devices: 12 us -> 16.3 us
    all_gather x1 -> x0, waiting for transfers between devices: 29.2 us -> none  [body(): packed = lax.all_gather(packed, 'seq', axis=0, tiled=False)]
    ppermute x0 -> x3, waiting for transfers between devices: none -> 22.6 us  [body(): lax.ppermute(packed, 'seq', perm=[(i, (i + k) % seq_count) for i in range...]
    ppermute x0 -> x3, starting transfers between devices: none -> 4.5 us  [body(): lax.ppermute(packed, 'seq', perm=[(i, (i + k) % seq_count) for i in range...]
    optimization_barrier x0 -> x3, local copies, waits for them, and re-layouts: none -> 3.73 us  [body(): lax.optimization_barrier((packed, query_up, key_up, value_up))]
    unnamed x28 -> x25, local copies, waits for them, and re-layouts: 7 us -> 3.37 us
  transfers between devices with their start and end apart: 11 -> 13, of which waited for: 8 -> 8; matrix products, arithmetic and copies ran while one was open for 6% -> 7% of each run, Pallas kernels for 0% -> 0%
where the time goes in v9:
time: 299 us; the launch traced here: 298 us
  waiting for transfers between devices  149 us (50%)
  blocking collectives  52.2 us (17%)
  local copies, waits for them, and re-layouts  25.1 us (8%)
  starting transfers between devices  16.3 us (5%)
  matrix products  15.2 us (5%)
  Pallas kernels  14.8 us (5%)
  between operations  13.6 us (5%)
  other arithmetic  12.2 us (4%)
    all_gather x1, waiting for transfers between devices, body(): own_all = lax.all_gather(own_rows, 'seq', axis=1, tiled=True)  52.8 us
    all_to_all x3, waiting for transfers between devices, head_columns(): own = lax.all_to_all(own, 'seq', split_axis=1, concat_axis=0, tiled=True)  35.3 us
    reduce_scatter x1, waiting for transfers between devices, body(): lax.psum_scatter(partial, 'tp', scatter_dimension=0, tiled=True)  34.6 us
    all_to_all x1, blocking collectives, body(): lax.all_to_all(head_output, 'seq', split_axis=1, concat_axis=0, tiled=True)  29.1 us
    ppermute x3, waiting for transfers between devices, body(): lax.ppermute(packed, 'seq', perm=[(i, (i + k) % seq_count) for i in range...  22.6 us
    pallas_call x1, Pallas kernels, heads_attention_kernel(): pl.pallas_call(kernel, grid=(heads, total_rows // block), in_specs=[pl.Bl...  14.8 us
    all_gather x1, blocking collectives, body(): group_ids = lax.all_gather(segment_ids, 'seq', axis=0, tiled=True)  11.7 us
    psum x1, blocking collectives, body(): square_sums = lax.psum(jnp.sum(inputs * inputs, 1), 'tp')  11.4 us
  transfers between devices with their start and end apart: 13, of which 8 were waited for; matrix products, arithmetic and copies ran while one was open for 7% of the time, Pallas kernels for 0%

profile of v9, /device:TPU:0, one launch (start us, length us, event | category | flops | bytes accessed | tf_op | source)
XLA Modules:
  0.0 298.1 jit_solution(9164775571344676877)
XLA Ops:
  10.2 11.4 %psum.7 = f32[256]{0:T(256)S(1)} all-reduce(f32[256]{0:T(256)S(1)} %fusion.2), channel_id=1, replica_groups=mesh['seq'=4,'tp'=4,'dp'=2] {'tp'}, use_global_device_ids=true, to_apply=%region_1.0 | all-reduce | flops 256 | bytes 2048 | tf_op jit(solution)/shard_map/psum | solution.py:168
  21.6 11.7 %all-gather.1 = s32[4,1,256]{2,1,0:T(1,128)S(1)} all-gather(s32[1,1,256]{2,1,0:T(1,128)S(1)} %bitcast.94), channel_id=1, replica_groups=mesh['seq'=4,'tp'=4,'dp'=2] {'seq'}, dimensions={0}, use_global_device_ids=true | all-gather | bytes 5120 | tf_op jit(solution)/shard_map/all_gather | solution.py:165
  33.5 52.8 %all-gather.5.cloned.1.call-done = bf16[896,2112]{0,1:T(8,128)(2,1)} async-done(((bf16[896,528]{0,1:T(8,128)(2,1)}), bf16[896,2112]{0,1:T(8,128)(2,1)}) %all-gather.5.cloned.1.call-update) | async-done | bytes 3784720 | tf_op jit(solution)/shard_map/all_gather | solution.py:178
  86.4 3.5 %fusion.9 = f32[256,2112]{1,0:T(8,128)S(1)} fusion(bf16[896,2112]{0,1:T(8,128)(2,1)} %all-gather.5.cloned.1.call-done, bf16[256,1792]{1,0:T(8,128)(2,1)S(1)} %fusion.4, s32[]{:T(128)S(6)} %select_n.121), kind=kOutput, calls=%fused_computation.32 | convolution fusion | flops 968884224 | bytes 6406148 | tf_op jit(solution)/shard_map/dot_general | solution.py:180
  89.8 3.4 %collective-permute-done = bf16[896,2112]{0,1:T(8,128)(2,1)} collective-permute-done((bf16[896,2112]{0,1:T(8,128)(2,1)}, bf16[896,2112]{0,1:T(8,128)(2,1)}, u32[]{:S(2)}, u32[]{:S(2)}) %collective-permute-start) | collective-permute-done | bytes 3784736 | tf_op jit(solution)/shard_map/ppermute | solution.py:187
  93.3 4.9 %convolution_add_fusion = f32[256,2112]{1,0:T(8,128)} fusion(f32[256,2112]{1,0:T(8,128)S(1)} %fusion.9, bf16[896,2112]{0,1:T(8,128)(2,1)} %collective-permute-done, bf16[256,1792]{1,0:T(8,128)(2,1)S(1)} %fusion.4, s32[]{:T(128)S(6)} %select_n.122), kind=kOutput, calls=%fused_computation.1 | convolution fusion | flops 969424896 | bytes 8634372 | tf_op jit(solution)/shard_map/dot_general | solution.py:190
  98.6 34.6 %reduce-scatter.2.cloned.1.call-done = f32[64,2112]{1,0:T(8,128)} async-done(((f32[256,2112]{1,0:T(8,128)}), f32[64,2112]{1,0:T(8,128)}) %reduce-scatter.2.cloned.1.call-update) | async-done | bytes 540688 | tf_op jit(solution)/shard_map/reduce_scatter | solution.py:195
  136.5 3.4 %collective-permute-start.3 = (bf16[64,2112]{1,0:T(8,128)(2,1)S(1)}, bf16[64,2112]{1,0:T(8,128)(2,1)S(1)}, u32[]{:S(2)}, u32[]{:S(2)}) collective-permute-start(bf16[64,2112]{1,0:T(8,128)(2,1)S(1)} %concatenate.23), channel_id=1, source_target_pairs={{0,24},{8,0},{16,8},{24,16},{1,25},{9,1},{17,9},{25,17},{2,26},{10... | collective-permute-start | bytes 811016 | tf_op jit(solution)/shard_map/ppermute | solution.py:213
  141.0 5.9 %collective-permute-done.3 = bf16[64,2112]{1,0:T(8,128)(2,1)S(1)} collective-permute-done((bf16[64,2112]{1,0:T(8,128)(2,1)S(1)}, bf16[64,2112]{1,0:T(8,128)(2,1)S(1)}, u32[]{:S(2)}, u32[]{:S(2)}) %collective-permute-start.3) | collective-permute-done | bytes 270368 | tf_op jit(solution)/shard_map/ppermute | solution.py:213
  147.0 16.6 %collective-permute-done.2 = bf16[64,2112]{1,0:T(8,128)(2,1)S(1)} collective-permute-done((bf16[64,2112]{1,0:T(8,128)(2,1)S(1)}, bf16[64,2112]{1,0:T(8,128)(2,1)S(1)}, u32[]{:S(2)}, u32[]{:S(2)}) %collective-permute-start.2) | collective-permute-done | bytes 270368 | tf_op jit(solution)/shard_map/ppermute | solution.py:213
  166.9 4.0 %all-to-all-start.2 = ((bf16[128,4,256]{2,0,1:T(8,128)(2,1)}), bf16[128,4,256]{2,0,1:T(8,128)(2,1)}, u32[]{:S(2)}, u32[]{:S(2)}) async-start(bf16[128,4,256]{2,0,1:T(8,128)(2,1)} %copy.129), calls=%async_computation.3 | async-start | bytes 524288 | tf_op jit(solution)/shard_map/all_to_all | solution.py:235
  170.9 3.2 %copy.115 = bf16[384,3072]{0,1:T(8,128)(2,1)S(1)} copy(bf16[384,3072]{1,0:T(8,128)(2,1)} %param.16) | data formatting | bytes 4718592 | tf_op jit(solution)/shard_map/optimization_barrier | solution.py:217
  175.7 4.0 %all-to-all-done.2 = bf16[128,4,256]{2,0,1:T(8,128)(2,1)} async-done(((bf16[128,4,256]{2,0,1:T(8,128)(2,1)}), bf16[128,4,256]{2,0,1:T(8,128)(2,1)}, u32[]{:S(2)}, u32[]{:S(2)}) %all-to-all-start.2) | async-done | bytes 262176 | tf_op jit(solution)/shard_map/all_to_all | solution.py:235
  179.7 3.5 %all-to-all-start = ((bf16[384,4,384]{2,0,1:T(8,128)(2,1)}), bf16[384,4,384]{2,0,1:T(8,128)(2,1)S(1)}, u32[]{:S(2)}, u32[]{:S(2)}) async-start(bf16[384,4,384]{2,0,1:T(8,128)(2,1)} %copy.116), calls=%async_computation.1 | async-start | bytes 2359296 | tf_op jit(solution)/shard_map/all_to_all | solution.py:235
  184.4 26.1 %all-to-all-done = bf16[384,4,384]{2,0,1:T(8,128)(2,1)S(1)} async-done(((bf16[384,4,384]{2,0,1:T(8,128)(2,1)}), bf16[384,4,384]{2,0,1:T(8,128)(2,1)S(1)}, u32[]{:S(2)}, u32[]{:S(2)}) %all-to-all-start) | async-done | bytes 1179680 | tf_op jit(solution)/shard_map/all_to_all | solution.py:235
  210.5 3.6 %all-to-all-start.1 = ((bf16[128,4,256]{2,0,1:T(8,128)(2,1)}), bf16[128,4,256]{2,0,1:T(8,128)(2,1)S(1)}, u32[]{:S(2)}, u32[]{:S(2)}) async-start(bf16[128,4,256]{2,0,1:T(8,128)(2,1)} %copy.123), calls=%async_computation.2 | async-start | bytes 524288 | tf_op jit(solution)/shard_map/all_to_all | solution.py:235
  217.1 5.2 %all-to-all-done.1 = bf16[128,4,256]{2,0,1:T(8,128)(2,1)S(1)} async-done(((bf16[128,4,256]{2,0,1:T(8,128)(2,1)}), bf16[128,4,256]{2,0,1:T(8,128)(2,1)S(1)}, u32[]{:S(2)}, u32[]{:S(2)}) %all-to-all-start.1) | async-done | bytes 262176 | tf_op jit(solution)/shard_map/all_to_all | solution.py:235
  224.3 1.9 multiply_cosine_fusion
  229.5 2.6 copy.120
  232.8 3.4 %fusion.1 = f32[4,1024,192]{2,1,0:T(8,128)S(1)} fusion(bf16[1536,4,192]{0,2,1:T(8,128)(2,1)S(1)} %bitcast.78, bf16[1024,2112]{1,0:T(8,128)(2,1)S(1)} %bitcast.67), kind=kOutput, calls=%fused_computation.7 | convolution fusion | flops 2415919104 | bytes 8650752 | tf_op jit(solution)/shard_map/td,dhe->hte/dot_general | solution.py:256
  241.5 2.0 pad_maximum_fusion.1.query_ref
  243.5 14.8 %shard_map.100 = bf16[4,1024,128]{2,1,0:T(8,128)(2,1)} custom-call(bf16[4,1024,192]{2,1,0:T(8,128)(2,1)} %pad_maximum_fusion.1.query_ref, bf16[4,1024,128]{2,1,0:T(8,128)(2,1)} %fusion.5.key_ref, bf16[1024,64]{1,0:T(8,128)(2,1)} %slice.63.rope_ref, bf16[4,1024,128]{2,1,0:T(8,128)(2,1)} %fusion.6.value_ref, s32[1024,1]{1,0:T(8,128)} %copy.134.ids_col_ref, ...), custom_call_target="tpu_custom_call" | custom-call | flops 1342177280 | bytes 4718592 | tf_op jit(solution)/shard_map/pallas_call | solution.py:112
  258.3 2.0 copy.135
  260.3 29.1 %all_to_all.63 = bf16[4,1024,128]{2,0,1:T(4,128)(2,1)S(1)} all-to-all(bf16[4,1024,128]{2,0,1:T(4,128)(2,1)S(1)} %copy.135), channel_id=1, replica_groups=mesh['seq'=4,'tp'=4,'dp'=2] {'seq'}, dimensions={1} | all-to-all | bytes 2097152 | tf_op jit(solution)/shard_map/all_to_all | solution.py:275
  (96 shorter events, 30.9 us)
Async XLA Ops:
  6.5 1.9 copy-start.5
  6.5 79.8 %all-gather.5.cloned.1.call-start = ((), (), s32[]{:S(2)}) async-start(), calls=%async_computation.5 | async-start | bytes 4730880 | tf_op jit(solution)/shard_map/all_gather | solution.py:178
  8.4 1.5 copy-start
  8.4 13.1 %copy-start.10 = (s32[256]{0:T(256)S(1)}, s32[256]{0:T(256)}, u32[]{:S(2)}) copy-start(s32[256]{0:T(256)} %param.19) | copy-start | bytes 3076
  8.4 24.8 %copy-start.7 = (f32[1792]{0:T(1024)S(1)}, f32[1792]{0:T(1024)}, u32[]{:S(2)}) copy-start(f32[1792]{0:T(1024)} %param.11) | copy-start | bytes 21508
  9.5 123.7 %reduce-scatter.2.cloned.1.call-start = ((), (), s32[]{:S(2)}) async-start(), calls=%async_computation.6 | async-start | bytes 2785280 | tf_op jit(solution)/shard_map/reduce_scatter | solution.py:195
  33.2 190.0 %copy-start.6 = (s32[4,1,256]{2,1,0:T(1,128)}, s32[4,1,256]{2,1,0:T(1,128)S(1)}, u32[]{:S(2)}) copy-start(s32[4,1,256]{2,1,0:T(1,128)S(1)} %all-gather.1) | copy-start | bytes 12292
  86.4 6.9 %collective-permute-start = (bf16[896,2112]{0,1:T(8,128)(2,1)}, bf16[896,2112]{0,1:T(8,128)(2,1)}, u32[]{:S(2)}, u32[]{:S(2)}) collective-permute-start(bf16[896,2112]{0,1:T(8,128)(2,1)} %all-gather.5.cloned.1.call-done), channel_id=1, source_target_pairs={{0,1},{1,0},{2,3},{3,2},{4,5},{5,4},{6,7},{7,6},{8,9},{9,8},{10,11... | collective-permute-start | bytes 11354120 | tf_op jit(solution)/shard_map/ppermute | solution.py:187
  98.2 131.3 %all-gather.7.cloned.1.call-start = ((), (), s32[]{:S(2)}) async-start(), calls=%async_computation.7 | async-start | bytes 5570560 | tf_op jit(solution)/shard_map/all_gather | solution.py:220
  98.2 37.4 %copy-start.9 = (f32[512]{0:T(512)S(1)}, f32[512]{0:T(512)}, u32[]{:S(2)}) copy-start(f32[512]{0:T(512)} %param.15) | copy-start | bytes 6148
  134.7 1.5 copy-start.8
  136.5 10.5 %collective-permute-start.3 = (bf16[64,2112]{1,0:T(8,128)(2,1)S(1)}, bf16[64,2112]{1,0:T(8,128)(2,1)S(1)}, u32[]{:S(2)}, u32[]{:S(2)}) collective-permute-start(bf16[64,2112]{1,0:T(8,128)(2,1)S(1)} %concatenate.23), channel_id=1, source_target_pairs={{0,24},{8,0},{16,8},{24,16},{1,25},{9,1},{17,9},{25,17},{2,26},{10... | collective-permute-start | bytes 811016 | tf_op jit(solution)/shard_map/ppermute | solution.py:213
  139.9 23.7 %collective-permute-start.2 = (bf16[64,2112]{1,0:T(8,128)(2,1)S(1)}, bf16[64,2112]{1,0:T(8,128)(2,1)S(1)}, u32[]{:S(2)}, u32[]{:S(2)}) collective-permute-start(bf16[64,2112]{1,0:T(8,128)(2,1)S(1)} %concatenate.23), channel_id=1, source_target_pairs={{0,16},{8,24},{16,0},{24,8},{1,17},{9,25},{17,1},{25,9},{2,18},{10... | collective-permute-start | bytes 811016 | tf_op jit(solution)/shard_map/ppermute | solution.py:213
  139.9 23.7 %collective-permute-start.1 = (bf16[64,2112]{1,0:T(8,128)(2,1)S(1)}, bf16[64,2112]{1,0:T(8,128)(2,1)S(1)}, u32[]{:S(2)}, u32[]{:S(2)}) collective-permute-start(bf16[64,2112]{1,0:T(8,128)(2,1)S(1)} %concatenate.23), channel_id=1, source_target_pairs={{0,8},{8,16},{16,24},{24,0},{1,9},{9,17},{17,25},{25,1},{2,10},{10... | collective-permute-start | bytes 811016 | tf_op jit(solution)/shard_map/ppermute | solution.py:213
  164.5 1.2 copy-start.1
  166.9 12.9 %all-to-all-start.2 = ((bf16[128,4,256]{2,0,1:T(8,128)(2,1)}), bf16[128,4,256]{2,0,1:T(8,128)(2,1)}, u32[]{:S(2)}, u32[]{:S(2)}) async-start(bf16[128,4,256]{2,0,1:T(8,128)(2,1)} %copy.129), calls=%async_computation.3 | async-start | bytes 524288 | tf_op jit(solution)/shard_map/all_to_all | solution.py:235
  174.2 9.0 %copy-start.2 = (bf16[128,2048]{1,0:T(8,128)(2,1)S(1)}, bf16[128,2048]{1,0:T(8,128)(2,1)}, u32[]{:S(2)}) copy-start(bf16[128,2048]{1,0:T(8,128)(2,1)} %param.17) | copy-start | bytes 1572868
  179.7 30.8 %all-to-all-start = ((bf16[384,4,384]{2,0,1:T(8,128)(2,1)}), bf16[384,4,384]{2,0,1:T(8,128)(2,1)S(1)}, u32[]{:S(2)}, u32[]{:S(2)}) async-start(bf16[384,4,384]{2,0,1:T(8,128)(2,1)} %copy.116), calls=%async_computation.1 | async-start | bytes 2359296 | tf_op jit(solution)/shard_map/all_to_all | solution.py:235
  210.5 11.8 %all-to-all-start.1 = ((bf16[128,4,256]{2,0,1:T(8,128)(2,1)}), bf16[128,4,256]{2,0,1:T(8,128)(2,1)S(1)}, u32[]{:S(2)}, u32[]{:S(2)}) async-start(bf16[128,4,256]{2,0,1:T(8,128)(2,1)} %copy.123), calls=%async_computation.2 | async-start | bytes 524288 | tf_op jit(solution)/shard_map/all_to_all | solution.py:235
  214.8 14.3 %collective-permute-start.4 = (bf16[1536,384]{0,1:T(8,128)(2,1)S(1)}, bf16[1536,384]{0,1:T(8,128)(2,1)S(1)}, u32[]{:S(2)}, u32[]{:S(2)}) collective-permute-start(bf16[1536,384]{0,1:T(8,128)(2,1)S(1)} %copy.117), channel_id=1, source_target_pairs={{0,1},{1,0},{2,3},{3,2},{4,5},{5,4},{6,7},{7,6},{8,9},{9,8},{10,11... | collective-permute-start | bytes 3538952 | tf_op jit(solution)/shard_map/ppermute | solution.py:240
  216.6 9.5 %collective-permute-start.6 = (bf16[512,256]{0,1:T(8,128)(2,1)}, bf16[512,256]{0,1:T(8,128)(2,1)}, u32[]{:S(2)}, u32[]{:S(2)}) collective-permute-start(bf16[512,256]{0,1:T(8,128)(2,1)} %copy.130), channel_id=1, source_target_pairs={{0,1},{1,0},{2,3},{3,2},{4,5},{5,4},{6,7},{7,6},{8,9},{9,8},{10,11... | collective-permute-start | bytes 786440 | tf_op jit(solution)/shard_map/ppermute | solution.py:240
  223.2 3.0 collective-permute-start.5
  236.3 1.0 copy-start.3
  236.3 2.8 copy-start.4
Sparse Core Ops, SparseCore 0:
  9.6 76.7 all-gather.4
  98.3 34.8 reduce-scatter.1
  165.8 54.1 all-gather.6

commit v10 on v9

--- a/solution.py
+++ b/solution.py
@@ -74,9 +74,9 @@
 
 
 def attention_kernel(
-    query_ref, key_ref, rope_ref, value_ref, ids_col_ref, ids_row_ref, out_ref, *, block, window, doc_most, scale
+    block_ref, query_ref, key_ref, rope_ref, value_ref, ids_col_ref, ids_row_ref, out_ref, *, block, window, doc_most, scale
 ):
-    lower = pl.program_id(1) * block
+    lower = block_ref[0] * block
     start = pl.multiple_of(jnp.maximum(lower - doc_most, 0), block)
     query = query_ref[0]
     keys = key_ref[0, pl.ds(start, window), :]
@@ -101,33 +101,36 @@
     out_ref[0] = (weighted / denominator).astype(out_ref.dtype)
 
 
-def heads_attention_kernel(query, key_nope, key_rope, value, group_ids, score_scale, doc_most):
+def block_attention(query, key_nope, key_rope, value, group_ids, score_scale, doc_most, block, index):
     heads, total_rows, _ = query.shape
-    block = min(256, total_rows)
     window = min(total_rows, doc_most + block)
     kernel = functools.partial(
         attention_kernel, block=block, window=window, doc_most=doc_most, scale=score_scale
     )
-    flops = 2 * heads * total_rows * window * (NOPE + ROPE + VDIM)
+    flops = 2 * heads * block * window * (NOPE + ROPE + VDIM)
     return pl.pallas_call(
         kernel,
-        grid=(heads, total_rows // block),
-        in_specs=[
-            pl.BlockSpec((1, block, NOPE + ROPE), lambda h, i: (h, i, 0)),
-            pl.BlockSpec((1, total_rows, NOPE), lambda h, i: (h, 0, 0)),
-            pl.BlockSpec((total_rows, ROPE), lambda h, i: (0, 0)),
-            pl.BlockSpec((1, total_rows, VDIM), lambda h, i: (h, 0, 0)),
-            pl.BlockSpec((block, 1), lambda h, i: (i, 0)),
-            pl.BlockSpec((1, total_rows), lambda h, i: (0, 0)),
-        ],
-        out_specs=pl.BlockSpec((1, block, VDIM), lambda h, i: (h, i, 0)),
-        out_shape=jax.ShapeDtypeStruct((heads, total_rows, VDIM), jnp.bfloat16),
+        grid_spec=pltpu.PrefetchScalarGridSpec(
+            num_scalar_prefetch=1,
+            grid=(heads,),
+            in_specs=[
+                pl.BlockSpec((1, block, NOPE + ROPE), lambda h, b: (h, b[0], 0)),
+                pl.BlockSpec((1, total_rows, NOPE), lambda h, b: (h, 0, 0)),
+                pl.BlockSpec((total_rows, ROPE), lambda h, b: (0, 0)),
+                pl.BlockSpec((1, total_rows, VDIM), lambda h, b: (h, 0, 0)),
+                pl.BlockSpec((block, 1), lambda h, b: (b[0], 0)),
+                pl.BlockSpec((1, total_rows), lambda h, b: (0, 0)),
+            ],
+            out_specs=pl.BlockSpec((1, block, VDIM), lambda h, b: (h, 0, 0)),
+        ),
+        out_shape=jax.ShapeDtypeStruct((heads, block, VDIM), jnp.bfloat16),
         cost_estimate=pl.CostEstimate(
             flops=flops,
-            transcendentals=heads * total_rows * window,
-            bytes_accessed=2 * heads * total_rows * (NOPE + ROPE + NOPE + VDIM + VDIM),
+            transcendentals=heads * block * window,
+            bytes_accessed=2 * heads * (block * (NOPE + ROPE + VDIM) + window * (NOPE + VDIM)),
         ),
     )(
+        jnp.reshape(index, (1,)).astype(jnp.int32),
         query,
         key_nope,
         key_rope,
@@ -269,11 +272,21 @@
         "td,dhe->hte", cm_all, value_w.reshape(KVRANK, heads, VDIM), preferred_element_type=jnp.float32
     ).astype(jnp.bfloat16)
     score_scale = (NOPE + ROPE) ** (-0.5)
-    head_output = heads_attention_kernel(
-        query, key_nope, rope_all, value, group_ids, score_scale, doc_most
-    )
-    attended = lax.all_to_all(head_output, "seq", split_axis=1, concat_axis=0, tiled=True)
-    attended = jnp.transpose(attended, (1, 0, 2))
+    received = [None] * seq_count
+    for k in list(range(1, seq_count)) + [0]:
+        rows = block_attention(
+            query, key_nope, rope_all, value, group_ids, score_scale, doc_most, tok_count,
+            (seq_index + k) % seq_count,
+        )
+        if k:
+            rows = lax.ppermute(
+                rows, "seq", perm=[(i, (i + k) % seq_count) for i in range(seq_count)]
+            )
+        received[k] = rows
+    attended = jnp.take(
+        jnp.stack(received), (seq_index - jnp.arange(seq_count)) % seq_count, axis=0
+    )
+    attended = jnp.transpose(attended, (2, 0, 1, 3))
     return attended.reshape(tok_count, local_heads * VDIM)
 
 

time: 299 us -> 287 us (0.960)
  blocking collectives: 52.2 us -> 23 us
  waiting for transfers between devices: 149 us -> 159 us
  Pallas kernels: 14.8 us -> 19.6 us
    all_to_all x1 -> x0, blocking collectives: 29.1 us -> none  [body(): lax.all_to_all(head_output, 'seq', split_axis=1, concat_axis=0, tiled=True)]
    ppermute x0 -> x3, waiting for transfers between devices: none -> 10.4 us  [body(): lax.ppermute(rows, 'seq', perm=[(i, (i + k) % seq_count) for i in range(s...]
    pallas_call x1 -> x4, Pallas kernels: 14.8 us -> 19.6 us  [block_attention(): pl.pallas_call(kernel, grid_spec=pltpu.PrefetchScalarGridSpec(num_scalar_...]
  transfers between devices with their start and end apart: 13 -> 16, of which waited for: 8 -> 9; matrix products, arithmetic and copies ran while one was open for 7% -> 7% of each run, Pallas kernels for 0% -> 5%
where the time goes in v10:
time: 287 us; the launch traced here: 286 us
  waiting for transfers between devices  159 us (55%)
  local copies, waits for them, and re-layouts  23.6 us (8%)
  blocking collectives  23 us (8%)
  Pallas kernels  19.6 us (7%)
  starting transfers between devices  18.4 us (6%)
  matrix products  15.3 us (5%)
  between operations  13.6 us (5%)
  other arithmetic  13.5 us (5%)
    all_gather x1, waiting for transfers between devices, body(): own_all = lax.all_gather(own_rows, 'seq', axis=1, tiled=True)  52.8 us
    all_to_all x3, waiting for transfers between devices, head_columns(): own = lax.all_to_all(own, 'seq', split_axis=1, concat_axis=0, tiled=True)  35.2 us
    reduce_scatter x1, waiting for transfers between devices, body(): lax.psum_scatter(partial, 'tp', scatter_dimension=0, tiled=True)  34.6 us
    ppermute x3, waiting for transfers between devices, body(): lax.ppermute(packed, 'seq', perm=[(i, (i + k) % seq_count) for i in range...  22.6 us
    pallas_call x4, Pallas kernels, block_attention(): pl.pallas_call(kernel, grid_spec=pltpu.PrefetchScalarGridSpec(num_scalar_...  19.6 us
    all_gather x1, blocking collectives, body(): group_ids = lax.all_gather(segment_ids, 'seq', axis=0, tiled=True)  11.7 us
    psum x1, blocking collectives, body(): square_sums = lax.psum(jnp.sum(inputs * inputs, 1), 'tp')  11.4 us
    all_to_all x3, starting transfers between devices, head_columns(): own = lax.all_to_all(own, 'seq', split_axis=1, concat_axis=0, tiled=True)  11.2 us
  transfers between devices with their start and end apart: 16, of which 9 were waited for; matrix products, arithmetic and copies ran while one was open for 7% of the time, Pallas kernels for 5%

profile of v10, /device:TPU:0, one launch (start us, length us, event | category | flops | bytes accessed | tf_op | source)
XLA Modules:
  0.0 286.1 jit_solution(5415547823491279136)
XLA Ops:
  10.2 11.4 %psum.7 = f32[256]{0:T(256)S(1)} all-reduce(f32[256]{0:T(256)S(1)} %fusion.2), channel_id=1, replica_groups=mesh['seq'=4,'tp'=4,'dp'=2] {'tp'}, use_global_device_ids=true, to_apply=%region_1.0 | all-reduce | flops 256 | bytes 2048 | tf_op jit(solution)/shard_map/psum | solution.py:171
  21.6 11.7 %all-gather.1 = s32[4,1,256]{2,1,0:T(1,128)S(1)} all-gather(s32[1,1,256]{2,1,0:T(1,128)S(1)} %bitcast.103), channel_id=1, replica_groups=mesh['seq'=4,'tp'=4,'dp'=2] {'seq'}, dimensions={0}, use_global_device_ids=true | all-gather | bytes 5120 | tf_op jit(solution)/shard_map/all_gather | solution.py:168
  33.5 52.8 %all-gather.5.cloned.1.call-done = bf16[896,2112]{0,1:T(8,128)(2,1)} async-done(((bf16[896,528]{0,1:T(8,128)(2,1)}), bf16[896,2112]{0,1:T(8,128)(2,1)}) %all-gather.5.cloned.1.call-update) | async-done | bytes 3784720 | tf_op jit(solution)/shard_map/all_gather | solution.py:181
  86.4 3.5 %fusion.9 = f32[256,2112]{1,0:T(8,128)S(1)} fusion(bf16[896,2112]{0,1:T(8,128)(2,1)} %all-gather.5.cloned.1.call-done, bf16[256,1792]{1,0:T(8,128)(2,1)S(1)} %fusion.4, s32[]{:T(128)S(6)} %select_n.150), kind=kOutput, calls=%fused_computation.35 | convolution fusion | flops 968884224 | bytes 6406148 | tf_op jit(solution)/shard_map/dot_general | solution.py:183
  89.9 3.4 %collective-permute-done = bf16[896,2112]{0,1:T(8,128)(2,1)} collective-permute-done((bf16[896,2112]{0,1:T(8,128)(2,1)}, bf16[896,2112]{0,1:T(8,128)(2,1)}, u32[]{:S(2)}, u32[]{:S(2)}) %collective-permute-start) | collective-permute-done | bytes 3784736 | tf_op jit(solution)/shard_map/ppermute | solution.py:190
  93.3 4.9 %convolution_add_fusion = f32[256,2112]{1,0:T(8,128)} fusion(f32[256,2112]{1,0:T(8,128)S(1)} %fusion.9, bf16[896,2112]{0,1:T(8,128)(2,1)} %collective-permute-done, bf16[256,1792]{1,0:T(8,128)(2,1)S(1)} %fusion.4, s32[]{:T(128)S(6)} %select_n.151), kind=kOutput, calls=%fused_computation.2 | convolution fusion | flops 969424896 | bytes 8634372 | tf_op jit(solution)/shard_map/dot_general | solution.py:193
  98.6 34.6 %reduce-scatter.2.cloned.1.call-done = f32[64,2112]{1,0:T(8,128)} async-done(((f32[256,2112]{1,0:T(8,128)}), f32[64,2112]{1,0:T(8,128)}) %reduce-scatter.2.cloned.1.call-update) | async-done | bytes 540688 | tf_op jit(solution)/shard_map/reduce_scatter | solution.py:198
  136.5 3.4 %collective-permute-start.3 = (bf16[64,2112]{1,0:T(8,128)(2,1)S(1)}, bf16[64,2112]{1,0:T(8,128)(2,1)S(1)}, u32[]{:S(2)}, u32[]{:S(2)}) collective-permute-start(bf16[64,2112]{1,0:T(8,128)(2,1)S(1)} %concatenate.23), channel_id=1, source_target_pairs={{0,24},{8,0},{16,8},{24,16},{1,25},{9,1},{17,9},{25,17},{2,26},{10... | collective-permute-start | bytes 811016 | tf_op jit(solution)/shard_map/ppermute | solution.py:216
  141.0 6.0 %collective-permute-done.3 = bf16[64,2112]{1,0:T(8,128)(2,1)S(1)} collective-permute-done((bf16[64,2112]{1,0:T(8,128)(2,1)S(1)}, bf16[64,2112]{1,0:T(8,128)(2,1)S(1)}, u32[]{:S(2)}, u32[]{:S(2)}) %collective-permute-start.3) | collective-permute-done | bytes 270368 | tf_op jit(solution)/shard_map/ppermute | solution.py:216
  147.0 16.6 %collective-permute-done.2 = bf16[64,2112]{1,0:T(8,128)(2,1)S(1)} collective-permute-done((bf16[64,2112]{1,0:T(8,128)(2,1)S(1)}, bf16[64,2112]{1,0:T(8,128)(2,1)S(1)}, u32[]{:S(2)}, u32[]{:S(2)}) %collective-permute-start.2) | collective-permute-done | bytes 270368 | tf_op jit(solution)/shard_map/ppermute | solution.py:216
  166.9 4.1 %all-to-all-start.2 = ((bf16[128,4,256]{2,0,1:T(8,128)(2,1)}), bf16[128,4,256]{2,0,1:T(8,128)(2,1)}, u32[]{:S(2)}, u32[]{:S(2)}) async-start(bf16[128,4,256]{2,0,1:T(8,128)(2,1)} %copy.123), calls=%async_computation.3 | async-start | bytes 524288 | tf_op jit(solution)/shard_map/all_to_all | solution.py:238
  171.0 3.2 %copy.109 = bf16[384,3072]{0,1:T(8,128)(2,1)S(1)} copy(bf16[384,3072]{1,0:T(8,128)(2,1)} %param.16) | data formatting | bytes 4718592 | tf_op jit(solution)/shard_map/optimization_barrier | solution.py:220
  175.8 4.0 %all-to-all-done.2 = bf16[128,4,256]{2,0,1:T(8,128)(2,1)} async-done(((bf16[128,4,256]{2,0,1:T(8,128)(2,1)}), bf16[128,4,256]{2,0,1:T(8,128)(2,1)}, u32[]{:S(2)}, u32[]{:S(2)}) %all-to-all-start.2) | async-done | bytes 262176 | tf_op jit(solution)/shard_map/all_to_all | solution.py:238
  179.8 3.5 %all-to-all-start = ((bf16[384,4,384]{2,0,1:T(8,128)(2,1)}), bf16[384,4,384]{2,0,1:T(8,128)(2,1)S(1)}, u32[]{:S(2)}, u32[]{:S(2)}) async-start(bf16[384,4,384]{2,0,1:T(8,128)(2,1)} %copy.110), calls=%async_computation.1 | async-start | bytes 2359296 | tf_op jit(solution)/shard_map/all_to_all | solution.py:238
  184.5 26.1 %all-to-all-done = bf16[384,4,384]{2,0,1:T(8,128)(2,1)S(1)} async-done(((bf16[384,4,384]{2,0,1:T(8,128)(2,1)}), bf16[384,4,384]{2,0,1:T(8,128)(2,1)S(1)}, u32[]{:S(2)}, u32[]{:S(2)}) %all-to-all-start) | async-done | bytes 1179680 | tf_op jit(solution)/shard_map/all_to_all | solution.py:238
  210.6 3.6 %all-to-all-start.1 = ((bf16[128,4,256]{2,0,1:T(8,128)(2,1)}), bf16[128,4,256]{2,0,1:T(8,128)(2,1)S(1)}, u32[]{:S(2)}, u32[]{:S(2)}) async-start(bf16[128,4,256]{2,0,1:T(8,128)(2,1)} %copy.117), calls=%async_computation.2 | async-start | bytes 524288 | tf_op jit(solution)/shard_map/all_to_all | solution.py:238
  217.2 5.2 %all-to-all-done.1 = bf16[128,4,256]{2,0,1:T(8,128)(2,1)S(1)} async-done(((bf16[128,4,256]{2,0,1:T(8,128)(2,1)}), bf16[128,4,256]{2,0,1:T(8,128)(2,1)S(1)}, u32[]{:S(2)}, u32[]{:S(2)}) %all-to-all-start.1) | async-done | bytes 262176 | tf_op jit(solution)/shard_map/all_to_all | solution.py:238
  229.5 2.6 copy.114
  232.9 3.4 %fusion.1 = f32[4,1024,192]{2,1,0:T(8,128)S(1)} fusion(bf16[1536,4,192]{0,2,1:T(8,128)(2,1)S(1)} %bitcast.80, bf16[1024,2112]{1,0:T(8,128)(2,1)S(1)} %bitcast.71), kind=kOutput, calls=%fused_computation.8 | convolution fusion | flops 2415919104 | bytes 8650752 | tf_op jit(solution)/shard_map/td,dhe->hte/dot_general | solution.py:259
  243.6 4.9 %shard_map.103 = bf16[4,256,128]{2,1,0:T(8,128)(2,1)} custom-call(s32[1]{0:T(128)} %bitcast.45.block_ref, bf16[4,1024,192]{2,1,0:T(8,128)(2,1)} %pad_maximum_fusion.1.query_ref, bf16[4,1024,128]{2,1,0:T(8,128)(2,1)} %fusion.5.key_ref, bf16[1024,64]{1,0:T(8,128)(2,1)} %slice.65.rope_ref, bf16[4,1024,128]{2,1,0:T(8,128)(2,1)} %fusion.6.value_ref, ...), custom_call_target="tpu_custom_call" | custom-call | flops 335544320 | bytes 1703936 | tf_op jit(solution)/shard_map/pallas_call | solution.py:111
  249.9 4.9 %shard_map.102 = bf16[4,256,128]{2,1,0:T(8,128)(2,1)} custom-call(s32[1]{0:T(128)} %bitcast.43.block_ref, bf16[4,1024,192]{2,1,0:T(8,128)(2,1)} %pad_maximum_fusion.1.query_ref, bf16[4,1024,128]{2,1,0:T(8,128)(2,1)} %fusion.5.key_ref, bf16[1024,64]{1,0:T(8,128)(2,1)} %slice.65.rope_ref, bf16[4,1024,128]{2,1,0:T(8,128)(2,1)} %fusion.6.value_ref, ...), custom_call_target="tpu_custom_call" | custom-call | flops 335544320 | bytes 1703936 | tf_op jit(solution)/shard_map/pallas_call | solution.py:111
  255.0 4.9 %shard_map.101 = bf16[4,256,128]{2,1,0:T(8,128)(2,1)} custom-call(s32[1]{0:T(128)} %bitcast.41.block_ref, bf16[4,1024,192]{2,1,0:T(8,128)(2,1)} %pad_maximum_fusion.1.query_ref, bf16[4,1024,128]{2,1,0:T(8,128)(2,1)} %fusion.5.key_ref, bf16[1024,64]{1,0:T(8,128)(2,1)} %slice.65.rope_ref, bf16[4,1024,128]{2,1,0:T(8,128)(2,1)} %fusion.6.value_ref, ...), custom_call_target="tpu_custom_call" | custom-call | flops 335544320 | bytes 1703936 | tf_op jit(solution)/shard_map/pallas_call | solution.py:111
  260.3 4.9 %shard_map.100 = bf16[4,256,128]{2,1,0:T(8,128)(2,1)} custom-call(s32[1]{0:T(128)} %bitcast.block_ref, bf16[4,1024,192]{2,1,0:T(8,128)(2,1)} %pad_maximum_fusion.1.query_ref, bf16[4,1024,128]{2,1,0:T(8,128)(2,1)} %fusion.5.key_ref, bf16[1024,64]{1,0:T(8,128)(2,1)} %slice.65.rope_ref, bf16[4,1024,128]{2,1,0:T(8,128)(2,1)} %fusion.6.value_ref, ...), custom_call_target="tpu_custom_call" | custom-call | flops 335544320 | bytes 1703936 | tf_op jit(solution)/shard_map/pallas_call | solution.py:111
  265.3 10.3 %collective-permute-done.8 = bf16[4,256,128]{2,1,0:T(8,128)(2,1)S(1)} collective-permute-done((bf16[4,256,128]{2,1,0:T(8,128)(2,1)}, bf16[4,256,128]{2,1,0:T(8,128)(2,1)S(1)}, u32[]{:S(2)}, u32[]{:S(2)}) %collective-permute-start.8) | collective-permute-done | bytes 262176 | tf_op jit(solution)/shard_map/ppermute | solution.py:282
  (108 shorter events, 38.6 us)
Async XLA Ops:
  6.5 79.8 %all-gather.5.cloned.1.call-start = ((), (), s32[]{:S(2)}) async-start(), calls=%async_computation.4 | async-start | bytes 4730880 | tf_op jit(solution)/shard_map/all_gather | solution.py:181
  8.4 13.1 %copy-start.12 = (s32[256]{0:T(256)S(1)}, s32[256]{0:T(256)}, u32[]{:S(2)}) copy-start(s32[256]{0:T(256)} %param.19) | copy-start | bytes 3076
  8.4 24.8 %copy-start.7 = (f32[1792]{0:T(1024)S(1)}, f32[1792]{0:T(1024)}, u32[]{:S(2)}) copy-start(f32[1792]{0:T(1024)} %param.11) | copy-start | bytes 21508
  9.5 123.8 %reduce-scatter.2.cloned.1.call-start = ((), (), s32[]{:S(2)}) async-start(), calls=%async_computation.5 | async-start | bytes 2785280 | tf_op jit(solution)/shard_map/reduce_scatter | solution.py:198
  33.2 190.0 %copy-start.6 = (s32[4,1,256]{2,1,0:T(1,128)}, s32[4,1,256]{2,1,0:T(1,128)S(1)}, u32[]{:S(2)}) copy-start(s32[4,1,256]{2,1,0:T(1,128)S(1)} %all-gather.1) | copy-start | bytes 12292
  86.4 6.9 %collective-permute-start = (bf16[896,2112]{0,1:T(8,128)(2,1)}, bf16[896,2112]{0,1:T(8,128)(2,1)}, u32[]{:S(2)}, u32[]{:S(2)}) collective-permute-start(bf16[896,2112]{0,1:T(8,128)(2,1)} %all-gather.5.cloned.1.call-done), channel_id=1, source_target_pairs={{0,1},{1,0},{2,3},{3,2},{4,5},{5,4},{6,7},{7,6},{8,9},{9,8},{10,11... | collective-permute-start | bytes 11354120 | tf_op jit(solution)/shard_map/ppermute | solution.py:190
  98.2 131.3 %all-gather.7.cloned.1.call-start = ((), (), s32[]{:S(2)}) async-start(), calls=%async_computation.6 | async-start | bytes 5570560 | tf_op jit(solution)/shard_map/all_gather | solution.py:223
  98.3 37.4 %copy-start.9 = (f32[512]{0:T(512)S(1)}, f32[512]{0:T(512)}, u32[]{:S(2)}) copy-start(f32[512]{0:T(512)} %param.15) | copy-start | bytes 6148
  98.3 37.6 %copy-start.10 = (f32[32]{0:T(128)}, f32[32]{0:T(128)S(1)}, u32[]{:S(2)}) copy-start(f32[32]{0:T(128)S(1)} %multiply_power_fusion) | copy-start | bytes 388
  136.5 10.5 %collective-permute-start.3 = (bf16[64,2112]{1,0:T(8,128)(2,1)S(1)}, bf16[64,2112]{1,0:T(8,128)(2,1)S(1)}, u32[]{:S(2)}, u32[]{:S(2)}) collective-permute-start(bf16[64,2112]{1,0:T(8,128)(2,1)S(1)} %concatenate.23), channel_id=1, source_target_pairs={{0,24},{8,0},{16,8},{24,16},{1,25},{9,1},{17,9},{25,17},{2,26},{10... | collective-permute-start | bytes 811016 | tf_op jit(solution)/shard_map/ppermute | solution.py:216
  139.9 23.7 %collective-permute-start.2 = (bf16[64,2112]{1,0:T(8,128)(2,1)S(1)}, bf16[64,2112]{1,0:T(8,128)(2,1)S(1)}, u32[]{:S(2)}, u32[]{:S(2)}) collective-permute-start(bf16[64,2112]{1,0:T(8,128)(2,1)S(1)} %concatenate.23), channel_id=1, source_target_pairs={{0,16},{8,24},{16,0},{24,8},{1,17},{9,25},{17,1},{25,9},{2,18},{10... | collective-permute-start | bytes 811016 | tf_op jit(solution)/shard_map/ppermute | solution.py:216
  139.9 23.7 %collective-permute-start.1 = (bf16[64,2112]{1,0:T(8,128)(2,1)S(1)}, bf16[64,2112]{1,0:T(8,128)(2,1)S(1)}, u32[]{:S(2)}, u32[]{:S(2)}) collective-permute-start(bf16[64,2112]{1,0:T(8,128)(2,1)S(1)} %concatenate.23), channel_id=1, source_target_pairs={{0,8},{8,16},{16,24},{24,0},{1,9},{9,17},{17,25},{25,1},{2,10},{10... | collective-permute-start | bytes 811016 | tf_op jit(solution)/shard_map/ppermute | solution.py:216
  166.9 12.9 %all-to-all-start.2 = ((bf16[128,4,256]{2,0,1:T(8,128)(2,1)}), bf16[128,4,256]{2,0,1:T(8,128)(2,1)}, u32[]{:S(2)}, u32[]{:S(2)}) async-start(bf16[128,4,256]{2,0,1:T(8,128)(2,1)} %copy.123), calls=%async_computation.3 | async-start | bytes 524288 | tf_op jit(solution)/shard_map/all_to_all | solution.py:238
  174.3 9.0 %copy-start.2 = (bf16[128,2048]{1,0:T(8,128)(2,1)S(1)}, bf16[128,2048]{1,0:T(8,128)(2,1)}, u32[]{:S(2)}) copy-start(bf16[128,2048]{1,0:T(8,128)(2,1)} %param.17) | copy-start | bytes 1572868
  179.8 30.8 %all-to-all-start = ((bf16[384,4,384]{2,0,1:T(8,128)(2,1)}), bf16[384,4,384]{2,0,1:T(8,128)(2,1)S(1)}, u32[]{:S(2)}, u32[]{:S(2)}) async-start(bf16[384,4,384]{2,0,1:T(8,128)(2,1)} %copy.110), calls=%async_computation.1 | async-start | bytes 2359296 | tf_op jit(solution)/shard_map/all_to_all | solution.py:238
  210.6 11.8 %all-to-all-start.1 = ((bf16[128,4,256]{2,0,1:T(8,128)(2,1)}), bf16[128,4,256]{2,0,1:T(8,128)(2,1)S(1)}, u32[]{:S(2)}, u32[]{:S(2)}) async-start(bf16[128,4,256]{2,0,1:T(8,128)(2,1)} %copy.117), calls=%async_computation.2 | async-start | bytes 524288 | tf_op jit(solution)/shard_map/all_to_all | solution.py:238
  214.2 10.1 %copy-start.11 = (f32[32]{0:T(128)S(1)}, f32[32]{0:T(128)}, u32[]{:S(2)}) copy-start(f32[32]{0:T(128)} %copy-done.10) | copy-start | bytes 388
  214.8 14.3 %collective-permute-start.4 = (bf16[1536,384]{0,1:T(8,128)(2,1)S(1)}, bf16[1536,384]{0,1:T(8,128)(2,1)S(1)}, u32[]{:S(2)}, u32[]{:S(2)}) collective-permute-start(bf16[1536,384]{0,1:T(8,128)(2,1)S(1)} %copy.111), channel_id=1, source_target_pairs={{0,1},{1,0},{2,3},{3,2},{4,5},{5,4},{6,7},{7,6},{8,9},{9,8},{10,11... | collective-permute-start | bytes 3538952 | tf_op jit(solution)/shard_map/ppermute | solution.py:243
  216.7 9.5 %collective-permute-start.6 = (bf16[512,256]{0,1:T(8,128)(2,1)}, bf16[512,256]{0,1:T(8,128)(2,1)}, u32[]{:S(2)}, u32[]{:S(2)}) collective-permute-start(bf16[512,256]{0,1:T(8,128)(2,1)} %copy.124), channel_id=1, source_target_pairs={{0,1},{1,0},{2,3},{3,2},{4,5},{5,4},{6,7},{7,6},{8,9},{9,8},{10,11... | collective-permute-start | bytes 786440 | tf_op jit(solution)/shard_map/ppermute | solution.py:243
  223.2 2.9 %collective-permute-start.5 = (bf16[512,256]{0,1:T(8,128)(2,1)}, bf16[512,256]{0,1:T(8,128)(2,1)}, u32[]{:S(2)}, u32[]{:S(2)}) collective-permute-start(bf16[512,256]{0,1:T(8,128)(2,1)} %copy.118), channel_id=1, source_target_pairs={{0,1},{1,0},{2,3},{3,2},{4,5},{5,4},{6,7},{7,6},{8,9},{9,8},{10,11... | collective-permute-start | bytes 786440 | tf_op jit(solution)/shard_map/ppermute | solution.py:243
  236.3 2.8 copy-start.4
  248.5 16.8 %collective-permute-start.9 = (bf16[4,256,128]{2,1,0:T(8,128)(2,1)}, bf16[4,256,128]{2,1,0:T(8,128)(2,1)S(1)}, u32[]{:S(2)}, u32[]{:S(2)}) collective-permute-start(bf16[4,256,128]{2,1,0:T(8,128)(2,1)} %shard_map.103), channel_id=1, source_target_pairs={{0,24},{8,0},{16,8},{24,16},{1,25},{9,1},{17,9},{25,17},{2,26},{10... | collective-permute-start | bytes 786440 | tf_op jit(solution)/shard_map/ppermute | solution.py:282
  254.8 20.8 %collective-permute-start.8 = (bf16[4,256,128]{2,1,0:T(8,128)(2,1)}, bf16[4,256,128]{2,1,0:T(8,128)(2,1)S(1)}, u32[]{:S(2)}, u32[]{:S(2)}) collective-permute-start(bf16[4,256,128]{2,1,0:T(8,128)(2,1)} %shard_map.102), channel_id=1, source_target_pairs={{0,16},{8,24},{16,0},{24,8},{1,17},{9,25},{17,1},{25,9},{2,18},{10... | collective-permute-start | bytes 786440 | tf_op jit(solution)/shard_map/ppermute | solution.py:282
  260.0 15.7 %collective-permute-start.7 = (bf16[4,256,128]{2,1,0:T(8,128)(2,1)}, bf16[4,256,128]{2,1,0:T(8,128)(2,1)S(1)}, u32[]{:S(2)}, u32[]{:S(2)}) collective-permute-start(bf16[4,256,128]{2,1,0:T(8,128)(2,1)} %shard_map.101), channel_id=1, source_target_pairs={{0,8},{8,16},{16,24},{24,0},{1,9},{9,17},{17,25},{25,1},{2,10},{10... | collective-permute-start | bytes 786440 | tf_op jit(solution)/shard_map/ppermute | solution.py:282
  (5 other events, 7.2 us)
Sparse Core Ops, SparseCore 0:
  9.6 76.7 all-gather.4
  98.4 34.8 reduce-scatter.1
  165.9 54.1 all-gather.6

commit v11 on v10

--- a/solution.py
+++ b/solution.py
@@ -74,10 +74,20 @@
 
 
 def attention_kernel(
-    block_ref, query_ref, key_ref, rope_ref, value_ref, ids_col_ref, ids_row_ref, out_ref, *, block, window, doc_most, scale
+    block_ref, query_ref, key_ref, rope_ref, value_ref, ids_col_ref, ids_row_ref, out_ref, bias_ref, *, block, window, doc_most, scale
 ):
     lower = block_ref[0] * block
     start = pl.multiple_of(jnp.maximum(lower - doc_most, 0), block)
+
+    @pl.when(pl.program_id(0) == 0)
+    def _():
+        query_index = lower + lax.broadcasted_iota(jnp.int32, (block, window), 0)
+        key_index = start + lax.broadcasted_iota(jnp.int32, (block, window), 1)
+        allowed = (ids_col_ref[...] == ids_row_ref[:, pl.ds(start, window)]) & (
+            query_index >= key_index
+        )
+        bias_ref[...] = jnp.where(allowed, 0.0, -jnp.inf).astype(jnp.float32)
+
     query = query_ref[0]
     keys = key_ref[0, pl.ds(start, window), :]
     rope = rope_ref[pl.ds(start, window), :]
@@ -87,13 +97,7 @@
     scores = scores + lax.dot_general(
         query[:, NOPE:], rope, dims, preferred_element_type=jnp.float32
     )
-    scores = scores * scale
-    query_index = lower + lax.broadcasted_iota(jnp.int32, (block, window), 0)
-    key_index = start + lax.broadcasted_iota(jnp.int32, (block, window), 1)
-    allowed = (ids_col_ref[...] == ids_row_ref[:, pl.ds(start, window)]) & (
-        query_index >= key_index
-    )
-    scores = jnp.where(allowed, scores, -jnp.inf)
+    scores = scores * scale + bias_ref[...]
     row_max = jnp.max(scores, -1, keepdims=True)
     probs = jnp.exp(scores - row_max)
     denominator = jnp.sum(probs, -1, keepdims=True)
@@ -122,6 +126,7 @@
                 pl.BlockSpec((1, total_rows), lambda h, b: (0, 0)),
             ],
             out_specs=pl.BlockSpec((1, block, VDIM), lambda h, b: (h, 0, 0)),
+            scratch_shapes=[pltpu.VMEM((block, window), jnp.float32)],
         ),
         out_shape=jax.ShapeDtypeStruct((heads, block, VDIM), jnp.bfloat16),
         cost_estimate=pl.CostEstimate(

time: 287 us -> 287 us (level)
  no operation moved by 1% of the time
where the time goes in v11:
time: 287 us; the launch traced here: 286 us
  waiting for transfers between devices  159 us (55%)
  local copies, waits for them, and re-layouts  23.6 us (8%)
  blocking collectives  23 us (8%)
  Pallas kernels  19.3 us (7%)
  starting transfers between devices  18.4 us (6%)
  matrix products  15.3 us (5%)
  between operations  13.6 us (5%)
  other arithmetic  13.5 us (5%)
    all_gather x1, waiting for transfers between devices, body(): own_all = lax.all_gather(own_rows, 'seq', axis=1, tiled=True)  52.8 us
    all_to_all x3, waiting for transfers between devices, head_columns(): own = lax.all_to_all(own, 'seq', split_axis=1, concat_axis=0, tiled=True)  35.2 us
    reduce_scatter x1, waiting for transfers between devices, body(): lax.psum_scatter(partial, 'tp', scatter_dimension=0, tiled=True)  34.6 us
    ppermute x3, waiting for transfers between devices, body(): lax.ppermute(packed, 'seq', perm=[(i, (i + k) % seq_count) for i in range...  22.6 us
    pallas_call x4, Pallas kernels, block_attention(): pl.pallas_call(kernel, grid_spec=pltpu.PrefetchScalarGridSpec(num_scalar_...  19.3 us
    all_gather x1, blocking collectives, body(): group_ids = lax.all_gather(segment_ids, 'seq', axis=0, tiled=True)  11.7 us
    psum x1, blocking collectives, body(): square_sums = lax.psum(jnp.sum(inputs * inputs, 1), 'tp')  11.4 us
    all_to_all x3, starting transfers between devices, head_columns(): own = lax.all_to_all(own, 'seq', split_axis=1, concat_axis=0, tiled=True)  11.2 us
  transfers between devices with their start and end apart: 16, of which 9 were waited for; matrix products, arithmetic and copies ran while one was open for 7% of the time, Pallas kernels for 5%

profile of v11, /device:TPU:0, one launch (start us, length us, event | category | flops | bytes accessed | tf_op | source)
XLA Modules:
  0.0 285.9 jit_solution(5892579988266465871)
XLA Ops:
  10.2 11.4 %psum.7 = f32[256]{0:T(256)S(1)} all-reduce(f32[256]{0:T(256)S(1)} %fusion.2), channel_id=1, replica_groups=mesh['seq'=4,'tp'=4,'dp'=2] {'tp'}, use_global_device_ids=true, to_apply=%region_1.0 | all-reduce | flops 256 | bytes 2048 | tf_op jit(solution)/shard_map/psum | solution.py:176
  21.6 11.7 %all-gather.1 = s32[4,1,256]{2,1,0:T(1,128)S(1)} all-gather(s32[1,1,256]{2,1,0:T(1,128)S(1)} %bitcast.103), channel_id=1, replica_groups=mesh['seq'=4,'tp'=4,'dp'=2] {'seq'}, dimensions={0}, use_global_device_ids=true | all-gather | bytes 5120 | tf_op jit(solution)/shard_map/all_gather | solution.py:173
  33.5 52.8 %all-gather.5.cloned.1.call-done = bf16[896,2112]{0,1:T(8,128)(2,1)} async-done(((bf16[896,528]{0,1:T(8,128)(2,1)}), bf16[896,2112]{0,1:T(8,128)(2,1)}) %all-gather.5.cloned.1.call-update) | async-done | bytes 3784720 | tf_op jit(solution)/shard_map/all_gather | solution.py:186
  86.4 3.5 %fusion.9 = f32[256,2112]{1,0:T(8,128)S(1)} fusion(bf16[896,2112]{0,1:T(8,128)(2,1)} %all-gather.5.cloned.1.call-done, bf16[256,1792]{1,0:T(8,128)(2,1)S(1)} %fusion.4, s32[]{:T(128)S(6)} %select_n.150), kind=kOutput, calls=%fused_computation.35 | convolution fusion | flops 968884224 | bytes 6406148 | tf_op jit(solution)/shard_map/dot_general | solution.py:188
  89.9 3.4 %collective-permute-done = bf16[896,2112]{0,1:T(8,128)(2,1)} collective-permute-done((bf16[896,2112]{0,1:T(8,128)(2,1)}, bf16[896,2112]{0,1:T(8,128)(2,1)}, u32[]{:S(2)}, u32[]{:S(2)}) %collective-permute-start) | collective-permute-done | bytes 3784736 | tf_op jit(solution)/shard_map/ppermute | solution.py:195
  93.3 4.9 %convolution_add_fusion = f32[256,2112]{1,0:T(8,128)} fusion(f32[256,2112]{1,0:T(8,128)S(1)} %fusion.9, bf16[896,2112]{0,1:T(8,128)(2,1)} %collective-permute-done, bf16[256,1792]{1,0:T(8,128)(2,1)S(1)} %fusion.4, s32[]{:T(128)S(6)} %select_n.151), kind=kOutput, calls=%fused_computation.2 | convolution fusion | flops 969424896 | bytes 8634372 | tf_op jit(solution)/shard_map/dot_general | solution.py:198
  98.6 34.6 %reduce-scatter.2.cloned.1.call-done = f32[64,2112]{1,0:T(8,128)} async-done(((f32[256,2112]{1,0:T(8,128)}), f32[64,2112]{1,0:T(8,128)}) %reduce-scatter.2.cloned.1.call-update) | async-done | bytes 540688 | tf_op jit(solution)/shard_map/reduce_scatter | solution.py:203
  136.5 3.4 %collective-permute-start.3 = (bf16[64,2112]{1,0:T(8,128)(2,1)S(1)}, bf16[64,2112]{1,0:T(8,128)(2,1)S(1)}, u32[]{:S(2)}, u32[]{:S(2)}) collective-permute-start(bf16[64,2112]{1,0:T(8,128)(2,1)S(1)} %concatenate.23), channel_id=1, source_target_pairs={{0,24},{8,0},{16,8},{24,16},{1,25},{9,1},{17,9},{25,17},{2,26},{10... | collective-permute-start | bytes 811016 | tf_op jit(solution)/shard_map/ppermute | solution.py:221
  141.0 6.0 %collective-permute-done.3 = bf16[64,2112]{1,0:T(8,128)(2,1)S(1)} collective-permute-done((bf16[64,2112]{1,0:T(8,128)(2,1)S(1)}, bf16[64,2112]{1,0:T(8,128)(2,1)S(1)}, u32[]{:S(2)}, u32[]{:S(2)}) %collective-permute-start.3) | collective-permute-done | bytes 270368 | tf_op jit(solution)/shard_map/ppermute | solution.py:221
  147.0 16.6 %collective-permute-done.2 = bf16[64,2112]{1,0:T(8,128)(2,1)S(1)} collective-permute-done((bf16[64,2112]{1,0:T(8,128)(2,1)S(1)}, bf16[64,2112]{1,0:T(8,128)(2,1)S(1)}, u32[]{:S(2)}, u32[]{:S(2)}) %collective-permute-start.2) | collective-permute-done | bytes 270368 | tf_op jit(solution)/shard_map/ppermute | solution.py:221
  166.9 4.1 %all-to-all-start.2 = ((bf16[128,4,256]{2,0,1:T(8,128)(2,1)}), bf16[128,4,256]{2,0,1:T(8,128)(2,1)}, u32[]{:S(2)}, u32[]{:S(2)}) async-start(bf16[128,4,256]{2,0,1:T(8,128)(2,1)} %copy.123), calls=%async_computation.3 | async-start | bytes 524288 | tf_op jit(solution)/shard_map/all_to_all | solution.py:243
  171.0 3.2 %copy.109 = bf16[384,3072]{0,1:T(8,128)(2,1)S(1)} copy(bf16[384,3072]{1,0:T(8,128)(2,1)} %param.16) | data formatting | bytes 4718592 | tf_op jit(solution)/shard_map/optimization_barrier | solution.py:225
  175.8 4.0 %all-to-all-done.2 = bf16[128,4,256]{2,0,1:T(8,128)(2,1)} async-done(((bf16[128,4,256]{2,0,1:T(8,128)(2,1)}), bf16[128,4,256]{2,0,1:T(8,128)(2,1)}, u32[]{:S(2)}, u32[]{:S(2)}) %all-to-all-start.2) | async-done | bytes 262176 | tf_op jit(solution)/shard_map/all_to_all | solution.py:243
  179.8 3.5 %all-to-all-start = ((bf16[384,4,384]{2,0,1:T(8,128)(2,1)}), bf16[384,4,384]{2,0,1:T(8,128)(2,1)S(1)}, u32[]{:S(2)}, u32[]{:S(2)}) async-start(bf16[384,4,384]{2,0,1:T(8,128)(2,1)} %copy.110), calls=%async_computation.1 | async-start | bytes 2359296 | tf_op jit(solution)/shard_map/all_to_all | solution.py:243
  184.5 26.1 %all-to-all-done = bf16[384,4,384]{2,0,1:T(8,128)(2,1)S(1)} async-done(((bf16[384,4,384]{2,0,1:T(8,128)(2,1)}), bf16[384,4,384]{2,0,1:T(8,128)(2,1)S(1)}, u32[]{:S(2)}, u32[]{:S(2)}) %all-to-all-start) | async-done | bytes 1179680 | tf_op jit(solution)/shard_map/all_to_all | solution.py:243
  210.6 3.6 %all-to-all-start.1 = ((bf16[128,4,256]{2,0,1:T(8,128)(2,1)}), bf16[128,4,256]{2,0,1:T(8,128)(2,1)S(1)}, u32[]{:S(2)}, u32[]{:S(2)}) async-start(bf16[128,4,256]{2,0,1:T(8,128)(2,1)} %copy.117), calls=%async_computation.2 | async-start | bytes 524288 | tf_op jit(solution)/shard_map/all_to_all | solution.py:243
  217.2 5.2 %all-to-all-done.1 = bf16[128,4,256]{2,0,1:T(8,128)(2,1)S(1)} async-done(((bf16[128,4,256]{2,0,1:T(8,128)(2,1)}), bf16[128,4,256]{2,0,1:T(8,128)(2,1)S(1)}, u32[]{:S(2)}, u32[]{:S(2)}) %all-to-all-start.1) | async-done | bytes 262176 | tf_op jit(solution)/shard_map/all_to_all | solution.py:243
  229.5 2.6 copy.114
  232.9 3.4 %fusion.1 = f32[4,1024,192]{2,1,0:T(8,128)S(1)} fusion(bf16[1536,4,192]{0,2,1:T(8,128)(2,1)S(1)} %bitcast.80, bf16[1024,2112]{1,0:T(8,128)(2,1)S(1)} %bitcast.71), kind=kOutput, calls=%fused_computation.8 | convolution fusion | flops 2415919104 | bytes 8650752 | tf_op jit(solution)/shard_map/td,dhe->hte/dot_general | solution.py:264
  243.6 4.8 %shard_map.103 = bf16[4,256,128]{2,1,0:T(8,128)(2,1)} custom-call(s32[1]{0:T(128)} %bitcast.45.block_ref, bf16[4,1024,192]{2,1,0:T(8,128)(2,1)} %pad_maximum_fusion.1.query_ref, bf16[4,1024,128]{2,1,0:T(8,128)(2,1)} %fusion.5.key_ref, bf16[1024,64]{1,0:T(8,128)(2,1)} %slice.65.rope_ref, bf16[4,1024,128]{2,1,0:T(8,128)(2,1)} %fusion.6.value_ref, ...), custom_call_target="tpu_custom_call" | custom-call | flops 335544320 | bytes 1703936 | tf_op jit(solution)/shard_map/pallas_call | solution.py:115
  249.8 4.8 %shard_map.102 = bf16[4,256,128]{2,1,0:T(8,128)(2,1)} custom-call(s32[1]{0:T(128)} %bitcast.43.block_ref, bf16[4,1024,192]{2,1,0:T(8,128)(2,1)} %pad_maximum_fusion.1.query_ref, bf16[4,1024,128]{2,1,0:T(8,128)(2,1)} %fusion.5.key_ref, bf16[1024,64]{1,0:T(8,128)(2,1)} %slice.65.rope_ref, bf16[4,1024,128]{2,1,0:T(8,128)(2,1)} %fusion.6.value_ref, ...), custom_call_target="tpu_custom_call" | custom-call | flops 335544320 | bytes 1703936 | tf_op jit(solution)/shard_map/pallas_call | solution.py:115
  254.9 4.8 %shard_map.101 = bf16[4,256,128]{2,1,0:T(8,128)(2,1)} custom-call(s32[1]{0:T(128)} %bitcast.41.block_ref, bf16[4,1024,192]{2,1,0:T(8,128)(2,1)} %pad_maximum_fusion.1.query_ref, bf16[4,1024,128]{2,1,0:T(8,128)(2,1)} %fusion.5.key_ref, bf16[1024,64]{1,0:T(8,128)(2,1)} %slice.65.rope_ref, bf16[4,1024,128]{2,1,0:T(8,128)(2,1)} %fusion.6.value_ref, ...), custom_call_target="tpu_custom_call" | custom-call | flops 335544320 | bytes 1703936 | tf_op jit(solution)/shard_map/pallas_call | solution.py:115
  260.1 4.8 %shard_map.100 = bf16[4,256,128]{2,1,0:T(8,128)(2,1)} custom-call(s32[1]{0:T(128)} %bitcast.block_ref, bf16[4,1024,192]{2,1,0:T(8,128)(2,1)} %pad_maximum_fusion.1.query_ref, bf16[4,1024,128]{2,1,0:T(8,128)(2,1)} %fusion.5.key_ref, bf16[1024,64]{1,0:T(8,128)(2,1)} %slice.65.rope_ref, bf16[4,1024,128]{2,1,0:T(8,128)(2,1)} %fusion.6.value_ref, ...), custom_call_target="tpu_custom_call" | custom-call | flops 335544320 | bytes 1703936 | tf_op jit(solution)/shard_map/pallas_call | solution.py:115
  264.9 10.5 %collective-permute-done.8 = bf16[4,256,128]{2,1,0:T(8,128)(2,1)S(1)} collective-permute-done((bf16[4,256,128]{2,1,0:T(8,128)(2,1)}, bf16[4,256,128]{2,1,0:T(8,128)(2,1)S(1)}, u32[]{:S(2)}, u32[]{:S(2)}) %collective-permute-start.8) | collective-permute-done | bytes 262176 | tf_op jit(solution)/shard_map/ppermute | solution.py:287
  (108 shorter events, 38.6 us)
Async XLA Ops:
  6.5 79.8 %all-gather.5.cloned.1.call-start = ((), (), s32[]{:S(2)}) async-start(), calls=%async_computation.4 | async-start | bytes 4730880 | tf_op jit(solution)/shard_map/all_gather | solution.py:186
  8.4 13.1 %copy-start.12 = (s32[256]{0:T(256)S(1)}, s32[256]{0:T(256)}, u32[]{:S(2)}) copy-start(s32[256]{0:T(256)} %param.19) | copy-start | bytes 3076
  8.4 24.8 %copy-start.7 = (f32[1792]{0:T(1024)S(1)}, f32[1792]{0:T(1024)}, u32[]{:S(2)}) copy-start(f32[1792]{0:T(1024)} %param.11) | copy-start | bytes 21508
  9.5 123.8 %reduce-scatter.2.cloned.1.call-start = ((), (), s32[]{:S(2)}) async-start(), calls=%async_computation.5 | async-start | bytes 2785280 | tf_op jit(solution)/shard_map/reduce_scatter | solution.py:203
  33.2 190.0 %copy-start.6 = (s32[4,1,256]{2,1,0:T(1,128)}, s32[4,1,256]{2,1,0:T(1,128)S(1)}, u32[]{:S(2)}) copy-start(s32[4,1,256]{2,1,0:T(1,128)S(1)} %all-gather.1) | copy-start | bytes 12292
  86.4 6.9 %collective-permute-start = (bf16[896,2112]{0,1:T(8,128)(2,1)}, bf16[896,2112]{0,1:T(8,128)(2,1)}, u32[]{:S(2)}, u32[]{:S(2)}) collective-permute-start(bf16[896,2112]{0,1:T(8,128)(2,1)} %all-gather.5.cloned.1.call-done), channel_id=1, source_target_pairs={{0,1},{1,0},{2,3},{3,2},{4,5},{5,4},{6,7},{7,6},{8,9},{9,8},{10,11... | collective-permute-start | bytes 11354120 | tf_op jit(solution)/shard_map/ppermute | solution.py:195
  98.2 131.3 %all-gather.7.cloned.1.call-start = ((), (), s32[]{:S(2)}) async-start(), calls=%async_computation.6 | async-start | bytes 5570560 | tf_op jit(solution)/shard_map/all_gather | solution.py:228
  98.3 37.4 %copy-start.9 = (f32[512]{0:T(512)S(1)}, f32[512]{0:T(512)}, u32[]{:S(2)}) copy-start(f32[512]{0:T(512)} %param.15) | copy-start | bytes 6148
  98.3 37.6 %copy-start.10 = (f32[32]{0:T(128)}, f32[32]{0:T(128)S(1)}, u32[]{:S(2)}) copy-start(f32[32]{0:T(128)S(1)} %multiply_power_fusion) | copy-start | bytes 388
  136.5 10.5 %collective-permute-start.3 = (bf16[64,2112]{1,0:T(8,128)(2,1)S(1)}, bf16[64,2112]{1,0:T(8,128)(2,1)S(1)}, u32[]{:S(2)}, u32[]{:S(2)}) collective-permute-start(bf16[64,2112]{1,0:T(8,128)(2,1)S(1)} %concatenate.23), channel_id=1, source_target_pairs={{0,24},{8,0},{16,8},{24,16},{1,25},{9,1},{17,9},{25,17},{2,26},{10... | collective-permute-start | bytes 811016 | tf_op jit(solution)/shard_map/ppermute | solution.py:221
  139.9 23.7 %collective-permute-start.2 = (bf16[64,2112]{1,0:T(8,128)(2,1)S(1)}, bf16[64,2112]{1,0:T(8,128)(2,1)S(1)}, u32[]{:S(2)}, u32[]{:S(2)}) collective-permute-start(bf16[64,2112]{1,0:T(8,128)(2,1)S(1)} %concatenate.23), channel_id=1, source_target_pairs={{0,16},{8,24},{16,0},{24,8},{1,17},{9,25},{17,1},{25,9},{2,18},{10... | collective-permute-start | bytes 811016 | tf_op jit(solution)/shard_map/ppermute | solution.py:221
  139.9 23.7 %collective-permute-start.1 = (bf16[64,2112]{1,0:T(8,128)(2,1)S(1)}, bf16[64,2112]{1,0:T(8,128)(2,1)S(1)}, u32[]{:S(2)}, u32[]{:S(2)}) collective-permute-start(bf16[64,2112]{1,0:T(8,128)(2,1)S(1)} %concatenate.23), channel_id=1, source_target_pairs={{0,8},{8,16},{16,24},{24,0},{1,9},{9,17},{17,25},{25,1},{2,10},{10... | collective-permute-start | bytes 811016 | tf_op jit(solution)/shard_map/ppermute | solution.py:221
  166.9 12.9 %all-to-all-start.2 = ((bf16[128,4,256]{2,0,1:T(8,128)(2,1)}), bf16[128,4,256]{2,0,1:T(8,128)(2,1)}, u32[]{:S(2)}, u32[]{:S(2)}) async-start(bf16[128,4,256]{2,0,1:T(8,128)(2,1)} %copy.123), calls=%async_computation.3 | async-start | bytes 524288 | tf_op jit(solution)/shard_map/all_to_all | solution.py:243
  174.3 9.0 %copy-start.2 = (bf16[128,2048]{1,0:T(8,128)(2,1)S(1)}, bf16[128,2048]{1,0:T(8,128)(2,1)}, u32[]{:S(2)}) copy-start(bf16[128,2048]{1,0:T(8,128)(2,1)} %param.17) | copy-start | bytes 1572868
  179.8 30.8 %all-to-all-start = ((bf16[384,4,384]{2,0,1:T(8,128)(2,1)}), bf16[384,4,384]{2,0,1:T(8,128)(2,1)S(1)}, u32[]{:S(2)}, u32[]{:S(2)}) async-start(bf16[384,4,384]{2,0,1:T(8,128)(2,1)} %copy.110), calls=%async_computation.1 | async-start | bytes 2359296 | tf_op jit(solution)/shard_map/all_to_all | solution.py:243
  210.6 11.8 %all-to-all-start.1 = ((bf16[128,4,256]{2,0,1:T(8,128)(2,1)}), bf16[128,4,256]{2,0,1:T(8,128)(2,1)S(1)}, u32[]{:S(2)}, u32[]{:S(2)}) async-start(bf16[128,4,256]{2,0,1:T(8,128)(2,1)} %copy.117), calls=%async_computation.2 | async-start | bytes 524288 | tf_op jit(solution)/shard_map/all_to_all | solution.py:243
  214.2 10.1 %copy-start.11 = (f32[32]{0:T(128)S(1)}, f32[32]{0:T(128)}, u32[]{:S(2)}) copy-start(f32[32]{0:T(128)} %copy-done.10) | copy-start | bytes 388
  214.8 14.3 %collective-permute-start.4 = (bf16[1536,384]{0,1:T(8,128)(2,1)S(1)}, bf16[1536,384]{0,1:T(8,128)(2,1)S(1)}, u32[]{:S(2)}, u32[]{:S(2)}) collective-permute-start(bf16[1536,384]{0,1:T(8,128)(2,1)S(1)} %copy.111), channel_id=1, source_target_pairs={{0,1},{1,0},{2,3},{3,2},{4,5},{5,4},{6,7},{7,6},{8,9},{9,8},{10,11... | collective-permute-start | bytes 3538952 | tf_op jit(solution)/shard_map/ppermute | solution.py:248
  216.7 9.5 %collective-permute-start.6 = (bf16[512,256]{0,1:T(8,128)(2,1)}, bf16[512,256]{0,1:T(8,128)(2,1)}, u32[]{:S(2)}, u32[]{:S(2)}) collective-permute-start(bf16[512,256]{0,1:T(8,128)(2,1)} %copy.124), channel_id=1, source_target_pairs={{0,1},{1,0},{2,3},{3,2},{4,5},{5,4},{6,7},{7,6},{8,9},{9,8},{10,11... | collective-permute-start | bytes 786440 | tf_op jit(solution)/shard_map/ppermute | solution.py:248
  223.2 2.9 %collective-permute-start.5 = (bf16[512,256]{0,1:T(8,128)(2,1)}, bf16[512,256]{0,1:T(8,128)(2,1)}, u32[]{:S(2)}, u32[]{:S(2)}) collective-permute-start(bf16[512,256]{0,1:T(8,128)(2,1)} %copy.118), channel_id=1, source_target_pairs={{0,1},{1,0},{2,3},{3,2},{4,5},{5,4},{6,7},{7,6},{8,9},{9,8},{10,11... | collective-permute-start | bytes 786440 | tf_op jit(solution)/shard_map/ppermute | solution.py:248
  236.3 2.8 copy-start.4
  248.4 16.5 %collective-permute-start.9 = (bf16[4,256,128]{2,1,0:T(8,128)(2,1)}, bf16[4,256,128]{2,1,0:T(8,128)(2,1)S(1)}, u32[]{:S(2)}, u32[]{:S(2)}) collective-permute-start(bf16[4,256,128]{2,1,0:T(8,128)(2,1)} %shard_map.103), channel_id=1, source_target_pairs={{0,24},{8,0},{16,8},{24,16},{1,25},{9,1},{17,9},{25,17},{2,26},{10... | collective-permute-start | bytes 786440 | tf_op jit(solution)/shard_map/ppermute | solution.py:287
  254.7 20.8 %collective-permute-start.8 = (bf16[4,256,128]{2,1,0:T(8,128)(2,1)}, bf16[4,256,128]{2,1,0:T(8,128)(2,1)S(1)}, u32[]{:S(2)}, u32[]{:S(2)}) collective-permute-start(bf16[4,256,128]{2,1,0:T(8,128)(2,1)} %shard_map.102), channel_id=1, source_target_pairs={{0,16},{8,24},{16,0},{24,8},{1,17},{9,25},{17,1},{25,9},{2,18},{10... | collective-permute-start | bytes 786440 | tf_op jit(solution)/shard_map/ppermute | solution.py:287
  259.7 15.8 %collective-permute-start.7 = (bf16[4,256,128]{2,1,0:T(8,128)(2,1)}, bf16[4,256,128]{2,1,0:T(8,128)(2,1)S(1)}, u32[]{:S(2)}, u32[]{:S(2)}) collective-permute-start(bf16[4,256,128]{2,1,0:T(8,128)(2,1)} %shard_map.101), channel_id=1, source_target_pairs={{0,8},{8,16},{16,24},{24,0},{1,9},{9,17},{17,25},{25,1},{2,10},{10... | collective-permute-start | bytes 786440 | tf_op jit(solution)/shard_map/ppermute | solution.py:287
  (5 other events, 7.2 us)
Sparse Core Ops, SparseCore 0:
  9.6 76.7 all-gather.4
  98.4 34.8 reduce-scatter.1
  165.9 54.1 all-gather.6

commit v12 on v11

--- a/solution.py
+++ b/solution.py
@@ -278,7 +278,9 @@
     ).astype(jnp.bfloat16)
     score_scale = (NOPE + ROPE) ** (-0.5)
     received = [None] * seq_count
-    for k in list(range(1, seq_count)) + [0]:
+    shifts = [k for k in range(seq_count - 1, 0, -1) if k % 2]
+    shifts = shifts + [k for k in range(seq_count - 1, 0, -1) if k % 2 == 0] + [0]
+    for k in shifts:
         rows = block_attention(
             query, key_nope, rope_all, value, group_ids, score_scale, doc_most, tok_count,
             (seq_index + k) % seq_count,

time: 287 us -> 287 us (level)
  no operation moved by 1% of the time
where the time goes in v12:
time: 287 us; the launch traced here: 286 us
  waiting for transfers between devices  159 us (55%)
  local copies, waits for them, and re-layouts  23.6 us (8%)
  blocking collectives  23 us (8%)
  Pallas kernels  19.3 us (7%)
  starting transfers between devices  18.4 us (6%)
  matrix products  15.3 us (5%)
  between operations  13.6 us (5%)
  other arithmetic  13.5 us (5%)
    all_gather x1, waiting for transfers between devices, body(): own_all = lax.all_gather(own_rows, 'seq', axis=1, tiled=True)  52.8 us
    all_to_all x3, waiting for transfers between devices, head_columns(): own = lax.all_to_all(own, 'seq', split_axis=1, concat_axis=0, tiled=True)  35.2 us
    reduce_scatter x1, waiting for transfers between devices, body(): lax.psum_scatter(partial, 'tp', scatter_dimension=0, tiled=True)  34.6 us
    ppermute x3, waiting for transfers between devices, body(): lax.ppermute(packed, 'seq', perm=[(i, (i + k) % seq_count) for i in range...  22.6 us
    pallas_call x4, Pallas kernels, block_attention(): pl.pallas_call(kernel, grid_spec=pltpu.PrefetchScalarGridSpec(num_scalar_...  19.3 us
    all_gather x1, blocking collectives, body(): group_ids = lax.all_gather(segment_ids, 'seq', axis=0, tiled=True)  11.7 us
    psum x1, blocking collectives, body(): square_sums = lax.psum(jnp.sum(inputs * inputs, 1), 'tp')  11.4 us
    all_to_all x3, starting transfers between devices, head_columns(): own = lax.all_to_all(own, 'seq', split_axis=1, concat_axis=0, tiled=True)  11.2 us
  transfers between devices with their start and end apart: 16, of which 9 were waited for; matrix products, arithmetic and copies ran while one was open for 7% of the time, Pallas kernels for 5%

profile of v12, /device:TPU:0, one launch (start us, length us, event | category | flops | bytes accessed | tf_op | source)
XLA Modules:
  0.0 285.9 jit_solution(5892579988266465871)
XLA Ops:
  10.2 11.4 %psum.7 = f32[256]{0:T(256)S(1)} all-reduce(f32[256]{0:T(256)S(1)} %fusion.2), channel_id=1, replica_groups=mesh['seq'=4,'tp'=4,'dp'=2] {'tp'}, use_global_device_ids=true, to_apply=%region_1.0 | all-reduce | flops 256 | bytes 2048 | tf_op jit(solution)/shard_map/psum | solution.py:176
  21.6 11.7 %all-gather.1 = s32[4,1,256]{2,1,0:T(1,128)S(1)} all-gather(s32[1,1,256]{2,1,0:T(1,128)S(1)} %bitcast.103), channel_id=1, replica_groups=mesh['seq'=4,'tp'=4,'dp'=2] {'seq'}, dimensions={0}, use_global_device_ids=true | all-gather | bytes 5120 | tf_op jit(solution)/shard_map/all_gather | solution.py:173
  33.5 52.8 %all-gather.5.cloned.1.call-done = bf16[896,2112]{0,1:T(8,128)(2,1)} async-done(((bf16[896,528]{0,1:T(8,128)(2,1)}), bf16[896,2112]{0,1:T(8,128)(2,1)}) %all-gather.5.cloned.1.call-update) | async-done | bytes 3784720 | tf_op jit(solution)/shard_map/all_gather | solution.py:186
  86.4 3.5 %fusion.9 = f32[256,2112]{1,0:T(8,128)S(1)} fusion(bf16[896,2112]{0,1:T(8,128)(2,1)} %all-gather.5.cloned.1.call-done, bf16[256,1792]{1,0:T(8,128)(2,1)S(1)} %fusion.4, s32[]{:T(128)S(6)} %select_n.150), kind=kOutput, calls=%fused_computation.35 | convolution fusion | flops 968884224 | bytes 6406148 | tf_op jit(solution)/shard_map/dot_general | solution.py:188
  89.9 3.4 %collective-permute-done = bf16[896,2112]{0,1:T(8,128)(2,1)} collective-permute-done((bf16[896,2112]{0,1:T(8,128)(2,1)}, bf16[896,2112]{0,1:T(8,128)(2,1)}, u32[]{:S(2)}, u32[]{:S(2)}) %collective-permute-start) | collective-permute-done | bytes 3784736 | tf_op jit(solution)/shard_map/ppermute | solution.py:195
  93.3 4.9 %convolution_add_fusion = f32[256,2112]{1,0:T(8,128)} fusion(f32[256,2112]{1,0:T(8,128)S(1)} %fusion.9, bf16[896,2112]{0,1:T(8,128)(2,1)} %collective-permute-done, bf16[256,1792]{1,0:T(8,128)(2,1)S(1)} %fusion.4, s32[]{:T(128)S(6)} %select_n.151), kind=kOutput, calls=%fused_computation.2 | convolution fusion | flops 969424896 | bytes 8634372 | tf_op jit(solution)/shard_map/dot_general | solution.py:198
  98.6 34.6 %reduce-scatter.2.cloned.1.call-done = f32[64,2112]{1,0:T(8,128)} async-done(((f32[256,2112]{1,0:T(8,128)}), f32[64,2112]{1,0:T(8,128)}) %reduce-scatter.2.cloned.1.call-update) | async-done | bytes 540688 | tf_op jit(solution)/shard_map/reduce_scatter | solution.py:203
  136.5 3.4 %collective-permute-start.3 = (bf16[64,2112]{1,0:T(8,128)(2,1)S(1)}, bf16[64,2112]{1,0:T(8,128)(2,1)S(1)}, u32[]{:S(2)}, u32[]{:S(2)}) collective-permute-start(bf16[64,2112]{1,0:T(8,128)(2,1)S(1)} %concatenate.23), channel_id=1, source_target_pairs={{0,24},{8,0},{16,8},{24,16},{1,25},{9,1},{17,9},{25,17},{2,26},{10... | collective-permute-start | bytes 811016 | tf_op jit(solution)/shard_map/ppermute | solution.py:221
  141.0 6.0 %collective-permute-done.3 = bf16[64,2112]{1,0:T(8,128)(2,1)S(1)} collective-permute-done((bf16[64,2112]{1,0:T(8,128)(2,1)S(1)}, bf16[64,2112]{1,0:T(8,128)(2,1)S(1)}, u32[]{:S(2)}, u32[]{:S(2)}) %collective-permute-start.3) | collective-permute-done | bytes 270368 | tf_op jit(solution)/shard_map/ppermute | solution.py:221
  147.0 16.6 %collective-permute-done.2 = bf16[64,2112]{1,0:T(8,128)(2,1)S(1)} collective-permute-done((bf16[64,2112]{1,0:T(8,128)(2,1)S(1)}, bf16[64,2112]{1,0:T(8,128)(2,1)S(1)}, u32[]{:S(2)}, u32[]{:S(2)}) %collective-permute-start.2) | collective-permute-done | bytes 270368 | tf_op jit(solution)/shard_map/ppermute | solution.py:221
  166.9 4.1 %all-to-all-start.2 = ((bf16[128,4,256]{2,0,1:T(8,128)(2,1)}), bf16[128,4,256]{2,0,1:T(8,128)(2,1)}, u32[]{:S(2)}, u32[]{:S(2)}) async-start(bf16[128,4,256]{2,0,1:T(8,128)(2,1)} %copy.123), calls=%async_computation.3 | async-start | bytes 524288 | tf_op jit(solution)/shard_map/all_to_all | solution.py:243
  171.0 3.2 %copy.109 = bf16[384,3072]{0,1:T(8,128)(2,1)S(1)} copy(bf16[384,3072]{1,0:T(8,128)(2,1)} %param.16) | data formatting | bytes 4718592 | tf_op jit(solution)/shard_map/optimization_barrier | solution.py:225
  175.8 4.0 %all-to-all-done.2 = bf16[128,4,256]{2,0,1:T(8,128)(2,1)} async-done(((bf16[128,4,256]{2,0,1:T(8,128)(2,1)}), bf16[128,4,256]{2,0,1:T(8,128)(2,1)}, u32[]{:S(2)}, u32[]{:S(2)}) %all-to-all-start.2) | async-done | bytes 262176 | tf_op jit(solution)/shard_map/all_to_all | solution.py:243
  179.8 3.5 %all-to-all-start = ((bf16[384,4,384]{2,0,1:T(8,128)(2,1)}), bf16[384,4,384]{2,0,1:T(8,128)(2,1)S(1)}, u32[]{:S(2)}, u32[]{:S(2)}) async-start(bf16[384,4,384]{2,0,1:T(8,128)(2,1)} %copy.110), calls=%async_computation.1 | async-start | bytes 2359296 | tf_op jit(solution)/shard_map/all_to_all | solution.py:243
  184.5 26.1 %all-to-all-done = bf16[384,4,384]{2,0,1:T(8,128)(2,1)S(1)} async-done(((bf16[384,4,384]{2,0,1:T(8,128)(2,1)}), bf16[384,4,384]{2,0,1:T(8,128)(2,1)S(1)}, u32[]{:S(2)}, u32[]{:S(2)}) %all-to-all-start) | async-done | bytes 1179680 | tf_op jit(solution)/shard_map/all_to_all | solution.py:243
  210.6 3.6 %all-to-all-start.1 = ((bf16[128,4,256]{2,0,1:T(8,128)(2,1)}), bf16[128,4,256]{2,0,1:T(8,128)(2,1)S(1)}, u32[]{:S(2)}, u32[]{:S(2)}) async-start(bf16[128,4,256]{2,0,1:T(8,128)(2,1)} %copy.117), calls=%async_computation.2 | async-start | bytes 524288 | tf_op jit(solution)/shard_map/all_to_all | solution.py:243
  217.2 5.2 %all-to-all-done.1 = bf16[128,4,256]{2,0,1:T(8,128)(2,1)S(1)} async-done(((bf16[128,4,256]{2,0,1:T(8,128)(2,1)}), bf16[128,4,256]{2,0,1:T(8,128)(2,1)S(1)}, u32[]{:S(2)}, u32[]{:S(2)}) %all-to-all-start.1) | async-done | bytes 262176 | tf_op jit(solution)/shard_map/all_to_all | solution.py:243
  229.5 2.6 copy.114
  232.9 3.4 %fusion.1 = f32[4,1024,192]{2,1,0:T(8,128)S(1)} fusion(bf16[1536,4,192]{0,2,1:T(8,128)(2,1)S(1)} %bitcast.80, bf16[1024,2112]{1,0:T(8,128)(2,1)S(1)} %bitcast.71), kind=kOutput, calls=%fused_computation.8 | convolution fusion | flops 2415919104 | bytes 8650752 | tf_op jit(solution)/shard_map/td,dhe->hte/dot_general | solution.py:264
  243.6 4.8 %shard_map.103 = bf16[4,256,128]{2,1,0:T(8,128)(2,1)} custom-call(s32[1]{0:T(128)} %bitcast.45.block_ref, bf16[4,1024,192]{2,1,0:T(8,128)(2,1)} %pad_maximum_fusion.1.query_ref, bf16[4,1024,128]{2,1,0:T(8,128)(2,1)} %fusion.5.key_ref, bf16[1024,64]{1,0:T(8,128)(2,1)} %slice.65.rope_ref, bf16[4,1024,128]{2,1,0:T(8,128)(2,1)} %fusion.6.value_ref, ...), custom_call_target="tpu_custom_call" | custom-call | flops 335544320 | bytes 1703936 | tf_op jit(solution)/shard_map/pallas_call | solution.py:115
  249.8 4.8 %shard_map.102 = bf16[4,256,128]{2,1,0:T(8,128)(2,1)} custom-call(s32[1]{0:T(128)} %bitcast.43.block_ref, bf16[4,1024,192]{2,1,0:T(8,128)(2,1)} %pad_maximum_fusion.1.query_ref, bf16[4,1024,128]{2,1,0:T(8,128)(2,1)} %fusion.5.key_ref, bf16[1024,64]{1,0:T(8,128)(2,1)} %slice.65.rope_ref, bf16[4,1024,128]{2,1,0:T(8,128)(2,1)} %fusion.6.value_ref, ...), custom_call_target="tpu_custom_call" | custom-call | flops 335544320 | bytes 1703936 | tf_op jit(solution)/shard_map/pallas_call | solution.py:115
  254.9 4.8 %shard_map.101 = bf16[4,256,128]{2,1,0:T(8,128)(2,1)} custom-call(s32[1]{0:T(128)} %bitcast.41.block_ref, bf16[4,1024,192]{2,1,0:T(8,128)(2,1)} %pad_maximum_fusion.1.query_ref, bf16[4,1024,128]{2,1,0:T(8,128)(2,1)} %fusion.5.key_ref, bf16[1024,64]{1,0:T(8,128)(2,1)} %slice.65.rope_ref, bf16[4,1024,128]{2,1,0:T(8,128)(2,1)} %fusion.6.value_ref, ...), custom_call_target="tpu_custom_call" | custom-call | flops 335544320 | bytes 1703936 | tf_op jit(solution)/shard_map/pallas_call | solution.py:115
  260.1 4.8 %shard_map.100 = bf16[4,256,128]{2,1,0:T(8,128)(2,1)} custom-call(s32[1]{0:T(128)} %bitcast.block_ref, bf16[4,1024,192]{2,1,0:T(8,128)(2,1)} %pad_maximum_fusion.1.query_ref, bf16[4,1024,128]{2,1,0:T(8,128)(2,1)} %fusion.5.key_ref, bf16[1024,64]{1,0:T(8,128)(2,1)} %slice.65.rope_ref, bf16[4,1024,128]{2,1,0:T(8,128)(2,1)} %fusion.6.value_ref, ...), custom_call_target="tpu_custom_call" | custom-call | flops 335544320 | bytes 1703936 | tf_op jit(solution)/shard_map/pallas_call | solution.py:115
  264.9 10.5 %collective-permute-done.8 = bf16[4,256,128]{2,1,0:T(8,128)(2,1)S(1)} collective-permute-done((bf16[4,256,128]{2,1,0:T(8,128)(2,1)}, bf16[4,256,128]{2,1,0:T(8,128)(2,1)S(1)}, u32[]{:S(2)}, u32[]{:S(2)}) %collective-permute-start.8) | collective-permute-done | bytes 262176 | tf_op jit(solution)/shard_map/ppermute | solution.py:289
  (108 shorter events, 38.6 us)
Async XLA Ops:
  6.5 79.8 %all-gather.5.cloned.1.call-start = ((), (), s32[]{:S(2)}) async-start(), calls=%async_computation.4 | async-start | bytes 4730880 | tf_op jit(solution)/shard_map/all_gather | solution.py:186
  8.4 13.1 %copy-start.12 = (s32[256]{0:T(256)S(1)}, s32[256]{0:T(256)}, u32[]{:S(2)}) copy-start(s32[256]{0:T(256)} %param.19) | copy-start | bytes 3076
  8.4 24.8 %copy-start.7 = (f32[1792]{0:T(1024)S(1)}, f32[1792]{0:T(1024)}, u32[]{:S(2)}) copy-start(f32[1792]{0:T(1024)} %param.11) | copy-start | bytes 21508
  9.5 123.8 %reduce-scatter.2.cloned.1.call-start = ((), (), s32[]{:S(2)}) async-start(), calls=%async_computation.5 | async-start | bytes 2785280 | tf_op jit(solution)/shard_map/reduce_scatter | solution.py:203
  33.2 190.0 %copy-start.6 = (s32[4,1,256]{2,1,0:T(1,128)}, s32[4,1,256]{2,1,0:T(1,128)S(1)}, u32[]{:S(2)}) copy-start(s32[4,1,256]{2,1,0:T(1,128)S(1)} %all-gather.1) | copy-start | bytes 12292
  86.4 6.9 %collective-permute-start = (bf16[896,2112]{0,1:T(8,128)(2,1)}, bf16[896,2112]{0,1:T(8,128)(2,1)}, u32[]{:S(2)}, u32[]{:S(2)}) collective-permute-start(bf16[896,2112]{0,1:T(8,128)(2,1)} %all-gather.5.cloned.1.call-done), channel_id=1, source_target_pairs={{0,1},{1,0},{2,3},{3,2},{4,5},{5,4},{6,7},{7,6},{8,9},{9,8},{10,11... | collective-permute-start | bytes 11354120 | tf_op jit(solution)/shard_map/ppermute | solution.py:195
  98.2 131.3 %all-gather.7.cloned.1.call-start = ((), (), s32[]{:S(2)}) async-start(), calls=%async_computation.6 | async-start | bytes 5570560 | tf_op jit(solution)/shard_map/all_gather | solution.py:228
  98.3 37.4 %copy-start.9 = (f32[512]{0:T(512)S(1)}, f32[512]{0:T(512)}, u32[]{:S(2)}) copy-start(f32[512]{0:T(512)} %param.15) | copy-start | bytes 6148
  98.3 37.6 %copy-start.10 = (f32[32]{0:T(128)}, f32[32]{0:T(128)S(1)}, u32[]{:S(2)}) copy-start(f32[32]{0:T(128)S(1)} %multiply_power_fusion) | copy-start | bytes 388
  136.5 10.5 %collective-permute-start.3 = (bf16[64,2112]{1,0:T(8,128)(2,1)S(1)}, bf16[64,2112]{1,0:T(8,128)(2,1)S(1)}, u32[]{:S(2)}, u32[]{:S(2)}) collective-permute-start(bf16[64,2112]{1,0:T(8,128)(2,1)S(1)} %concatenate.23), channel_id=1, source_target_pairs={{0,24},{8,0},{16,8},{24,16},{1,25},{9,1},{17,9},{25,17},{2,26},{10... | collective-permute-start | bytes 811016 | tf_op jit(solution)/shard_map/ppermute | solution.py:221
  139.9 23.7 %collective-permute-start.2 = (bf16[64,2112]{1,0:T(8,128)(2,1)S(1)}, bf16[64,2112]{1,0:T(8,128)(2,1)S(1)}, u32[]{:S(2)}, u32[]{:S(2)}) collective-permute-start(bf16[64,2112]{1,0:T(8,128)(2,1)S(1)} %concatenate.23), channel_id=1, source_target_pairs={{0,16},{8,24},{16,0},{24,8},{1,17},{9,25},{17,1},{25,9},{2,18},{10... | collective-permute-start | bytes 811016 | tf_op jit(solution)/shard_map/ppermute | solution.py:221
  139.9 23.7 %collective-permute-start.1 = (bf16[64,2112]{1,0:T(8,128)(2,1)S(1)}, bf16[64,2112]{1,0:T(8,128)(2,1)S(1)}, u32[]{:S(2)}, u32[]{:S(2)}) collective-permute-start(bf16[64,2112]{1,0:T(8,128)(2,1)S(1)} %concatenate.23), channel_id=1, source_target_pairs={{0,8},{8,16},{16,24},{24,0},{1,9},{9,17},{17,25},{25,1},{2,10},{10... | collective-permute-start | bytes 811016 | tf_op jit(solution)/shard_map/ppermute | solution.py:221
  166.9 12.9 %all-to-all-start.2 = ((bf16[128,4,256]{2,0,1:T(8,128)(2,1)}), bf16[128,4,256]{2,0,1:T(8,128)(2,1)}, u32[]{:S(2)}, u32[]{:S(2)}) async-start(bf16[128,4,256]{2,0,1:T(8,128)(2,1)} %copy.123), calls=%async_computation.3 | async-start | bytes 524288 | tf_op jit(solution)/shard_map/all_to_all | solution.py:243
  174.3 9.0 %copy-start.2 = (bf16[128,2048]{1,0:T(8,128)(2,1)S(1)}, bf16[128,2048]{1,0:T(8,128)(2,1)}, u32[]{:S(2)}) copy-start(bf16[128,2048]{1,0:T(8,128)(2,1)} %param.17) | copy-start | bytes 1572868
  179.8 30.8 %all-to-all-start = ((bf16[384,4,384]{2,0,1:T(8,128)(2,1)}), bf16[384,4,384]{2,0,1:T(8,128)(2,1)S(1)}, u32[]{:S(2)}, u32[]{:S(2)}) async-start(bf16[384,4,384]{2,0,1:T(8,128)(2,1)} %copy.110), calls=%async_computation.1 | async-start | bytes 2359296 | tf_op jit(solution)/shard_map/all_to_all | solution.py:243
  210.6 11.8 %all-to-all-start.1 = ((bf16[128,4,256]{2,0,1:T(8,128)(2,1)}), bf16[128,4,256]{2,0,1:T(8,128)(2,1)S(1)}, u32[]{:S(2)}, u32[]{:S(2)}) async-start(bf16[128,4,256]{2,0,1:T(8,128)(2,1)} %copy.117), calls=%async_computation.2 | async-start | bytes 524288 | tf_op jit(solution)/shard_map/all_to_all | solution.py:243
  214.2 10.1 %copy-start.11 = (f32[32]{0:T(128)S(1)}, f32[32]{0:T(128)}, u32[]{:S(2)}) copy-start(f32[32]{0:T(128)} %copy-done.10) | copy-start | bytes 388
  214.8 14.3 %collective-permute-start.4 = (bf16[1536,384]{0,1:T(8,128)(2,1)S(1)}, bf16[1536,384]{0,1:T(8,128)(2,1)S(1)}, u32[]{:S(2)}, u32[]{:S(2)}) collective-permute-start(bf16[1536,384]{0,1:T(8,128)(2,1)S(1)} %copy.111), channel_id=1, source_target_pairs={{0,1},{1,0},{2,3},{3,2},{4,5},{5,4},{6,7},{7,6},{8,9},{9,8},{10,11... | collective-permute-start | bytes 3538952 | tf_op jit(solution)/shard_map/ppermute | solution.py:248
  216.7 9.5 %collective-permute-start.6 = (bf16[512,256]{0,1:T(8,128)(2,1)}, bf16[512,256]{0,1:T(8,128)(2,1)}, u32[]{:S(2)}, u32[]{:S(2)}) collective-permute-start(bf16[512,256]{0,1:T(8,128)(2,1)} %copy.124), channel_id=1, source_target_pairs={{0,1},{1,0},{2,3},{3,2},{4,5},{5,4},{6,7},{7,6},{8,9},{9,8},{10,11... | collective-permute-start | bytes 786440 | tf_op jit(solution)/shard_map/ppermute | solution.py:248
  223.2 2.9 %collective-permute-start.5 = (bf16[512,256]{0,1:T(8,128)(2,1)}, bf16[512,256]{0,1:T(8,128)(2,1)}, u32[]{:S(2)}, u32[]{:S(2)}) collective-permute-start(bf16[512,256]{0,1:T(8,128)(2,1)} %copy.118), channel_id=1, source_target_pairs={{0,1},{1,0},{2,3},{3,2},{4,5},{5,4},{6,7},{7,6},{8,9},{9,8},{10,11... | collective-permute-start | bytes 786440 | tf_op jit(solution)/shard_map/ppermute | solution.py:248
  236.3 2.8 copy-start.4
  248.4 16.5 %collective-permute-start.9 = (bf16[4,256,128]{2,1,0:T(8,128)(2,1)}, bf16[4,256,128]{2,1,0:T(8,128)(2,1)S(1)}, u32[]{:S(2)}, u32[]{:S(2)}) collective-permute-start(bf16[4,256,128]{2,1,0:T(8,128)(2,1)} %shard_map.103), channel_id=1, source_target_pairs={{0,24},{8,0},{16,8},{24,16},{1,25},{9,1},{17,9},{25,17},{2,26},{10... | collective-permute-start | bytes 786440 | tf_op jit(solution)/shard_map/ppermute | solution.py:289
  254.7 20.8 %collective-permute-start.8 = (bf16[4,256,128]{2,1,0:T(8,128)(2,1)}, bf16[4,256,128]{2,1,0:T(8,128)(2,1)S(1)}, u32[]{:S(2)}, u32[]{:S(2)}) collective-permute-start(bf16[4,256,128]{2,1,0:T(8,128)(2,1)} %shard_map.102), channel_id=1, source_target_pairs={{0,16},{8,24},{16,0},{24,8},{1,17},{9,25},{17,1},{25,9},{2,18},{10... | collective-permute-start | bytes 786440 | tf_op jit(solution)/shard_map/ppermute | solution.py:289
  259.7 15.8 %collective-permute-start.7 = (bf16[4,256,128]{2,1,0:T(8,128)(2,1)}, bf16[4,256,128]{2,1,0:T(8,128)(2,1)S(1)}, u32[]{:S(2)}, u32[]{:S(2)}) collective-permute-start(bf16[4,256,128]{2,1,0:T(8,128)(2,1)} %shard_map.101), channel_id=1, source_target_pairs={{0,8},{8,16},{16,24},{24,0},{1,9},{9,17},{17,25},{25,1},{2,10},{10... | collective-permute-start | bytes 786440 | tf_op jit(solution)/shard_map/ppermute | solution.py:289
  (5 other events, 7.2 us)
Sparse Core Ops, SparseCore 0:
  9.6 76.7 all-gather.4
  98.4 34.8 reduce-scatter.1
  165.9 54.1 all-gather.6

commit v13 on v12

--- a/solution.py
+++ b/solution.py
@@ -234,14 +234,26 @@
     local_heads = query_up.shape[1] // (NOPE + ROPE)
     heads = local_heads // seq_count
 
-    def head_columns(weight, head_width):
+    def own_columns(weight, head_width):
         rows = weight.shape[0]
         cols = heads * head_width // dp_count
         own = lax.dynamic_slice_in_dim(
             weight.reshape(rows, seq_count, heads * head_width), dp_index * cols, cols, 2
         )
-        own = lax.all_to_all(own, "seq", split_axis=1, concat_axis=0, tiled=True)
-        own = own.reshape(rows * seq_count, cols)
+        return jnp.transpose(own, (1, 0, 2)).reshape(seq_count, rows * cols), (rows, cols)
+
+    packed_w = [
+        own_columns(query_up, NOPE + ROPE),
+        own_columns(key_up, NOPE),
+        own_columns(value_up, VDIM),
+    ]
+    moved = lax.all_to_all(
+        jnp.concatenate([p for p, _ in packed_w], 1), "seq", split_axis=0, concat_axis=0, tiled=True
+    )
+
+    def head_columns(offset, shape):
+        rows, cols = shape
+        own = moved[:, offset : offset + rows * cols].reshape(seq_count * rows, cols)
         pieces = [own]
         for shift in range(1, dp_count):
             pieces.append(
@@ -257,9 +269,12 @@
             ordered.append(pick)
         return jnp.concatenate(ordered, 1)
 
-    query_w = head_columns(query_up, NOPE + ROPE)
-    key_w = head_columns(key_up, NOPE)
-    value_w = head_columns(value_up, VDIM)
+    offsets = [0]
+    for _, (rows, cols) in packed_w:
+        offsets.append(offsets[-1] + rows * cols)
+    query_w = head_columns(offsets[0], packed_w[0][1])
+    key_w = head_columns(offsets[1], packed_w[1][1])
+    value_w = head_columns(offsets[2], packed_w[2][1])
 
     query_full = jnp.einsum(
         "td,dhe->hte",

time: 287 us -> 314 us (1.094)
  other arithmetic: 13.5 us -> 29 us
  local copies, waits for them, and re-layouts: 23.6 us -> 38 us
  starting transfers between devices: 18.4 us -> 11.8 us
  waiting for transfers between devices: 159 us -> 163 us
    all_to_all x0 -> x2, other arithmetic: none -> 15 us  [body(): lax.all_to_all(jnp.concatenate([p for p, _ in packed_w], 1), 'seq', split...]
    unnamed x29 -> x32, local copies, waits for them, and re-layouts: 3.38 us -> 14.2 us
    all_to_all x3 -> x1, starting transfers between devices: 11.2 us -> 4.4 us  [body(): lax.all_to_all(jnp.concatenate([p for p, _ in packed_w], 1), 'seq', split...]
    concatenate x0 -> x3, local copies, waits for them, and re-layouts: none -> 4.47 us  [head_columns(): return jnp.concatenate(ordered, 1)]
    optimization_barrier x3 -> x0, local copies, waits for them, and re-layouts: 3.74 us -> none  [body(): lax.optimization_barrier((packed, query_up, key_up, value_up))]
    all_to_all x3 -> x1, waiting for transfers between devices: 35.2 us -> 39 us  [body(): lax.all_to_all(jnp.concatenate([p for p, _ in packed_w], 1), 'seq', split...]
    reshape x3 -> x6, local copies, waits for them, and re-layouts: 3.29 us -> 6.56 us  [the longest x3 5.47 us: own_columns(): weight.reshape(rows, seq_count, heads * head_width)]
  transfers between devices with their start and end apart: 16 -> 14, of which waited for: 9 -> 7; matrix products, arithmetic and copies ran while one was open for 7% -> 8% of each run, Pallas kernels for 5% -> 5%
where the time goes in v13:
time: 314 us; the launch traced here: 313 us
  waiting for transfers between devices  163 us (52%)
  local copies, waits for them, and re-layouts  38 us (12%)
  other arithmetic  29 us (9%)
  blocking collectives  23 us (7%)
  Pallas kernels  19.3 us (6%)
  matrix products  15.2 us (5%)
  between operations  13.6 us (4%)
  starting transfers between devices  11.8 us (4%)
    all_gather x1, waiting for transfers between devices, body(): own_all = lax.all_gather(own_rows, 'seq', axis=1, tiled=True)  52.8 us
    all_to_all x1, waiting for transfers between devices, body(): lax.all_to_all(jnp.concatenate([p for p, _ in packed_w], 1), 'seq', split...  39 us
    reduce_scatter x1, waiting for transfers between devices, body(): lax.psum_scatter(partial, 'tp', scatter_dimension=0, tiled=True)  34.7 us
    ppermute x3, waiting for transfers between devices, body(): lax.ppermute(packed, 'seq', perm=[(i, (i + k) % seq_count) for i in range...  22.6 us
    pallas_call x4, Pallas kernels, block_attention(): pl.pallas_call(kernel, grid_spec=pltpu.PrefetchScalarGridSpec(num_scalar_...  19.3 us
    all_to_all x2, other arithmetic, body(): lax.all_to_all(jnp.concatenate([p for p, _ in packed_w], 1), 'seq', split...  15 us
    unnamed x32, local copies, waits for them, and re-layouts  14.2 us
    all_gather x1, blocking collectives, body(): group_ids = lax.all_gather(segment_ids, 'seq', axis=0, tiled=True)  11.7 us
  transfers between devices with their start and end apart: 14, of which 7 were waited for; matrix products, arithmetic and copies ran while one was open for 8% of the time, Pallas kernels for 5%

profile of v13, /device:TPU:0, one launch (start us, length us, event | category | flops | bytes accessed | tf_op | source)
XLA Modules:
  0.0 313.0 jit_solution(16794509151005260206)
XLA Ops:
  10.2 11.4 %psum.7 = f32[256]{0:T(256)S(1)} all-reduce(f32[256]{0:T(256)S(1)} %fusion.2), channel_id=1, replica_groups=mesh['seq'=4,'tp'=4,'dp'=2] {'tp'}, use_global_device_ids=true, to_apply=%region_1.0 | all-reduce | flops 256 | bytes 2048 | tf_op jit(solution)/shard_map/psum | solution.py:176
  21.6 11.7 %all-gather.1 = s32[4,1,256]{2,1,0:T(1,128)S(1)} all-gather(s32[1,1,256]{2,1,0:T(1,128)S(1)} %bitcast.99), channel_id=1, replica_groups=mesh['seq'=4,'tp'=4,'dp'=2] {'seq'}, dimensions={0}, use_global_device_ids=true | all-gather | bytes 5120 | tf_op jit(solution)/shard_map/all_gather | solution.py:173
  33.5 52.8 %all-gather.5.cloned.1.call-done = bf16[896,2112]{0,1:T(8,128)(2,1)} async-done(((bf16[896,528]{0,1:T(8,128)(2,1)}), bf16[896,2112]{0,1:T(8,128)(2,1)}) %all-gather.5.cloned.1.call-update) | async-done | bytes 3784720 | tf_op jit(solution)/shard_map/all_gather | solution.py:186
  86.4 3.5 %fusion.9 = f32[256,2112]{1,0:T(8,128)S(1)} fusion(bf16[896,2112]{0,1:T(8,128)(2,1)} %all-gather.5.cloned.1.call-done, bf16[256,1792]{1,0:T(8,128)(2,1)S(1)} %fusion.4, s32[]{:T(128)S(6)} %select_n.150), kind=kOutput, calls=%fused_computation.37 | convolution fusion | flops 968884224 | bytes 6406148 | tf_op jit(solution)/shard_map/dot_general | solution.py:188
  89.8 3.4 %collective-permute-done = bf16[896,2112]{0,1:T(8,128)(2,1)} collective-permute-done((bf16[896,2112]{0,1:T(8,128)(2,1)}, bf16[896,2112]{0,1:T(8,128)(2,1)}, u32[]{:S(2)}, u32[]{:S(2)}) %collective-permute-start) | collective-permute-done | bytes 3784736 | tf_op jit(solution)/shard_map/ppermute | solution.py:195
  93.3 4.9 %convolution_add_fusion = f32[256,2112]{1,0:T(8,128)} fusion(f32[256,2112]{1,0:T(8,128)S(1)} %fusion.9, bf16[896,2112]{0,1:T(8,128)(2,1)} %collective-permute-done, bf16[256,1792]{1,0:T(8,128)(2,1)S(1)} %fusion.4, s32[]{:T(128)S(6)} %select_n.151), kind=kOutput, calls=%fused_computation.2 | convolution fusion | flops 969424896 | bytes 8634372 | tf_op jit(solution)/shard_map/dot_general | solution.py:198
  98.6 34.7 %reduce-scatter.2.cloned.1.call-done = f32[64,2112]{1,0:T(8,128)} async-done(((f32[256,2112]{1,0:T(8,128)}), f32[64,2112]{1,0:T(8,128)}) %reduce-scatter.2.cloned.1.call-update) | async-done | bytes 540688 | tf_op jit(solution)/shard_map/reduce_scatter | solution.py:203
  136.5 3.4 %collective-permute-start.3 = (bf16[64,2112]{1,0:T(8,128)(2,1)S(1)}, bf16[64,2112]{1,0:T(8,128)(2,1)S(1)}, u32[]{:S(2)}, u32[]{:S(2)}) collective-permute-start(bf16[64,2112]{1,0:T(8,128)(2,1)S(1)} %concatenate.26), channel_id=1, source_target_pairs={{0,24},{8,0},{16,8},{24,16},{1,25},{9,1},{17,9},{25,17},{2,26},{10... | collective-permute-start | bytes 811016 | tf_op jit(solution)/shard_map/ppermute | solution.py:221
  141.0 5.9 %collective-permute-done.3 = bf16[64,2112]{1,0:T(8,128)(2,1)S(1)} collective-permute-done((bf16[64,2112]{1,0:T(8,128)(2,1)S(1)}, bf16[64,2112]{1,0:T(8,128)(2,1)S(1)}, u32[]{:S(2)}, u32[]{:S(2)}) %collective-permute-start.3) | collective-permute-done | bytes 270368 | tf_op jit(solution)/shard_map/ppermute | solution.py:221
  147.0 16.6 %collective-permute-done.2 = bf16[64,2112]{1,0:T(8,128)(2,1)S(1)} collective-permute-done((bf16[64,2112]{1,0:T(8,128)(2,1)S(1)}, bf16[64,2112]{1,0:T(8,128)(2,1)S(1)}, u32[]{:S(2)}, u32[]{:S(2)}) %collective-permute-start.2) | collective-permute-done | bytes 270368 | tf_op jit(solution)/shard_map/ppermute | solution.py:221
  166.5 4.7 %reshape.238 = bf16[384,4,768]{2,1,0:T(4,128)(2,1)S(1)} reshape(bf16[384,3072]{1,0:T(8,128)(2,1)} %param.16) | data formatting | bytes 4718592 | tf_op jit(solution)/shard_map/reshape | solution.py:241
  171.9 12.2 %maximum_bitcast_fusion = bf16[4,1,212992]{2,0,1:T(4,128)(2,1)S(1)} fusion(bf16[4,32768]{1,0:T(4,128)(2,1)S(1)} %bitcast.82, bf16[4,32768]{1,0:T(4,128)(2,1)S(1)} %bitcast.83, bf16[4,147456]{1,0:T(4,128)(2,1)S(1)} %bitcast.71), kind=kLoop, calls=%fused_computation.18 | loop fusion | flops 5111808 | bytes 3407872 | tf_op jit(solution)/shard_map/all_to_all | solution.py:250
  184.6 2.8 reduce.1
  187.4 2.9 reshape.277
  190.3 4.4 %all-to-all-start = ((bf16[4,2,106496]{2,1,0:T(2,128)(2,1)}), bf16[4,2,106496]{2,1,0:T(2,128)(2,1)}, u32[]{:S(2)}, u32[]{:S(2)}) async-start(bf16[4,2,106496]{2,1,0:T(2,128)(2,1)} %reshape.277), calls=%async_computation.1 | async-start | bytes 3407872 | tf_op jit(solution)/shard_map/all_to_all | solution.py:250
  195.5 39.0 %all-to-all-done = bf16[4,2,106496]{2,1,0:T(2,128)(2,1)} async-done(((bf16[4,2,106496]{2,1,0:T(2,128)(2,1)}), bf16[4,2,106496]{2,1,0:T(2,128)(2,1)}, u32[]{:S(2)}, u32[]{:S(2)}) %all-to-all-start) | async-done | bytes 1703968 | tf_op jit(solution)/shard_map/all_to_all | solution.py:250
  234.4 3.2 %reshape.278 = bf16[4,1,212992]{2,1,0:T(2,128)(2,1)S(1)} reshape(bf16[4,2,106496]{2,1,0:T(2,128)(2,1)} %all-to-all-done) | data formatting | bytes 3407872
  237.6 3.6 %copy.102 = bf16[4,1,212992]{2,0,1:T(4,128)(2,1)S(1)} copy(bf16[4,1,212992]{2,1,0:T(2,128)(2,1)S(1)} %reshape.278) | data formatting | bytes 3407872
  260.6 3.4 %fusion.1 = f32[4,1024,192]{2,1,0:T(8,128)S(1)} fusion(bf16[1536,4,192]{0,2,1:T(8,128)(2,1)S(1)} %bitcast.77, bf16[1024,2112]{1,0:T(8,128)(2,1)S(1)} %bitcast.68), kind=kOutput, calls=%fused_computation.8 | convolution fusion | flops 2415919104 | bytes 8650752 | tf_op jit(solution)/shard_map/td,dhe->hte/dot_general | solution.py:279
  271.2 4.8 %shard_map.103 = bf16[4,256,128]{2,1,0:T(8,128)(2,1)} custom-call(s32[1]{0:T(128)} %bitcast.34.block_ref, bf16[4,1024,192]{2,1,0:T(8,128)(2,1)} %pad_maximum_fusion.1.query_ref, bf16[4,1024,128]{2,1,0:T(8,128)(2,1)} %fusion.5.key_ref, bf16[1024,64]{1,0:T(8,128)(2,1)} %slice.79.rope_ref, bf16[4,1024,128]{2,1,0:T(8,128)(2,1)} %fusion.6.value_ref, ...), custom_call_target="tpu_custom_call" | custom-call | flops 335544320 | bytes 1703936 | tf_op jit(solution)/shard_map/pallas_call | solution.py:115
  276.9 4.8 %shard_map.102 = bf16[4,256,128]{2,1,0:T(8,128)(2,1)} custom-call(s32[1]{0:T(128)} %bitcast.32.block_ref, bf16[4,1024,192]{2,1,0:T(8,128)(2,1)} %pad_maximum_fusion.1.query_ref, bf16[4,1024,128]{2,1,0:T(8,128)(2,1)} %fusion.5.key_ref, bf16[1024,64]{1,0:T(8,128)(2,1)} %slice.79.rope_ref, bf16[4,1024,128]{2,1,0:T(8,128)(2,1)} %fusion.6.value_ref, ...), custom_call_target="tpu_custom_call" | custom-call | flops 335544320 | bytes 1703936 | tf_op jit(solution)/shard_map/pallas_call | solution.py:115
  281.7 4.8 %shard_map.101 = bf16[4,256,128]{2,1,0:T(8,128)(2,1)} custom-call(s32[1]{0:T(128)} %bitcast.30.block_ref, bf16[4,1024,192]{2,1,0:T(8,128)(2,1)} %pad_maximum_fusion.1.query_ref, bf16[4,1024,128]{2,1,0:T(8,128)(2,1)} %fusion.5.key_ref, bf16[1024,64]{1,0:T(8,128)(2,1)} %slice.79.rope_ref, bf16[4,1024,128]{2,1,0:T(8,128)(2,1)} %fusion.6.value_ref, ...), custom_call_target="tpu_custom_call" | custom-call | flops 335544320 | bytes 1703936 | tf_op jit(solution)/shard_map/pallas_call | solution.py:115
  287.7 4.8 %shard_map.100 = bf16[4,256,128]{2,1,0:T(8,128)(2,1)} custom-call(s32[1]{0:T(128)} %bitcast.block_ref, bf16[4,1024,192]{2,1,0:T(8,128)(2,1)} %pad_maximum_fusion.1.query_ref, bf16[4,1024,128]{2,1,0:T(8,128)(2,1)} %fusion.5.key_ref, bf16[1024,64]{1,0:T(8,128)(2,1)} %slice.79.rope_ref, bf16[4,1024,128]{2,1,0:T(8,128)(2,1)} %fusion.6.value_ref, ...), custom_call_target="tpu_custom_call" | custom-call | flops 335544320 | bytes 1703936 | tf_op jit(solution)/shard_map/pallas_call | solution.py:115
  292.6 9.9 %collective-permute-done.8 = bf16[4,256,128]{2,1,0:T(8,128)(2,1)S(1)} collective-permute-done((bf16[4,256,128]{2,1,0:T(8,128)(2,1)}, bf16[4,256,128]{2,1,0:T(8,128)(2,1)S(1)}, u32[]{:S(2)}, u32[]{:S(2)}) %collective-permute-start.8) | collective-permute-done | bytes 262176 | tf_op jit(solution)/shard_map/ppermute | solution.py:304
  (112 shorter events, 45.8 us)
Async XLA Ops:
  6.5 1.9 copy-start.7
  6.5 79.8 %all-gather.5.cloned.1.call-start = ((), (), s32[]{:S(2)}) async-start(), calls=%async_computation.2 | async-start | bytes 4730880 | tf_op jit(solution)/shard_map/all_gather | solution.py:186
  8.4 13.1 %copy-start.12 = (s32[256]{0:T(256)S(1)}, s32[256]{0:T(256)}, u32[]{:S(2)}) copy-start(s32[256]{0:T(256)} %param.19) | copy-start | bytes 3076
  8.4 24.8 %copy-start.9 = (f32[1792]{0:T(1024)S(1)}, f32[1792]{0:T(1024)}, u32[]{:S(2)}) copy-start(f32[1792]{0:T(1024)} %param.11) | copy-start | bytes 21508
  9.5 123.7 %reduce-scatter.2.cloned.1.call-start = ((), (), s32[]{:S(2)}) async-start(), calls=%async_computation.3 | async-start | bytes 2785280 | tf_op jit(solution)/shard_map/reduce_scatter | solution.py:203
  33.2 212.4 %copy-start.8 = (s32[4,1,256]{2,1,0:T(1,128)}, s32[4,1,256]{2,1,0:T(1,128)S(1)}, u32[]{:S(2)}) copy-start(s32[4,1,256]{2,1,0:T(1,128)S(1)} %all-gather.1) | copy-start | bytes 12292
  86.4 6.9 %collective-permute-start = (bf16[896,2112]{0,1:T(8,128)(2,1)}, bf16[896,2112]{0,1:T(8,128)(2,1)}, u32[]{:S(2)}, u32[]{:S(2)}) collective-permute-start(bf16[896,2112]{0,1:T(8,128)(2,1)} %all-gather.5.cloned.1.call-done), channel_id=1, source_target_pairs={{0,1},{1,0},{2,3},{3,2},{4,5},{5,4},{6,7},{7,6},{8,9},{9,8},{10,11... | collective-permute-start | bytes 11354120 | tf_op jit(solution)/shard_map/ppermute | solution.py:195
  98.2 37.4 %copy-start.11 = (f32[512]{0:T(512)S(1)}, f32[512]{0:T(512)}, u32[]{:S(2)}) copy-start(f32[512]{0:T(512)} %param.15) | copy-start | bytes 6148
  134.7 1.5 copy-start.10
  136.5 10.5 %collective-permute-start.3 = (bf16[64,2112]{1,0:T(8,128)(2,1)S(1)}, bf16[64,2112]{1,0:T(8,128)(2,1)S(1)}, u32[]{:S(2)}, u32[]{:S(2)}) collective-permute-start(bf16[64,2112]{1,0:T(8,128)(2,1)S(1)} %concatenate.26), channel_id=1, source_target_pairs={{0,24},{8,0},{16,8},{24,16},{1,25},{9,1},{17,9},{25,17},{2,26},{10... | collective-permute-start | bytes 811016 | tf_op jit(solution)/shard_map/ppermute | solution.py:221
  139.9 23.7 %collective-permute-start.2 = (bf16[64,2112]{1,0:T(8,128)(2,1)S(1)}, bf16[64,2112]{1,0:T(8,128)(2,1)S(1)}, u32[]{:S(2)}, u32[]{:S(2)}) collective-permute-start(bf16[64,2112]{1,0:T(8,128)(2,1)S(1)} %concatenate.26), channel_id=1, source_target_pairs={{0,16},{8,24},{16,0},{24,8},{1,17},{9,25},{17,1},{25,9},{2,18},{10... | collective-permute-start | bytes 811016 | tf_op jit(solution)/shard_map/ppermute | solution.py:221
  139.9 23.7 %collective-permute-start.1 = (bf16[64,2112]{1,0:T(8,128)(2,1)S(1)}, bf16[64,2112]{1,0:T(8,128)(2,1)S(1)}, u32[]{:S(2)}, u32[]{:S(2)}) collective-permute-start(bf16[64,2112]{1,0:T(8,128)(2,1)S(1)} %concatenate.26), channel_id=1, source_target_pairs={{0,8},{8,16},{16,24},{24,0},{1,9},{9,17},{17,25},{25,1},{2,10},{10... | collective-permute-start | bytes 811016 | tf_op jit(solution)/shard_map/ppermute | solution.py:221
  163.8 2.0 copy-start.3
  164.5 1.7 copy-start.4
  190.3 44.1 %all-to-all-start = ((bf16[4,2,106496]{2,1,0:T(2,128)(2,1)}), bf16[4,2,106496]{2,1,0:T(2,128)(2,1)}, u32[]{:S(2)}, u32[]{:S(2)}) async-start(bf16[4,2,106496]{2,1,0:T(2,128)(2,1)} %reshape.277), calls=%async_computation.1 | async-start | bytes 3407872 | tf_op jit(solution)/shard_map/all_to_all | solution.py:250
  194.7 62.3 %all-gather.7.cloned.1.call-start = ((), (), s32[]{:S(2)}) async-start(), calls=%async_computation.4 | async-start | bytes 5570560 | tf_op jit(solution)/shard_map/all_gather | solution.py:228
  243.6 9.4 %collective-permute-start.4 = (bf16[1536,384]{1,0:T(8,128)(2,1)S(1)}, bf16[1536,384]{1,0:T(8,128)(2,1)}, u32[]{:S(2)}, u32[]{:S(2)}) collective-permute-start(bf16[1536,384]{1,0:T(8,128)(2,1)S(1)} %reshape.244), channel_id=1, source_target_pairs={{0,1},{1,0},{2,3},{3,2},{4,5},{5,4},{6,7},{7,6},{8,9},{9,8},{10,11... | collective-permute-start | bytes 3538952 | tf_op jit(solution)/shard_map/ppermute | solution.py:260
  245.0 3.8 %collective-permute-start.5 = (bf16[512,256]{1,0:T(8,128)(2,1)S(1)}, bf16[512,256]{1,0:T(8,128)(2,1)}, u32[]{:S(2)}, u32[]{:S(2)}) collective-permute-start(bf16[512,256]{1,0:T(8,128)(2,1)S(1)} %reshape.247), channel_id=1, source_target_pairs={{0,1},{1,0},{2,3},{3,2},{4,5},{5,4},{6,7},{7,6},{8,9},{9,8},{10,11... | collective-permute-start | bytes 786440 | tf_op jit(solution)/shard_map/ppermute | solution.py:260
  248.7 2.2 collective-permute-start.6
  257.1 3.5 %copy-start.2 = (bf16[1536,768]{0,1:T(8,128)(2,1)S(1)}, bf16[1536,768]{0,1:T(8,128)(2,1)}, u32[]{:S(2)}) copy-start(bf16[1536,768]{0,1:T(8,128)(2,1)} %copy.82) | copy-start | bytes 7077892
  264.0 2.8 copy-start.6
  276.1 16.5 %collective-permute-start.9 = (bf16[4,256,128]{2,1,0:T(8,128)(2,1)}, bf16[4,256,128]{2,1,0:T(8,128)(2,1)S(1)}, u32[]{:S(2)}, u32[]{:S(2)}) collective-permute-start(bf16[4,256,128]{2,1,0:T(8,128)(2,1)} %shard_map.103), channel_id=1, source_target_pairs={{0,24},{8,0},{16,8},{24,16},{1,25},{9,1},{17,9},{25,17},{2,26},{10... | collective-permute-start | bytes 786440 | tf_op jit(solution)/shard_map/ppermute | solution.py:304
  281.7 20.7 %collective-permute-start.8 = (bf16[4,256,128]{2,1,0:T(8,128)(2,1)}, bf16[4,256,128]{2,1,0:T(8,128)(2,1)S(1)}, u32[]{:S(2)}, u32[]{:S(2)}) collective-permute-start(bf16[4,256,128]{2,1,0:T(8,128)(2,1)} %shard_map.102), channel_id=1, source_target_pairs={{0,16},{8,24},{16,0},{24,8},{1,17},{9,25},{17,1},{25,9},{2,18},{10... | collective-permute-start | bytes 786440 | tf_op jit(solution)/shard_map/ppermute | solution.py:304
  286.6 15.9 %collective-permute-start.7 = (bf16[4,256,128]{2,1,0:T(8,128)(2,1)}, bf16[4,256,128]{2,1,0:T(8,128)(2,1)S(1)}, u32[]{:S(2)}, u32[]{:S(2)}) collective-permute-start(bf16[4,256,128]{2,1,0:T(8,128)(2,1)} %shard_map.101), channel_id=1, source_target_pairs={{0,8},{8,16},{16,24},{24,0},{1,9},{9,17},{17,25},{25,1},{2,10},{10... | collective-permute-start | bytes 786440 | tf_op jit(solution)/shard_map/ppermute | solution.py:304
  (3 other events, 3.8 us)
Sparse Core Ops, SparseCore 0:
  9.6 76.7 all-gather.4
  98.3 34.8 reduce-scatter.1
  197.4 55.1 all-gather.6

commit v14 on v12

--- a/solution.py
+++ b/solution.py
@@ -200,7 +200,13 @@
             peer_all,
             preferred_element_type=jnp.float32,
         )
-    latent_rows = lax.psum_scatter(partial, "tp", scatter_dimension=0, tiled=True)
+    pieces = partial.reshape(tp_count, partial.shape[0] // tp_count, partial.shape[1])
+    latent_rows = lax.dynamic_index_in_dim(pieces, tp_index, 0, keepdims=False)
+    for k in range(1, tp_count):
+        sent = lax.dynamic_index_in_dim(pieces, (tp_index + k) % tp_count, 0, keepdims=False)
+        latent_rows = latent_rows + lax.ppermute(
+            sent, "tp", perm=[(i, (i + k) % tp_count) for i in range(tp_count)]
+        )
 
     token_index = jnp.arange(total_rows, dtype=jnp.int32)
     onehot = group_ids[:, None] == jnp.arange(DOCS, dtype=jnp.int32)[None, :]

time: 287 us -> 281 us (0.979)
  waiting for transfers between devices: 159 us -> 149 us
    reduce_scatter x1 -> x0, waiting for transfers between devices: 34.6 us -> none  [body(): lax.psum_scatter(partial, 'tp', scatter_dimension=0, tiled=True)]
    ppermute x0 -> x3, waiting for transfers between devices: none -> 24.9 us  [body(): lax.ppermute(sent, 'tp', perm=[(i, (i + k) % tp_count) for i in range(tp_...]
    ppermute x0 -> x3, starting transfers between devices: none -> 3.59 us  [body(): lax.ppermute(sent, 'tp', perm=[(i, (i + k) % tp_count) for i in range(tp_...]
  transfers between devices with their start and end apart: 16 -> 18, of which waited for: 9 -> 10; matrix products, arithmetic and copies ran while one was open for 7% -> 7% of each run, Pallas kernels for 5% -> 5%
where the time goes in v14:
time: 281 us; the launch traced here: 280 us
  waiting for transfers between devices  149 us (53%)
  local copies, waits for them, and re-layouts  24.7 us (9%)
  blocking collectives  23 us (8%)
  starting transfers between devices  20.6 us (7%)
  Pallas kernels  19.3 us (7%)
  matrix products  15.2 us (5%)
  between operations  13.9 us (5%)
  other arithmetic  13.6 us (5%)
    all_gather x1, waiting for transfers between devices, body(): own_all = lax.all_gather(own_rows, 'seq', axis=1, tiled=True)  52.8 us
    all_to_all x3, waiting for transfers between devices, head_columns(): own = lax.all_to_all(own, 'seq', split_axis=1, concat_axis=0, tiled=True)  36.7 us
    ppermute x3, waiting for transfers between devices, body(): lax.ppermute(sent, 'tp', perm=[(i, (i + k) % tp_count) for i in range(tp_...  24.9 us
    ppermute x3, waiting for transfers between devices, body(): lax.ppermute(packed, 'seq', perm=[(i, (i + k) % seq_count) for i in range...  20.8 us
    pallas_call x4, Pallas kernels, block_attention(): pl.pallas_call(kernel, grid_spec=pltpu.PrefetchScalarGridSpec(num_scalar_...  19.3 us
    all_gather x1, blocking collectives, body(): group_ids = lax.all_gather(segment_ids, 'seq', axis=0, tiled=True)  11.7 us
    psum x1, blocking collectives, body(): square_sums = lax.psum(jnp.sum(inputs * inputs, 1), 'tp')  11.4 us
    all_to_all x3, starting transfers between devices, head_columns(): own = lax.all_to_all(own, 'seq', split_axis=1, concat_axis=0, tiled=True)  11.3 us
  transfers between devices with their start and end apart: 18, of which 10 were waited for; matrix products, arithmetic and copies ran while one was open for 7% of the time, Pallas kernels for 5%

profile of v14, /device:TPU:0, one launch (start us, length us, event | category | flops | bytes accessed | tf_op | source)
XLA Modules:
  0.0 279.6 jit_solution(14887316919693023927)
XLA Ops:
  10.2 11.4 %psum.7 = f32[256]{0:T(256)S(1)} all-reduce(f32[256]{0:T(256)S(1)} %fusion.2), channel_id=1, replica_groups=mesh['seq'=4,'tp'=4,'dp'=2] {'tp'}, use_global_device_ids=true, to_apply=%region_1.0 | all-reduce | flops 256 | bytes 2048 | tf_op jit(solution)/shard_map/psum | solution.py:176
  21.6 11.7 %all-gather.1 = s32[4,1,256]{2,1,0:T(1,128)S(1)} all-gather(s32[1,1,256]{2,1,0:T(1,128)S(1)} %bitcast.118), channel_id=1, replica_groups=mesh['seq'=4,'tp'=4,'dp'=2] {'seq'}, dimensions={0}, use_global_device_ids=true | all-gather | bytes 5120 | tf_op jit(solution)/shard_map/all_gather | solution.py:173
  33.5 52.8 %all-gather.5.cloned.1.call-done = bf16[896,2112]{0,1:T(8,128)(2,1)} async-done(((bf16[896,528]{0,1:T(8,128)(2,1)}), bf16[896,2112]{0,1:T(8,128)(2,1)}) %all-gather.5.cloned.1.call-update) | async-done | bytes 3784720 | tf_op jit(solution)/shard_map/all_gather | solution.py:186
  86.4 3.5 %fusion.11 = f32[256,2112]{0,1:T(8,128)S(1)} fusion(bf16[896,2112]{0,1:T(8,128)(2,1)} %all-gather.5.cloned.1.call-done, bf16[256,1792]{1,0:T(8,128)(2,1)S(1)} %fusion.4, s32[]{:T(128)S(6)} %select_n.175), kind=kOutput, calls=%fused_computation.41 | convolution fusion | flops 968884224 | bytes 6406148 | tf_op jit(solution)/shard_map/dot_general | solution.py:188
  89.9 3.4 %collective-permute-done = bf16[896,2112]{0,1:T(8,128)(2,1)} collective-permute-done((bf16[896,2112]{0,1:T(8,128)(2,1)}, bf16[896,2112]{0,1:T(8,128)(2,1)}, u32[]{:S(2)}, u32[]{:S(2)}) %collective-permute-start) | collective-permute-done | bytes 3784736 | tf_op jit(solution)/shard_map/ppermute | solution.py:195
  93.3 4.8 %convolution_add_fusion = f32[256,2112]{0,1:T(8,128)} fusion(f32[256,2112]{0,1:T(8,128)S(1)} %fusion.11, bf16[896,2112]{0,1:T(8,128)(2,1)} %collective-permute-done, bf16[256,1792]{1,0:T(8,128)(2,1)S(1)} %fusion.4, s32[]{:T(128)S(6)} %select_n.176), kind=kOutput, calls=%fused_computation.2 | convolution fusion | flops 969424896 | bytes 8568836 | tf_op jit(solution)/shard_map/dot_general | solution.py:198
  104.1 11.7 %collective-permute-done.3 = f32[64,2112]{1,0:T(8,128)S(1)} collective-permute-done((f32[64,2112]{1,0:T(8,128)S(1)}, f32[64,2112]{1,0:T(8,128)S(1)}, u32[]{:S(2)}, u32[]{:S(2)}) %collective-permute-start.3) | collective-permute-done | bytes 540704 | tf_op jit(solution)/shard_map/ppermute | solution.py:207
  115.8 13.2 %collective-permute-done.2 = f32[64,2112]{1,0:T(8,128)S(1)} collective-permute-done((f32[64,2112]{1,0:T(8,128)S(1)}, f32[64,2112]{1,0:T(8,128)S(1)}, u32[]{:S(2)}, u32[]{:S(2)}) %collective-permute-start.2) | collective-permute-done | bytes 540704 | tf_op jit(solution)/shard_map/ppermute | solution.py:207
  134.5 5.1 %collective-permute-done.6 = bf16[64,2112]{1,0:T(8,128)(2,1)S(1)} collective-permute-done((bf16[64,2112]{1,0:T(8,128)(2,1)S(1)}, bf16[64,2112]{1,0:T(8,128)(2,1)S(1)}, u32[]{:S(2)}, u32[]{:S(2)}) %collective-permute-start.6) | collective-permute-done | bytes 270368 | tf_op jit(solution)/shard_map/ppermute | solution.py:227
  139.5 15.7 %collective-permute-done.5 = bf16[64,2112]{1,0:T(8,128)(2,1)S(1)} collective-permute-done((bf16[64,2112]{1,0:T(8,128)(2,1)S(1)}, bf16[64,2112]{1,0:T(8,128)(2,1)S(1)}, u32[]{:S(2)}, u32[]{:S(2)}) %collective-permute-start.5) | collective-permute-done | bytes 270368 | tf_op jit(solution)/shard_map/ppermute | solution.py:227
  158.6 4.2 %all-to-all-start.2 = ((bf16[128,4,256]{2,0,1:T(8,128)(2,1)}), bf16[128,4,256]{2,0,1:T(8,128)(2,1)}, u32[]{:S(2)}, u32[]{:S(2)}) async-start(bf16[128,4,256]{2,0,1:T(8,128)(2,1)} %copy.156), calls=%async_computation.2 | async-start | bytes 524288 | tf_op jit(solution)/shard_map/all_to_all | solution.py:249
  162.8 3.2 %copy.142 = bf16[384,3072]{0,1:T(8,128)(2,1)S(1)} copy(bf16[384,3072]{1,0:T(8,128)(2,1)} %param.16) | data formatting | bytes 4718592 | tf_op jit(solution)/shard_map/optimization_barrier | solution.py:231
  167.6 4.2 %all-to-all-done.2 = bf16[128,4,256]{2,0,1:T(8,128)(2,1)} async-done(((bf16[128,4,256]{2,0,1:T(8,128)(2,1)}), bf16[128,4,256]{2,0,1:T(8,128)(2,1)}, u32[]{:S(2)}, u32[]{:S(2)}) %all-to-all-start.2) | async-done | bytes 262176 | tf_op jit(solution)/shard_map/all_to_all | solution.py:249
  171.9 3.5 %all-to-all-start = ((bf16[384,4,384]{2,0,1:T(8,128)(2,1)}), bf16[384,4,384]{2,0,1:T(8,128)(2,1)S(1)}, u32[]{:S(2)}, u32[]{:S(2)}) async-start(bf16[384,4,384]{2,0,1:T(8,128)(2,1)} %copy.143), calls=%async_computation | async-start | bytes 2359296 | tf_op jit(solution)/shard_map/all_to_all | solution.py:249
  176.6 27.3 %all-to-all-done = bf16[384,4,384]{2,0,1:T(8,128)(2,1)S(1)} async-done(((bf16[384,4,384]{2,0,1:T(8,128)(2,1)}), bf16[384,4,384]{2,0,1:T(8,128)(2,1)S(1)}, u32[]{:S(2)}, u32[]{:S(2)}) %all-to-all-start) | async-done | bytes 1179680 | tf_op jit(solution)/shard_map/all_to_all | solution.py:249
  203.9 3.6 %all-to-all-start.1 = ((bf16[128,4,256]{2,0,1:T(8,128)(2,1)}), bf16[128,4,256]{2,0,1:T(8,128)(2,1)S(1)}, u32[]{:S(2)}, u32[]{:S(2)}) async-start(bf16[128,4,256]{2,0,1:T(8,128)(2,1)} %copy.150), calls=%async_computation.1 | async-start | bytes 524288 | tf_op jit(solution)/shard_map/all_to_all | solution.py:249
  210.5 5.2 %all-to-all-done.1 = bf16[128,4,256]{2,0,1:T(8,128)(2,1)S(1)} async-done(((bf16[128,4,256]{2,0,1:T(8,128)(2,1)}), bf16[128,4,256]{2,0,1:T(8,128)(2,1)S(1)}, u32[]{:S(2)}, u32[]{:S(2)}) %all-to-all-start.1) | async-done | bytes 262176 | tf_op jit(solution)/shard_map/all_to_all | solution.py:249
  222.8 2.6 copy.147
  226.2 3.4 %fusion.1 = f32[4,1024,192]{2,1,0:T(8,128)S(1)} fusion(bf16[1536,4,192]{0,2,1:T(8,128)(2,1)S(1)} %bitcast.95, bf16[1024,2112]{1,0:T(8,128)(2,1)S(1)} %bitcast.86), kind=kOutput, calls=%fused_computation.8 | convolution fusion | flops 2415919104 | bytes 8650752 | tf_op jit(solution)/shard_map/td,dhe->hte/dot_general | solution.py:270
  236.9 4.8 %shard_map.103 = bf16[4,256,128]{2,1,0:T(8,128)(2,1)} custom-call(s32[1]{0:T(128)} %bitcast.50.block_ref, bf16[4,1024,192]{2,1,0:T(8,128)(2,1)} %pad_maximum_fusion.1.query_ref, bf16[4,1024,128]{2,1,0:T(8,128)(2,1)} %fusion.5.key_ref, bf16[1024,64]{1,0:T(8,128)(2,1)} %slice.65.rope_ref, bf16[4,1024,128]{2,1,0:T(8,128)(2,1)} %fusion.6.value_ref, ...), custom_call_target="tpu_custom_call" | custom-call | flops 335544320 | bytes 1703936 | tf_op jit(solution)/shard_map/pallas_call | solution.py:115
  243.2 4.8 %shard_map.102 = bf16[4,256,128]{2,1,0:T(8,128)(2,1)} custom-call(s32[1]{0:T(128)} %bitcast.48.block_ref, bf16[4,1024,192]{2,1,0:T(8,128)(2,1)} %pad_maximum_fusion.1.query_ref, bf16[4,1024,128]{2,1,0:T(8,128)(2,1)} %fusion.5.key_ref, bf16[1024,64]{1,0:T(8,128)(2,1)} %slice.65.rope_ref, bf16[4,1024,128]{2,1,0:T(8,128)(2,1)} %fusion.6.value_ref, ...), custom_call_target="tpu_custom_call" | custom-call | flops 335544320 | bytes 1703936 | tf_op jit(solution)/shard_map/pallas_call | solution.py:115
  248.2 4.8 %shard_map.101 = bf16[4,256,128]{2,1,0:T(8,128)(2,1)} custom-call(s32[1]{0:T(128)} %bitcast.46.block_ref, bf16[4,1024,192]{2,1,0:T(8,128)(2,1)} %pad_maximum_fusion.1.query_ref, bf16[4,1024,128]{2,1,0:T(8,128)(2,1)} %fusion.5.key_ref, bf16[1024,64]{1,0:T(8,128)(2,1)} %slice.65.rope_ref, bf16[4,1024,128]{2,1,0:T(8,128)(2,1)} %fusion.6.value_ref, ...), custom_call_target="tpu_custom_call" | custom-call | flops 335544320 | bytes 1703936 | tf_op jit(solution)/shard_map/pallas_call | solution.py:115
  253.4 4.8 %shard_map.100 = bf16[4,256,128]{2,1,0:T(8,128)(2,1)} custom-call(s32[1]{0:T(128)} %bitcast.block_ref, bf16[4,1024,192]{2,1,0:T(8,128)(2,1)} %pad_maximum_fusion.1.query_ref, bf16[4,1024,128]{2,1,0:T(8,128)(2,1)} %fusion.5.key_ref, bf16[1024,64]{1,0:T(8,128)(2,1)} %slice.65.rope_ref, bf16[4,1024,128]{2,1,0:T(8,128)(2,1)} %fusion.6.value_ref, ...), custom_call_target="tpu_custom_call" | custom-call | flops 335544320 | bytes 1703936 | tf_op jit(solution)/shard_map/pallas_call | solution.py:115
  258.2 10.5 %collective-permute-done.11 = bf16[4,256,128]{2,1,0:T(8,128)(2,1)S(1)} collective-permute-done((bf16[4,256,128]{2,1,0:T(8,128)(2,1)}, bf16[4,256,128]{2,1,0:T(8,128)(2,1)S(1)}, u32[]{:S(2)}, u32[]{:S(2)}) %collective-permute-start.11) | collective-permute-done | bytes 262176 | tf_op jit(solution)/shard_map/ppermute | solution.py:295
  (114 shorter events, 45.3 us)
Async XLA Ops:
  6.5 79.8 %all-gather.5.cloned.1.call-start = ((), (), s32[]{:S(2)}) async-start(), calls=%async_computation.3 | async-start | bytes 4730880 | tf_op jit(solution)/shard_map/all_gather | solution.py:186
  8.4 13.1 %copy-start.12 = (s32[256]{0:T(256)S(1)}, s32[256]{0:T(256)}, u32[]{:S(2)}) copy-start(s32[256]{0:T(256)} %param.19) | copy-start | bytes 3076
  8.4 24.8 %copy-start.7 = (f32[1792]{0:T(1024)S(1)}, f32[1792]{0:T(1024)}, u32[]{:S(2)}) copy-start(f32[1792]{0:T(1024)} %param.11) | copy-start | bytes 21508
  9.5 213.3 %all-gather.7.cloned.1.call-start = ((), (), s32[]{:S(2)}) async-start(), calls=%async_computation.4 | async-start | bytes 5570560 | tf_op jit(solution)/shard_map/all_gather | solution.py:234
  33.2 183.3 %copy-start.6 = (s32[4,1,256]{2,1,0:T(1,128)}, s32[4,1,256]{2,1,0:T(1,128)S(1)}, u32[]{:S(2)}) copy-start(s32[4,1,256]{2,1,0:T(1,128)S(1)} %all-gather.1) | copy-start | bytes 12292
  86.4 6.9 %collective-permute-start = (bf16[896,2112]{0,1:T(8,128)(2,1)}, bf16[896,2112]{0,1:T(8,128)(2,1)}, u32[]{:S(2)}, u32[]{:S(2)}) collective-permute-start(bf16[896,2112]{0,1:T(8,128)(2,1)} %all-gather.5.cloned.1.call-done), channel_id=1, source_target_pairs={{0,1},{1,0},{2,3},{3,2},{4,5},{5,4},{6,7},{7,6},{8,9},{9,8},{10,11... | collective-permute-start | bytes 11354120 | tf_op jit(solution)/shard_map/ppermute | solution.py:195
  86.4 44.4 %copy-start.10 = (f32[32]{0:T(128)}, f32[32]{0:T(128)S(1)}, u32[]{:S(2)}) copy-start(f32[32]{0:T(128)S(1)} %multiply_power_fusion) | copy-start | bytes 388
  100.2 15.5 %collective-permute-start.3 = (f32[64,2112]{1,0:T(8,128)S(1)}, f32[64,2112]{1,0:T(8,128)S(1)}, u32[]{:S(2)}, u32[]{:S(2)}) collective-permute-start(f32[64,2112]{1,0:T(8,128)S(1)} %get-tuple-element.24), channel_id=1, source_target_pairs={{0,6},{2,0},{4,2},{6,4},{1,7},{3,1},{5,3},{7,5},{8,14},{10,8},{12,... | collective-permute-start | bytes 1622024 | tf_op jit(solution)/shard_map/ppermute | solution.py:207
  102.7 26.3 %collective-permute-start.2 = (f32[64,2112]{1,0:T(8,128)S(1)}, f32[64,2112]{1,0:T(8,128)S(1)}, u32[]{:S(2)}, u32[]{:S(2)}) collective-permute-start(f32[64,2112]{1,0:T(8,128)S(1)} %get-tuple-element.25), channel_id=1, source_target_pairs={{0,4},{2,6},{4,0},{6,2},{1,5},{3,7},{5,1},{7,3},{8,12},{10,14},{12... | collective-permute-start | bytes 1622024 | tf_op jit(solution)/shard_map/ppermute | solution.py:207
  103.2 25.8 %collective-permute-start.1 = (f32[64,2112]{1,0:T(8,128)S(1)}, f32[64,2112]{1,0:T(8,128)S(1)}, u32[]{:S(2)}, u32[]{:S(2)}) collective-permute-start(f32[64,2112]{1,0:T(8,128)S(1)} %get-tuple-element.23), channel_id=1, source_target_pairs={{0,2},{2,4},{4,6},{6,0},{1,3},{3,5},{5,7},{7,1},{8,10},{10,12},{12... | collective-permute-start | bytes 1622024 | tf_op jit(solution)/shard_map/ppermute | solution.py:207
  131.4 8.1 %collective-permute-start.6 = (bf16[64,2112]{1,0:T(8,128)(2,1)S(1)}, bf16[64,2112]{1,0:T(8,128)(2,1)S(1)}, u32[]{:S(2)}, u32[]{:S(2)}) collective-permute-start(bf16[64,2112]{1,0:T(8,128)(2,1)S(1)} %concatenate.23), channel_id=1, source_target_pairs={{0,24},{8,0},{16,8},{24,16},{1,25},{9,1},{17,9},{25,17},{2,26},{10... | collective-permute-start | bytes 811016 | tf_op jit(solution)/shard_map/ppermute | solution.py:227
  132.3 23.0 %collective-permute-start.5 = (bf16[64,2112]{1,0:T(8,128)(2,1)S(1)}, bf16[64,2112]{1,0:T(8,128)(2,1)S(1)}, u32[]{:S(2)}, u32[]{:S(2)}) collective-permute-start(bf16[64,2112]{1,0:T(8,128)(2,1)S(1)} %concatenate.23), channel_id=1, source_target_pairs={{0,16},{8,24},{16,0},{24,8},{1,17},{9,25},{17,1},{25,9},{2,18},{10... | collective-permute-start | bytes 811016 | tf_op jit(solution)/shard_map/ppermute | solution.py:227
  132.5 22.8 %collective-permute-start.4 = (bf16[64,2112]{1,0:T(8,128)(2,1)S(1)}, bf16[64,2112]{1,0:T(8,128)(2,1)S(1)}, u32[]{:S(2)}, u32[]{:S(2)}) collective-permute-start(bf16[64,2112]{1,0:T(8,128)(2,1)S(1)} %concatenate.23), channel_id=1, source_target_pairs={{0,8},{8,16},{16,24},{24,0},{1,9},{9,17},{17,25},{25,1},{2,10},{10... | collective-permute-start | bytes 811016 | tf_op jit(solution)/shard_map/ppermute | solution.py:227
  158.6 13.3 %all-to-all-start.2 = ((bf16[128,4,256]{2,0,1:T(8,128)(2,1)}), bf16[128,4,256]{2,0,1:T(8,128)(2,1)}, u32[]{:S(2)}, u32[]{:S(2)}) async-start(bf16[128,4,256]{2,0,1:T(8,128)(2,1)} %copy.156), calls=%async_computation.2 | async-start | bytes 524288 | tf_op jit(solution)/shard_map/all_to_all | solution.py:249
  166.1 9.3 %copy-start.2 = (bf16[128,2048]{1,0:T(8,128)(2,1)S(1)}, bf16[128,2048]{1,0:T(8,128)(2,1)}, u32[]{:S(2)}) copy-start(bf16[128,2048]{1,0:T(8,128)(2,1)} %param.17) | copy-start | bytes 1572868
  171.9 32.0 %all-to-all-start = ((bf16[384,4,384]{2,0,1:T(8,128)(2,1)}), bf16[384,4,384]{2,0,1:T(8,128)(2,1)S(1)}, u32[]{:S(2)}, u32[]{:S(2)}) async-start(bf16[384,4,384]{2,0,1:T(8,128)(2,1)} %copy.143), calls=%async_computation | async-start | bytes 2359296 | tf_op jit(solution)/shard_map/all_to_all | solution.py:249
  203.9 11.8 %all-to-all-start.1 = ((bf16[128,4,256]{2,0,1:T(8,128)(2,1)}), bf16[128,4,256]{2,0,1:T(8,128)(2,1)S(1)}, u32[]{:S(2)}, u32[]{:S(2)}) async-start(bf16[128,4,256]{2,0,1:T(8,128)(2,1)} %copy.150), calls=%async_computation.1 | async-start | bytes 524288 | tf_op jit(solution)/shard_map/all_to_all | solution.py:249
  207.5 10.1 %copy-start.11 = (f32[32]{0:T(128)S(1)}, f32[32]{0:T(128)}, u32[]{:S(2)}) copy-start(f32[32]{0:T(128)} %copy-done.10) | copy-start | bytes 388
  208.1 14.3 %collective-permute-start.7 = (bf16[1536,384]{0,1:T(8,128)(2,1)S(1)}, bf16[1536,384]{0,1:T(8,128)(2,1)S(1)}, u32[]{:S(2)}, u32[]{:S(2)}) collective-permute-start(bf16[1536,384]{0,1:T(8,128)(2,1)S(1)} %copy.144), channel_id=1, source_target_pairs={{0,1},{1,0},{2,3},{3,2},{4,5},{5,4},{6,7},{7,6},{8,9},{9,8},{10,11... | collective-permute-start | bytes 3538952 | tf_op jit(solution)/shard_map/ppermute | solution.py:254
  210.0 9.5 %collective-permute-start.9 = (bf16[512,256]{0,1:T(8,128)(2,1)}, bf16[512,256]{0,1:T(8,128)(2,1)}, u32[]{:S(2)}, u32[]{:S(2)}) collective-permute-start(bf16[512,256]{0,1:T(8,128)(2,1)} %copy.157), channel_id=1, source_target_pairs={{0,1},{1,0},{2,3},{3,2},{4,5},{5,4},{6,7},{7,6},{8,9},{9,8},{10,11... | collective-permute-start | bytes 786440 | tf_op jit(solution)/shard_map/ppermute | solution.py:254
  216.6 2.9 %collective-permute-start.8 = (bf16[512,256]{0,1:T(8,128)(2,1)}, bf16[512,256]{0,1:T(8,128)(2,1)}, u32[]{:S(2)}, u32[]{:S(2)}) collective-permute-start(bf16[512,256]{0,1:T(8,128)(2,1)} %copy.151), channel_id=1, source_target_pairs={{0,1},{1,0},{2,3},{3,2},{4,5},{5,4},{6,7},{7,6},{8,9},{9,8},{10,11... | collective-permute-start | bytes 786440 | tf_op jit(solution)/shard_map/ppermute | solution.py:254
  241.7 16.5 %collective-permute-start.12 = (bf16[4,256,128]{2,1,0:T(8,128)(2,1)}, bf16[4,256,128]{2,1,0:T(8,128)(2,1)S(1)}, u32[]{:S(2)}, u32[]{:S(2)}) collective-permute-start(bf16[4,256,128]{2,1,0:T(8,128)(2,1)} %shard_map.103), channel_id=1, source_target_pairs={{0,24},{8,0},{16,8},{24,16},{1,25},{9,1},{17,9},{25,17},{2,26},{10... | collective-permute-start | bytes 786440 | tf_op jit(solution)/shard_map/ppermute | solution.py:295
  248.0 20.8 %collective-permute-start.11 = (bf16[4,256,128]{2,1,0:T(8,128)(2,1)}, bf16[4,256,128]{2,1,0:T(8,128)(2,1)S(1)}, u32[]{:S(2)}, u32[]{:S(2)}) collective-permute-start(bf16[4,256,128]{2,1,0:T(8,128)(2,1)} %shard_map.102), channel_id=1, source_target_pairs={{0,16},{8,24},{16,0},{24,8},{1,17},{9,25},{17,1},{25,9},{2,18},{10... | collective-permute-start | bytes 786440 | tf_op jit(solution)/shard_map/ppermute | solution.py:295
  253.0 15.7 %collective-permute-start.10 = (bf16[4,256,128]{2,1,0:T(8,128)(2,1)}, bf16[4,256,128]{2,1,0:T(8,128)(2,1)S(1)}, u32[]{:S(2)}, u32[]{:S(2)}) collective-permute-start(bf16[4,256,128]{2,1,0:T(8,128)(2,1)} %shard_map.101), channel_id=1, source_target_pairs={{0,8},{8,16},{16,24},{24,0},{1,9},{9,17},{17,25},{25,1},{2,10},{10... | collective-permute-start | bytes 786440 | tf_op jit(solution)/shard_map/ppermute | solution.py:295
  (7 other events, 11.4 us)
Sparse Core Ops, SparseCore 0:
  9.6 76.7 all-gather.4
  157.5 54.2 all-gather.6

commit v15 on v14

--- a/solution.py
+++ b/solution.py
@@ -231,7 +231,11 @@
     packed, query_up, key_up, value_up = lax.optimization_barrier(
         (packed, query_up, key_up, value_up)
     )
-    packed = lax.all_gather(packed, "tp", axis=0, tiled=False)
+    from_tp = [packed] + [
+        lax.ppermute(packed, "tp", perm=[(i, (i + k) % tp_count) for i in range(tp_count)])
+        for k in range(1, tp_count)
+    ]
+    packed = jnp.take(jnp.stack(from_tp), (tp_index - jnp.arange(tp_count)) % tp_count, axis=0)
     latent = jnp.transpose(packed, (1, 0, 2, 3)).reshape(total_rows, packed.shape[-1])
     cq_all = latent[:, :qrank]
     cm_all = latent[:, qrank : qrank + KVRANK]

time: 281 us -> 303 us (1.078)
  waiting for transfers between devices: 149 us -> 157 us
  other arithmetic: 13.6 us -> 20.6 us
  starting transfers between devices: 20.6 us -> 26.2 us
    ppermute x0 -> x3, waiting for transfers between devices: none -> 36.9 us  [body(): lax.ppermute(packed, 'tp', perm=[(i, (i + k) % tp_count) for i in range(t...]
    all_to_all x3, waiting for transfers between devices: 36.7 us -> 10.3 us  [head_columns(): own = lax.all_to_all(own, 'seq', split_axis=1, concat_axis=0, tiled=True)]
    gather x0 -> x1, local copies, waits for them, and re-layouts: none -> 5.36 us  [body(): jnp.take(jnp.stack(from_tp), (tp_index - jnp.arange(tp_count)) % tp_count...]
    another operation x2 -> x3, other arithmetic: 0.91 us -> 4.71 us  [the longest x1 3.82 us: body(): jnp.stack(from_tp)]
  transfers between devices with their start and end apart: 18 -> 20, of which waited for: 10 -> 11; matrix products, arithmetic and copies ran while one was open for 7% -> 12% of each run, Pallas kernels for 5% -> 5%
where the time goes in v15:
time: 303 us; the launch traced here: 302 us
  waiting for transfers between devices  157 us (52%)
  local copies, waits for them, and re-layouts  26.7 us (9%)
  starting transfers between devices  26.2 us (9%)
  blocking collectives  23 us (8%)
  other arithmetic  20.6 us (7%)
  Pallas kernels  19.3 us (6%)
  matrix products  15.2 us (5%)
  between operations  13.9 us (5%)
    all_gather x1, waiting for transfers between devices, body(): own_all = lax.all_gather(own_rows, 'seq', axis=1, tiled=True)  52.8 us
    ppermute x3, waiting for transfers between devices, body(): lax.ppermute(packed, 'tp', perm=[(i, (i + k) % tp_count) for i in range(t...  36.9 us
    ppermute x3, waiting for transfers between devices, body(): lax.ppermute(sent, 'tp', perm=[(i, (i + k) % tp_count) for i in range(tp_...  24.9 us
    ppermute x3, waiting for transfers between devices, body(): lax.ppermute(packed, 'seq', perm=[(i, (i + k) % seq_count) for i in range...  20.2 us
    pallas_call x4, Pallas kernels, block_attention(): pl.pallas_call(kernel, grid_spec=pltpu.PrefetchScalarGridSpec(num_scalar_...  19.3 us
    all_gather x1, blocking collectives, body(): group_ids = lax.all_gather(segment_ids, 'seq', axis=0, tiled=True)  11.7 us
    all_to_all x3, starting transfers between devices, head_columns(): own = lax.all_to_all(own, 'seq', split_axis=1, concat_axis=0, tiled=True)  11.4 us
    psum x1, blocking collectives, body(): square_sums = lax.psum(jnp.sum(inputs * inputs, 1), 'tp')  11.4 us
  transfers between devices with their start and end apart: 20, of which 11 were waited for; matrix products, arithmetic and copies ran while one was open for 12% of the time, Pallas kernels for 5%

profile of v15, /device:TPU:0, one launch (start us, length us, event | category | flops | bytes accessed | tf_op | source)
XLA Modules:
  0.0 302.3 jit_solution(11826194114740545217)
XLA Ops:
  10.2 11.4 %psum.7 = f32[256]{0:T(256)S(1)} all-reduce(f32[256]{0:T(256)S(1)} %fusion.2), channel_id=1, replica_groups=mesh['seq'=4,'tp'=4,'dp'=2] {'tp'}, use_global_device_ids=true, to_apply=%region_1.0 | all-reduce | flops 256 | bytes 2048 | tf_op jit(solution)/shard_map/psum | solution.py:176
  21.6 11.7 %all-gather = s32[4,1,256]{2,1,0:T(1,128)S(1)} all-gather(s32[1,1,256]{2,1,0:T(1,128)S(1)} %bitcast.123), channel_id=1, replica_groups=mesh['seq'=4,'tp'=4,'dp'=2] {'seq'}, dimensions={0}, use_global_device_ids=true | all-gather | bytes 5120 | tf_op jit(solution)/shard_map/all_gather | solution.py:173
  33.5 52.8 %all-gather.3.cloned.1.call-done = bf16[896,2112]{0,1:T(8,128)(2,1)} async-done(((bf16[896,528]{0,1:T(8,128)(2,1)}), bf16[896,2112]{0,1:T(8,128)(2,1)}) %all-gather.3.cloned.1.call-update) | async-done | bytes 3784720 | tf_op jit(solution)/shard_map/all_gather | solution.py:186
  86.4 3.4 %fusion.11 = f32[256,2112]{0,1:T(8,128)S(1)} fusion(bf16[896,2112]{0,1:T(8,128)(2,1)} %all-gather.3.cloned.1.call-done, bf16[256,1792]{1,0:T(8,128)(2,1)S(1)} %fusion.4, s32[]{:T(128)S(6)} %select_n.213), kind=kOutput, calls=%fused_computation.44 | convolution fusion | flops 968884224 | bytes 6406148 | tf_op jit(solution)/shard_map/dot_general | solution.py:188
  89.8 3.4 %collective-permute-done = bf16[896,2112]{0,1:T(8,128)(2,1)} collective-permute-done((bf16[896,2112]{0,1:T(8,128)(2,1)}, bf16[896,2112]{0,1:T(8,128)(2,1)}, u32[]{:S(2)}, u32[]{:S(2)}) %collective-permute-start) | collective-permute-done | bytes 3784736 | tf_op jit(solution)/shard_map/ppermute | solution.py:195
  93.3 4.8 %convolution_add_fusion = f32[256,2112]{0,1:T(8,128)} fusion(f32[256,2112]{0,1:T(8,128)S(1)} %fusion.11, bf16[896,2112]{0,1:T(8,128)(2,1)} %collective-permute-done, bf16[256,1792]{1,0:T(8,128)(2,1)S(1)} %fusion.4, s32[]{:T(128)S(6)} %select_n.214), kind=kOutput, calls=%fused_computation.5 | convolution fusion | flops 969424896 | bytes 8568836 | tf_op jit(solution)/shard_map/dot_general | solution.py:198
  104.1 11.7 %collective-permute-done.3 = f32[64,2112]{1,0:T(8,128)S(1)} collective-permute-done((f32[64,2112]{1,0:T(8,128)S(1)}, f32[64,2112]{1,0:T(8,128)S(1)}, u32[]{:S(2)}, u32[]{:S(2)}) %collective-permute-start.3) | collective-permute-done | bytes 540704 | tf_op jit(solution)/shard_map/ppermute | solution.py:207
  115.8 13.2 %collective-permute-done.2 = f32[64,2112]{1,0:T(8,128)S(1)} collective-permute-done((f32[64,2112]{1,0:T(8,128)S(1)}, f32[64,2112]{1,0:T(8,128)S(1)}, u32[]{:S(2)}, u32[]{:S(2)}) %collective-permute-start.2) | collective-permute-done | bytes 540704 | tf_op jit(solution)/shard_map/ppermute | solution.py:207
  135.1 4.5 %collective-permute-done.6 = bf16[64,2112]{1,0:T(8,128)(2,1)S(1)} collective-permute-done((bf16[64,2112]{1,0:T(8,128)(2,1)S(1)}, bf16[64,2112]{1,0:T(8,128)(2,1)S(1)}, u32[]{:S(2)}, u32[]{:S(2)}) %collective-permute-start.6) | collective-permute-done | bytes 270368 | tf_op jit(solution)/shard_map/ppermute | solution.py:227
  139.5 15.7 %collective-permute-done.5 = bf16[64,2112]{1,0:T(8,128)(2,1)S(1)} collective-permute-done((bf16[64,2112]{1,0:T(8,128)(2,1)S(1)}, bf16[64,2112]{1,0:T(8,128)(2,1)S(1)}, u32[]{:S(2)}, u32[]{:S(2)}) %collective-permute-start.5) | collective-permute-done | bytes 270368 | tf_op jit(solution)/shard_map/ppermute | solution.py:227
  158.5 3.8 %all-to-all-start.1 = ((bf16[128,4,256]{2,0,1:T(8,128)(2,1)}), bf16[128,4,256]{2,0,1:T(8,128)(2,1)S(1)}, u32[]{:S(2)}, u32[]{:S(2)}) async-start(bf16[128,4,256]{2,0,1:T(8,128)(2,1)} %copy.150), calls=%async_computation.1 | async-start | bytes 524288 | tf_op jit(solution)/shard_map/all_to_all | solution.py:253
  163.5 7.9 %all-to-all-done.1 = bf16[128,4,256]{2,0,1:T(8,128)(2,1)S(1)} async-done(((bf16[128,4,256]{2,0,1:T(8,128)(2,1)}), bf16[128,4,256]{2,0,1:T(8,128)(2,1)S(1)}, u32[]{:S(2)}, u32[]{:S(2)}) %all-to-all-start.1) | async-done | bytes 262176 | tf_op jit(solution)/shard_map/all_to_all | solution.py:253
  171.5 4.1 %all-to-all-start.2 = ((bf16[128,4,256]{2,0,1:T(8,128)(2,1)}), bf16[128,4,256]{2,0,1:T(8,128)(2,1)}, u32[]{:S(2)}, u32[]{:S(2)}) async-start(bf16[128,4,256]{2,0,1:T(8,128)(2,1)} %copy.156), calls=%async_computation.2 | async-start | bytes 524288 | tf_op jit(solution)/shard_map/all_to_all | solution.py:253
  182.5 3.5 %all-to-all-start = ((bf16[384,4,384]{2,0,1:T(8,128)(2,1)}), bf16[384,4,384]{2,0,1:T(8,128)(2,1)S(1)}, u32[]{:S(2)}, u32[]{:S(2)}) async-start(bf16[384,4,384]{2,0,1:T(8,128)(2,1)} %copy.143), calls=%async_computation | async-start | bytes 2359296 | tf_op jit(solution)/shard_map/all_to_all | solution.py:253
  198.0 15.7 %collective-permute-done.10 = bf16[4,64,2112]{2,1,0:T(8,128)(2,1)} collective-permute-done((bf16[4,64,2112]{2,1,0:T(8,128)(2,1)S(1)}, bf16[4,64,2112]{2,1,0:T(8,128)(2,1)}, u32[]{:S(2)}, u32[]{:S(2)}) %collective-permute-start.10) | collective-permute-done | bytes 1081376 | tf_op jit(solution)/shard_map/ppermute | solution.py:235
  213.7 21.2 %collective-permute-done.9 = bf16[4,64,2112]{2,1,0:T(8,128)(2,1)} collective-permute-done((bf16[4,64,2112]{2,1,0:T(8,128)(2,1)S(1)}, bf16[4,64,2112]{2,1,0:T(8,128)(2,1)}, u32[]{:S(2)}, u32[]{:S(2)}) %collective-permute-start.9) | collective-permute-done | bytes 1081376 | tf_op jit(solution)/shard_map/ppermute | solution.py:235
  234.9 3.8 %pad_maximum_fusion = bf16[4,4,64,2112]{3,2,1,0:T(8,128)(2,1)} fusion(bf16[1,4,64,2112]{3,2,1,0:T(8,128)(2,1)} %bitcast.24, bf16[1,4,64,2112]{3,2,1,0:T(8,128)(2,1)} %bitcast.23, bf16[1,4,64,2112]{3,2,1,0:T(8,128)(2,1)} %bitcast.22, bf16[1,4,64,2112]{3,2,1,0:T(8,128)(2,1)S(1)} %bitcast.95), kind=kLoop, calls=%fused_computation.3 | loop fusion | flops 6488064 | bytes 8650752 | tf_op jit(solution)/shard_map/stack | solution.py:238
  238.7 5.4 %gather_fusion.1 = bf16[4,4,64,2112]{3,2,1,0:T(8,128)(2,1)} fusion(bf16[4,4,64,2112]{3,2,1,0:T(8,128)(2,1)} %pad_maximum_fusion, s32[1024]{0:T(1024)S(1)} %pad_clamp_fusion), kind=kCustom, calls=%fused_computation.1 | custom fusion | bytes 8650768 | tf_op jit(solution)/shard_map/jit(_take)/gather | solution.py:238
  258.8 4.8 %shard_map.103 = bf16[4,256,128]{2,1,0:T(8,128)(2,1)} custom-call(s32[1]{0:T(128)} %bitcast.54.block_ref, bf16[4,1024,192]{2,1,0:T(8,128)(2,1)} %pad_maximum_fusion.2.query_ref, bf16[4,1024,128]{2,1,0:T(8,128)(2,1)} %fusion.5.key_ref, bf16[1024,64]{1,0:T(8,128)(2,1)} %slice.67.rope_ref, bf16[4,1024,128]{2,1,0:T(8,128)(2,1)} %fusion.6.value_ref, ...), custom_call_target="tpu_custom_call" | custom-call | flops 335544320 | bytes 1703936 | tf_op jit(solution)/shard_map/pallas_call | solution.py:115
  263.6 3.5 %collective-permute-start.15 = (bf16[4,256,128]{2,1,0:T(8,128)(2,1)}, bf16[4,256,128]{2,1,0:T(8,128)(2,1)S(1)}, u32[]{:S(2)}, u32[]{:S(2)}) collective-permute-start(bf16[4,256,128]{2,1,0:T(8,128)(2,1)} %shard_map.103), channel_id=1, source_target_pairs={{0,24},{8,0},{16,8},{24,16},{1,25},{9,1},{17,9},{25,17},{2,26},{10... | collective-permute-start | bytes 786440 | tf_op jit(solution)/shard_map/ppermute | solution.py:299
  267.2 4.8 %shard_map.102 = bf16[4,256,128]{2,1,0:T(8,128)(2,1)} custom-call(s32[1]{0:T(128)} %bitcast.52.block_ref, bf16[4,1024,192]{2,1,0:T(8,128)(2,1)} %pad_maximum_fusion.2.query_ref, bf16[4,1024,128]{2,1,0:T(8,128)(2,1)} %fusion.5.key_ref, bf16[1024,64]{1,0:T(8,128)(2,1)} %slice.67.rope_ref, bf16[4,1024,128]{2,1,0:T(8,128)(2,1)} %fusion.6.value_ref, ...), custom_call_target="tpu_custom_call" | custom-call | flops 335544320 | bytes 1703936 | tf_op jit(solution)/shard_map/pallas_call | solution.py:115
  272.0 4.8 %shard_map.101 = bf16[4,256,128]{2,1,0:T(8,128)(2,1)} custom-call(s32[1]{0:T(128)} %bitcast.50.block_ref, bf16[4,1024,192]{2,1,0:T(8,128)(2,1)} %pad_maximum_fusion.2.query_ref, bf16[4,1024,128]{2,1,0:T(8,128)(2,1)} %fusion.5.key_ref, bf16[1024,64]{1,0:T(8,128)(2,1)} %slice.67.rope_ref, bf16[4,1024,128]{2,1,0:T(8,128)(2,1)} %fusion.6.value_ref, ...), custom_call_target="tpu_custom_call" | custom-call | flops 335544320 | bytes 1703936 | tf_op jit(solution)/shard_map/pallas_call | solution.py:115
  277.9 4.8 %shard_map.100 = bf16[4,256,128]{2,1,0:T(8,128)(2,1)} custom-call(s32[1]{0:T(128)} %bitcast.block_ref, bf16[4,1024,192]{2,1,0:T(8,128)(2,1)} %pad_maximum_fusion.2.query_ref, bf16[4,1024,128]{2,1,0:T(8,128)(2,1)} %fusion.5.key_ref, bf16[1024,64]{1,0:T(8,128)(2,1)} %slice.67.rope_ref, bf16[4,1024,128]{2,1,0:T(8,128)(2,1)} %fusion.6.value_ref, ...), custom_call_target="tpu_custom_call" | custom-call | flops 335544320 | bytes 1703936 | tf_op jit(solution)/shard_map/pallas_call | solution.py:115
  282.8 8.7 %collective-permute-done.14 = bf16[4,256,128]{2,1,0:T(8,128)(2,1)S(1)} collective-permute-done((bf16[4,256,128]{2,1,0:T(8,128)(2,1)}, bf16[4,256,128]{2,1,0:T(8,128)(2,1)S(1)}, u32[]{:S(2)}, u32[]{:S(2)}) %collective-permute-start.14) | collective-permute-done | bytes 262176 | tf_op jit(solution)/shard_map/ppermute | solution.py:299
  (133 shorter events, 58.7 us)
Async XLA Ops:
  6.5 79.8 %all-gather.3.cloned.1.call-start = ((), (), s32[]{:S(2)}) async-start(), calls=%async_computation.3 | async-start | bytes 4730880 | tf_op jit(solution)/shard_map/all_gather | solution.py:186
  8.4 13.1 %copy-start.17 = (s32[256]{0:T(256)S(1)}, s32[256]{0:T(256)}, u32[]{:S(2)}) copy-start(s32[256]{0:T(256)} %param.19) | copy-start | bytes 3076
  8.4 24.8 %copy-start.11 = (f32[1792]{0:T(1024)S(1)}, f32[1792]{0:T(1024)}, u32[]{:S(2)}) copy-start(f32[1792]{0:T(1024)} %param.11) | copy-start | bytes 21508
  33.2 156.8 %copy-start.10 = (s32[4,1,256]{2,1,0:T(1,128)}, s32[4,1,256]{2,1,0:T(1,128)S(1)}, u32[]{:S(2)}) copy-start(s32[4,1,256]{2,1,0:T(1,128)S(1)} %all-gather) | copy-start | bytes 12292
  86.4 6.9 %collective-permute-start = (bf16[896,2112]{0,1:T(8,128)(2,1)}, bf16[896,2112]{0,1:T(8,128)(2,1)}, u32[]{:S(2)}, u32[]{:S(2)}) collective-permute-start(bf16[896,2112]{0,1:T(8,128)(2,1)} %all-gather.3.cloned.1.call-done), channel_id=1, source_target_pairs={{0,1},{1,0},{2,3},{3,2},{4,5},{5,4},{6,7},{7,6},{8,9},{9,8},{10,11... | collective-permute-start | bytes 11354120 | tf_op jit(solution)/shard_map/ppermute | solution.py:195
  86.4 44.5 %copy-start.14 = (f32[32]{0:T(128)}, f32[32]{0:T(128)S(1)}, u32[]{:S(2)}) copy-start(f32[32]{0:T(128)S(1)} %multiply_power_fusion) | copy-start | bytes 388
  100.2 15.6 %collective-permute-start.3 = (f32[64,2112]{1,0:T(8,128)S(1)}, f32[64,2112]{1,0:T(8,128)S(1)}, u32[]{:S(2)}, u32[]{:S(2)}) collective-permute-start(f32[64,2112]{1,0:T(8,128)S(1)} %get-tuple-element.24), channel_id=1, source_target_pairs={{0,6},{2,0},{4,2},{6,4},{1,7},{3,1},{5,3},{7,5},{8,14},{10,8},{12,... | collective-permute-start | bytes 1622024 | tf_op jit(solution)/shard_map/ppermute | solution.py:207
  102.7 26.3 %collective-permute-start.2 = (f32[64,2112]{1,0:T(8,128)S(1)}, f32[64,2112]{1,0:T(8,128)S(1)}, u32[]{:S(2)}, u32[]{:S(2)}) collective-permute-start(f32[64,2112]{1,0:T(8,128)S(1)} %get-tuple-element.25), channel_id=1, source_target_pairs={{0,4},{2,6},{4,0},{6,2},{1,5},{3,7},{5,1},{7,3},{8,12},{10,14},{12... | collective-permute-start | bytes 1622024 | tf_op jit(solution)/shard_map/ppermute | solution.py:207
  103.3 25.8 %collective-permute-start.1 = (f32[64,2112]{1,0:T(8,128)S(1)}, f32[64,2112]{1,0:T(8,128)S(1)}, u32[]{:S(2)}, u32[]{:S(2)}) collective-permute-start(f32[64,2112]{1,0:T(8,128)S(1)} %get-tuple-element.23), channel_id=1, source_target_pairs={{0,2},{2,4},{4,6},{6,0},{1,3},{3,5},{5,7},{7,1},{8,10},{10,12},{12... | collective-permute-start | bytes 1622024 | tf_op jit(solution)/shard_map/ppermute | solution.py:207
  131.4 8.1 %collective-permute-start.6 = (bf16[64,2112]{1,0:T(8,128)(2,1)S(1)}, bf16[64,2112]{1,0:T(8,128)(2,1)S(1)}, u32[]{:S(2)}, u32[]{:S(2)}) collective-permute-start(bf16[64,2112]{1,0:T(8,128)(2,1)S(1)} %concatenate.23), channel_id=1, source_target_pairs={{0,24},{8,0},{16,8},{24,16},{1,25},{9,1},{17,9},{25,17},{2,26},{10... | collective-permute-start | bytes 811016 | tf_op jit(solution)/shard_map/ppermute | solution.py:227
  132.3 23.0 %collective-permute-start.5 = (bf16[64,2112]{1,0:T(8,128)(2,1)S(1)}, bf16[64,2112]{1,0:T(8,128)(2,1)S(1)}, u32[]{:S(2)}, u32[]{:S(2)}) collective-permute-start(bf16[64,2112]{1,0:T(8,128)(2,1)S(1)} %concatenate.23), channel_id=1, source_target_pairs={{0,16},{8,24},{16,0},{24,8},{1,17},{9,25},{17,1},{25,9},{2,18},{10... | collective-permute-start | bytes 811016 | tf_op jit(solution)/shard_map/ppermute | solution.py:227
  132.5 22.8 %collective-permute-start.4 = (bf16[64,2112]{1,0:T(8,128)(2,1)S(1)}, bf16[64,2112]{1,0:T(8,128)(2,1)S(1)}, u32[]{:S(2)}, u32[]{:S(2)}) collective-permute-start(bf16[64,2112]{1,0:T(8,128)(2,1)S(1)} %concatenate.23), channel_id=1, source_target_pairs={{0,8},{8,16},{16,24},{24,0},{1,9},{9,17},{17,25},{25,1},{2,10},{10... | collective-permute-start | bytes 811016 | tf_op jit(solution)/shard_map/ppermute | solution.py:227
  158.5 12.9 %all-to-all-start.1 = ((bf16[128,4,256]{2,0,1:T(8,128)(2,1)}), bf16[128,4,256]{2,0,1:T(8,128)(2,1)S(1)}, u32[]{:S(2)}, u32[]{:S(2)}) async-start(bf16[128,4,256]{2,0,1:T(8,128)(2,1)} %copy.150), calls=%async_computation.1 | async-start | bytes 524288 | tf_op jit(solution)/shard_map/all_to_all | solution.py:253
  171.5 11.1 %all-to-all-start.2 = ((bf16[128,4,256]{2,0,1:T(8,128)(2,1)}), bf16[128,4,256]{2,0,1:T(8,128)(2,1)}, u32[]{:S(2)}, u32[]{:S(2)}) async-start(bf16[128,4,256]{2,0,1:T(8,128)(2,1)} %copy.156), calls=%async_computation.2 | async-start | bytes 524288 | tf_op jit(solution)/shard_map/all_to_all | solution.py:253
  182.5 61.6 %all-to-all-start = ((bf16[384,4,384]{2,0,1:T(8,128)(2,1)}), bf16[384,4,384]{2,0,1:T(8,128)(2,1)S(1)}, u32[]{:S(2)}, u32[]{:S(2)}) async-start(bf16[384,4,384]{2,0,1:T(8,128)(2,1)} %copy.143), calls=%async_computation | async-start | bytes 2359296 | tf_op jit(solution)/shard_map/all_to_all | solution.py:253
  186.1 27.6 %collective-permute-start.10 = (bf16[4,64,2112]{2,1,0:T(8,128)(2,1)S(1)}, bf16[4,64,2112]{2,1,0:T(8,128)(2,1)}, u32[]{:S(2)}, u32[]{:S(2)}) collective-permute-start(bf16[4,64,2112]{2,1,0:T(8,128)(2,1)S(1)} %copy-done), channel_id=1, source_target_pairs={{0,6},{2,0},{4,2},{6,4},{1,7},{3,1},{5,3},{7,5},{8,14},{10,8},{12,... | collective-permute-start | bytes 3244040 | tf_op jit(solution)/shard_map/ppermute | solution.py:235
  187.9 47.0 %collective-permute-start.9 = (bf16[4,64,2112]{2,1,0:T(8,128)(2,1)S(1)}, bf16[4,64,2112]{2,1,0:T(8,128)(2,1)}, u32[]{:S(2)}, u32[]{:S(2)}) collective-permute-start(bf16[4,64,2112]{2,1,0:T(8,128)(2,1)S(1)} %copy-done), channel_id=1, source_target_pairs={{0,4},{2,6},{4,0},{6,2},{1,5},{3,7},{5,1},{7,3},{8,12},{10,14},{12... | collective-permute-start | bytes 3244040 | tf_op jit(solution)/shard_map/ppermute | solution.py:235
  189.1 45.8 %collective-permute-start.8 = (bf16[4,64,2112]{2,1,0:T(8,128)(2,1)S(1)}, bf16[4,64,2112]{2,1,0:T(8,128)(2,1)}, u32[]{:S(2)}, u32[]{:S(2)}) collective-permute-start(bf16[4,64,2112]{2,1,0:T(8,128)(2,1)S(1)} %copy-done), channel_id=1, source_target_pairs={{0,2},{2,4},{4,6},{6,0},{1,3},{3,5},{5,7},{7,1},{8,10},{10,12},{12... | collective-permute-start | bytes 3244040 | tf_op jit(solution)/shard_map/ppermute | solution.py:235
  189.9 5.3 %collective-permute-start.11 = (bf16[512,256]{0,1:T(8,128)(2,1)}, bf16[512,256]{0,1:T(8,128)(2,1)}, u32[]{:S(2)}, u32[]{:S(2)}) collective-permute-start(bf16[512,256]{0,1:T(8,128)(2,1)} %copy.151), channel_id=1, source_target_pairs={{0,1},{1,0},{2,3},{3,2},{4,5},{5,4},{6,7},{7,6},{8,9},{9,8},{10,11... | collective-permute-start | bytes 786440 | tf_op jit(solution)/shard_map/ppermute | solution.py:258
  194.7 2.4 collective-permute-start.12
  244.7 7.4 %collective-permute-start.7 = (bf16[1536,384]{0,1:T(8,128)(2,1)S(1)}, bf16[1536,384]{0,1:T(8,128)(2,1)S(1)}, u32[]{:S(2)}, u32[]{:S(2)}) collective-permute-start(bf16[1536,384]{0,1:T(8,128)(2,1)S(1)} %copy.144), channel_id=1, source_target_pairs={{0,1},{1,0},{2,3},{3,2},{4,5},{5,4},{6,7},{7,6},{8,9},{9,8},{10,11... | collective-permute-start | bytes 3538952 | tf_op jit(solution)/shard_map/ppermute | solution.py:258
  263.6 19.1 %collective-permute-start.15 = (bf16[4,256,128]{2,1,0:T(8,128)(2,1)}, bf16[4,256,128]{2,1,0:T(8,128)(2,1)S(1)}, u32[]{:S(2)}, u32[]{:S(2)}) collective-permute-start(bf16[4,256,128]{2,1,0:T(8,128)(2,1)} %shard_map.103), channel_id=1, source_target_pairs={{0,24},{8,0},{16,8},{24,16},{1,25},{9,1},{17,9},{25,17},{2,26},{10... | collective-permute-start | bytes 786440 | tf_op jit(solution)/shard_map/ppermute | solution.py:299
  272.0 19.5 %collective-permute-start.14 = (bf16[4,256,128]{2,1,0:T(8,128)(2,1)}, bf16[4,256,128]{2,1,0:T(8,128)(2,1)S(1)}, u32[]{:S(2)}, u32[]{:S(2)}) collective-permute-start(bf16[4,256,128]{2,1,0:T(8,128)(2,1)} %shard_map.102), channel_id=1, source_target_pairs={{0,16},{8,24},{16,0},{24,8},{1,17},{9,25},{17,1},{25,9},{2,18},{10... | collective-permute-start | bytes 786440 | tf_op jit(solution)/shard_map/ppermute | solution.py:299
  276.8 14.7 %collective-permute-start.13 = (bf16[4,256,128]{2,1,0:T(8,128)(2,1)}, bf16[4,256,128]{2,1,0:T(8,128)(2,1)S(1)}, u32[]{:S(2)}, u32[]{:S(2)}) collective-permute-start(bf16[4,256,128]{2,1,0:T(8,128)(2,1)} %shard_map.101), channel_id=1, source_target_pairs={{0,8},{8,16},{16,24},{24,0},{1,9},{9,17},{17,25},{25,1},{2,10},{10... | collective-permute-start | bytes 786440 | tf_op jit(solution)/shard_map/ppermute | solution.py:299
  (14 other events, 52.4 us)
Sparse Core Ops, SparseCore 0:
  9.6 76.7 all-gather.2

commit v16 on v14

--- a/solution.py
+++ b/solution.py
@@ -207,6 +207,9 @@
         latent_rows = latent_rows + lax.ppermute(
             sent, "tp", perm=[(i, (i + k) % tp_count) for i in range(tp_count)]
         )
+    latent_rows, query_up, key_up, value_up = lax.optimization_barrier(
+        (latent_rows, query_up, key_up, value_up)
+    )
 
     token_index = jnp.arange(total_rows, dtype=jnp.int32)
     onehot = group_ids[:, None] == jnp.arange(DOCS, dtype=jnp.int32)[None, :]
@@ -228,9 +231,6 @@
         for k in range(1, seq_count)
     ]
     packed = jnp.take(jnp.stack(from_seq), (seq_index - jnp.arange(seq_count)) % seq_count, axis=0)
-    packed, query_up, key_up, value_up = lax.optimization_barrier(
-        (packed, query_up, key_up, value_up)
-    )
     packed = lax.all_gather(packed, "tp", axis=0, tiled=False)
     latent = jnp.transpose(packed, (1, 0, 2, 3)).reshape(total_rows, packed.shape[-1])
     cq_all = latent[:, :qrank]

time: 281 us -> 281 us (level)
  no operation moved by 1% of the time
where the time goes in v16:
time: 281 us; the launch traced here: 280 us
  waiting for transfers between devices  149 us (53%)
  local copies, waits for them, and re-layouts  24.7 us (9%)
  blocking collectives  23 us (8%)
  starting transfers between devices  20.6 us (7%)
  Pallas kernels  19.3 us (7%)
  matrix products  15.2 us (5%)
  between operations  13.9 us (5%)
  other arithmetic  13.6 us (5%)
    all_gather x1, waiting for transfers between devices, body(): own_all = lax.all_gather(own_rows, 'seq', axis=1, tiled=True)  52.8 us
    all_to_all x3, waiting for transfers between devices, head_columns(): own = lax.all_to_all(own, 'seq', split_axis=1, concat_axis=0, tiled=True)  36.7 us
    ppermute x3, waiting for transfers between devices, body(): lax.ppermute(sent, 'tp', perm=[(i, (i + k) % tp_count) for i in range(tp_...  24.9 us
    ppermute x3, waiting for transfers between devices, body(): lax.ppermute(packed, 'seq', perm=[(i, (i + k) % seq_count) for i in range...  20.8 us
    pallas_call x4, Pallas kernels, block_attention(): pl.pallas_call(kernel, grid_spec=pltpu.PrefetchScalarGridSpec(num_scalar_...  19.3 us
    all_gather x1, blocking collectives, body(): group_ids = lax.all_gather(segment_ids, 'seq', axis=0, tiled=True)  11.7 us
    psum x1, blocking collectives, body(): square_sums = lax.psum(jnp.sum(inputs * inputs, 1), 'tp')  11.4 us
    all_to_all x3, starting transfers between devices, head_columns(): own = lax.all_to_all(own, 'seq', split_axis=1, concat_axis=0, tiled=True)  11.3 us
  transfers between devices with their start and end apart: 18, of which 10 were waited for; matrix products, arithmetic and copies ran while one was open for 7% of the time, Pallas kernels for 5%

profile of v16, /device:TPU:0, one launch (start us, length us, event | category | flops | bytes accessed | tf_op | source)
XLA Modules:
  0.0 279.6 jit_solution(14887316919693023927)
XLA Ops:
  10.2 11.4 %psum.7 = f32[256]{0:T(256)S(1)} all-reduce(f32[256]{0:T(256)S(1)} %fusion.2), channel_id=1, replica_groups=mesh['seq'=4,'tp'=4,'dp'=2] {'tp'}, use_global_device_ids=true, to_apply=%region_1.0 | all-reduce | flops 256 | bytes 2048 | tf_op jit(solution)/shard_map/psum | solution.py:176
  21.6 11.7 %all-gather = s32[4,1,256]{2,1,0:T(1,128)S(1)} all-gather(s32[1,1,256]{2,1,0:T(1,128)S(1)} %bitcast.118), channel_id=1, replica_groups=mesh['seq'=4,'tp'=4,'dp'=2] {'seq'}, dimensions={0}, use_global_device_ids=true | all-gather | bytes 5120 | tf_op jit(solution)/shard_map/all_gather | solution.py:173
  33.5 52.8 %all-gather.4.cloned.1.call-done = bf16[896,2112]{0,1:T(8,128)(2,1)} async-done(((bf16[896,528]{0,1:T(8,128)(2,1)}), bf16[896,2112]{0,1:T(8,128)(2,1)}) %all-gather.4.cloned.1.call-update) | async-done | bytes 3784720 | tf_op jit(solution)/shard_map/all_gather | solution.py:186
  86.4 3.5 %fusion.11 = f32[256,2112]{0,1:T(8,128)S(1)} fusion(bf16[896,2112]{0,1:T(8,128)(2,1)} %all-gather.4.cloned.1.call-done, bf16[256,1792]{1,0:T(8,128)(2,1)S(1)} %fusion.4, s32[]{:T(128)S(6)} %select_n.182), kind=kOutput, calls=%fused_computation.41 | convolution fusion | flops 968884224 | bytes 6406148 | tf_op jit(solution)/shard_map/dot_general | solution.py:188
  89.9 3.4 %collective-permute-done = bf16[896,2112]{0,1:T(8,128)(2,1)} collective-permute-done((bf16[896,2112]{0,1:T(8,128)(2,1)}, bf16[896,2112]{0,1:T(8,128)(2,1)}, u32[]{:S(2)}, u32[]{:S(2)}) %collective-permute-start) | collective-permute-done | bytes 3784736 | tf_op jit(solution)/shard_map/ppermute | solution.py:195
  93.3 4.8 %convolution_add_fusion = f32[256,2112]{0,1:T(8,128)} fusion(f32[256,2112]{0,1:T(8,128)S(1)} %fusion.11, bf16[896,2112]{0,1:T(8,128)(2,1)} %collective-permute-done, bf16[256,1792]{1,0:T(8,128)(2,1)S(1)} %fusion.4, s32[]{:T(128)S(6)} %select_n.183), kind=kOutput, calls=%fused_computation.2 | convolution fusion | flops 969424896 | bytes 8568836 | tf_op jit(solution)/shard_map/dot_general | solution.py:198
  104.1 11.7 %collective-permute-done.3 = f32[64,2112]{1,0:T(8,128)S(1)} collective-permute-done((f32[64,2112]{1,0:T(8,128)S(1)}, f32[64,2112]{1,0:T(8,128)S(1)}, u32[]{:S(2)}, u32[]{:S(2)}) %collective-permute-start.3) | collective-permute-done | bytes 540704 | tf_op jit(solution)/shard_map/ppermute | solution.py:207
  115.8 13.2 %collective-permute-done.2 = f32[64,2112]{1,0:T(8,128)S(1)} collective-permute-done((f32[64,2112]{1,0:T(8,128)S(1)}, f32[64,2112]{1,0:T(8,128)S(1)}, u32[]{:S(2)}, u32[]{:S(2)}) %collective-permute-start.2) | collective-permute-done | bytes 540704 | tf_op jit(solution)/shard_map/ppermute | solution.py:207
  134.5 5.1 %collective-permute-done.7 = bf16[64,2112]{1,0:T(8,128)(2,1)S(1)} collective-permute-done((bf16[64,2112]{1,0:T(8,128)(2,1)S(1)}, bf16[64,2112]{1,0:T(8,128)(2,1)S(1)}, u32[]{:S(2)}, u32[]{:S(2)}) %collective-permute-start.7) | collective-permute-done | bytes 270368 | tf_op jit(solution)/shard_map/ppermute | solution.py:230
  139.5 15.7 %collective-permute-done.6 = bf16[64,2112]{1,0:T(8,128)(2,1)S(1)} collective-permute-done((bf16[64,2112]{1,0:T(8,128)(2,1)S(1)}, bf16[64,2112]{1,0:T(8,128)(2,1)S(1)}, u32[]{:S(2)}, u32[]{:S(2)}) %collective-permute-start.6) | collective-permute-done | bytes 270368 | tf_op jit(solution)/shard_map/ppermute | solution.py:230
  158.6 4.2 %all-to-all-start.2 = ((bf16[128,4,256]{2,0,1:T(8,128)(2,1)}), bf16[128,4,256]{2,0,1:T(8,128)(2,1)}, u32[]{:S(2)}, u32[]{:S(2)}) async-start(bf16[128,4,256]{2,0,1:T(8,128)(2,1)} %copy.160), calls=%async_computation.2 | async-start | bytes 524288 | tf_op jit(solution)/shard_map/all_to_all | solution.py:249
  162.8 3.2 %copy.142 = bf16[384,3072]{0,1:T(8,128)(2,1)S(1)} copy(bf16[384,3072]{1,0:T(8,128)(2,1)} %param.16) | data formatting | bytes 4718592 | tf_op jit(solution)/shard_map/optimization_barrier | solution.py:210
  167.6 4.2 %all-to-all-done.2 = bf16[128,4,256]{2,0,1:T(8,128)(2,1)} async-done(((bf16[128,4,256]{2,0,1:T(8,128)(2,1)}), bf16[128,4,256]{2,0,1:T(8,128)(2,1)}, u32[]{:S(2)}, u32[]{:S(2)}) %all-to-all-start.2) | async-done | bytes 262176 | tf_op jit(solution)/shard_map/all_to_all | solution.py:249
  171.9 3.5 %all-to-all-start = ((bf16[384,4,384]{2,0,1:T(8,128)(2,1)}), bf16[384,4,384]{2,0,1:T(8,128)(2,1)S(1)}, u32[]{:S(2)}, u32[]{:S(2)}) async-start(bf16[384,4,384]{2,0,1:T(8,128)(2,1)} %copy.143), calls=%async_computation | async-start | bytes 2359296 | tf_op jit(solution)/shard_map/all_to_all | solution.py:249
  176.6 27.3 %all-to-all-done = bf16[384,4,384]{2,0,1:T(8,128)(2,1)S(1)} async-done(((bf16[384,4,384]{2,0,1:T(8,128)(2,1)}), bf16[384,4,384]{2,0,1:T(8,128)(2,1)S(1)}, u32[]{:S(2)}, u32[]{:S(2)}) %all-to-all-start) | async-done | bytes 1179680 | tf_op jit(solution)/shard_map/all_to_all | solution.py:249
  203.9 3.6 %all-to-all-start.1 = ((bf16[128,4,256]{2,0,1:T(8,128)(2,1)}), bf16[128,4,256]{2,0,1:T(8,128)(2,1)S(1)}, u32[]{:S(2)}, u32[]{:S(2)}) async-start(bf16[128,4,256]{2,0,1:T(8,128)(2,1)} %copy.154), calls=%async_computation.1 | async-start | bytes 524288 | tf_op jit(solution)/shard_map/all_to_all | solution.py:249
  210.5 5.2 %all-to-all-done.1 = bf16[128,4,256]{2,0,1:T(8,128)(2,1)S(1)} async-done(((bf16[128,4,256]{2,0,1:T(8,128)(2,1)}), bf16[128,4,256]{2,0,1:T(8,128)(2,1)S(1)}, u32[]{:S(2)}, u32[]{:S(2)}) %all-to-all-start.1) | async-done | bytes 262176 | tf_op jit(solution)/shard_map/all_to_all | solution.py:249
  222.8 2.6 copy.151
  226.2 3.4 %fusion.1 = f32[4,1024,192]{2,1,0:T(8,128)S(1)} fusion(bf16[1536,4,192]{0,2,1:T(8,128)(2,1)S(1)} %bitcast.95, bf16[1024,2112]{1,0:T(8,128)(2,1)S(1)} %bitcast.86), kind=kOutput, calls=%fused_computation.8 | convolution fusion | flops 2415919104 | bytes 8650752 | tf_op jit(solution)/shard_map/td,dhe->hte/dot_general | solution.py:270
  236.9 4.8 %shard_map.103 = bf16[4,256,128]{2,1,0:T(8,128)(2,1)} custom-call(s32[1]{0:T(128)} %bitcast.50.block_ref, bf16[4,1024,192]{2,1,0:T(8,128)(2,1)} %pad_maximum_fusion.1.query_ref, bf16[4,1024,128]{2,1,0:T(8,128)(2,1)} %fusion.5.key_ref, bf16[1024,64]{1,0:T(8,128)(2,1)} %slice.65.rope_ref, bf16[4,1024,128]{2,1,0:T(8,128)(2,1)} %fusion.6.value_ref, ...), custom_call_target="tpu_custom_call" | custom-call | flops 335544320 | bytes 1703936 | tf_op jit(solution)/shard_map/pallas_call | solution.py:115
  243.2 4.8 %shard_map.102 = bf16[4,256,128]{2,1,0:T(8,128)(2,1)} custom-call(s32[1]{0:T(128)} %bitcast.48.block_ref, bf16[4,1024,192]{2,1,0:T(8,128)(2,1)} %pad_maximum_fusion.1.query_ref, bf16[4,1024,128]{2,1,0:T(8,128)(2,1)} %fusion.5.key_ref, bf16[1024,64]{1,0:T(8,128)(2,1)} %slice.65.rope_ref, bf16[4,1024,128]{2,1,0:T(8,128)(2,1)} %fusion.6.value_ref, ...), custom_call_target="tpu_custom_call" | custom-call | flops 335544320 | bytes 1703936 | tf_op jit(solution)/shard_map/pallas_call | solution.py:115
  248.2 4.8 %shard_map.101 = bf16[4,256,128]{2,1,0:T(8,128)(2,1)} custom-call(s32[1]{0:T(128)} %bitcast.46.block_ref, bf16[4,1024,192]{2,1,0:T(8,128)(2,1)} %pad_maximum_fusion.1.query_ref, bf16[4,1024,128]{2,1,0:T(8,128)(2,1)} %fusion.5.key_ref, bf16[1024,64]{1,0:T(8,128)(2,1)} %slice.65.rope_ref, bf16[4,1024,128]{2,1,0:T(8,128)(2,1)} %fusion.6.value_ref, ...), custom_call_target="tpu_custom_call" | custom-call | flops 335544320 | bytes 1703936 | tf_op jit(solution)/shard_map/pallas_call | solution.py:115
  253.4 4.8 %shard_map.100 = bf16[4,256,128]{2,1,0:T(8,128)(2,1)} custom-call(s32[1]{0:T(128)} %bitcast.block_ref, bf16[4,1024,192]{2,1,0:T(8,128)(2,1)} %pad_maximum_fusion.1.query_ref, bf16[4,1024,128]{2,1,0:T(8,128)(2,1)} %fusion.5.key_ref, bf16[1024,64]{1,0:T(8,128)(2,1)} %slice.65.rope_ref, bf16[4,1024,128]{2,1,0:T(8,128)(2,1)} %fusion.6.value_ref, ...), custom_call_target="tpu_custom_call" | custom-call | flops 335544320 | bytes 1703936 | tf_op jit(solution)/shard_map/pallas_call | solution.py:115
  258.2 10.5 %collective-permute-done.11 = bf16[4,256,128]{2,1,0:T(8,128)(2,1)S(1)} collective-permute-done((bf16[4,256,128]{2,1,0:T(8,128)(2,1)}, bf16[4,256,128]{2,1,0:T(8,128)(2,1)S(1)}, u32[]{:S(2)}, u32[]{:S(2)}) %collective-permute-start.11) | collective-permute-done | bytes 262176 | tf_op jit(solution)/shard_map/ppermute | solution.py:295
  (114 shorter events, 45.3 us)
Async XLA Ops:
  6.5 79.8 %all-gather.4.cloned.1.call-start = ((), (), s32[]{:S(2)}) async-start(), calls=%async_computation.3 | async-start | bytes 4730880 | tf_op jit(solution)/shard_map/all_gather | solution.py:186
  8.4 13.1 %copy-start.12 = (s32[256]{0:T(256)S(1)}, s32[256]{0:T(256)}, u32[]{:S(2)}) copy-start(s32[256]{0:T(256)} %param.19) | copy-start | bytes 3076
  8.4 24.8 %copy-start.7 = (f32[1792]{0:T(1024)S(1)}, f32[1792]{0:T(1024)}, u32[]{:S(2)}) copy-start(f32[1792]{0:T(1024)} %param.11) | copy-start | bytes 21508
  9.5 213.3 %all-gather.6.cloned.1.call-start = ((), (), s32[]{:S(2)}) async-start(), calls=%async_computation.4 | async-start | bytes 5570560 | tf_op jit(solution)/shard_map/all_gather | solution.py:234
  33.2 183.3 %copy-start.6 = (s32[4,1,256]{2,1,0:T(1,128)}, s32[4,1,256]{2,1,0:T(1,128)S(1)}, u32[]{:S(2)}) copy-start(s32[4,1,256]{2,1,0:T(1,128)S(1)} %all-gather) | copy-start | bytes 12292
  86.4 6.9 %collective-permute-start = (bf16[896,2112]{0,1:T(8,128)(2,1)}, bf16[896,2112]{0,1:T(8,128)(2,1)}, u32[]{:S(2)}, u32[]{:S(2)}) collective-permute-start(bf16[896,2112]{0,1:T(8,128)(2,1)} %all-gather.4.cloned.1.call-done), channel_id=1, source_target_pairs={{0,1},{1,0},{2,3},{3,2},{4,5},{5,4},{6,7},{7,6},{8,9},{9,8},{10,11... | collective-permute-start | bytes 11354120 | tf_op jit(solution)/shard_map/ppermute | solution.py:195
  86.4 44.4 %copy-start.10 = (f32[32]{0:T(128)}, f32[32]{0:T(128)S(1)}, u32[]{:S(2)}) copy-start(f32[32]{0:T(128)S(1)} %multiply_power_fusion) | copy-start | bytes 388
  100.2 15.5 %collective-permute-start.3 = (f32[64,2112]{1,0:T(8,128)S(1)}, f32[64,2112]{1,0:T(8,128)S(1)}, u32[]{:S(2)}, u32[]{:S(2)}) collective-permute-start(f32[64,2112]{1,0:T(8,128)S(1)} %get-tuple-element.24), channel_id=1, source_target_pairs={{0,6},{2,0},{4,2},{6,4},{1,7},{3,1},{5,3},{7,5},{8,14},{10,8},{12,... | collective-permute-start | bytes 1622024 | tf_op jit(solution)/shard_map/ppermute | solution.py:207
  102.7 26.3 %collective-permute-start.2 = (f32[64,2112]{1,0:T(8,128)S(1)}, f32[64,2112]{1,0:T(8,128)S(1)}, u32[]{:S(2)}, u32[]{:S(2)}) collective-permute-start(f32[64,2112]{1,0:T(8,128)S(1)} %get-tuple-element.25), channel_id=1, source_target_pairs={{0,4},{2,6},{4,0},{6,2},{1,5},{3,7},{5,1},{7,3},{8,12},{10,14},{12... | collective-permute-start | bytes 1622024 | tf_op jit(solution)/shard_map/ppermute | solution.py:207
  103.2 25.8 %collective-permute-start.1 = (f32[64,2112]{1,0:T(8,128)S(1)}, f32[64,2112]{1,0:T(8,128)S(1)}, u32[]{:S(2)}, u32[]{:S(2)}) collective-permute-start(f32[64,2112]{1,0:T(8,128)S(1)} %get-tuple-element.23), channel_id=1, source_target_pairs={{0,2},{2,4},{4,6},{6,0},{1,3},{3,5},{5,7},{7,1},{8,10},{10,12},{12... | collective-permute-start | bytes 1622024 | tf_op jit(solution)/shard_map/ppermute | solution.py:207
  131.4 8.1 %collective-permute-start.7 = (bf16[64,2112]{1,0:T(8,128)(2,1)S(1)}, bf16[64,2112]{1,0:T(8,128)(2,1)S(1)}, u32[]{:S(2)}, u32[]{:S(2)}) collective-permute-start(bf16[64,2112]{1,0:T(8,128)(2,1)S(1)} %concatenate.24), channel_id=1, source_target_pairs={{0,24},{8,0},{16,8},{24,16},{1,25},{9,1},{17,9},{25,17},{2,26},{10... | collective-permute-start | bytes 811016 | tf_op jit(solution)/shard_map/ppermute | solution.py:230
  132.3 23.0 %collective-permute-start.6 = (bf16[64,2112]{1,0:T(8,128)(2,1)S(1)}, bf16[64,2112]{1,0:T(8,128)(2,1)S(1)}, u32[]{:S(2)}, u32[]{:S(2)}) collective-permute-start(bf16[64,2112]{1,0:T(8,128)(2,1)S(1)} %concatenate.24), channel_id=1, source_target_pairs={{0,16},{8,24},{16,0},{24,8},{1,17},{9,25},{17,1},{25,9},{2,18},{10... | collective-permute-start | bytes 811016 | tf_op jit(solution)/shard_map/ppermute | solution.py:230
  132.5 22.8 %collective-permute-start.5 = (bf16[64,2112]{1,0:T(8,128)(2,1)S(1)}, bf16[64,2112]{1,0:T(8,128)(2,1)S(1)}, u32[]{:S(2)}, u32[]{:S(2)}) collective-permute-start(bf16[64,2112]{1,0:T(8,128)(2,1)S(1)} %concatenate.24), channel_id=1, source_target_pairs={{0,8},{8,16},{16,24},{24,0},{1,9},{9,17},{17,25},{25,1},{2,10},{10... | collective-permute-start | bytes 811016 | tf_op jit(solution)/shard_map/ppermute | solution.py:230
  158.6 13.3 %all-to-all-start.2 = ((bf16[128,4,256]{2,0,1:T(8,128)(2,1)}), bf16[128,4,256]{2,0,1:T(8,128)(2,1)}, u32[]{:S(2)}, u32[]{:S(2)}) async-start(bf16[128,4,256]{2,0,1:T(8,128)(2,1)} %copy.160), calls=%async_computation.2 | async-start | bytes 524288 | tf_op jit(solution)/shard_map/all_to_all | solution.py:249
  166.1 9.3 %copy-start.2 = (bf16[128,2048]{1,0:T(8,128)(2,1)S(1)}, bf16[128,2048]{1,0:T(8,128)(2,1)}, u32[]{:S(2)}) copy-start(bf16[128,2048]{1,0:T(8,128)(2,1)} %param.17) | copy-start | bytes 1572868
  171.9 32.0 %all-to-all-start = ((bf16[384,4,384]{2,0,1:T(8,128)(2,1)}), bf16[384,4,384]{2,0,1:T(8,128)(2,1)S(1)}, u32[]{:S(2)}, u32[]{:S(2)}) async-start(bf16[384,4,384]{2,0,1:T(8,128)(2,1)} %copy.143), calls=%async_computation | async-start | bytes 2359296 | tf_op jit(solution)/shard_map/all_to_all | solution.py:249
  203.9 11.8 %all-to-all-start.1 = ((bf16[128,4,256]{2,0,1:T(8,128)(2,1)}), bf16[128,4,256]{2,0,1:T(8,128)(2,1)S(1)}, u32[]{:S(2)}, u32[]{:S(2)}) async-start(bf16[128,4,256]{2,0,1:T(8,128)(2,1)} %copy.154), calls=%async_computation.1 | async-start | bytes 524288 | tf_op jit(solution)/shard_map/all_to_all | solution.py:249
  207.5 10.1 %copy-start.11 = (f32[32]{0:T(128)S(1)}, f32[32]{0:T(128)}, u32[]{:S(2)}) copy-start(f32[32]{0:T(128)} %copy-done.10) | copy-start | bytes 388
  208.1 14.3 %collective-permute-start.4 = (bf16[1536,384]{0,1:T(8,128)(2,1)S(1)}, bf16[1536,384]{0,1:T(8,128)(2,1)S(1)}, u32[]{:S(2)}, u32[]{:S(2)}) collective-permute-start(bf16[1536,384]{0,1:T(8,128)(2,1)S(1)} %copy.144), channel_id=1, source_target_pairs={{0,1},{1,0},{2,3},{3,2},{4,5},{5,4},{6,7},{7,6},{8,9},{9,8},{10,11... | collective-permute-start | bytes 3538952 | tf_op jit(solution)/shard_map/ppermute | solution.py:254
  210.0 9.5 %collective-permute-start.9 = (bf16[512,256]{0,1:T(8,128)(2,1)}, bf16[512,256]{0,1:T(8,128)(2,1)}, u32[]{:S(2)}, u32[]{:S(2)}) collective-permute-start(bf16[512,256]{0,1:T(8,128)(2,1)} %copy.161), channel_id=1, source_target_pairs={{0,1},{1,0},{2,3},{3,2},{4,5},{5,4},{6,7},{7,6},{8,9},{9,8},{10,11... | collective-permute-start | bytes 786440 | tf_op jit(solution)/shard_map/ppermute | solution.py:254
  216.6 2.9 %collective-permute-start.8 = (bf16[512,256]{0,1:T(8,128)(2,1)}, bf16[512,256]{0,1:T(8,128)(2,1)}, u32[]{:S(2)}, u32[]{:S(2)}) collective-permute-start(bf16[512,256]{0,1:T(8,128)(2,1)} %copy.155), channel_id=1, source_target_pairs={{0,1},{1,0},{2,3},{3,2},{4,5},{5,4},{6,7},{7,6},{8,9},{9,8},{10,11... | collective-permute-start | bytes 786440 | tf_op jit(solution)/shard_map/ppermute | solution.py:254
  241.7 16.5 %collective-permute-start.12 = (bf16[4,256,128]{2,1,0:T(8,128)(2,1)}, bf16[4,256,128]{2,1,0:T(8,128)(2,1)S(1)}, u32[]{:S(2)}, u32[]{:S(2)}) collective-permute-start(bf16[4,256,128]{2,1,0:T(8,128)(2,1)} %shard_map.103), channel_id=1, source_target_pairs={{0,24},{8,0},{16,8},{24,16},{1,25},{9,1},{17,9},{25,17},{2,26},{10... | collective-permute-start | bytes 786440 | tf_op jit(solution)/shard_map/ppermute | solution.py:295
  248.0 20.8 %collective-permute-start.11 = (bf16[4,256,128]{2,1,0:T(8,128)(2,1)}, bf16[4,256,128]{2,1,0:T(8,128)(2,1)S(1)}, u32[]{:S(2)}, u32[]{:S(2)}) collective-permute-start(bf16[4,256,128]{2,1,0:T(8,128)(2,1)} %shard_map.102), channel_id=1, source_target_pairs={{0,16},{8,24},{16,0},{24,8},{1,17},{9,25},{17,1},{25,9},{2,18},{10... | collective-permute-start | bytes 786440 | tf_op jit(solution)/shard_map/ppermute | solution.py:295
  253.0 15.7 %collective-permute-start.10 = (bf16[4,256,128]{2,1,0:T(8,128)(2,1)}, bf16[4,256,128]{2,1,0:T(8,128)(2,1)S(1)}, u32[]{:S(2)}, u32[]{:S(2)}) collective-permute-start(bf16[4,256,128]{2,1,0:T(8,128)(2,1)} %shard_map.101), channel_id=1, source_target_pairs={{0,8},{8,16},{16,24},{24,0},{1,9},{9,17},{17,25},{25,1},{2,10},{10... | collective-permute-start | bytes 786440 | tf_op jit(solution)/shard_map/ppermute | solution.py:295
  (7 other events, 11.4 us)
Sparse Core Ops, SparseCore 0:
  9.6 76.7 all-gather.3
  157.5 54.2 all-gather.5

commit v17 on v14

--- a/solution.py
+++ b/solution.py
@@ -202,10 +202,13 @@
         )
     pieces = partial.reshape(tp_count, partial.shape[0] // tp_count, partial.shape[1])
     latent_rows = lax.dynamic_index_in_dim(pieces, tp_index, 0, keepdims=False)
+    by_xor = tp_count & (tp_count - 1) == 0
     for k in range(1, tp_count):
-        sent = lax.dynamic_index_in_dim(pieces, (tp_index + k) % tp_count, 0, keepdims=False)
+        partner = [(i ^ k) if by_xor else (i + k) % tp_count for i in range(tp_count)]
+        target = (tp_index ^ k) if by_xor else (tp_index + k) % tp_count
+        sent = lax.dynamic_index_in_dim(pieces, target, 0, keepdims=False)
         latent_rows = latent_rows + lax.ppermute(
-            sent, "tp", perm=[(i, (i + k) % tp_count) for i in range(tp_count)]
+            sent, "tp", perm=[(i, partner[i]) for i in range(tp_count)]
         )
 
     token_index = jnp.arange(total_rows, dtype=jnp.int32)

time: 281 us -> 281 us (level)
  transfers between devices with their start and end apart: 18 -> 18, of which waited for: 10 -> 11; matrix products, arithmetic and copies ran while one was open for 7% -> 7% of each run, Pallas kernels for 5% -> 5%
where the time goes in v17:
time: 281 us; the launch traced here: 280 us
  waiting for transfers between devices  150 us (53%)
  local copies, waits for them, and re-layouts  24.7 us (9%)
  blocking collectives  23 us (8%)
  starting transfers between devices  20.4 us (7%)
  Pallas kernels  19.3 us (7%)
  matrix products  15.2 us (5%)
  between operations  13.9 us (5%)
  other arithmetic  13.6 us (5%)
    all_gather x1, waiting for transfers between devices, body(): own_all = lax.all_gather(own_rows, 'seq', axis=1, tiled=True)  52.8 us
    all_to_all x3, waiting for transfers between devices, head_columns(): own = lax.all_to_all(own, 'seq', split_axis=1, concat_axis=0, tiled=True)  36.8 us
    ppermute x3, waiting for transfers between devices, body(): lax.ppermute(sent, 'tp', perm=[(i, partner[i]) for i in range(tp_count)])  23.8 us
    ppermute x3, waiting for transfers between devices, body(): lax.ppermute(packed, 'seq', perm=[(i, (i + k) % seq_count) for i in range...  22.6 us
    pallas_call x4, Pallas kernels, block_attention(): pl.pallas_call(kernel, grid_spec=pltpu.PrefetchScalarGridSpec(num_scalar_...  19.3 us
    all_gather x1, blocking collectives, body(): group_ids = lax.all_gather(segment_ids, 'seq', axis=0, tiled=True)  11.7 us
    psum x1, blocking collectives, body(): square_sums = lax.psum(jnp.sum(inputs * inputs, 1), 'tp')  11.4 us
    all_to_all x3, starting transfers between devices, head_columns(): own = lax.all_to_all(own, 'seq', split_axis=1, concat_axis=0, tiled=True)  11.2 us
  transfers between devices with their start and end apart: 18, of which 11 were waited for; matrix products, arithmetic and copies ran while one was open for 7% of the time, Pallas kernels for 5%

profile of v17, /device:TPU:0, one launch (start us, length us, event | category | flops | bytes accessed | tf_op | source)
XLA Modules:
  0.0 280.2 jit_solution(8093404992782492876)
XLA Ops:
  10.2 11.4 %psum.7 = f32[256]{0:T(256)S(1)} all-reduce(f32[256]{0:T(256)S(1)} %fusion.2), channel_id=1, replica_groups=mesh['seq'=4,'tp'=4,'dp'=2] {'tp'}, use_global_device_ids=true, to_apply=%region_1.0 | all-reduce | flops 256 | bytes 2048 | tf_op jit(solution)/shard_map/psum | solution.py:176
  21.6 11.7 %all-gather.1 = s32[4,1,256]{2,1,0:T(1,128)S(1)} all-gather(s32[1,1,256]{2,1,0:T(1,128)S(1)} %bitcast.118), channel_id=1, replica_groups=mesh['seq'=4,'tp'=4,'dp'=2] {'seq'}, dimensions={0}, use_global_device_ids=true | all-gather | bytes 5120 | tf_op jit(solution)/shard_map/all_gather | solution.py:173
  33.5 52.8 %all-gather.5.cloned.1.call-done = bf16[896,2112]{0,1:T(8,128)(2,1)} async-done(((bf16[896,528]{0,1:T(8,128)(2,1)}), bf16[896,2112]{0,1:T(8,128)(2,1)}) %all-gather.5.cloned.1.call-update) | async-done | bytes 3784720 | tf_op jit(solution)/shard_map/all_gather | solution.py:186
  86.4 3.5 %fusion.11 = f32[256,2112]{0,1:T(8,128)S(1)} fusion(bf16[896,2112]{0,1:T(8,128)(2,1)} %all-gather.5.cloned.1.call-done, bf16[256,1792]{1,0:T(8,128)(2,1)S(1)} %fusion.4, s32[]{:T(128)S(6)} %select_n.163), kind=kOutput, calls=%fused_computation.41 | convolution fusion | flops 968884224 | bytes 6406148 | tf_op jit(solution)/shard_map/dot_general | solution.py:188
  89.9 3.4 %collective-permute-done = bf16[896,2112]{0,1:T(8,128)(2,1)} collective-permute-done((bf16[896,2112]{0,1:T(8,128)(2,1)}, bf16[896,2112]{0,1:T(8,128)(2,1)}, u32[]{:S(2)}, u32[]{:S(2)}) %collective-permute-start) | collective-permute-done | bytes 3784736 | tf_op jit(solution)/shard_map/ppermute | solution.py:195
  93.3 4.8 %convolution_add_fusion = f32[256,2112]{0,1:T(8,128)} fusion(f32[256,2112]{0,1:T(8,128)S(1)} %fusion.11, bf16[896,2112]{0,1:T(8,128)(2,1)} %collective-permute-done, bf16[256,1792]{1,0:T(8,128)(2,1)S(1)} %fusion.4, s32[]{:T(128)S(6)} %select_n.164), kind=kOutput, calls=%fused_computation.2 | convolution fusion | flops 969424896 | bytes 8568836 | tf_op jit(solution)/shard_map/dot_general | solution.py:198
  104.1 12.6 %collective-permute-done.3 = f32[64,2112]{1,0:T(8,128)S(1)} collective-permute-done((f32[64,2112]{1,0:T(8,128)S(1)}, f32[64,2112]{1,0:T(8,128)S(1)}, u32[]{:S(2)}, u32[]{:S(2)}) %collective-permute-start.3) | collective-permute-done | bytes 540704 | tf_op jit(solution)/shard_map/ppermute | solution.py:210
  116.7 11.1 %collective-permute-done.2 = f32[64,2112]{1,0:T(8,128)S(1)} collective-permute-done((f32[64,2112]{1,0:T(8,128)S(1)}, f32[64,2112]{1,0:T(8,128)S(1)}, u32[]{:S(2)}, u32[]{:S(2)}) %collective-permute-start.2) | collective-permute-done | bytes 540704 | tf_op jit(solution)/shard_map/ppermute | solution.py:210
  133.3 6.4 %collective-permute-done.6 = bf16[64,2112]{1,0:T(8,128)(2,1)S(1)} collective-permute-done((bf16[64,2112]{1,0:T(8,128)(2,1)S(1)}, bf16[64,2112]{1,0:T(8,128)(2,1)S(1)}, u32[]{:S(2)}, u32[]{:S(2)}) %collective-permute-start.6) | collective-permute-done | bytes 270368 | tf_op jit(solution)/shard_map/ppermute | solution.py:230
  139.7 16.3 %collective-permute-done.5 = bf16[64,2112]{1,0:T(8,128)(2,1)S(1)} collective-permute-done((bf16[64,2112]{1,0:T(8,128)(2,1)S(1)}, bf16[64,2112]{1,0:T(8,128)(2,1)S(1)}, u32[]{:S(2)}, u32[]{:S(2)}) %collective-permute-start.5) | collective-permute-done | bytes 270368 | tf_op jit(solution)/shard_map/ppermute | solution.py:230
  159.3 4.0 %all-to-all-start.2 = ((bf16[128,4,256]{2,0,1:T(8,128)(2,1)}), bf16[128,4,256]{2,0,1:T(8,128)(2,1)}, u32[]{:S(2)}, u32[]{:S(2)}) async-start(bf16[128,4,256]{2,0,1:T(8,128)(2,1)} %copy.156), calls=%async_computation.2 | async-start | bytes 524288 | tf_op jit(solution)/shard_map/all_to_all | solution.py:252
  163.3 3.2 %copy.142 = bf16[384,3072]{0,1:T(8,128)(2,1)S(1)} copy(bf16[384,3072]{1,0:T(8,128)(2,1)} %param.16) | data formatting | bytes 4718592 | tf_op jit(solution)/shard_map/optimization_barrier | solution.py:234
  168.2 4.3 %all-to-all-done.2 = bf16[128,4,256]{2,0,1:T(8,128)(2,1)} async-done(((bf16[128,4,256]{2,0,1:T(8,128)(2,1)}), bf16[128,4,256]{2,0,1:T(8,128)(2,1)}, u32[]{:S(2)}, u32[]{:S(2)}) %all-to-all-start.2) | async-done | bytes 262176 | tf_op jit(solution)/shard_map/all_to_all | solution.py:252
  172.5 3.5 %all-to-all-start = ((bf16[384,4,384]{2,0,1:T(8,128)(2,1)}), bf16[384,4,384]{2,0,1:T(8,128)(2,1)S(1)}, u32[]{:S(2)}, u32[]{:S(2)}) async-start(bf16[384,4,384]{2,0,1:T(8,128)(2,1)} %copy.143), calls=%async_computation | async-start | bytes 2359296 | tf_op jit(solution)/shard_map/all_to_all | solution.py:252
  177.2 27.3 %all-to-all-done = bf16[384,4,384]{2,0,1:T(8,128)(2,1)S(1)} async-done(((bf16[384,4,384]{2,0,1:T(8,128)(2,1)}), bf16[384,4,384]{2,0,1:T(8,128)(2,1)S(1)}, u32[]{:S(2)}, u32[]{:S(2)}) %all-to-all-start) | async-done | bytes 1179680 | tf_op jit(solution)/shard_map/all_to_all | solution.py:252
  204.4 3.6 %all-to-all-start.1 = ((bf16[128,4,256]{2,0,1:T(8,128)(2,1)}), bf16[128,4,256]{2,0,1:T(8,128)(2,1)S(1)}, u32[]{:S(2)}, u32[]{:S(2)}) async-start(bf16[128,4,256]{2,0,1:T(8,128)(2,1)} %copy.150), calls=%async_computation.1 | async-start | bytes 524288 | tf_op jit(solution)/shard_map/all_to_all | solution.py:252
  211.1 5.2 %all-to-all-done.1 = bf16[128,4,256]{2,0,1:T(8,128)(2,1)S(1)} async-done(((bf16[128,4,256]{2,0,1:T(8,128)(2,1)}), bf16[128,4,256]{2,0,1:T(8,128)(2,1)S(1)}, u32[]{:S(2)}, u32[]{:S(2)}) %all-to-all-start.1) | async-done | bytes 262176 | tf_op jit(solution)/shard_map/all_to_all | solution.py:252
  223.4 2.6 copy.147
  226.8 3.4 %fusion.1 = f32[4,1024,192]{2,1,0:T(8,128)S(1)} fusion(bf16[1536,4,192]{0,2,1:T(8,128)(2,1)S(1)} %bitcast.95, bf16[1024,2112]{1,0:T(8,128)(2,1)S(1)} %bitcast.86), kind=kOutput, calls=%fused_computation.8 | convolution fusion | flops 2415919104 | bytes 8650752 | tf_op jit(solution)/shard_map/td,dhe->hte/dot_general | solution.py:273
  237.4 4.8 %shard_map.103 = bf16[4,256,128]{2,1,0:T(8,128)(2,1)} custom-call(s32[1]{0:T(128)} %bitcast.50.block_ref, bf16[4,1024,192]{2,1,0:T(8,128)(2,1)} %pad_maximum_fusion.1.query_ref, bf16[4,1024,128]{2,1,0:T(8,128)(2,1)} %fusion.5.key_ref, bf16[1024,64]{1,0:T(8,128)(2,1)} %slice.65.rope_ref, bf16[4,1024,128]{2,1,0:T(8,128)(2,1)} %fusion.6.value_ref, ...), custom_call_target="tpu_custom_call" | custom-call | flops 335544320 | bytes 1703936 | tf_op jit(solution)/shard_map/pallas_call | solution.py:115
  243.7 4.8 %shard_map.102 = bf16[4,256,128]{2,1,0:T(8,128)(2,1)} custom-call(s32[1]{0:T(128)} %bitcast.48.block_ref, bf16[4,1024,192]{2,1,0:T(8,128)(2,1)} %pad_maximum_fusion.1.query_ref, bf16[4,1024,128]{2,1,0:T(8,128)(2,1)} %fusion.5.key_ref, bf16[1024,64]{1,0:T(8,128)(2,1)} %slice.65.rope_ref, bf16[4,1024,128]{2,1,0:T(8,128)(2,1)} %fusion.6.value_ref, ...), custom_call_target="tpu_custom_call" | custom-call | flops 335544320 | bytes 1703936 | tf_op jit(solution)/shard_map/pallas_call | solution.py:115
  248.8 4.8 %shard_map.101 = bf16[4,256,128]{2,1,0:T(8,128)(2,1)} custom-call(s32[1]{0:T(128)} %bitcast.46.block_ref, bf16[4,1024,192]{2,1,0:T(8,128)(2,1)} %pad_maximum_fusion.1.query_ref, bf16[4,1024,128]{2,1,0:T(8,128)(2,1)} %fusion.5.key_ref, bf16[1024,64]{1,0:T(8,128)(2,1)} %slice.65.rope_ref, bf16[4,1024,128]{2,1,0:T(8,128)(2,1)} %fusion.6.value_ref, ...), custom_call_target="tpu_custom_call" | custom-call | flops 335544320 | bytes 1703936 | tf_op jit(solution)/shard_map/pallas_call | solution.py:115
  254.0 4.8 %shard_map.100 = bf16[4,256,128]{2,1,0:T(8,128)(2,1)} custom-call(s32[1]{0:T(128)} %bitcast.block_ref, bf16[4,1024,192]{2,1,0:T(8,128)(2,1)} %pad_maximum_fusion.1.query_ref, bf16[4,1024,128]{2,1,0:T(8,128)(2,1)} %fusion.5.key_ref, bf16[1024,64]{1,0:T(8,128)(2,1)} %slice.65.rope_ref, bf16[4,1024,128]{2,1,0:T(8,128)(2,1)} %fusion.6.value_ref, ...), custom_call_target="tpu_custom_call" | custom-call | flops 335544320 | bytes 1703936 | tf_op jit(solution)/shard_map/pallas_call | solution.py:115
  258.8 10.5 %collective-permute-done.11 = bf16[4,256,128]{2,1,0:T(8,128)(2,1)S(1)} collective-permute-done((bf16[4,256,128]{2,1,0:T(8,128)(2,1)}, bf16[4,256,128]{2,1,0:T(8,128)(2,1)S(1)}, u32[]{:S(2)}, u32[]{:S(2)}) %collective-permute-start.11) | collective-permute-done | bytes 262176 | tf_op jit(solution)/shard_map/ppermute | solution.py:298
  (114 shorter events, 45.4 us)
Async XLA Ops:
  6.5 79.8 %all-gather.5.cloned.1.call-start = ((), (), s32[]{:S(2)}) async-start(), calls=%async_computation.3 | async-start | bytes 4730880 | tf_op jit(solution)/shard_map/all_gather | solution.py:186
  8.4 13.1 %copy-start.12 = (s32[256]{0:T(256)S(1)}, s32[256]{0:T(256)}, u32[]{:S(2)}) copy-start(s32[256]{0:T(256)} %param.19) | copy-start | bytes 3076
  8.4 24.8 %copy-start.7 = (f32[1792]{0:T(1024)S(1)}, f32[1792]{0:T(1024)}, u32[]{:S(2)}) copy-start(f32[1792]{0:T(1024)} %param.11) | copy-start | bytes 21508
  9.5 213.9 %all-gather.7.cloned.1.call-start = ((), (), s32[]{:S(2)}) async-start(), calls=%async_computation.4 | async-start | bytes 5570560 | tf_op jit(solution)/shard_map/all_gather | solution.py:237
  33.2 183.9 %copy-start.6 = (s32[4,1,256]{2,1,0:T(1,128)}, s32[4,1,256]{2,1,0:T(1,128)S(1)}, u32[]{:S(2)}) copy-start(s32[4,1,256]{2,1,0:T(1,128)S(1)} %all-gather.1) | copy-start | bytes 12292
  86.4 6.9 %collective-permute-start = (bf16[896,2112]{0,1:T(8,128)(2,1)}, bf16[896,2112]{0,1:T(8,128)(2,1)}, u32[]{:S(2)}, u32[]{:S(2)}) collective-permute-start(bf16[896,2112]{0,1:T(8,128)(2,1)} %all-gather.5.cloned.1.call-done), channel_id=1, source_target_pairs={{0,1},{1,0},{2,3},{3,2},{4,5},{5,4},{6,7},{7,6},{8,9},{9,8},{10,11... | collective-permute-start | bytes 11354120 | tf_op jit(solution)/shard_map/ppermute | solution.py:195
  86.4 43.3 %copy-start.10 = (f32[32]{0:T(128)}, f32[32]{0:T(128)S(1)}, u32[]{:S(2)}) copy-start(f32[32]{0:T(128)S(1)} %multiply_power_fusion) | copy-start | bytes 388
  100.2 16.5 %collective-permute-start.3 = (f32[64,2112]{1,0:T(8,128)S(1)}, f32[64,2112]{1,0:T(8,128)S(1)}, u32[]{:S(2)}, u32[]{:S(2)}) collective-permute-start(f32[64,2112]{1,0:T(8,128)S(1)} %get-tuple-element.24), channel_id=1, source_target_pairs={{0,6},{2,4},{4,2},{6,0},{1,7},{3,5},{5,3},{7,1},{8,14},{10,12},{12... | collective-permute-start | bytes 1622024 | tf_op jit(solution)/shard_map/ppermute | solution.py:210
  102.7 25.1 %collective-permute-start.2 = (f32[64,2112]{1,0:T(8,128)S(1)}, f32[64,2112]{1,0:T(8,128)S(1)}, u32[]{:S(2)}, u32[]{:S(2)}) collective-permute-start(f32[64,2112]{1,0:T(8,128)S(1)} %get-tuple-element.25), channel_id=1, source_target_pairs={{0,4},{2,6},{4,0},{6,2},{1,5},{3,7},{5,1},{7,3},{8,12},{10,14},{12... | collective-permute-start | bytes 1622024 | tf_op jit(solution)/shard_map/ppermute | solution.py:210
  103.2 24.6 %collective-permute-start.1 = (f32[64,2112]{1,0:T(8,128)S(1)}, f32[64,2112]{1,0:T(8,128)S(1)}, u32[]{:S(2)}, u32[]{:S(2)}) collective-permute-start(f32[64,2112]{1,0:T(8,128)S(1)} %get-tuple-element.23), channel_id=1, source_target_pairs={{0,2},{2,0},{4,6},{6,4},{1,3},{3,1},{5,7},{7,5},{8,10},{10,8},{12,... | collective-permute-start | bytes 1622024 | tf_op jit(solution)/shard_map/ppermute | solution.py:210
  130.2 9.5 %collective-permute-start.6 = (bf16[64,2112]{1,0:T(8,128)(2,1)S(1)}, bf16[64,2112]{1,0:T(8,128)(2,1)S(1)}, u32[]{:S(2)}, u32[]{:S(2)}) collective-permute-start(bf16[64,2112]{1,0:T(8,128)(2,1)S(1)} %concatenate.23), channel_id=1, source_target_pairs={{0,24},{8,0},{16,8},{24,16},{1,25},{9,1},{17,9},{25,17},{2,26},{10... | collective-permute-start | bytes 811016 | tf_op jit(solution)/shard_map/ppermute | solution.py:230
  131.1 24.8 %collective-permute-start.5 = (bf16[64,2112]{1,0:T(8,128)(2,1)S(1)}, bf16[64,2112]{1,0:T(8,128)(2,1)S(1)}, u32[]{:S(2)}, u32[]{:S(2)}) collective-permute-start(bf16[64,2112]{1,0:T(8,128)(2,1)S(1)} %concatenate.23), channel_id=1, source_target_pairs={{0,16},{8,24},{16,0},{24,8},{1,17},{9,25},{17,1},{25,9},{2,18},{10... | collective-permute-start | bytes 811016 | tf_op jit(solution)/shard_map/ppermute | solution.py:230
  131.3 24.6 %collective-permute-start.4 = (bf16[64,2112]{1,0:T(8,128)(2,1)S(1)}, bf16[64,2112]{1,0:T(8,128)(2,1)S(1)}, u32[]{:S(2)}, u32[]{:S(2)}) collective-permute-start(bf16[64,2112]{1,0:T(8,128)(2,1)S(1)} %concatenate.23), channel_id=1, source_target_pairs={{0,8},{8,16},{16,24},{24,0},{1,9},{9,17},{17,25},{25,1},{2,10},{10... | collective-permute-start | bytes 811016 | tf_op jit(solution)/shard_map/ppermute | solution.py:230
  159.3 13.2 %all-to-all-start.2 = ((bf16[128,4,256]{2,0,1:T(8,128)(2,1)}), bf16[128,4,256]{2,0,1:T(8,128)(2,1)}, u32[]{:S(2)}, u32[]{:S(2)}) async-start(bf16[128,4,256]{2,0,1:T(8,128)(2,1)} %copy.156), calls=%async_computation.2 | async-start | bytes 524288 | tf_op jit(solution)/shard_map/all_to_all | solution.py:252
  166.6 9.4 %copy-start.2 = (bf16[128,2048]{1,0:T(8,128)(2,1)S(1)}, bf16[128,2048]{1,0:T(8,128)(2,1)}, u32[]{:S(2)}) copy-start(bf16[128,2048]{1,0:T(8,128)(2,1)} %param.17) | copy-start | bytes 1572868
  172.5 32.0 %all-to-all-start = ((bf16[384,4,384]{2,0,1:T(8,128)(2,1)}), bf16[384,4,384]{2,0,1:T(8,128)(2,1)S(1)}, u32[]{:S(2)}, u32[]{:S(2)}) async-start(bf16[384,4,384]{2,0,1:T(8,128)(2,1)} %copy.143), calls=%async_computation | async-start | bytes 2359296 | tf_op jit(solution)/shard_map/all_to_all | solution.py:252
  204.4 11.8 %all-to-all-start.1 = ((bf16[128,4,256]{2,0,1:T(8,128)(2,1)}), bf16[128,4,256]{2,0,1:T(8,128)(2,1)S(1)}, u32[]{:S(2)}, u32[]{:S(2)}) async-start(bf16[128,4,256]{2,0,1:T(8,128)(2,1)} %copy.150), calls=%async_computation.1 | async-start | bytes 524288 | tf_op jit(solution)/shard_map/all_to_all | solution.py:252
  208.0 10.1 %copy-start.11 = (f32[32]{0:T(128)S(1)}, f32[32]{0:T(128)}, u32[]{:S(2)}) copy-start(f32[32]{0:T(128)} %copy-done.10) | copy-start | bytes 388
  208.7 14.3 %collective-permute-start.7 = (bf16[1536,384]{0,1:T(8,128)(2,1)S(1)}, bf16[1536,384]{0,1:T(8,128)(2,1)S(1)}, u32[]{:S(2)}, u32[]{:S(2)}) collective-permute-start(bf16[1536,384]{0,1:T(8,128)(2,1)S(1)} %copy.144), channel_id=1, source_target_pairs={{0,1},{1,0},{2,3},{3,2},{4,5},{5,4},{6,7},{7,6},{8,9},{9,8},{10,11... | collective-permute-start | bytes 3538952 | tf_op jit(solution)/shard_map/ppermute | solution.py:257
  210.6 9.5 %collective-permute-start.9 = (bf16[512,256]{0,1:T(8,128)(2,1)}, bf16[512,256]{0,1:T(8,128)(2,1)}, u32[]{:S(2)}, u32[]{:S(2)}) collective-permute-start(bf16[512,256]{0,1:T(8,128)(2,1)} %copy.157), channel_id=1, source_target_pairs={{0,1},{1,0},{2,3},{3,2},{4,5},{5,4},{6,7},{7,6},{8,9},{9,8},{10,11... | collective-permute-start | bytes 786440 | tf_op jit(solution)/shard_map/ppermute | solution.py:257
  217.1 2.9 %collective-permute-start.8 = (bf16[512,256]{0,1:T(8,128)(2,1)}, bf16[512,256]{0,1:T(8,128)(2,1)}, u32[]{:S(2)}, u32[]{:S(2)}) collective-permute-start(bf16[512,256]{0,1:T(8,128)(2,1)} %copy.151), channel_id=1, source_target_pairs={{0,1},{1,0},{2,3},{3,2},{4,5},{5,4},{6,7},{7,6},{8,9},{9,8},{10,11... | collective-permute-start | bytes 786440 | tf_op jit(solution)/shard_map/ppermute | solution.py:257
  242.3 16.5 %collective-permute-start.12 = (bf16[4,256,128]{2,1,0:T(8,128)(2,1)}, bf16[4,256,128]{2,1,0:T(8,128)(2,1)S(1)}, u32[]{:S(2)}, u32[]{:S(2)}) collective-permute-start(bf16[4,256,128]{2,1,0:T(8,128)(2,1)} %shard_map.103), channel_id=1, source_target_pairs={{0,24},{8,0},{16,8},{24,16},{1,25},{9,1},{17,9},{25,17},{2,26},{10... | collective-permute-start | bytes 786440 | tf_op jit(solution)/shard_map/ppermute | solution.py:298
  248.6 20.8 %collective-permute-start.11 = (bf16[4,256,128]{2,1,0:T(8,128)(2,1)}, bf16[4,256,128]{2,1,0:T(8,128)(2,1)S(1)}, u32[]{:S(2)}, u32[]{:S(2)}) collective-permute-start(bf16[4,256,128]{2,1,0:T(8,128)(2,1)} %shard_map.102), channel_id=1, source_target_pairs={{0,16},{8,24},{16,0},{24,8},{1,17},{9,25},{17,1},{25,9},{2,18},{10... | collective-permute-start | bytes 786440 | tf_op jit(solution)/shard_map/ppermute | solution.py:298
  253.6 15.8 %collective-permute-start.10 = (bf16[4,256,128]{2,1,0:T(8,128)(2,1)}, bf16[4,256,128]{2,1,0:T(8,128)(2,1)S(1)}, u32[]{:S(2)}, u32[]{:S(2)}) collective-permute-start(bf16[4,256,128]{2,1,0:T(8,128)(2,1)} %shard_map.101), channel_id=1, source_target_pairs={{0,8},{8,16},{16,24},{24,0},{1,9},{9,17},{17,25},{25,1},{2,10},{10... | collective-permute-start | bytes 786440 | tf_op jit(solution)/shard_map/ppermute | solution.py:298
  (7 other events, 11.4 us)
Sparse Core Ops, SparseCore 0:
  9.6 76.7 all-gather.4
  158.2 53.9 all-gather.6

commit v18 on v14

--- a/solution.py
+++ b/solution.py
@@ -88,21 +88,22 @@
         )
         bias_ref[...] = jnp.where(allowed, 0.0, -jnp.inf).astype(jnp.float32)
 
-    query = query_ref[0]
-    keys = key_ref[0, pl.ds(start, window), :]
     rope = rope_ref[pl.ds(start, window), :]
-    values = value_ref[0, pl.ds(start, window), :]
     dims = (((1,), (1,)), ((), ()))
-    scores = lax.dot_general(query[:, :NOPE], keys, dims, preferred_element_type=jnp.float32)
-    scores = scores + lax.dot_general(
-        query[:, NOPE:], rope, dims, preferred_element_type=jnp.float32
-    )
-    scores = scores * scale + bias_ref[...]
-    row_max = jnp.max(scores, -1, keepdims=True)
-    probs = jnp.exp(scores - row_max)
-    denominator = jnp.sum(probs, -1, keepdims=True)
-    weighted = jnp.dot(probs.astype(jnp.bfloat16), values, preferred_element_type=jnp.float32)
-    out_ref[0] = (weighted / denominator).astype(out_ref.dtype)
+    for head in range(query_ref.shape[0]):
+        query = query_ref[head]
+        keys = key_ref[head, pl.ds(start, window), :]
+        values = value_ref[head, pl.ds(start, window), :]
+        scores = lax.dot_general(query[:, :NOPE], keys, dims, preferred_element_type=jnp.float32)
+        scores = scores + lax.dot_general(
+            query[:, NOPE:], rope, dims, preferred_element_type=jnp.float32
+        )
+        scores = scores * scale + bias_ref[...]
+        row_max = jnp.max(scores, -1, keepdims=True)
+        probs = jnp.exp(scores - row_max)
+        denominator = jnp.sum(probs, -1, keepdims=True)
+        weighted = jnp.dot(probs.astype(jnp.bfloat16), values, preferred_element_type=jnp.float32)
+        out_ref[head] = (weighted / denominator).astype(out_ref.dtype)
 
 
 def block_attention(query, key_nope, key_rope, value, group_ids, score_scale, doc_most, block, index):
@@ -112,20 +113,21 @@
         attention_kernel, block=block, window=window, doc_most=doc_most, scale=score_scale
     )
     flops = 2 * heads * block * window * (NOPE + ROPE + VDIM)
+    step = 2 if heads % 2 == 0 else 1
     return pl.pallas_call(
         kernel,
         grid_spec=pltpu.PrefetchScalarGridSpec(
             num_scalar_prefetch=1,
-            grid=(heads,),
+            grid=(heads // step,),
             in_specs=[
-                pl.BlockSpec((1, block, NOPE + ROPE), lambda h, b: (h, b[0], 0)),
-                pl.BlockSpec((1, total_rows, NOPE), lambda h, b: (h, 0, 0)),
+                pl.BlockSpec((step, block, NOPE + ROPE), lambda h, b: (h, b[0], 0)),
+                pl.BlockSpec((step, total_rows, NOPE), lambda h, b: (h, 0, 0)),
                 pl.BlockSpec((total_rows, ROPE), lambda h, b: (0, 0)),
-                pl.BlockSpec((1, total_rows, VDIM), lambda h, b: (h, 0, 0)),
+                pl.BlockSpec((step, total_rows, VDIM), lambda h, b: (h, 0, 0)),
                 pl.BlockSpec((block, 1), lambda h, b: (b[0], 0)),
                 pl.BlockSpec((1, total_rows), lambda h, b: (0, 0)),
             ],
-            out_specs=pl.BlockSpec((1, block, VDIM), lambda h, b: (h, 0, 0)),
+            out_specs=pl.BlockSpec((step, block, VDIM), lambda h, b: (h, 0, 0)),
             scratch_shapes=[pltpu.VMEM((block, window), jnp.float32)],
         ),
         out_shape=jax.ShapeDtypeStruct((heads, block, VDIM), jnp.bfloat16),

time: 281 us -> 279 us (level)
  Pallas kernels: 19.3 us -> 16.1 us
    pallas_call x4, Pallas kernels: 19.3 us -> 16.1 us  [block_attention(): pl.pallas_call(kernel, grid_spec=pltpu.PrefetchScalarGridSpec(num_scalar_...]
  transfers between devices with their start and end apart: 18 -> 18, of which waited for: 10 -> 10; matrix products, arithmetic and copies ran while one was open for 7% -> 8% of each run, Pallas kernels for 5% -> 4%
where the time goes in v18:
time: 279 us; the launch traced here: 278 us
  waiting for transfers between devices  151 us (54%)
  local copies, waits for them, and re-layouts  24.7 us (9%)
  blocking collectives  23 us (8%)
  starting transfers between devices  20.7 us (7%)
  Pallas kernels  16.1 us (6%)
  matrix products  15.2 us (5%)
  between operations  13.9 us (5%)
  other arithmetic  13.6 us (5%)
    all_gather x1, waiting for transfers between devices, body(): own_all = lax.all_gather(own_rows, 'seq', axis=1, tiled=True)  52.8 us
    all_to_all x3, waiting for transfers between devices, head_columns(): own = lax.all_to_all(own, 'seq', split_axis=1, concat_axis=0, tiled=True)  36.7 us
    ppermute x3, waiting for transfers between devices, body(): lax.ppermute(sent, 'tp', perm=[(i, (i + k) % tp_count) for i in range(tp_...  24.9 us
    ppermute x3, waiting for transfers between devices, body(): lax.ppermute(packed, 'seq', perm=[(i, (i + k) % seq_count) for i in range...  20.8 us
    pallas_call x4, Pallas kernels, block_attention(): pl.pallas_call(kernel, grid_spec=pltpu.PrefetchScalarGridSpec(num_scalar_...  16.1 us
    ppermute x3, waiting for transfers between devices, body(): lax.ppermute(rows, 'seq', perm=[(i, (i + k) % seq_count) for i in range(s...  12.2 us
    all_gather x1, blocking collectives, body(): group_ids = lax.all_gather(segment_ids, 'seq', axis=0, tiled=True)  11.7 us
    psum x1, blocking collectives, body(): square_sums = lax.psum(jnp.sum(inputs * inputs, 1), 'tp')  11.4 us
  transfers between devices with their start and end apart: 18, of which 10 were waited for; matrix products, arithmetic and copies ran while one was open for 8% of the time, Pallas kernels for 4%

profile of v18, /device:TPU:0, one launch (start us, length us, event | category | flops | bytes accessed | tf_op | source)
XLA Modules:
  0.0 278.0 jit_solution(696334796453766912)
XLA Ops:
  10.2 11.4 %psum.7 = f32[256]{0:T(256)S(1)} all-reduce(f32[256]{0:T(256)S(1)} %fusion.2), channel_id=1, replica_groups=mesh['seq'=4,'tp'=4,'dp'=2] {'tp'}, use_global_device_ids=true, to_apply=%region_1.0 | all-reduce | flops 256 | bytes 2048 | tf_op jit(solution)/shard_map/psum | solution.py:178
  21.6 11.7 %all-gather.1 = s32[4,1,256]{2,1,0:T(1,128)S(1)} all-gather(s32[1,1,256]{2,1,0:T(1,128)S(1)} %bitcast.118), channel_id=1, replica_groups=mesh['seq'=4,'tp'=4,'dp'=2] {'seq'}, dimensions={0}, use_global_device_ids=true | all-gather | bytes 5120 | tf_op jit(solution)/shard_map/all_gather | solution.py:175
  33.5 52.8 %all-gather.5.cloned.1.call-done = bf16[896,2112]{0,1:T(8,128)(2,1)} async-done(((bf16[896,528]{0,1:T(8,128)(2,1)}), bf16[896,2112]{0,1:T(8,128)(2,1)}) %all-gather.5.cloned.1.call-update) | async-done | bytes 3784720 | tf_op jit(solution)/shard_map/all_gather | solution.py:188
  86.4 3.5 %fusion.11 = f32[256,2112]{0,1:T(8,128)S(1)} fusion(bf16[896,2112]{0,1:T(8,128)(2,1)} %all-gather.5.cloned.1.call-done, bf16[256,1792]{1,0:T(8,128)(2,1)S(1)} %fusion.4, s32[]{:T(128)S(6)} %select_n.175), kind=kOutput, calls=%fused_computation.41 | convolution fusion | flops 968884224 | bytes 6406148 | tf_op jit(solution)/shard_map/dot_general | solution.py:190
  89.9 3.4 %collective-permute-done = bf16[896,2112]{0,1:T(8,128)(2,1)} collective-permute-done((bf16[896,2112]{0,1:T(8,128)(2,1)}, bf16[896,2112]{0,1:T(8,128)(2,1)}, u32[]{:S(2)}, u32[]{:S(2)}) %collective-permute-start) | collective-permute-done | bytes 3784736 | tf_op jit(solution)/shard_map/ppermute | solution.py:197
  93.3 4.8 %convolution_add_fusion = f32[256,2112]{0,1:T(8,128)} fusion(f32[256,2112]{0,1:T(8,128)S(1)} %fusion.11, bf16[896,2112]{0,1:T(8,128)(2,1)} %collective-permute-done, bf16[256,1792]{1,0:T(8,128)(2,1)S(1)} %fusion.4, s32[]{:T(128)S(6)} %select_n.176), kind=kOutput, calls=%fused_computation.2 | convolution fusion | flops 969424896 | bytes 8568836 | tf_op jit(solution)/shard_map/dot_general | solution.py:200
  104.1 11.7 %collective-permute-done.3 = f32[64,2112]{1,0:T(8,128)S(1)} collective-permute-done((f32[64,2112]{1,0:T(8,128)S(1)}, f32[64,2112]{1,0:T(8,128)S(1)}, u32[]{:S(2)}, u32[]{:S(2)}) %collective-permute-start.3) | collective-permute-done | bytes 540704 | tf_op jit(solution)/shard_map/ppermute | solution.py:209
  115.8 13.2 %collective-permute-done.2 = f32[64,2112]{1,0:T(8,128)S(1)} collective-permute-done((f32[64,2112]{1,0:T(8,128)S(1)}, f32[64,2112]{1,0:T(8,128)S(1)}, u32[]{:S(2)}, u32[]{:S(2)}) %collective-permute-start.2) | collective-permute-done | bytes 540704 | tf_op jit(solution)/shard_map/ppermute | solution.py:209
  134.5 5.1 %collective-permute-done.6 = bf16[64,2112]{1,0:T(8,128)(2,1)S(1)} collective-permute-done((bf16[64,2112]{1,0:T(8,128)(2,1)S(1)}, bf16[64,2112]{1,0:T(8,128)(2,1)S(1)}, u32[]{:S(2)}, u32[]{:S(2)}) %collective-permute-start.6) | collective-permute-done | bytes 270368 | tf_op jit(solution)/shard_map/ppermute | solution.py:229
  139.5 15.7 %collective-permute-done.5 = bf16[64,2112]{1,0:T(8,128)(2,1)S(1)} collective-permute-done((bf16[64,2112]{1,0:T(8,128)(2,1)S(1)}, bf16[64,2112]{1,0:T(8,128)(2,1)S(1)}, u32[]{:S(2)}, u32[]{:S(2)}) %collective-permute-start.5) | collective-permute-done | bytes 270368 | tf_op jit(solution)/shard_map/ppermute | solution.py:229
  158.6 4.2 %all-to-all-start.2 = ((bf16[128,4,256]{2,0,1:T(8,128)(2,1)}), bf16[128,4,256]{2,0,1:T(8,128)(2,1)}, u32[]{:S(2)}, u32[]{:S(2)}) async-start(bf16[128,4,256]{2,0,1:T(8,128)(2,1)} %copy.156), calls=%async_computation.2 | async-start | bytes 524288 | tf_op jit(solution)/shard_map/all_to_all | solution.py:251
  162.8 3.2 %copy.142 = bf16[384,3072]{0,1:T(8,128)(2,1)S(1)} copy(bf16[384,3072]{1,0:T(8,128)(2,1)} %param.16) | data formatting | bytes 4718592 | tf_op jit(solution)/shard_map/optimization_barrier | solution.py:233
  167.6 4.2 %all-to-all-done.2 = bf16[128,4,256]{2,0,1:T(8,128)(2,1)} async-done(((bf16[128,4,256]{2,0,1:T(8,128)(2,1)}), bf16[128,4,256]{2,0,1:T(8,128)(2,1)}, u32[]{:S(2)}, u32[]{:S(2)}) %all-to-all-start.2) | async-done | bytes 262176 | tf_op jit(solution)/shard_map/all_to_all | solution.py:251
  171.9 3.5 %all-to-all-start = ((bf16[384,4,384]{2,0,1:T(8,128)(2,1)}), bf16[384,4,384]{2,0,1:T(8,128)(2,1)S(1)}, u32[]{:S(2)}, u32[]{:S(2)}) async-start(bf16[384,4,384]{2,0,1:T(8,128)(2,1)} %copy.143), calls=%async_computation | async-start | bytes 2359296 | tf_op jit(solution)/shard_map/all_to_all | solution.py:251
  176.6 27.3 %all-to-all-done = bf16[384,4,384]{2,0,1:T(8,128)(2,1)S(1)} async-done(((bf16[384,4,384]{2,0,1:T(8,128)(2,1)}), bf16[384,4,384]{2,0,1:T(8,128)(2,1)S(1)}, u32[]{:S(2)}, u32[]{:S(2)}) %all-to-all-start) | async-done | bytes 1179680 | tf_op jit(solution)/shard_map/all_to_all | solution.py:251
  203.9 3.6 %all-to-all-start.1 = ((bf16[128,4,256]{2,0,1:T(8,128)(2,1)}), bf16[128,4,256]{2,0,1:T(8,128)(2,1)S(1)}, u32[]{:S(2)}, u32[]{:S(2)}) async-start(bf16[128,4,256]{2,0,1:T(8,128)(2,1)} %copy.150), calls=%async_computation.1 | async-start | bytes 524288 | tf_op jit(solution)/shard_map/all_to_all | solution.py:251
  210.5 5.2 %all-to-all-done.1 = bf16[128,4,256]{2,0,1:T(8,128)(2,1)S(1)} async-done(((bf16[128,4,256]{2,0,1:T(8,128)(2,1)}), bf16[128,4,256]{2,0,1:T(8,128)(2,1)S(1)}, u32[]{:S(2)}, u32[]{:S(2)}) %all-to-all-start.1) | async-done | bytes 262176 | tf_op jit(solution)/shard_map/all_to_all | solution.py:251
  222.8 2.6 copy.147
  226.2 3.4 %fusion.1 = f32[4,1024,192]{2,1,0:T(8,128)S(1)} fusion(bf16[1536,4,192]{0,2,1:T(8,128)(2,1)S(1)} %bitcast.95, bf16[1024,2112]{1,0:T(8,128)(2,1)S(1)} %bitcast.86), kind=kOutput, calls=%fused_computation.8 | convolution fusion | flops 2415919104 | bytes 8650752 | tf_op jit(solution)/shard_map/td,dhe->hte/dot_general | solution.py:272
  236.9 4.0 %shard_map.103 = bf16[4,256,128]{2,1,0:T(8,128)(2,1)} custom-call(s32[1]{0:T(128)} %bitcast.50.block_ref, bf16[4,1024,192]{2,1,0:T(8,128)(2,1)} %pad_maximum_fusion.1.query_ref, bf16[4,1024,128]{2,1,0:T(8,128)(2,1)} %fusion.5.key_ref, bf16[1024,64]{1,0:T(8,128)(2,1)} %slice.65.rope_ref, bf16[4,1024,128]{2,1,0:T(8,128)(2,1)} %fusion.6.value_ref, ...), custom_call_target="tpu_custom_call" | custom-call | flops 335544320 | bytes 1703936 | tf_op jit(solution)/shard_map/pallas_call | solution.py:117
  242.4 4.0 %shard_map.102 = bf16[4,256,128]{2,1,0:T(8,128)(2,1)} custom-call(s32[1]{0:T(128)} %bitcast.48.block_ref, bf16[4,1024,192]{2,1,0:T(8,128)(2,1)} %pad_maximum_fusion.1.query_ref, bf16[4,1024,128]{2,1,0:T(8,128)(2,1)} %fusion.5.key_ref, bf16[1024,64]{1,0:T(8,128)(2,1)} %slice.65.rope_ref, bf16[4,1024,128]{2,1,0:T(8,128)(2,1)} %fusion.6.value_ref, ...), custom_call_target="tpu_custom_call" | custom-call | flops 335544320 | bytes 1703936 | tf_op jit(solution)/shard_map/pallas_call | solution.py:117
  246.6 4.0 %shard_map.101 = bf16[4,256,128]{2,1,0:T(8,128)(2,1)} custom-call(s32[1]{0:T(128)} %bitcast.46.block_ref, bf16[4,1024,192]{2,1,0:T(8,128)(2,1)} %pad_maximum_fusion.1.query_ref, bf16[4,1024,128]{2,1,0:T(8,128)(2,1)} %fusion.5.key_ref, bf16[1024,64]{1,0:T(8,128)(2,1)} %slice.65.rope_ref, bf16[4,1024,128]{2,1,0:T(8,128)(2,1)} %fusion.6.value_ref, ...), custom_call_target="tpu_custom_call" | custom-call | flops 335544320 | bytes 1703936 | tf_op jit(solution)/shard_map/pallas_call | solution.py:117
  251.0 4.0 %shard_map.100 = bf16[4,256,128]{2,1,0:T(8,128)(2,1)} custom-call(s32[1]{0:T(128)} %bitcast.block_ref, bf16[4,1024,192]{2,1,0:T(8,128)(2,1)} %pad_maximum_fusion.1.query_ref, bf16[4,1024,128]{2,1,0:T(8,128)(2,1)} %fusion.5.key_ref, bf16[1024,64]{1,0:T(8,128)(2,1)} %slice.65.rope_ref, bf16[4,1024,128]{2,1,0:T(8,128)(2,1)} %fusion.6.value_ref, ...), custom_call_target="tpu_custom_call" | custom-call | flops 335544320 | bytes 1703936 | tf_op jit(solution)/shard_map/pallas_call | solution.py:117
  255.0 12.1 %collective-permute-done.11 = bf16[4,256,128]{2,1,0:T(8,128)(2,1)S(1)} collective-permute-done((bf16[4,256,128]{2,1,0:T(8,128)(2,1)}, bf16[4,256,128]{2,1,0:T(8,128)(2,1)S(1)}, u32[]{:S(2)}, u32[]{:S(2)}) %collective-permute-start.11) | collective-permute-done | bytes 262176 | tf_op jit(solution)/shard_map/ppermute | solution.py:297
  (114 shorter events, 45.4 us)
Async XLA Ops:
  6.5 79.8 %all-gather.5.cloned.1.call-start = ((), (), s32[]{:S(2)}) async-start(), calls=%async_computation.3 | async-start | bytes 4730880 | tf_op jit(solution)/shard_map/all_gather | solution.py:188
  8.4 13.1 %copy-start.12 = (s32[256]{0:T(256)S(1)}, s32[256]{0:T(256)}, u32[]{:S(2)}) copy-start(s32[256]{0:T(256)} %param.19) | copy-start | bytes 3076
  8.4 24.8 %copy-start.7 = (f32[1792]{0:T(1024)S(1)}, f32[1792]{0:T(1024)}, u32[]{:S(2)}) copy-start(f32[1792]{0:T(1024)} %param.11) | copy-start | bytes 21508
  9.5 213.3 %all-gather.7.cloned.1.call-start = ((), (), s32[]{:S(2)}) async-start(), calls=%async_computation.4 | async-start | bytes 5570560 | tf_op jit(solution)/shard_map/all_gather | solution.py:236
  33.2 183.3 %copy-start.6 = (s32[4,1,256]{2,1,0:T(1,128)}, s32[4,1,256]{2,1,0:T(1,128)S(1)}, u32[]{:S(2)}) copy-start(s32[4,1,256]{2,1,0:T(1,128)S(1)} %all-gather.1) | copy-start | bytes 12292
  86.4 6.9 %collective-permute-start = (bf16[896,2112]{0,1:T(8,128)(2,1)}, bf16[896,2112]{0,1:T(8,128)(2,1)}, u32[]{:S(2)}, u32[]{:S(2)}) collective-permute-start(bf16[896,2112]{0,1:T(8,128)(2,1)} %all-gather.5.cloned.1.call-done), channel_id=1, source_target_pairs={{0,1},{1,0},{2,3},{3,2},{4,5},{5,4},{6,7},{7,6},{8,9},{9,8},{10,11... | collective-permute-start | bytes 11354120 | tf_op jit(solution)/shard_map/ppermute | solution.py:197
  86.4 44.4 %copy-start.10 = (f32[32]{0:T(128)}, f32[32]{0:T(128)S(1)}, u32[]{:S(2)}) copy-start(f32[32]{0:T(128)S(1)} %multiply_power_fusion) | copy-start | bytes 388
  100.2 15.5 %collective-permute-start.3 = (f32[64,2112]{1,0:T(8,128)S(1)}, f32[64,2112]{1,0:T(8,128)S(1)}, u32[]{:S(2)}, u32[]{:S(2)}) collective-permute-start(f32[64,2112]{1,0:T(8,128)S(1)} %get-tuple-element.24), channel_id=1, source_target_pairs={{0,6},{2,0},{4,2},{6,4},{1,7},{3,1},{5,3},{7,5},{8,14},{10,8},{12,... | collective-permute-start | bytes 1622024 | tf_op jit(solution)/shard_map/ppermute | solution.py:209
  102.7 26.3 %collective-permute-start.2 = (f32[64,2112]{1,0:T(8,128)S(1)}, f32[64,2112]{1,0:T(8,128)S(1)}, u32[]{:S(2)}, u32[]{:S(2)}) collective-permute-start(f32[64,2112]{1,0:T(8,128)S(1)} %get-tuple-element.25), channel_id=1, source_target_pairs={{0,4},{2,6},{4,0},{6,2},{1,5},{3,7},{5,1},{7,3},{8,12},{10,14},{12... | collective-permute-start | bytes 1622024 | tf_op jit(solution)/shard_map/ppermute | solution.py:209
  103.2 25.8 %collective-permute-start.1 = (f32[64,2112]{1,0:T(8,128)S(1)}, f32[64,2112]{1,0:T(8,128)S(1)}, u32[]{:S(2)}, u32[]{:S(2)}) collective-permute-start(f32[64,2112]{1,0:T(8,128)S(1)} %get-tuple-element.23), channel_id=1, source_target_pairs={{0,2},{2,4},{4,6},{6,0},{1,3},{3,5},{5,7},{7,1},{8,10},{10,12},{12... | collective-permute-start | bytes 1622024 | tf_op jit(solution)/shard_map/ppermute | solution.py:209
  131.4 8.1 %collective-permute-start.6 = (bf16[64,2112]{1,0:T(8,128)(2,1)S(1)}, bf16[64,2112]{1,0:T(8,128)(2,1)S(1)}, u32[]{:S(2)}, u32[]{:S(2)}) collective-permute-start(bf16[64,2112]{1,0:T(8,128)(2,1)S(1)} %concatenate.23), channel_id=1, source_target_pairs={{0,24},{8,0},{16,8},{24,16},{1,25},{9,1},{17,9},{25,17},{2,26},{10... | collective-permute-start | bytes 811016 | tf_op jit(solution)/shard_map/ppermute | solution.py:229
  132.3 23.0 %collective-permute-start.5 = (bf16[64,2112]{1,0:T(8,128)(2,1)S(1)}, bf16[64,2112]{1,0:T(8,128)(2,1)S(1)}, u32[]{:S(2)}, u32[]{:S(2)}) collective-permute-start(bf16[64,2112]{1,0:T(8,128)(2,1)S(1)} %concatenate.23), channel_id=1, source_target_pairs={{0,16},{8,24},{16,0},{24,8},{1,17},{9,25},{17,1},{25,9},{2,18},{10... | collective-permute-start | bytes 811016 | tf_op jit(solution)/shard_map/ppermute | solution.py:229
  132.5 22.8 %collective-permute-start.4 = (bf16[64,2112]{1,0:T(8,128)(2,1)S(1)}, bf16[64,2112]{1,0:T(8,128)(2,1)S(1)}, u32[]{:S(2)}, u32[]{:S(2)}) collective-permute-start(bf16[64,2112]{1,0:T(8,128)(2,1)S(1)} %concatenate.23), channel_id=1, source_target_pairs={{0,8},{8,16},{16,24},{24,0},{1,9},{9,17},{17,25},{25,1},{2,10},{10... | collective-permute-start | bytes 811016 | tf_op jit(solution)/shard_map/ppermute | solution.py:229
  158.6 13.3 %all-to-all-start.2 = ((bf16[128,4,256]{2,0,1:T(8,128)(2,1)}), bf16[128,4,256]{2,0,1:T(8,128)(2,1)}, u32[]{:S(2)}, u32[]{:S(2)}) async-start(bf16[128,4,256]{2,0,1:T(8,128)(2,1)} %copy.156), calls=%async_computation.2 | async-start | bytes 524288 | tf_op jit(solution)/shard_map/all_to_all | solution.py:251
  166.1 9.3 %copy-start.2 = (bf16[128,2048]{1,0:T(8,128)(2,1)S(1)}, bf16[128,2048]{1,0:T(8,128)(2,1)}, u32[]{:S(2)}) copy-start(bf16[128,2048]{1,0:T(8,128)(2,1)} %param.17) | copy-start | bytes 1572868
  171.9 32.0 %all-to-all-start = ((bf16[384,4,384]{2,0,1:T(8,128)(2,1)}), bf16[384,4,384]{2,0,1:T(8,128)(2,1)S(1)}, u32[]{:S(2)}, u32[]{:S(2)}) async-start(bf16[384,4,384]{2,0,1:T(8,128)(2,1)} %copy.143), calls=%async_computation | async-start | bytes 2359296 | tf_op jit(solution)/shard_map/all_to_all | solution.py:251
  203.9 11.8 %all-to-all-start.1 = ((bf16[128,4,256]{2,0,1:T(8,128)(2,1)}), bf16[128,4,256]{2,0,1:T(8,128)(2,1)S(1)}, u32[]{:S(2)}, u32[]{:S(2)}) async-start(bf16[128,4,256]{2,0,1:T(8,128)(2,1)} %copy.150), calls=%async_computation.1 | async-start | bytes 524288 | tf_op jit(solution)/shard_map/all_to_all | solution.py:251
  207.5 10.1 %copy-start.11 = (f32[32]{0:T(128)S(1)}, f32[32]{0:T(128)}, u32[]{:S(2)}) copy-start(f32[32]{0:T(128)} %copy-done.10) | copy-start | bytes 388
  208.1 14.3 %collective-permute-start.7 = (bf16[1536,384]{0,1:T(8,128)(2,1)S(1)}, bf16[1536,384]{0,1:T(8,128)(2,1)S(1)}, u32[]{:S(2)}, u32[]{:S(2)}) collective-permute-start(bf16[1536,384]{0,1:T(8,128)(2,1)S(1)} %copy.144), channel_id=1, source_target_pairs={{0,1},{1,0},{2,3},{3,2},{4,5},{5,4},{6,7},{7,6},{8,9},{9,8},{10,11... | collective-permute-start | bytes 3538952 | tf_op jit(solution)/shard_map/ppermute | solution.py:256
  210.0 9.5 %collective-permute-start.9 = (bf16[512,256]{0,1:T(8,128)(2,1)}, bf16[512,256]{0,1:T(8,128)(2,1)}, u32[]{:S(2)}, u32[]{:S(2)}) collective-permute-start(bf16[512,256]{0,1:T(8,128)(2,1)} %copy.157), channel_id=1, source_target_pairs={{0,1},{1,0},{2,3},{3,2},{4,5},{5,4},{6,7},{7,6},{8,9},{9,8},{10,11... | collective-permute-start | bytes 786440 | tf_op jit(solution)/shard_map/ppermute | solution.py:256
  216.6 2.9 %collective-permute-start.8 = (bf16[512,256]{0,1:T(8,128)(2,1)}, bf16[512,256]{0,1:T(8,128)(2,1)}, u32[]{:S(2)}, u32[]{:S(2)}) collective-permute-start(bf16[512,256]{0,1:T(8,128)(2,1)} %copy.151), channel_id=1, source_target_pairs={{0,1},{1,0},{2,3},{3,2},{4,5},{5,4},{6,7},{7,6},{8,9},{9,8},{10,11... | collective-permute-start | bytes 786440 | tf_op jit(solution)/shard_map/ppermute | solution.py:256
  240.9 14.1 %collective-permute-start.12 = (bf16[4,256,128]{2,1,0:T(8,128)(2,1)}, bf16[4,256,128]{2,1,0:T(8,128)(2,1)S(1)}, u32[]{:S(2)}, u32[]{:S(2)}) collective-permute-start(bf16[4,256,128]{2,1,0:T(8,128)(2,1)} %shard_map.103), channel_id=1, source_target_pairs={{0,24},{8,0},{16,8},{24,16},{1,25},{9,1},{17,9},{25,17},{2,26},{10... | collective-permute-start | bytes 786440 | tf_op jit(solution)/shard_map/ppermute | solution.py:297
  246.4 20.8 %collective-permute-start.11 = (bf16[4,256,128]{2,1,0:T(8,128)(2,1)}, bf16[4,256,128]{2,1,0:T(8,128)(2,1)S(1)}, u32[]{:S(2)}, u32[]{:S(2)}) collective-permute-start(bf16[4,256,128]{2,1,0:T(8,128)(2,1)} %shard_map.102), channel_id=1, source_target_pairs={{0,16},{8,24},{16,0},{24,8},{1,17},{9,25},{17,1},{25,9},{2,18},{10... | collective-permute-start | bytes 786440 | tf_op jit(solution)/shard_map/ppermute | solution.py:297
  250.6 16.6 %collective-permute-start.10 = (bf16[4,256,128]{2,1,0:T(8,128)(2,1)}, bf16[4,256,128]{2,1,0:T(8,128)(2,1)S(1)}, u32[]{:S(2)}, u32[]{:S(2)}) collective-permute-start(bf16[4,256,128]{2,1,0:T(8,128)(2,1)} %shard_map.101), channel_id=1, source_target_pairs={{0,8},{8,16},{16,24},{24,0},{1,9},{9,17},{17,25},{25,1},{2,10},{10... | collective-permute-start | bytes 786440 | tf_op jit(solution)/shard_map/ppermute | solution.py:297
  (7 other events, 11.4 us)
Sparse Core Ops, SparseCore 0:
  9.6 76.7 all-gather.4
  157.5 54.2 all-gather.6

commit v19 on v18

--- a/solution.py
+++ b/solution.py
@@ -113,7 +113,7 @@
         attention_kernel, block=block, window=window, doc_most=doc_most, scale=score_scale
     )
     flops = 2 * heads * block * window * (NOPE + ROPE + VDIM)
-    step = 2 if heads % 2 == 0 else 1
+    step = heads
     return pl.pallas_call(
         kernel,
         grid_spec=pltpu.PrefetchScalarGridSpec(

time: 279 us -> 279 us (level)
  transfers between devices with their start and end apart: 18 -> 18, of which waited for: 10 -> 10; matrix products, arithmetic and copies ran while one was open for 8% -> 8% of each run, Pallas kernels for 4% -> 5%
where the time goes in v19:
time: 279 us; the launch traced here: 278 us
  waiting for transfers between devices  151 us (54%)
  local copies, waits for them, and re-layouts  24.7 us (9%)
  blocking collectives  23 us (8%)
  starting transfers between devices  20.6 us (7%)
  Pallas kernels  16.8 us (6%)
  matrix products  15.1 us (5%)
  between operations  13.9 us (5%)
  other arithmetic  13.6 us (5%)
    all_gather x1, waiting for transfers between devices, body(): own_all = lax.all_gather(own_rows, 'seq', axis=1, tiled=True)  52.8 us
    all_to_all x3, waiting for transfers between devices, head_columns(): own = lax.all_to_all(own, 'seq', split_axis=1, concat_axis=0, tiled=True)  36.7 us
    ppermute x3, waiting for transfers between devices, body(): lax.ppermute(sent, 'tp', perm=[(i, (i + k) % tp_count) for i in range(tp_...  24.9 us
    ppermute x3, waiting for transfers between devices, body(): lax.ppermute(packed, 'seq', perm=[(i, (i + k) % seq_count) for i in range...  20.8 us
    pallas_call x4, Pallas kernels, block_attention(): pl.pallas_call(kernel, grid_spec=pltpu.PrefetchScalarGridSpec(num_scalar_...  16.8 us
    ppermute x3, waiting for transfers between devices, body(): lax.ppermute(rows, 'seq', perm=[(i, (i + k) % seq_count) for i in range(s...  11.8 us
    all_gather x1, blocking collectives, body(): group_ids = lax.all_gather(segment_ids, 'seq', axis=0, tiled=True)  11.7 us
    psum x1, blocking collectives, body(): square_sums = lax.psum(jnp.sum(inputs * inputs, 1), 'tp')  11.4 us
  transfers between devices with their start and end apart: 18, of which 10 were waited for; matrix products, arithmetic and copies ran while one was open for 8% of the time, Pallas kernels for 5%

profile of v19, /device:TPU:0, one launch (start us, length us, event | category | flops | bytes accessed | tf_op | source)
XLA Modules:
  0.0 278.3 jit_solution(7139287371354162273)
XLA Ops:
  10.2 11.4 %psum.7 = f32[256]{0:T(256)S(1)} all-reduce(f32[256]{0:T(256)S(1)} %fusion.2), channel_id=1, replica_groups=mesh['seq'=4,'tp'=4,'dp'=2] {'tp'}, use_global_device_ids=true, to_apply=%region_1.0 | all-reduce | flops 256 | bytes 2048 | tf_op jit(solution)/shard_map/psum | solution.py:178
  21.6 11.7 %all-gather.1 = s32[4,1,256]{2,1,0:T(1,128)S(1)} all-gather(s32[1,1,256]{2,1,0:T(1,128)S(1)} %bitcast.118), channel_id=1, replica_groups=mesh['seq'=4,'tp'=4,'dp'=2] {'seq'}, dimensions={0}, use_global_device_ids=true | all-gather | bytes 5120 | tf_op jit(solution)/shard_map/all_gather | solution.py:175
  33.5 52.8 %all-gather.5.cloned.1.call-done = bf16[896,2112]{0,1:T(8,128)(2,1)} async-done(((bf16[896,528]{0,1:T(8,128)(2,1)}), bf16[896,2112]{0,1:T(8,128)(2,1)}) %all-gather.5.cloned.1.call-update) | async-done | bytes 3784720 | tf_op jit(solution)/shard_map/all_gather | solution.py:188
  86.4 3.5 %fusion.11 = f32[256,2112]{0,1:T(8,128)S(1)} fusion(bf16[896,2112]{0,1:T(8,128)(2,1)} %all-gather.5.cloned.1.call-done, bf16[256,1792]{1,0:T(8,128)(2,1)S(1)} %fusion.4, s32[]{:T(128)S(6)} %select_n.175), kind=kOutput, calls=%fused_computation.41 | convolution fusion | flops 968884224 | bytes 6406148 | tf_op jit(solution)/shard_map/dot_general | solution.py:190
  89.9 3.4 %collective-permute-done = bf16[896,2112]{0,1:T(8,128)(2,1)} collective-permute-done((bf16[896,2112]{0,1:T(8,128)(2,1)}, bf16[896,2112]{0,1:T(8,128)(2,1)}, u32[]{:S(2)}, u32[]{:S(2)}) %collective-permute-start) | collective-permute-done | bytes 3784736 | tf_op jit(solution)/shard_map/ppermute | solution.py:197
  93.3 4.8 %convolution_add_fusion = f32[256,2112]{0,1:T(8,128)} fusion(f32[256,2112]{0,1:T(8,128)S(1)} %fusion.11, bf16[896,2112]{0,1:T(8,128)(2,1)} %collective-permute-done, bf16[256,1792]{1,0:T(8,128)(2,1)S(1)} %fusion.4, s32[]{:T(128)S(6)} %select_n.176), kind=kOutput, calls=%fused_computation.2 | convolution fusion | flops 969424896 | bytes 8568836 | tf_op jit(solution)/shard_map/dot_general | solution.py:200
  104.1 11.7 %collective-permute-done.3 = f32[64,2112]{1,0:T(8,128)S(1)} collective-permute-done((f32[64,2112]{1,0:T(8,128)S(1)}, f32[64,2112]{1,0:T(8,128)S(1)}, u32[]{:S(2)}, u32[]{:S(2)}) %collective-permute-start.3) | collective-permute-done | bytes 540704 | tf_op jit(solution)/shard_map/ppermute | solution.py:209
  115.8 13.2 %collective-permute-done.2 = f32[64,2112]{1,0:T(8,128)S(1)} collective-permute-done((f32[64,2112]{1,0:T(8,128)S(1)}, f32[64,2112]{1,0:T(8,128)S(1)}, u32[]{:S(2)}, u32[]{:S(2)}) %collective-permute-start.2) | collective-permute-done | bytes 540704 | tf_op jit(solution)/shard_map/ppermute | solution.py:209
  134.5 5.1 %collective-permute-done.6 = bf16[64,2112]{1,0:T(8,128)(2,1)S(1)} collective-permute-done((bf16[64,2112]{1,0:T(8,128)(2,1)S(1)}, bf16[64,2112]{1,0:T(8,128)(2,1)S(1)}, u32[]{:S(2)}, u32[]{:S(2)}) %collective-permute-start.6) | collective-permute-done | bytes 270368 | tf_op jit(solution)/shard_map/ppermute | solution.py:229
  139.5 15.7 %collective-permute-done.5 = bf16[64,2112]{1,0:T(8,128)(2,1)S(1)} collective-permute-done((bf16[64,2112]{1,0:T(8,128)(2,1)S(1)}, bf16[64,2112]{1,0:T(8,128)(2,1)S(1)}, u32[]{:S(2)}, u32[]{:S(2)}) %collective-permute-start.5) | collective-permute-done | bytes 270368 | tf_op jit(solution)/shard_map/ppermute | solution.py:229
  158.6 4.2 %all-to-all-start.2 = ((bf16[128,4,256]{2,0,1:T(8,128)(2,1)}), bf16[128,4,256]{2,0,1:T(8,128)(2,1)}, u32[]{:S(2)}, u32[]{:S(2)}) async-start(bf16[128,4,256]{2,0,1:T(8,128)(2,1)} %copy.156), calls=%async_computation.2 | async-start | bytes 524288 | tf_op jit(solution)/shard_map/all_to_all | solution.py:251
  162.8 3.2 %copy.142 = bf16[384,3072]{0,1:T(8,128)(2,1)S(1)} copy(bf16[384,3072]{1,0:T(8,128)(2,1)} %param.16) | data formatting | bytes 4718592 | tf_op jit(solution)/shard_map/optimization_barrier | solution.py:233
  167.6 4.2 %all-to-all-done.2 = bf16[128,4,256]{2,0,1:T(8,128)(2,1)} async-done(((bf16[128,4,256]{2,0,1:T(8,128)(2,1)}), bf16[128,4,256]{2,0,1:T(8,128)(2,1)}, u32[]{:S(2)}, u32[]{:S(2)}) %all-to-all-start.2) | async-done | bytes 262176 | tf_op jit(solution)/shard_map/all_to_all | solution.py:251
  171.9 3.5 %all-to-all-start = ((bf16[384,4,384]{2,0,1:T(8,128)(2,1)}), bf16[384,4,384]{2,0,1:T(8,128)(2,1)S(1)}, u32[]{:S(2)}, u32[]{:S(2)}) async-start(bf16[384,4,384]{2,0,1:T(8,128)(2,1)} %copy.143), calls=%async_computation | async-start | bytes 2359296 | tf_op jit(solution)/shard_map/all_to_all | solution.py:251
  176.6 27.3 %all-to-all-done = bf16[384,4,384]{2,0,1:T(8,128)(2,1)S(1)} async-done(((bf16[384,4,384]{2,0,1:T(8,128)(2,1)}), bf16[384,4,384]{2,0,1:T(8,128)(2,1)S(1)}, u32[]{:S(2)}, u32[]{:S(2)}) %all-to-all-start) | async-done | bytes 1179680 | tf_op jit(solution)/shard_map/all_to_all | solution.py:251
  203.9 3.6 %all-to-all-start.1 = ((bf16[128,4,256]{2,0,1:T(8,128)(2,1)}), bf16[128,4,256]{2,0,1:T(8,128)(2,1)S(1)}, u32[]{:S(2)}, u32[]{:S(2)}) async-start(bf16[128,4,256]{2,0,1:T(8,128)(2,1)} %copy.150), calls=%async_computation.1 | async-start | bytes 524288 | tf_op jit(solution)/shard_map/all_to_all | solution.py:251
  210.5 5.2 %all-to-all-done.1 = bf16[128,4,256]{2,0,1:T(8,128)(2,1)S(1)} async-done(((bf16[128,4,256]{2,0,1:T(8,128)(2,1)}), bf16[128,4,256]{2,0,1:T(8,128)(2,1)S(1)}, u32[]{:S(2)}, u32[]{:S(2)}) %all-to-all-start.1) | async-done | bytes 262176 | tf_op jit(solution)/shard_map/all_to_all | solution.py:251
  222.8 2.6 copy.147
  226.2 3.4 %fusion.1 = f32[4,1024,192]{2,1,0:T(8,128)S(1)} fusion(bf16[1536,4,192]{0,2,1:T(8,128)(2,1)S(1)} %bitcast.95, bf16[1024,2112]{1,0:T(8,128)(2,1)S(1)} %bitcast.86), kind=kOutput, calls=%fused_computation.8 | convolution fusion | flops 2415919104 | bytes 8650752 | tf_op jit(solution)/shard_map/td,dhe->hte/dot_general | solution.py:272
  236.9 4.2 %shard_map.103 = bf16[4,256,128]{2,1,0:T(8,128)(2,1)} custom-call(s32[1]{0:T(128)} %bitcast.50.block_ref, bf16[4,1024,192]{2,1,0:T(8,128)(2,1)} %pad_maximum_fusion.1.query_ref, bf16[4,1024,128]{2,1,0:T(8,128)(2,1)} %fusion.5.key_ref, bf16[1024,64]{1,0:T(8,128)(2,1)} %slice.65.rope_ref, bf16[4,1024,128]{2,1,0:T(8,128)(2,1)} %fusion.6.value_ref, ...), custom_call_target="tpu_custom_call" | custom-call | flops 335544320 | bytes 1703936 | tf_op jit(solution)/shard_map/pallas_call | solution.py:117
  242.6 4.2 %shard_map.102 = bf16[4,256,128]{2,1,0:T(8,128)(2,1)} custom-call(s32[1]{0:T(128)} %bitcast.48.block_ref, bf16[4,1024,192]{2,1,0:T(8,128)(2,1)} %pad_maximum_fusion.1.query_ref, bf16[4,1024,128]{2,1,0:T(8,128)(2,1)} %fusion.5.key_ref, bf16[1024,64]{1,0:T(8,128)(2,1)} %slice.65.rope_ref, bf16[4,1024,128]{2,1,0:T(8,128)(2,1)} %fusion.6.value_ref, ...), custom_call_target="tpu_custom_call" | custom-call | flops 335544320 | bytes 1703936 | tf_op jit(solution)/shard_map/pallas_call | solution.py:117
  246.9 4.2 %shard_map.101 = bf16[4,256,128]{2,1,0:T(8,128)(2,1)} custom-call(s32[1]{0:T(128)} %bitcast.46.block_ref, bf16[4,1024,192]{2,1,0:T(8,128)(2,1)} %pad_maximum_fusion.1.query_ref, bf16[4,1024,128]{2,1,0:T(8,128)(2,1)} %fusion.5.key_ref, bf16[1024,64]{1,0:T(8,128)(2,1)} %slice.65.rope_ref, bf16[4,1024,128]{2,1,0:T(8,128)(2,1)} %fusion.6.value_ref, ...), custom_call_target="tpu_custom_call" | custom-call | flops 335544320 | bytes 1703936 | tf_op jit(solution)/shard_map/pallas_call | solution.py:117
  251.5 4.2 %shard_map.100 = bf16[4,256,128]{2,1,0:T(8,128)(2,1)} custom-call(s32[1]{0:T(128)} %bitcast.block_ref, bf16[4,1024,192]{2,1,0:T(8,128)(2,1)} %pad_maximum_fusion.1.query_ref, bf16[4,1024,128]{2,1,0:T(8,128)(2,1)} %fusion.5.key_ref, bf16[1024,64]{1,0:T(8,128)(2,1)} %slice.65.rope_ref, bf16[4,1024,128]{2,1,0:T(8,128)(2,1)} %fusion.6.value_ref, ...), custom_call_target="tpu_custom_call" | custom-call | flops 335544320 | bytes 1703936 | tf_op jit(solution)/shard_map/pallas_call | solution.py:117
  255.7 11.8 %collective-permute-done.11 = bf16[4,256,128]{2,1,0:T(8,128)(2,1)S(1)} collective-permute-done((bf16[4,256,128]{2,1,0:T(8,128)(2,1)}, bf16[4,256,128]{2,1,0:T(8,128)(2,1)S(1)}, u32[]{:S(2)}, u32[]{:S(2)}) %collective-permute-start.11) | collective-permute-done | bytes 262176 | tf_op jit(solution)/shard_map/ppermute | solution.py:297
  (114 shorter events, 45.3 us)
Async XLA Ops:
  6.5 79.8 %all-gather.5.cloned.1.call-start = ((), (), s32[]{:S(2)}) async-start(), calls=%async_computation.3 | async-start | bytes 4730880 | tf_op jit(solution)/shard_map/all_gather | solution.py:188
  8.4 13.1 %copy-start.12 = (s32[256]{0:T(256)S(1)}, s32[256]{0:T(256)}, u32[]{:S(2)}) copy-start(s32[256]{0:T(256)} %param.19) | copy-start | bytes 3076
  8.4 24.8 %copy-start.7 = (f32[1792]{0:T(1024)S(1)}, f32[1792]{0:T(1024)}, u32[]{:S(2)}) copy-start(f32[1792]{0:T(1024)} %param.11) | copy-start | bytes 21508
  9.5 213.3 %all-gather.7.cloned.1.call-start = ((), (), s32[]{:S(2)}) async-start(), calls=%async_computation.4 | async-start | bytes 5570560 | tf_op jit(solution)/shard_map/all_gather | solution.py:236
  33.2 183.3 %copy-start.6 = (s32[4,1,256]{2,1,0:T(1,128)}, s32[4,1,256]{2,1,0:T(1,128)S(1)}, u32[]{:S(2)}) copy-start(s32[4,1,256]{2,1,0:T(1,128)S(1)} %all-gather.1) | copy-start | bytes 12292
  86.4 6.9 %collective-permute-start = (bf16[896,2112]{0,1:T(8,128)(2,1)}, bf16[896,2112]{0,1:T(8,128)(2,1)}, u32[]{:S(2)}, u32[]{:S(2)}) collective-permute-start(bf16[896,2112]{0,1:T(8,128)(2,1)} %all-gather.5.cloned.1.call-done), channel_id=1, source_target_pairs={{0,1},{1,0},{2,3},{3,2},{4,5},{5,4},{6,7},{7,6},{8,9},{9,8},{10,11... | collective-permute-start | bytes 11354120 | tf_op jit(solution)/shard_map/ppermute | solution.py:197
  86.4 44.4 %copy-start.10 = (f32[32]{0:T(128)}, f32[32]{0:T(128)S(1)}, u32[]{:S(2)}) copy-start(f32[32]{0:T(128)S(1)} %multiply_power_fusion) | copy-start | bytes 388
  100.2 15.5 %collective-permute-start.3 = (f32[64,2112]{1,0:T(8,128)S(1)}, f32[64,2112]{1,0:T(8,128)S(1)}, u32[]{:S(2)}, u32[]{:S(2)}) collective-permute-start(f32[64,2112]{1,0:T(8,128)S(1)} %get-tuple-element.24), channel_id=1, source_target_pairs={{0,6},{2,0},{4,2},{6,4},{1,7},{3,1},{5,3},{7,5},{8,14},{10,8},{12,... | collective-permute-start | bytes 1622024 | tf_op jit(solution)/shard_map/ppermute | solution.py:209
  102.7 26.3 %collective-permute-start.2 = (f32[64,2112]{1,0:T(8,128)S(1)}, f32[64,2112]{1,0:T(8,128)S(1)}, u32[]{:S(2)}, u32[]{:S(2)}) collective-permute-start(f32[64,2112]{1,0:T(8,128)S(1)} %get-tuple-element.25), channel_id=1, source_target_pairs={{0,4},{2,6},{4,0},{6,2},{1,5},{3,7},{5,1},{7,3},{8,12},{10,14},{12... | collective-permute-start | bytes 1622024 | tf_op jit(solution)/shard_map/ppermute | solution.py:209
  103.2 25.8 %collective-permute-start.1 = (f32[64,2112]{1,0:T(8,128)S(1)}, f32[64,2112]{1,0:T(8,128)S(1)}, u32[]{:S(2)}, u32[]{:S(2)}) collective-permute-start(f32[64,2112]{1,0:T(8,128)S(1)} %get-tuple-element.23), channel_id=1, source_target_pairs={{0,2},{2,4},{4,6},{6,0},{1,3},{3,5},{5,7},{7,1},{8,10},{10,12},{12... | collective-permute-start | bytes 1622024 | tf_op jit(solution)/shard_map/ppermute | solution.py:209
  131.4 8.1 %collective-permute-start.6 = (bf16[64,2112]{1,0:T(8,128)(2,1)S(1)}, bf16[64,2112]{1,0:T(8,128)(2,1)S(1)}, u32[]{:S(2)}, u32[]{:S(2)}) collective-permute-start(bf16[64,2112]{1,0:T(8,128)(2,1)S(1)} %concatenate.23), channel_id=1, source_target_pairs={{0,24},{8,0},{16,8},{24,16},{1,25},{9,1},{17,9},{25,17},{2,26},{10... | collective-permute-start | bytes 811016 | tf_op jit(solution)/shard_map/ppermute | solution.py:229
  132.3 23.0 %collective-permute-start.5 = (bf16[64,2112]{1,0:T(8,128)(2,1)S(1)}, bf16[64,2112]{1,0:T(8,128)(2,1)S(1)}, u32[]{:S(2)}, u32[]{:S(2)}) collective-permute-start(bf16[64,2112]{1,0:T(8,128)(2,1)S(1)} %concatenate.23), channel_id=1, source_target_pairs={{0,16},{8,24},{16,0},{24,8},{1,17},{9,25},{17,1},{25,9},{2,18},{10... | collective-permute-start | bytes 811016 | tf_op jit(solution)/shard_map/ppermute | solution.py:229
  132.5 22.8 %collective-permute-start.4 = (bf16[64,2112]{1,0:T(8,128)(2,1)S(1)}, bf16[64,2112]{1,0:T(8,128)(2,1)S(1)}, u32[]{:S(2)}, u32[]{:S(2)}) collective-permute-start(bf16[64,2112]{1,0:T(8,128)(2,1)S(1)} %concatenate.23), channel_id=1, source_target_pairs={{0,8},{8,16},{16,24},{24,0},{1,9},{9,17},{17,25},{25,1},{2,10},{10... | collective-permute-start | bytes 811016 | tf_op jit(solution)/shard_map/ppermute | solution.py:229
  158.6 13.3 %all-to-all-start.2 = ((bf16[128,4,256]{2,0,1:T(8,128)(2,1)}), bf16[128,4,256]{2,0,1:T(8,128)(2,1)}, u32[]{:S(2)}, u32[]{:S(2)}) async-start(bf16[128,4,256]{2,0,1:T(8,128)(2,1)} %copy.156), calls=%async_computation.2 | async-start | bytes 524288 | tf_op jit(solution)/shard_map/all_to_all | solution.py:251
  166.1 9.3 %copy-start.2 = (bf16[128,2048]{1,0:T(8,128)(2,1)S(1)}, bf16[128,2048]{1,0:T(8,128)(2,1)}, u32[]{:S(2)}) copy-start(bf16[128,2048]{1,0:T(8,128)(2,1)} %param.17) | copy-start | bytes 1572868
  171.9 32.0 %all-to-all-start = ((bf16[384,4,384]{2,0,1:T(8,128)(2,1)}), bf16[384,4,384]{2,0,1:T(8,128)(2,1)S(1)}, u32[]{:S(2)}, u32[]{:S(2)}) async-start(bf16[384,4,384]{2,0,1:T(8,128)(2,1)} %copy.143), calls=%async_computation | async-start | bytes 2359296 | tf_op jit(solution)/shard_map/all_to_all | solution.py:251
  203.9 11.8 %all-to-all-start.1 = ((bf16[128,4,256]{2,0,1:T(8,128)(2,1)}), bf16[128,4,256]{2,0,1:T(8,128)(2,1)S(1)}, u32[]{:S(2)}, u32[]{:S(2)}) async-start(bf16[128,4,256]{2,0,1:T(8,128)(2,1)} %copy.150), calls=%async_computation.1 | async-start | bytes 524288 | tf_op jit(solution)/shard_map/all_to_all | solution.py:251
  207.5 10.1 %copy-start.11 = (f32[32]{0:T(128)S(1)}, f32[32]{0:T(128)}, u32[]{:S(2)}) copy-start(f32[32]{0:T(128)} %copy-done.10) | copy-start | bytes 388
  208.1 14.3 %collective-permute-start.7 = (bf16[1536,384]{0,1:T(8,128)(2,1)S(1)}, bf16[1536,384]{0,1:T(8,128)(2,1)S(1)}, u32[]{:S(2)}, u32[]{:S(2)}) collective-permute-start(bf16[1536,384]{0,1:T(8,128)(2,1)S(1)} %copy.144), channel_id=1, source_target_pairs={{0,1},{1,0},{2,3},{3,2},{4,5},{5,4},{6,7},{7,6},{8,9},{9,8},{10,11... | collective-permute-start | bytes 3538952 | tf_op jit(solution)/shard_map/ppermute | solution.py:256
  210.0 9.5 %collective-permute-start.9 = (bf16[512,256]{0,1:T(8,128)(2,1)}, bf16[512,256]{0,1:T(8,128)(2,1)}, u32[]{:S(2)}, u32[]{:S(2)}) collective-permute-start(bf16[512,256]{0,1:T(8,128)(2,1)} %copy.157), channel_id=1, source_target_pairs={{0,1},{1,0},{2,3},{3,2},{4,5},{5,4},{6,7},{7,6},{8,9},{9,8},{10,11... | collective-permute-start | bytes 786440 | tf_op jit(solution)/shard_map/ppermute | solution.py:256
  216.6 2.9 %collective-permute-start.8 = (bf16[512,256]{0,1:T(8,128)(2,1)}, bf16[512,256]{0,1:T(8,128)(2,1)}, u32[]{:S(2)}, u32[]{:S(2)}) collective-permute-start(bf16[512,256]{0,1:T(8,128)(2,1)} %copy.151), channel_id=1, source_target_pairs={{0,1},{1,0},{2,3},{3,2},{4,5},{5,4},{6,7},{7,6},{8,9},{9,8},{10,11... | collective-permute-start | bytes 786440 | tf_op jit(solution)/shard_map/ppermute | solution.py:256
  241.1 14.6 %collective-permute-start.12 = (bf16[4,256,128]{2,1,0:T(8,128)(2,1)}, bf16[4,256,128]{2,1,0:T(8,128)(2,1)S(1)}, u32[]{:S(2)}, u32[]{:S(2)}) collective-permute-start(bf16[4,256,128]{2,1,0:T(8,128)(2,1)} %shard_map.103), channel_id=1, source_target_pairs={{0,24},{8,0},{16,8},{24,16},{1,25},{9,1},{17,9},{25,17},{2,26},{10... | collective-permute-start | bytes 786440 | tf_op jit(solution)/shard_map/ppermute | solution.py:297
  246.7 20.8 %collective-permute-start.11 = (bf16[4,256,128]{2,1,0:T(8,128)(2,1)}, bf16[4,256,128]{2,1,0:T(8,128)(2,1)S(1)}, u32[]{:S(2)}, u32[]{:S(2)}) collective-permute-start(bf16[4,256,128]{2,1,0:T(8,128)(2,1)} %shard_map.102), channel_id=1, source_target_pairs={{0,16},{8,24},{16,0},{24,8},{1,17},{9,25},{17,1},{25,9},{2,18},{10... | collective-permute-start | bytes 786440 | tf_op jit(solution)/shard_map/ppermute | solution.py:297
  251.1 16.4 %collective-permute-start.10 = (bf16[4,256,128]{2,1,0:T(8,128)(2,1)}, bf16[4,256,128]{2,1,0:T(8,128)(2,1)S(1)}, u32[]{:S(2)}, u32[]{:S(2)}) collective-permute-start(bf16[4,256,128]{2,1,0:T(8,128)(2,1)} %shard_map.101), channel_id=1, source_target_pairs={{0,8},{8,16},{16,24},{24,0},{1,9},{9,17},{17,25},{25,1},{2,10},{10... | collective-permute-start | bytes 786440 | tf_op jit(solution)/shard_map/ppermute | solution.py:297
  (7 other events, 11.4 us)
Sparse Core Ops, SparseCore 0:
  9.6 76.7 all-gather.4
  157.5 54.2 all-gather.6
